TPU v7x, 32 devices: a whole 2x2x4 slice. The times are simulated.
32 devices in a mesh: groups: 2 (over x), row: 16 (over z, y, core).
Axes of the slice: x: 2, y: 2, z: 4, core: 2. Of those that a mesh axis runs over, the one named last changes fastest.
Arguments:
- atom_feat: bfloat16 [4096, 2, 128], P(('groups', 'row')), parts along dimension 0, may hold values from -6 to 6
- window_shift: int32 [128], P(('groups', 'row')), parts along dimension 0, may hold values from -16 to 16, as said below
- atom_token: int32 [4096], P('groups'), parts along dimension 0, may hold values from 0 to 255, as said below
- token_in: bfloat16 [512, 2, 768], P(('groups', 'row')), parts along dimension 0, may hold values from -6 to 6
- pair: bfloat16 [512, 256, 128], P(('groups', 'row')), parts along dimension 0, may hold values from -6 to 6
- key_mask: int32 [512], P('groups'), parts along dimension 0, may hold values from 0 to 1, as said below
- w_atom_query: bfloat16 [128, 128], replicated, may hold values from -2 to 2
- w_atom_key: bfloat16 [128, 128], replicated, may hold values from -2 to 2
- w_atom_value: bfloat16 [128, 128], replicated, may hold values from -0.5 to 0.5
- w_atom_out: bfloat16 [128, 128], replicated, may hold values from -0.5 to 0.5
- w_to_token: bfloat16 [128, 768], replicated, may hold values from -0.5 to 0.5
- w_query: bfloat16 [768, 768], replicated, may hold values from -0.21875 to 0.21875
- w_key: bfloat16 [768, 768], replicated, may hold values from -0.21875 to 0.21875
- w_value: bfloat16 [768, 768], replicated, may hold values from -0.21875 to 0.21875
- w_out: bfloat16 [768, 768], replicated, may hold values from -0.21875 to 0.21875
- w_bias: bfloat16 [128, 16], replicated, may hold values from -4 to 4
Outputs:
- atom_out: bfloat16 [4096, 2, 128], P(('groups', 'row')), parts along dimension 0
- token_out: bfloat16 [512, 2, 768], P(('groups', 'row')), parts along dimension 0
There are 2 independent parts, one for each index of `groups`. A program takes and returns all parts, laid end to end along the dimension named above; an argument that names none is the same for every part. Nothing has to cross between parts.
Inputs may be any that keep to these rules, and one draw needn't show every extreme that they name: `window_shift`: one entry per query block, moving its key window. `atom_token`: never falls along the atoms; token 0 starts at atom 0 and token t's first atom is 8 t + r with r from -3 to 3, and with r from 1 to 3 where t is a positive multiple of 16. `key_mask`: token 0 is always kept.
All inputs are finite; a program needn't handle non-finite values.
Results may differ from a plain program's by a relative error of at most 0.0095.
Values may be sent and summed in bfloat16 or wider, within the bound.
No kernel may reach another device: no remote copies, remote signals or barrier semaphores. Data moves between devices by JAX's collectives and lax.ppermute only.
A program may use at most 64 MiB of HBM per device.

v0:
```python
import jax
import jax.numpy as jnp
from jax import lax
from jax.sharding import PartitionSpec as P

ATOM_HEADS = 4
QBLOCK = 32
KWIN = 128
SHIFT = 16
TOKEN_HEADS = 16


def extended(block, sides, width):
    for axis, dim in sides:
        count = lax.axis_size(axis)
        forward = [(i, i + 1) for i in range(count - 1)]
        backward = [(target, source) for source, target in forward]
        low = lax.ppermute(
            lax.slice_in_dim(block, block.shape[dim] - width, None, axis=dim), axis, forward
        )
        high = lax.ppermute(lax.slice_in_dim(block, 0, width, axis=dim), axis, backward)
        block = jnp.concatenate([low, block, high], axis=dim)
    return block


def from_behind(block, axis, distance):
    devices = range(lax.axis_size(axis))
    route = [(i - distance, i) for i in devices if i - distance in devices]
    return lax.ppermute(block, axis, route)


def layer_norm(values):
    values = values.astype(jnp.float32)
    mean = jnp.mean(values, axis=-1, keepdims=True)
    var = jnp.mean((values - mean) ** 2, axis=-1, keepdims=True)
    return (values - mean) / jnp.sqrt(var + 1e-05)


def project(values, weight):
    return jnp.einsum("asc,cd->asd", values, weight, preferred_element_type=jnp.float32)


def on_device(
    atom_feat,
    window_shift,
    atom_token,
    token_in,
    pair,
    key_mask,
    w_atom_query,
    w_atom_key,
    w_atom_value,
    w_atom_out,
    w_to_token,
    w_query,
    w_key,
    w_value,
    w_out,
    w_bias,
):
    high = lax.Precision.HIGHEST
    atom_dev, samples, width = atom_feat.shape
    tok_dev = token_in.shape[0]
    tok_width = token_in.shape[2]
    devices = lax.axis_size("row")
    rank = lax.axis_index("row")
    atom_base = rank * atom_dev
    total_atoms = atom_dev * devices
    normed = layer_norm(atom_feat).astype(jnp.bfloat16)
    query = project(normed, w_atom_query).astype(jnp.bfloat16)
    margin = (KWIN - QBLOCK) // 2
    border = margin + SHIFT
    keyed = project(normed, w_atom_key).astype(jnp.bfloat16)
    valued = project(normed, w_atom_value).astype(jnp.bfloat16)
    stacked = extended(jnp.stack([keyed, valued], 0), (("row", 1),), border)
    key_pad = stacked[0]
    value_pad = stacked[1]
    blocks = atom_dev // QBLOCK
    starts = jnp.arange(blocks, dtype=jnp.int32) * QBLOCK - margin + window_shift
    places = starts[:, None] + jnp.arange(KWIN, dtype=jnp.int32)[None, :]
    absolute = places + atom_base
    valid = (absolute >= 0) & (absolute < total_atoms)
    window_k = jnp.take(key_pad, places + border, axis=0)
    window_v = jnp.take(value_pad, places + border, axis=0)
    head_dim = width // ATOM_HEADS
    qblock = query.reshape(blocks, QBLOCK, samples, ATOM_HEADS, head_dim)
    kblock = window_k.reshape(blocks, KWIN, samples, ATOM_HEADS, head_dim)
    vblock = window_v.reshape(blocks, KWIN, samples, ATOM_HEADS, head_dim)
    scores = jnp.einsum(
        "bqshd,bkshd->bshqk", qblock, kblock, preferred_element_type=jnp.float32
    ) / jnp.sqrt(jnp.float32(head_dim))
    keep = valid[:, None, None, None, :]
    scores = jnp.where(keep, scores, -1e30)
    top = jnp.max(scores, axis=-1, keepdims=True)
    expo = jnp.where(keep, jnp.exp(scores - top), 0.0)
    total = jnp.sum(expo, axis=-1)
    mixed = jnp.einsum(
        "bshqk,bkshd->bqshd", expo.astype(jnp.bfloat16), vblock, preferred_element_type=jnp.float32
    )
    mixed = mixed / jnp.transpose(total, (0, 3, 1, 2))[..., None]
    mixed = mixed.astype(jnp.bfloat16).reshape(atom_dev, samples, width)
    atom_out = (atom_feat.astype(jnp.float32) + project(mixed, w_atom_out)).astype(jnp.bfloat16)
    own_ids = rank * tok_dev + jnp.arange(tok_dev, dtype=jnp.int32)
    counts = jnp.sum((atom_token[None, :] == own_ids[:, None]).astype(jnp.float32), axis=1)
    local_ids = lax.dynamic_slice_in_dim(atom_token, atom_base, atom_dev)
    edge_rows = 8
    passed_atoms = from_behind(atom_out[:edge_rows], "row", -1)
    next_ids = lax.dynamic_slice_in_dim(atom_token, atom_base + atom_dev, edge_rows)
    rows = jnp.concatenate([atom_out, passed_atoms], axis=0)
    row_ids = jnp.concatenate([local_ids, next_ids], axis=0)
    hidden = jax.nn.relu(project(rows, w_to_token))
    onehot = (own_ids[:, None] == row_ids[None, :]).astype(jnp.float32)
    sums = jnp.einsum("ta,asd->tsd", onehot, hidden, precision=high)
    state = (token_in.astype(jnp.float32) + sums / counts[:, None, None]).astype(jnp.bfloat16)
    tnorm = layer_norm(state).astype(jnp.bfloat16)
    tdim = tok_width // TOKEN_HEADS
    tq = project(tnorm, w_query).astype(jnp.bfloat16).reshape(tok_dev, samples, TOKEN_HEADS, tdim)
    tk = project(tnorm, w_key).astype(jnp.bfloat16)
    tv = project(tnorm, w_value).astype(jnp.bfloat16)
    scale = 1.0 / jnp.sqrt(jnp.float32(tdim))
    running = jnp.full((samples, TOKEN_HEADS, tok_dev), -1e30, jnp.float32)
    kpiece = lax.all_gather(tk, "row", axis=0, tiled=True)
    vpiece = lax.all_gather(tv, "row", axis=0, tiled=True)
    count = kpiece.shape[0]
    kheads = kpiece.reshape(count, samples, TOKEN_HEADS, tdim)
    vheads = vpiece.reshape(count, samples, TOKEN_HEADS, tdim)
    bias = jnp.einsum("qkc,ch->hqk", pair, w_bias, preferred_element_type=jnp.float32)
    flags = (key_mask > 0)[None, None, None, :]
    score = (
        jnp.einsum("qshd,kshd->shqk", tq, kheads, preferred_element_type=jnp.float32) * scale
        + bias[None]
    )
    score = jnp.where(flags, score, -1e30)
    fresh = jnp.maximum(running, jnp.max(score, axis=-1))
    expo_t = jnp.where(flags, jnp.exp(score - fresh[..., None]), 0.0)
    denom = jnp.sum(expo_t, axis=-1)
    accum = jnp.einsum(
        "shqk,kshd->shqd", expo_t.astype(jnp.bfloat16), vheads, preferred_element_type=jnp.float32
    )
    running, denom, accum = (fresh, denom, accum)
    tmix = (accum / denom[..., None]).astype(jnp.bfloat16)
    tmix = jnp.transpose(tmix, (2, 0, 1, 3)).reshape(tok_dev, samples, tok_width)
    token_out = (state.astype(jnp.float32) + project(tmix, w_out)).astype(jnp.bfloat16)
    return (atom_out, token_out)


def solution(mesh):
    return jax.shard_map(
        on_device,
        mesh=mesh,
        in_specs=(
            P(("groups", "row"), None, None),
            P(("groups", "row")),
            P("groups"),
            P(("groups", "row"), None, None),
            P(("groups", "row"), None, None),
            P("groups"),
            P(),
            P(),
            P(),
            P(),
            P(),
            P(),
            P(),
            P(),
            P(),
            P(),
        ),
        out_specs=(P(("groups", "row"), None, None), P(("groups", "row"), None, None)),
        check_vma=False,
    )
```

profile of v0, /device:TPU:0, one launch (start us, length us, event | category | flops | bytes accessed | tf_op | source)
XLA Modules:
  0.0 78.8 jit_solution(695110558038212447)
XLA Ops:
  0.6 0.0 copy-start
  0.6 0.0 copy-start.5
  0.7 1.0 %convert_reduce_fusion = f32[128,2]{0,1:T(2,128)S(1)} fusion(bf16[128,2,128]{2,1,0:T(2,128)(2,1)} %param.18), kind=kLoop, calls=%fused_computation.55 | loop fusion | flops 65280 | bytes 66560 | tf_op jit(solution)/shard_map/reduce_sum | solution.py:34
  1.7 1.0 %fusion.51 = f32[128,2]{0,1:T(2,128)S(1)} fusion(f32[128,2]{0,1:T(2,128)S(1)} %broadcast_multiply_fusion.1, bf16[128,2,128]{2,1,0:T(2,128)(2,1)} %param.18), kind=kLoop, calls=%fused_computation.58 | loop fusion | flops 130816 | bytes 67584 | tf_op jit(solution)/shard_map/reduce_sum | solution.py:35
  2.8 0.0 copy-start.9
  2.8 0.0 copy-start.12
  2.8 0.0 copy-start.4
  2.8 0.0 copy-start.10
  2.8 1.2 %fusion.39 = bf16[1,128,2,128]{3,1,2,0:T(8,128)(2,1)S(1)} fusion(bf16[128,128]{1,0:T(8,128)(2,1)} %param.26, f32[128,2]{0,1:T(2,128)S(1)} %add_sqrt_fusion.1, f32[128,2]{0,1:T(2,128)S(1)} %broadcast_multiply_fusion.1, bf16[128,2,128]{2,1,0:T(2,128)(2,1)} %param.18), kind=kOutput, calls=%fused_computation.41 | convolution fusion | flops 8552448 | bytes 165888 | tf_op jit(solution)/shard_map/asc,cd->asd/dot_general | solution.py:40
  4.0 1.1 %fusion.38 = bf16[1,128,2,128]{3,1,2,0:T(8,128)(2,1)S(1)} fusion(bf16[128,128]{1,0:T(8,128)(2,1)} %param.25, f32[128,2]{0,1:T(2,128)S(1)} %add_sqrt_fusion.1, f32[128,2]{0,1:T(2,128)S(1)} %broadcast_multiply_fusion.1, bf16[128,2,128]{2,1,0:T(2,128)(2,1)} %param.18), kind=kOutput, calls=%fused_computation.40 | convolution fusion | flops 8552448 | bytes 165888 | tf_op jit(solution)/shard_map/asc,cd->asd/dot_general | solution.py:40
  5.1 2.4 %collective-permute-start = (bf16[2,64,2,128]{3,1,2,0:T(8,128)(2,1)S(1)}, bf16[2,64,2,128]{3,1,2,0:T(8,128)(2,1)S(1)}, u32[]{:S(2)}, u32[]{:S(2)}) collective-permute-start(bf16[2,64,2,128]{3,1,2,0:T(8,128)(2,1)S(1)} %get-tuple-element.11), channel_id=1, source_target_pairs={{0,1},{1,2},{2,3},{3,4},{4,5},{5,6},{6,7},{7,8},{8,9},{9,10},{10,1... | collective-permute-start | bytes 196616 | tf_op jit(solution)/shard_map/ppermute | solution.py:18
  7.5 1.3 %collective-permute-start.1 = (bf16[2,64,2,128]{3,1,2,0:T(8,128)(2,1)S(1)}, bf16[2,64,2,128]{3,1,2,0:T(8,128)(2,1)S(1)}, u32[]{:S(2)}, u32[]{:S(2)}) collective-permute-start(bf16[2,64,2,128]{3,1,2,0:T(8,128)(2,1)S(1)} %get-tuple-element.12), channel_id=1, source_target_pairs={{1,0},{2,1},{3,2},{4,3},{5,4},{6,5},{7,6},{8,7},{9,8},{10,9},{11,1... | collective-permute-start | bytes 196616 | tf_op jit(solution)/shard_map/ppermute | solution.py:21
  8.8 0.1 fusion.72
  8.9 0.1 fusion.71
  9.0 0.0 copy-done.5
  9.0 0.2 convolution_convert_fusion
  9.2 0.2 reshape.93
  9.4 0.1 dynamic_slice.7
  9.5 0.1 dynamic_slice.6
  9.6 0.2 convert_reduce_fusion.1
  9.8 0.4 fusion.66
  10.2 0.0 collective-permute-done
  10.2 2.6 %collective-permute-done.1 = bf16[2,64,2,128]{3,1,2,0:T(8,128)(2,1)S(1)} collective-permute-done((bf16[2,64,2,128]{3,1,2,0:T(8,128)(2,1)S(1)}, bf16[2,64,2,128]{3,1,2,0:T(8,128)(2,1)S(1)}, u32[]{:S(2)}, u32[]{:S(2)}) %collective-permute-start.1) | collective-permute-done | bytes 65568 | tf_op jit(solution)/shard_map/ppermute | solution.py:21
  12.8 0.1 copy.47
  13.0 0.1 copy.45
  13.1 2.1 %gather_fusion.1 = bf16[512,2,128]{2,1,0:T(2,128)(2,1)S(1)} fusion(bf16[256,2,128]{2,1,0:T(2,128)(2,1)S(1)} %copy.47, s32[1024]{0:T(1024)S(1)} %pad_clamp_fusion), kind=kCustom, calls=%fused_computation.1.clone | custom fusion | bytes 526336 | tf_op jit(solution)/shard_map/jit(_take)/gather | solution.py:83
  15.2 2.1 %gather_fusion = bf16[512,2,128]{2,1,0:T(2,128)(2,1)S(1)} fusion(bf16[256,2,128]{2,1,0:T(2,128)(2,1)S(1)} %copy.45, s32[1024]{0:T(1024)S(1)} %pad_clamp_fusion), kind=kCustom, calls=%fused_computation.clone | custom fusion | bytes 526336 | tf_op jit(solution)/shard_map/jit(_take)/gather | solution.py:84
  17.4 1.1 %broadcast_select_fusion = (bf16[4,128,2,128]{3,2,1,0:T(2,128)(2,1)S(1)}, bf16[4,128,2,128]{3,2,1,0:T(2,128)(2,1)S(1)}) fusion(bf16[4,128,2,128]{3,2,1,0:T(2,128)(2,1)S(1)} %bitcast.97, pred[4,128]{1,0:T(4,128)(4,1)S(1)} %get-tuple-element.16, bf16[4,128,2,128]{3,2,1,0:T(2,128)(2,1)S(1)} %bitcast.98), kind=kLoop, calls=%fused_computation.43 | loop fusion | flops 262144 | bytes 1049088 | tf_op jit(solution)/shard_map/jit(_take)/select_n | solution.py:83
  18.5 0.2 copy.48
  18.7 0.2 fusion.7
  18.9 0.5 fusion.82
  19.4 0.2 copy.46
  19.6 0.0 copy-start.8
  19.6 0.3 fusion.8
  19.9 0.0 copy-start.6
  20.0 0.2 copy.50
  20.2 0.0 copy-start.7
  20.2 0.2 reshape.95
  20.4 0.2 fusion.20
  20.5 1.3 %collective-permute-start.2 = (bf16[8,2,128]{2,0,1:T(8,128)(2,1)S(1)}, bf16[8,2,128]{2,0,1:T(8,128)(2,1)S(1)}, u32[]{:S(2)}, u32[]{:S(2)}) collective-permute-start(bf16[8,2,128]{2,0,1:T(8,128)(2,1)S(1)} %slice.28), channel_id=1, source_target_pairs={{1,0},{2,1},{3,2},{4,3},{5,4},{6,5},{7,6},{8,7},{9,8},{10,9},{11,1... | collective-permute-start | bytes 12296 | tf_op jit(solution)/shard_map/ppermute | solution.py:29
  21.8 0.8 %copy.54 = f32[16,16,256]{2,1,0:T(8,128)} copy(f32[16,16,256]{2,0,1:T(8,128)S(1)} %fusion.66) | data formatting | bytes 524288 | tf_op jit(solution)/shard_map/qkc,ch->hqk/dot_general | solution.py:127
  22.7 0.7 copy.57
  23.4 2.6 %collective-permute-done.2 = bf16[8,2,128]{2,0,1:T(8,128)(2,1)S(1)} collective-permute-done((bf16[8,2,128]{2,0,1:T(8,128)(2,1)S(1)}, bf16[8,2,128]{2,0,1:T(8,128)(2,1)S(1)}, u32[]{:S(2)}, u32[]{:S(2)}) %collective-permute-start.2) | collective-permute-done | bytes 4128 | tf_op jit(solution)/shard_map/ppermute | solution.py:29
  26.0 0.3 convolution_maximum_fusion
  26.3 0.0 copy-start.1
  26.3 0.5 fusion.85
  26.8 0.2 multiply_reduce_fusion
  27.0 0.4 fusion.29
  27.4 0.2 reshape.96
  27.5 0.0 copy-done.1
  27.6 0.4 fusion.32
  27.9 24.9 %all_gather.6 = bf16[256,2,768]{2,0,1:T(8,128)(2,1)S(1)} all-gather(bf16[16,2,768]{2,0,1:T(8,128)(2,1)S(1)} %fusion.32), channel_id=1, replica_groups=mesh['groups'=2,'row'=16] {'row'}, dimensions={0}, use_global_device_ids=true | all-gather | bytes 835584 | tf_op jit(solution)/shard_map/all_gather | solution.py:122
  52.9 0.3 copy.52
  53.1 0.0 copy-start.2
  53.2 1.4 %fusion.86 = (f32[2,16,16]{2,1,0:T(8,128)S(1)}, f32[2,16,16,256]{3,2,1,0:T(8,128)S(1)}) fusion(f32[16,16,256]{2,1,0:T(8,128)} %copy.54, bf16[256,2,16,48]{0,3,2,1:T(8,128)(2,1)S(1)} %bitcast.96, bf16[16,2,16,48]{3,2,0,1:T(8,128)(2,1)S(1)} %reshape.96, pred[256]{0:T(512)(128)(4,1)S(1)} %broadcast_compare_fusion), kind=kOutput, calls=%fused_computation.107 | convolution fusion | flops 13106688 | bytes 1624320 | tf_op jit(solution)/shard_map/qshd,kshd->shqk/dot_general | solution.py:130
  54.5 0.4 fusion.35
  54.9 19.6 %all_gather.7 = bf16[256,2,768]{2,0,1:T(8,128)(2,1)S(1)} all-gather(bf16[16,2,768]{2,0,1:T(8,128)(2,1)S(1)} %fusion.35), channel_id=1, replica_groups=mesh['groups'=2,'row'=16] {'row'}, dimensions={0}, use_global_device_ids=true | all-gather | bytes 835584 | tf_op jit(solution)/shard_map/all_gather | solution.py:123
  74.5 1.1 %copy.55 = bf16[256,2,768]{0,2,1:T(8,128)(2,1)} copy(bf16[256,2,768]{2,0,1:T(8,128)(2,1)S(1)} %all_gather.7) | data formatting | bytes 1572864 | tf_op jit(solution)/shard_map/all_gather | solution.py:123
  75.7 0.2 fusion.40
  75.9 0.0 copy-start.3
  75.9 1.6 %fusion.18 = bf16[16,2,16,48]{3,0,2,1:T(8,128)(2,1)S(1)} fusion(bf16[256,2,16,48]{0,3,2,1:T(8,128)(2,1)} %bitcast.101, f32[2,16,16,256]{3,2,1,0:T(8,128)S(1)} %get-tuple-element.20, f32[2,16,16]{2,1,0:T(8,128)S(1)} %broadcast_maximum_fusion, pred[256]{0:T(512)(128)(4,1)S(1)} %broadcast_compare_fusion, f32[16,2,16]{0,2,1:T(8,128)S(1)} %bitcast.103), kind=kOutput, calls=%fused_computation.25 | convolution fusion | flops 13025280 | bytes 1364224 | tf_op jit(solution)/shard_map/shqk,kshd->shqd/dot_general | solution.py:137
  77.6 0.2 reshape.99
  77.8 0.3 fusion.24
  78.1 0.7 copy.58
  (29 shorter events, 0.2 us)
Async XLA Ops:
  0.6 26.3 %copy-start = (bf16[768,768]{1,0:T(8,128)(2,1)S(1)}, bf16[768,768]{1,0:T(8,128)(2,1)}, u32[]{:S(2)}) copy-start(bf16[768,768]{1,0:T(8,128)(2,1)} %param.29) | copy-start | bytes 3538948
  0.6 8.3 %copy-start.5 = (bf16[128,2,128]{2,1,0:T(2,128)(2,1)S(1)}, bf16[128,2,128]{2,1,0:T(2,128)(2,1)}, u32[]{:S(2)}) copy-start(bf16[128,2,128]{2,1,0:T(2,128)(2,1)} %param.18) | copy-start | bytes 196612
  0.7 8.1 %copy-start.13 = (s32[4]{0:T(128)S(1)}, s32[4]{0:T(128)}, u32[]{:S(2)}) copy-start(s32[4]{0:T(128)} %param.19) | copy-start | bytes 52
  0.7 8.3 %copy-start.11 = (bf16[128,128]{1,0:T(8,128)(2,1)S(1)}, bf16[128,128]{1,0:T(8,128)(2,1)}, u32[]{:S(2)}) copy-start(bf16[128,128]{1,0:T(8,128)(2,1)} %param.24) | copy-start | bytes 98308
  2.8 6.6 %copy-start.9 = (s32[2048]{0:T(1024)S(1)}, s32[2048]{0:T(1024)}, u32[]{:S(2)}) copy-start(s32[2048]{0:T(1024)} %param.20) | copy-start | bytes 24580
  2.8 7.0 %copy-start.12 = (s32[256]{0:T(256)S(1)}, s32[256]{0:T(256)}, u32[]{:S(2)}) copy-start(s32[256]{0:T(256)} %param.23) | copy-start | bytes 3076
  2.8 7.0 %copy-start.4 = (bf16[16,256,128]{2,1,0:T(8,128)(2,1)S(1)}, bf16[16,256,128]{2,1,0:T(8,128)(2,1)}, u32[]{:S(2)}) copy-start(bf16[16,256,128]{2,1,0:T(8,128)(2,1)} %param.22) | copy-start | bytes 3145732
  2.8 7.0 %copy-start.10 = (bf16[128,16]{0,1:T(8,128)(2,1)S(1)}, bf16[128,16]{0,1:T(8,128)(2,1)}, u32[]{:S(2)}) copy-start(bf16[128,16]{0,1:T(8,128)(2,1)} %param.33) | copy-start | bytes 12292
  5.1 5.1 %collective-permute-start = (bf16[2,64,2,128]{3,1,2,0:T(8,128)(2,1)S(1)}, bf16[2,64,2,128]{3,1,2,0:T(8,128)(2,1)S(1)}, u32[]{:S(2)}, u32[]{:S(2)}) collective-permute-start(bf16[2,64,2,128]{3,1,2,0:T(8,128)(2,1)S(1)} %get-tuple-element.11), channel_id=1, source_target_pairs={{0,1},{1,2},{2,3},{3,4},{4,5},{5,6},{6,7},{7,8},{8,9},{9,10},{10,1... | collective-permute-start | bytes 196616 | tf_op jit(solution)/shard_map/ppermute | solution.py:18
  7.5 5.3 %collective-permute-start.1 = (bf16[2,64,2,128]{3,1,2,0:T(8,128)(2,1)S(1)}, bf16[2,64,2,128]{3,1,2,0:T(8,128)(2,1)S(1)}, u32[]{:S(2)}, u32[]{:S(2)}) collective-permute-start(bf16[2,64,2,128]{3,1,2,0:T(8,128)(2,1)S(1)} %get-tuple-element.12), channel_id=1, source_target_pairs={{1,0},{2,1},{3,2},{4,3},{5,4},{6,5},{7,6},{8,7},{9,8},{10,9},{11,1... | collective-permute-start | bytes 196616 | tf_op jit(solution)/shard_map/ppermute | solution.py:21
  19.6 0.8 copy-start.8
  19.9 6.1 %copy-start.6 = (bf16[128,768]{1,0:T(8,128)(2,1)S(1)}, bf16[128,768]{1,0:T(8,128)(2,1)}, u32[]{:S(2)}) copy-start(bf16[128,768]{1,0:T(8,128)(2,1)} %param.28) | copy-start | bytes 589828
  20.2 6.1 %copy-start.7 = (bf16[16,2,768]{2,1,0:T(2,128)(2,1)S(1)}, bf16[16,2,768]{2,1,0:T(2,128)(2,1)}, u32[]{:S(2)}) copy-start(bf16[16,2,768]{2,1,0:T(2,128)(2,1)} %param.21) | copy-start | bytes 147460
  20.5 5.5 %collective-permute-start.2 = (bf16[8,2,128]{2,0,1:T(8,128)(2,1)S(1)}, bf16[8,2,128]{2,0,1:T(8,128)(2,1)S(1)}, u32[]{:S(2)}, u32[]{:S(2)}) collective-permute-start(bf16[8,2,128]{2,0,1:T(8,128)(2,1)S(1)} %slice.28), channel_id=1, source_target_pairs={{1,0},{2,1},{3,2},{4,3},{5,4},{6,5},{7,6},{8,7},{9,8},{10,9},{11,1... | collective-permute-start | bytes 12296 | tf_op jit(solution)/shard_map/ppermute | solution.py:29
  26.3 1.3 %copy-start.1 = (bf16[768,768]{1,0:T(8,128)(2,1)S(1)}, bf16[768,768]{1,0:T(8,128)(2,1)}, u32[]{:S(2)}) copy-start(bf16[768,768]{1,0:T(8,128)(2,1)} %param.30) | copy-start | bytes 3538948
  53.1 1.4 %copy-start.2 = (bf16[768,768]{1,0:T(8,128)(2,1)S(1)}, bf16[768,768]{1,0:T(8,128)(2,1)}, u32[]{:S(2)}) copy-start(bf16[768,768]{1,0:T(8,128)(2,1)} %param.31) | copy-start | bytes 3538948
  75.9 1.8 %copy-start.3 = (bf16[768,768]{1,0:T(8,128)(2,1)S(1)}, bf16[768,768]{1,0:T(8,128)(2,1)}, u32[]{:S(2)}) copy-start(bf16[768,768]{1,0:T(8,128)(2,1)} %param.32) | copy-start | bytes 3538948
where the time goes:
time: 79.2 us; the launch traced here: 78.8 us
  blocking collectives  44.5 us (56%)
  local copies, waits for them, and re-layouts  9.67 us (12%)
  matrix products  9.26 us (12%)
  waiting for transfers between devices  5.23 us (7%)
  starting transfers between devices  4.94 us (6%)
  other arithmetic  4.04 us (5%)
  between operations  1.09 us (1%)
    all_gather x1, blocking collectives, on_device(): kpiece = lax.all_gather(tk, 'row', axis=0, tiled=True)  24.9 us
    all_gather x1, blocking collectives, on_device(): vpiece = lax.all_gather(tv, 'row', axis=0, tiled=True)  19.6 us
    dot_general x9, matrix products, project(): jnp.einsum('asc,cd->asd', values, weight, preferred_element_type=jnp.floa...  4.36 us
    ppermute x1, waiting for transfers between devices, from_behind(): return lax.ppermute(block, axis, route)  2.64 us
    ppermute x1, waiting for transfers between devices, extended(): lax.ppermute(lax.slice_in_dim(block, 0, width, axis=dim), axis, backward)  2.57 us
    ppermute x1, starting transfers between devices, extended(): lax.ppermute(lax.slice_in_dim(block, block.shape[dim] - width, None, axis...  2.36 us
    gather x1, local copies, waits for them, and re-layouts, on_device(): window_k = jnp.take(key_pad, places + border, axis=0)  2.11 us
    gather x1, local copies, waits for them, and re-layouts, on_device(): window_v = jnp.take(value_pad, places + border, axis=0)  2.11 us
  transfers between devices with their start and end apart: 3, of which 2 were waited for; matrix products, arithmetic and copies ran while one was open for 4% of the time, Pallas kernels for 0%

commit v1 on v0

v1 whole, which is shorter than its diff:
```python
import jax
import jax.numpy as jnp
from jax import lax
from jax.sharding import PartitionSpec as P

ATOM_HEADS = 4
QBLOCK = 32
KWIN = 128
SHIFT = 16
TOKEN_HEADS = 16


def layer_norm(values):
    values = values.astype(jnp.float32)
    mean = jnp.mean(values, axis=-1, keepdims=True)
    var = jnp.mean((values - mean) ** 2, axis=-1, keepdims=True)
    return (values - mean) / jnp.sqrt(var + 1e-05)


def project(values, weight):
    return jnp.einsum("asc,cd->asd", values, weight, preferred_element_type=jnp.float32)


def shifted(block, axis, step):
    count = lax.axis_size(axis)
    route = [(i, i + step) for i in range(count) if 0 <= i + step < count]
    return lax.ppermute(block, axis, route)


def on_device(
    atom_feat,
    window_shift,
    atom_token,
    token_in,
    pair,
    key_mask,
    w_atom_query,
    w_atom_key,
    w_atom_value,
    w_atom_out,
    w_to_token,
    w_query,
    w_key,
    w_value,
    w_out,
    w_bias,
):
    high = lax.Precision.HIGHEST
    atom_dev, samples, width = atom_feat.shape
    tok_dev = token_in.shape[0]
    tok_width = token_in.shape[2]
    devices = lax.axis_size("row")
    rank = lax.axis_index("row")
    atom_base = rank * atom_dev
    total_atoms = atom_dev * devices
    margin = (KWIN - QBLOCK) // 2
    low_rows = margin + SHIFT
    span = KWIN + 2 * SHIFT
    high_rows = span - low_rows
    blocks = atom_dev // QBLOCK + 1

    shift_row = jnp.broadcast_to(
        window_shift[0].astype(jnp.bfloat16), (1, samples, width)
    )
    low = shifted(atom_feat[atom_dev - low_rows :], "row", 1)
    upper = shifted(
        jnp.concatenate([atom_feat[:high_rows], shift_row], axis=0), "row", -1
    )
    next_shift = upper[high_rows, 0, 0].astype(jnp.int32)
    upper = upper[:high_rows]

    w_qkv = jnp.concatenate([w_atom_query, w_atom_key, w_atom_value], axis=1)
    w_kv = jnp.concatenate([w_atom_key, w_atom_value], axis=1)
    own_p = project(layer_norm(atom_feat).astype(jnp.bfloat16), w_qkv).astype(jnp.bfloat16)
    low_p = project(layer_norm(low).astype(jnp.bfloat16), w_kv).astype(jnp.bfloat16)
    high_p = project(layer_norm(upper).astype(jnp.bfloat16), w_qkv).astype(jnp.bfloat16)
    query = jnp.concatenate([own_p[..., :width], high_p[:QBLOCK, :, :width]], axis=0)
    kv = jnp.concatenate([low_p, own_p[..., width:], high_p[..., width:]], axis=0)

    head_dim = width // ATOM_HEADS
    shifts = jnp.concatenate([window_shift, next_shift[None]], axis=0)
    kwin = jnp.stack([kv[j * QBLOCK : j * QBLOCK + span] for j in range(blocks)], axis=0)
    position = jnp.arange(span, dtype=jnp.int32)
    first = (SHIFT + shifts)[:, None]
    absolute = (
        atom_base
        + jnp.arange(blocks, dtype=jnp.int32)[:, None] * QBLOCK
        - low_rows
        + position[None, :]
    )
    valid = (
        (position[None, :] >= first)
        & (position[None, :] < first + KWIN)
        & (absolute >= 0)
        & (absolute < total_atoms)
    )
    qblock = query.reshape(blocks, QBLOCK, samples, ATOM_HEADS, head_dim)
    kblock = kwin[..., :width].reshape(blocks, span, samples, ATOM_HEADS, head_dim)
    vblock = kwin[..., width:].reshape(blocks, span, samples, ATOM_HEADS, head_dim)
    scores = jnp.einsum(
        "bqshd,bkshd->bshqk", qblock, kblock, preferred_element_type=jnp.float32
    ) / jnp.sqrt(jnp.float32(head_dim))
    keep = valid[:, None, None, None, :]
    scores = jnp.where(keep, scores, -1e30)
    top = jnp.max(scores, axis=-1, keepdims=True)
    expo = jnp.where(keep, jnp.exp(scores - top), 0.0)
    total = jnp.sum(expo, axis=-1)
    mixed = jnp.einsum(
        "bshqk,bkshd->bqshd", expo.astype(jnp.bfloat16), vblock, preferred_element_type=jnp.float32
    )
    mixed = mixed / jnp.transpose(total, (0, 3, 1, 2))[..., None]
    rows = blocks * QBLOCK
    mixed = mixed.astype(jnp.bfloat16).reshape(rows, samples, width)
    feat = jnp.concatenate([atom_feat, upper[:QBLOCK]], axis=0)
    atom_rows = (feat.astype(jnp.float32) + project(mixed, w_atom_out)).astype(jnp.bfloat16)
    atom_out = atom_rows[:atom_dev]

    own_ids = rank * tok_dev + jnp.arange(tok_dev, dtype=jnp.int32)
    row_ids = lax.dynamic_slice_in_dim(
        jnp.concatenate([atom_token, jnp.full((QBLOCK,), -1, jnp.int32)]), atom_base, rows
    )
    hidden = jax.nn.relu(project(atom_rows, w_to_token))
    onehot = (own_ids[:, None] == row_ids[None, :]).astype(jnp.float32)
    counts = jnp.sum(onehot, axis=1)
    sums = jnp.einsum("ta,asd->tsd", onehot, hidden, precision=high)
    state = (token_in.astype(jnp.float32) + sums / counts[:, None, None]).astype(jnp.bfloat16)

    tdim = tok_width // TOKEN_HEADS
    tq = project(layer_norm(state).astype(jnp.bfloat16), w_query).astype(jnp.bfloat16)
    tq = tq.reshape(tok_dev, samples, TOKEN_HEADS, tdim)
    bias = jnp.einsum("qkc,ch->hqk", pair, w_bias, preferred_element_type=jnp.float32)
    scale = 1.0 / jnp.sqrt(jnp.float32(tdim))

    every = lax.all_gather(state, "row", axis=0, tiled=True)
    count = every.shape[0]
    tkv = project(layer_norm(every).astype(jnp.bfloat16), jnp.concatenate([w_key, w_value], axis=1))
    tkv = tkv.astype(jnp.bfloat16)
    kheads = tkv[..., :tok_width].reshape(count, samples, TOKEN_HEADS, tdim)
    vheads = tkv[..., tok_width:].reshape(count, samples, TOKEN_HEADS, tdim)
    flags = (key_mask > 0)[None, None, None, :]
    score = (
        jnp.einsum("qshd,kshd->shqk", tq, kheads, preferred_element_type=jnp.float32) * scale
        + bias[None]
    )
    score = jnp.where(flags, score, -1e30)
    peak = jnp.max(score, axis=-1)
    expo_t = jnp.where(flags, jnp.exp(score - peak[..., None]), 0.0)
    denom = jnp.sum(expo_t, axis=-1)
    accum = jnp.einsum(
        "shqk,kshd->shqd", expo_t.astype(jnp.bfloat16), vheads, preferred_element_type=jnp.float32
    )
    tmix = (accum / denom[..., None]).astype(jnp.bfloat16)
    tmix = jnp.transpose(tmix, (2, 0, 1, 3)).reshape(tok_dev, samples, tok_width)
    token_out = (state.astype(jnp.float32) + project(tmix, w_out)).astype(jnp.bfloat16)
    return (atom_out, token_out)


def solution(mesh):
    return jax.shard_map(
        on_device,
        mesh=mesh,
        in_specs=(
            P(("groups", "row"), None, None),
            P(("groups", "row")),
            P("groups"),
            P(("groups", "row"), None, None),
            P(("groups", "row"), None, None),
            P("groups"),
            P(),
            P(),
            P(),
            P(),
            P(),
            P(),
            P(),
            P(),
            P(),
            P(),
        ),
        out_specs=(P(("groups", "row"), None, None), P(("groups", "row"), None, None)),
        check_vma=False,
    )
```

time: 79.2 us -> 65.1 us (0.82)
  blocking collectives: 44.5 us -> 25.4 us
  waiting for transfers between devices: 5.23 us -> 0.01 us
  other arithmetic: 4.04 us -> 8.99 us
  matrix products: 9.26 us -> 12 us
  local copies, waits for them, and re-layouts: 9.67 us -> 11.7 us
  between operations: 1.09 us -> 1.94 us
    all_gather x2 -> x1, blocking collectives: 44.5 us -> 25.4 us  [on_device(): every = lax.all_gather(state, 'row', axis=0, tiled=True)]
    ppermute x3 -> x2, waiting for transfers between devices: 5.23 us -> 0.01 us  [shifted(): return lax.ppermute(block, axis, route)]
    slice x1 -> x15, local copies, waits for them, and re-layouts: 0.01 us -> 4.24 us  [the longest x1 1.15 us: on_device(): vheads = tkv[..., tok_width:].reshape(count, samples, TOKEN_HEADS, tdim)]
    gather x2 -> x0, local copies, waits for them, and re-layouts: 4.23 us -> none  [the longest x1 2.11 us: on_device(): window_k = jnp.take(key_pad, places + border, axis=0)]
    unnamed x30 -> x55, local copies, waits for them, and re-layouts: 1.47 us -> 3.9 us
    dot_general x1, matrix products: 0.35 us -> 1.94 us  [on_device(): jnp.einsum('bshqk,bkshd->bqshd', expo.astype(jnp.bfloat16), vblock, prefe...]
    all_gather x2 -> x0, local copies, waits for them, and re-layouts: 1.42 us -> none  [the longest x1 1.15 us: on_device(): vpiece = lax.all_gather(tv, 'row', axis=0, tiled=True)]
    convert_element_type x0 -> x2, other arithmetic: none -> 1.38 us  [the longest x1 1.18 us: on_device(): layer_norm(atom_feat).astype(jnp.bfloat16)]
  transfers between devices with their start and end apart: 3 -> 2, of which waited for: 2 -> 0; matrix products, arithmetic and copies ran while one was open for 4% -> 15% of each run, Pallas kernels for 0% -> 0%
where the time goes in v1:
time: 65.1 us; the launch traced here: 64.4 us
  blocking collectives  25.4 us (39%)
  matrix products  12 us (18%)
  local copies, waits for them, and re-layouts  11.7 us (18%)
  other arithmetic  8.99 us (14%)
  starting transfers between devices  4.32 us (7%)
  between operations  1.94 us (3%)
    all_gather x1, blocking collectives, on_device(): every = lax.all_gather(state, 'row', axis=0, tiled=True)  25.4 us
    ppermute x2, starting transfers between devices, shifted(): return lax.ppermute(block, axis, route)  4.32 us
    dot_general x8, matrix products, project(): jnp.einsum('asc,cd->asd', values, weight, preferred_element_type=jnp.floa...  3.99 us
    unnamed x55, local copies, waits for them, and re-layouts  3.9 us
    reduce_sum x5, other arithmetic, layer_norm(): var = jnp.mean((values - mean) ** 2, axis=-1, keepdims=True)  2.14 us
    dot_general x1, matrix products, on_device(): jnp.einsum('bshqk,bkshd->bqshd', expo.astype(jnp.bfloat16), vblock, prefe...  1.94 us
    dot_general x1, matrix products, on_device(): jnp.einsum('shqk,kshd->shqd', expo_t.astype(jnp.bfloat16), vheads, prefer...  1.69 us
    reduce_sum x4, other arithmetic, layer_norm(): mean = jnp.mean(values, axis=-1, keepdims=True)  1.48 us
  transfers between devices with their start and end apart: 2, of which 0 were waited for; matrix products, arithmetic and copies ran while one was open for 15% of the time, Pallas kernels for 0%

profile of v1, /device:TPU:0, one launch (start us, length us, event | category | flops | bytes accessed | tf_op | source)
XLA Modules:
  0.0 64.4 jit_solution(1307241648718720969)
XLA Ops:
  0.6 0.0 copy-start
  0.7 1.0 %copy.33 = bf16[128,2,128]{2,0,1:T(8,128)(2,1)S(1)} copy(bf16[128,2,128]{2,1,0:T(2,128)(2,1)} %param.16) | data formatting | bytes 131072 | tf_op args[0]
  1.7 0.0 copy-start.8
  1.7 0.7 %convert.4 = bf16[4]{0:T(256)(128)(2,1)S(1)} convert(s32[4]{0:T(128)} %param.17) | non-fusion elementwise | flops 4 | bytes 24 | tf_op jit(solution)/shard_map/convert.1
  2.4 0.8 %slice_select_fusion = bf16[97,2,128]{2,0,1:T(8,128)(2,1)S(1)} fusion(bf16[128,2,128]{2,0,1:T(8,128)(2,1)S(1)} %copy.33, pred[97]{0:T(512)(128)(4,1)} %constant.19.clone.1, bf16[]{:T(256)S(1)} %bitcast.108), kind=kLoop, calls=%fused_computation.103 | loop fusion | flops 24832 | bytes 99427 | tf_op jit(solution)/shard_map/concatenate | solution.py:67
  3.2 1.3 %collective-permute-start = (bf16[97,2,128]{2,0,1:T(8,128)(2,1)S(1)}, bf16[97,2,128]{2,0,1:T(8,128)(2,1)S(1)}, u32[]{:S(2)}, u32[]{:S(2)}) collective-permute-start(bf16[97,2,128]{2,0,1:T(8,128)(2,1)S(1)} %slice_select_fusion), channel_id=1, source_target_pairs={{1,0},{2,1},{3,2},{4,3},{5,4},{6,5},{7,6},{8,7},{9,8},{10,9},{11,1... | collective-permute-start | bytes 149000 | tf_op jit(solution)/shard_map/ppermute | solution.py:27
  4.5 0.8 %slice.71 = bf16[64,2,128]{2,1,0:T(2,128)(2,1)S(1)} slice(bf16[128,2,128]{2,1,0:T(2,128)(2,1)} %param.16), slice={[64:128], [0:2], [0:128]} | slice | bytes 65536 | tf_op jit(solution)/shard_map/slice | solution.py:65
  5.3 3.0 %collective-permute-start.1 = (bf16[64,2,128]{2,1,0:T(2,128)(2,1)S(1)}, bf16[64,2,128]{2,1,0:T(2,128)(2,1)S(1)}, u32[]{:S(2)}, u32[]{:S(2)}) collective-permute-start(bf16[64,2,128]{2,1,0:T(2,128)(2,1)S(1)} %slice.71), channel_id=1, source_target_pairs={{0,1},{1,2},{2,3},{3,4},{4,5},{5,6},{6,7},{7,8},{8,9},{9,10},{10,1... | collective-permute-start | bytes 98312 | tf_op jit(solution)/shard_map/ppermute | solution.py:27
  8.3 1.0 %convert_reduce_fusion.1 = f32[128,2]{1,0:T(8,128)S(1)} fusion(bf16[128,2,128]{2,1,0:T(2,128)(2,1)} %param.16), kind=kLoop, calls=%fused_computation.56 | loop fusion | flops 65280 | bytes 66560 | tf_op jit(solution)/shard_map/reduce_sum | solution.py:15
  9.4 1.2 %fusion.58 = f32[128,2]{1,0:T(8,128)S(1)} fusion(bf16[128,2,128]{2,1,0:T(2,128)(2,1)} %param.16, f32[128,2]{1,0:T(8,128)S(1)} %broadcast_multiply_fusion), kind=kLoop, calls=%fused_computation.77 | loop fusion | flops 130816 | bytes 67584 | tf_op jit(solution)/shard_map/reduce_sum | solution.py:16
  10.6 1.2 %fusion.59 = bf16[128,2,128]{2,1,0:T(2,128)(2,1)S(1)} fusion(bf16[128,2,128]{2,1,0:T(2,128)(2,1)} %param.16, f32[128,2]{1,0:T(8,128)S(1)} %add_sqrt_fusion, f32[128,2]{1,0:T(8,128)S(1)} %broadcast_multiply_fusion), kind=kLoop, calls=%fused_computation.78 | loop fusion | flops 131072 | bytes 133120 | tf_op jit(solution)/shard_map/convert_element_type | solution.py:74
  11.8 1.3 %broadcast_compare_fusion = pred[256]{0:T(512)(128)(4,1)} fusion(s32[256]{0:T(256)} %param.21), kind=kLoop, calls=%fused_computation.139 | loop fusion | flops 256 | bytes 1280 | tf_op jit(solution)/shard_map/gt | solution.py:140
  13.1 0.8 %pad_dynamic-slice_fusion = s32[160]{0:T(256)S(1)} fusion(s32[]{:T(128)S(6)} %select_n.19, s32[2048]{0:T(1024)} %param.18), kind=kLoop, calls=%fused_computation.118 | loop fusion | bytes 8836 | tf_op jit(solution)/shard_map/dynamic_slice | solution.py:119
  13.9 1.1 %fusion.98 = f32[16,16,256]{2,0,1:T(8,128)S(1)} fusion(bf16[16,256,128]{2,1,0:T(8,128)(2,1)S(1)} %copy-done.3, bf16[128,16]{0,1:T(8,128)(2,1)} %param.31), kind=kOutput, calls=%fused_computation.129 | convolution fusion | flops 16777216 | bytes 1314816 | tf_op jit(solution)/shard_map/qkc,ch->hqk/dot_general | solution.py:131
  14.9 0.0 copy-done.15
  15.0 0.2 convolution_convert_fusion.1
  15.2 0.7 %fusion.90 = f32[16]{0:T(128)} fusion(s32[160]{0:T(256)S(1)} %pad_dynamic-slice_fusion, s32[16]{0:T(128)S(1)} %iota_add_fusion.1), kind=kLoop, calls=%fused_computation.116 | loop fusion | flops 7664 | bytes 768 | tf_op jit(solution)/shard_map/reduce_sum | solution.py:124
  15.9 0.9 %copy.43 = f32[16,16,256]{2,1,0:T(8,128)} copy(f32[16,16,256]{2,0,1:T(8,128)S(1)} %fusion.98) | data formatting | bytes 524288 | tf_op jit(solution)/shard_map/qkc,ch->hqk/dot_general | solution.py:131
  16.8 0.0 collective-permute-done.1
  16.8 0.1 convert_reduce_fusion.4
  16.9 0.2 fusion.71
  17.2 0.2 fusion.72
  17.4 0.1 convolution_convert_fusion.3
  17.6 0.1 convert_reduce_fusion.3
  17.7 0.2 fusion.67
  17.9 0.3 convolution_convert_fusion.2
  18.3 0.0 copy-start.23
  18.3 0.2 fusion.111
  18.5 0.2 copy.37
  18.8 0.5 slice.100
  20.0 0.1 broadcast_add_fusion.1
  20.0 0.2 reshape.203
  20.2 0.1 fusion.97
  20.3 0.6 copy-done.1
  20.9 1.3 %fusion.112 = f32[5,2,4,32]{3,2,1,0:T(4,128)} fusion(bf16[5,160,2,4,32]{1,4,3,2,0:T(8,128)(2,1)S(1)} %bitcast.104, pred[5,160]{1,0:T(8,128)(4,1)S(1)} %fusion.97, bf16[5,32,2,4,32]{4,3,1,0,2:T(4,128)(2,1)S(1)} %reshape.203), kind=kOutput, calls=%fused_computation.155 | convolution fusion | flops 14131359 | bytes 497440 | tf_op jit(solution)/shard_map/sub | solution.py:106
  22.2 1.3 %fusion.10 = f32[5,2,4,32,160]{4,3,2,1,0:T(8,128)S(1)} fusion(bf16[5,160,2,4,32]{1,4,3,2,0:T(8,128)(2,1)S(1)} %bitcast.105, pred[5,160]{1,0:T(8,128)(4,1)} %copy-done.18, bf16[5,32,2,4,32]{4,3,1,0,2:T(4,128)(2,1)} %copy-done.1), kind=kOutput, calls=%fused_computation.15 | convolution fusion | flops 13516800 | bytes 1311520 | tf_op jit(solution)/shard_map/bqshd,bkshd->bshqk/dot_general | solution.py:100
  23.5 0.2 copy.36
  23.8 0.0 copy-start.9
  23.8 1.9 %fusion.18 = bf16[5,32,2,4,32]{1,4,3,2,0:T(8,128)(2,1)} fusion(bf16[5,160,2,4,32]{1,4,3,2,0:T(8,128)(2,1)S(1)} %bitcast.107, f32[5,32,2,4]{1,3,2,0:T(4,128)} %bitcast.109, f32[5,2,4,32,160]{4,3,2,1,0:T(8,128)S(1)} %fusion.10, pred[5,160]{1,0:T(8,128)(4,1)} %copy-done.18), kind=kOutput, calls=%fused_computation.26 | convolution fusion | flops 13804959 | bytes 1316640 | tf_op jit(solution)/shard_map/bshqk,bkshd->bqshd/dot_general | solution.py:108
  25.7 1.2 %copy.39 = bf16[5,32,2,4,32]{4,3,1,0,2:T(4,128)(2,1)S(1)} copy(bf16[5,32,2,4,32]{1,4,3,2,0:T(8,128)(2,1)} %fusion.18) | data formatting | bytes 163840 | tf_op jit(solution)/shard_map/convert_element_type | solution.py:113
  27.0 0.2 reshape.205
  27.2 0.7 %slice.89 = bf16[32,2,128]{2,0,1:T(8,128)(2,1)S(1)} slice(bf16[97,2,128]{2,0,1:T(8,128)(2,1)} %copy-done.10), slice={[0:32], [0:2], [0:128]} | slice | bytes 32768 | tf_op jit(solution)/shard_map/slice | solution.py:114
  27.9 0.9 %add_convert_fusion = bf16[160,2,128]{2,0,1:T(8,128)(2,1)S(1)} fusion(bf16[32,2,128]{2,0,1:T(8,128)(2,1)S(1)} %slice.89, bf16[128,2,128]{2,0,1:T(8,128)(2,1)S(1)} %copy-done.9, bf16[160,2,128]{2,0,1:T(8,128)(2,1)S(1)} %reshape.205, bf16[128,128]{1,0:T(8,128)(2,1)} %param.25), kind=kOutput, calls=%fused_computation.72 | convolution fusion | flops 10731520 | bytes 278528 | tf_op jit(solution)/shard_map/asc,cd->asd/dot_general | solution.py:21
  28.8 0.7 %copy.46 = bf16[128,2,128]{2,1,0:T(2,128)(2,1)} copy(bf16[128,2,128]{2,0,1:T(8,128)(2,1)S(1)} %slice.104) | data formatting | bytes 131072
  29.5 0.3 convolution_maximum_fusion
  29.9 0.5 convert_reduce_fusion.2
  30.4 25.4 %all_gather.3 = bf16[256,2,768]{2,0,1:T(8,128)(2,1)S(1)} all-gather(bf16[16,2,768]{2,0,1:T(8,128)(2,1)S(1)} %get-tuple-element.13), channel_id=1, replica_groups=mesh['groups'=2,'row'=16] {'row'}, dimensions={0}, use_global_device_ids=true | all-gather | bytes 835584 | tf_op jit(solution)/shard_map/all_gather | solution.py:134
  55.8 0.2 convert_reduce_fusion
  55.9 0.4 fusion.7
  56.4 1.5 %convolution_convert_fusion = bf16[256,2,1536]{2,0,1:T(8,128)(2,1)S(1)} fusion(bf16[768,768]{1,0:T(8,128)(2,1)S(1)} %copy-done.24, bf16[768,768]{1,0:T(8,128)(2,1)S(1)} %copy-done.25, bf16[256,2,768]{2,0,1:T(8,128)(2,1)S(1)} %all_gather.3, f32[256,2]{0,1:T(2,128)S(1)} %add_sqrt_fusion.2, f32[256,2]{0,1:T(2,128)S(1)} %broadcast_multiply_fusion.2), kind=kOutput, calls=%fused_computation.2 | convolution fusion | flops 1215037440 | bytes 4722688 | tf_op jit(solution)/shard_map/asc,cd->asd/dot_general | solution.py:21
  57.9 0.1 fusion.110
  58.0 1.2 %copy.44 = bf16[256,2,768]{0,2,1:T(8,128)(2,1)} copy(bf16[256,2,768]{2,0,1:T(8,128)(2,1)S(1)} %get-tuple-element.7) | data formatting | bytes 1572864 | tf_op jit(solution)/shard_map/slice | solution.py:139
  59.1 0.3 copy.41
  59.4 0.2 fusion.65
  59.6 0.4 fusion.33
  60.0 0.2 reshape.206
  60.2 0.2 fusion.17
  60.4 0.8 %copy-done.7 = f32[2,16,16,256]{3,2,1,0:T(8,128)} copy-done((f32[2,16,16,256]{3,2,1,0:T(8,128)}, f32[2,16,16,256]{3,2,1,0:T(8,128)S(1)}, u32[]{:S(2)}) %copy-start.7) | copy-done | bytes 524312
  61.2 0.2 fusion.115
  61.5 0.0 copy-start.2
  61.5 1.7 %fusion.24 = bf16[16,2,16,48]{3,0,2,1:T(8,128)(2,1)S(1)} fusion(bf16[256,2,16,48]{0,3,2,1:T(8,128)(2,1)S(1)} %bitcast.106, f32[16,2,16]{0,2,1:T(8,128)S(1)} %bitcast.110, f32[2,16,16,256]{3,2,1,0:T(8,128)} %copy-done.7, pred[256]{0:T(512)(128)(4,1)S(1)} %copy-done.22), kind=kOutput, calls=%fused_computation.35 | convolution fusion | flops 13026047 | bytes 1362176 | tf_op jit(solution)/shard_map/shqk,kshd->shqd/dot_general | solution.py:149
  63.2 0.2 reshape.209
  63.4 0.3 fusion.29
  63.7 0.7 %copy.47 = bf16[16,2,768]{2,1,0:T(2,128)(2,1)} copy(bf16[16,2,768]{2,0,1:T(8,128)(2,1)S(1)} %fusion.29) | data formatting | bytes 98304
  (69 shorter events, 0.3 us)
Async XLA Ops:
  0.6 59.0 %copy-start = (bf16[768,768]{1,0:T(8,128)(2,1)S(1)}, bf16[768,768]{1,0:T(8,128)(2,1)}, u32[]{:S(2)}) copy-start(bf16[768,768]{1,0:T(8,128)(2,1)} %param.27) | copy-start | bytes 3538948
  0.6 13.2 %copy-start.3 = (bf16[16,256,128]{2,1,0:T(8,128)(2,1)S(1)}, bf16[16,256,128]{2,1,0:T(8,128)(2,1)}, u32[]{:S(2)}) copy-start(bf16[16,256,128]{2,1,0:T(8,128)(2,1)} %param.20) | copy-start | bytes 3145732
  0.7 14.3 %copy-start.12 = (bf16[128,128]{1,0:T(8,128)(2,1)S(1)}, bf16[128,128]{1,0:T(8,128)(2,1)}, u32[]{:S(2)}) copy-start(bf16[128,128]{1,0:T(8,128)(2,1)} %param.24) | copy-start | bytes 98308
  0.7 14.3 %copy-start.13 = (bf16[128,128]{1,0:T(8,128)(2,1)S(1)}, bf16[128,128]{1,0:T(8,128)(2,1)}, u32[]{:S(2)}) copy-start(bf16[128,128]{1,0:T(8,128)(2,1)} %param.23) | copy-start | bytes 98308
  0.7 14.3 %copy-start.15 = (bf16[128,128]{1,0:T(8,128)(2,1)S(1)}, bf16[128,128]{1,0:T(8,128)(2,1)}, u32[]{:S(2)}) copy-start(bf16[128,128]{1,0:T(8,128)(2,1)} %param.22) | copy-start | bytes 98308
  1.7 7.7 %copy-start.8 = (bf16[128,2,128]{2,0,1:T(8,128)(2,1)}, bf16[128,2,128]{2,0,1:T(8,128)(2,1)S(1)}, u32[]{:S(2)}) copy-start(bf16[128,2,128]{2,0,1:T(8,128)(2,1)S(1)} %copy.33) | copy-start | bytes 196612
  3.2 14.4 %collective-permute-start = (bf16[97,2,128]{2,0,1:T(8,128)(2,1)S(1)}, bf16[97,2,128]{2,0,1:T(8,128)(2,1)S(1)}, u32[]{:S(2)}, u32[]{:S(2)}) collective-permute-start(bf16[97,2,128]{2,0,1:T(8,128)(2,1)S(1)} %slice_select_fusion), channel_id=1, source_target_pairs={{1,0},{2,1},{3,2},{4,3},{5,4},{6,5},{7,6},{8,7},{9,8},{10,9},{11,1... | collective-permute-start | bytes 149000 | tf_op jit(solution)/shard_map/ppermute | solution.py:27
  5.3 11.5 %collective-permute-start.1 = (bf16[64,2,128]{2,1,0:T(2,128)(2,1)S(1)}, bf16[64,2,128]{2,1,0:T(2,128)(2,1)S(1)}, u32[]{:S(2)}, u32[]{:S(2)}) collective-permute-start(bf16[64,2,128]{2,1,0:T(2,128)(2,1)S(1)} %slice.71), channel_id=1, source_target_pairs={{0,1},{1,2},{2,3},{3,4},{4,5},{5,6},{6,7},{7,8},{8,9},{9,10},{10,1... | collective-permute-start | bytes 98312 | tf_op jit(solution)/shard_map/ppermute | solution.py:27
  11.8 5.1 %copy-start.19 = (s32[16]{0:T(128)}, s32[16]{0:T(128)S(1)}, u32[]{:S(2)}) copy-start(s32[16]{0:T(128)S(1)} %iota_add_fusion.1) | copy-start | bytes 196
  13.9 3.0 %copy-start.16 = (s32[160]{0:T(256)}, s32[160]{0:T(256)S(1)}, u32[]{:S(2)}) copy-start(s32[160]{0:T(256)S(1)} %pad_dynamic-slice_fusion) | copy-start | bytes 1924
  15.2 3.0 %copy-start.6 = (bf16[128,2,384]{2,0,1:T(8,128)(2,1)}, bf16[128,2,384]{2,0,1:T(8,128)(2,1)S(1)}, u32[]{:S(2)}) copy-start(bf16[128,2,384]{2,0,1:T(8,128)(2,1)S(1)} %convolution_convert_fusion.1) | copy-start | bytes 589828
  17.6 1.2 %copy-start.10 = (bf16[97,2,128]{2,0,1:T(8,128)(2,1)}, bf16[97,2,128]{2,0,1:T(8,128)(2,1)S(1)}, u32[]{:S(2)}) copy-start(bf16[97,2,128]{2,0,1:T(8,128)(2,1)S(1)} %collective-permute-done) | copy-start | bytes 148996
  18.3 1.6 %copy-start.23 = (s32[4]{0:T(128)S(1)}, s32[4]{0:T(128)}, u32[]{:S(2)}) copy-start(s32[4]{0:T(128)} %param.17) | copy-start | bytes 52
  18.3 1.7 %slice-start = ((bf16[128,2,384]{2,0,1:T(8,128)(2,1)}), bf16[128,2,128]{2,0,1:T(8,128)(2,1)S(1)}, s32[]{:S(2)}) async-start(bf16[128,2,384]{2,0,1:T(8,128)(2,1)} %copy-done.6), calls=%async_computation | async-start | bytes 131072 | tf_op jit(solution)/shard_map/slice | solution.py:77
  20.2 0.7 %copy-start.1 = (bf16[5,32,2,4,32]{4,3,1,0,2:T(4,128)(2,1)}, bf16[5,32,2,4,32]{4,3,1,0,2:T(4,128)(2,1)S(1)}, u32[]{:S(2)}) copy-start(bf16[5,32,2,4,32]{4,3,1,0,2:T(4,128)(2,1)S(1)} %reshape.203) | copy-start | bytes 245764
  20.3 0.6 copy-start.18
  23.8 4.1 %copy-start.9 = (bf16[128,2,128]{2,0,1:T(8,128)(2,1)S(1)}, bf16[128,2,128]{2,0,1:T(8,128)(2,1)}, u32[]{:S(2)}) copy-start(bf16[128,2,128]{2,0,1:T(8,128)(2,1)} %copy-done.8) | copy-start | bytes 196612
  25.7 3.8 %copy-start.11 = (bf16[128,768]{1,0:T(8,128)(2,1)S(1)}, bf16[128,768]{1,0:T(8,128)(2,1)}, u32[]{:S(2)}) copy-start(bf16[128,768]{1,0:T(8,128)(2,1)} %param.26) | copy-start | bytes 589828
  25.7 4.1 %copy-start.14 = (bf16[16,2,768]{2,1,0:T(2,128)(2,1)S(1)}, bf16[16,2,768]{2,1,0:T(2,128)(2,1)}, u32[]{:S(2)}) copy-start(bf16[16,2,768]{2,1,0:T(2,128)(2,1)} %param.19) | copy-start | bytes 147460
  25.7 4.1 %copy-start.17 = (s32[160]{0:T(256)S(1)}, s32[160]{0:T(256)}, u32[]{:S(2)}) copy-start(s32[160]{0:T(256)} %copy-done.16) | copy-start | bytes 1924
  25.7 4.1 %copy-start.20 = (s32[16]{0:T(128)S(1)}, s32[16]{0:T(128)}, u32[]{:S(2)}) copy-start(s32[16]{0:T(128)} %copy-done.19) | copy-start | bytes 196
  25.7 4.1 %copy-start.21 = (f32[16]{0:T(128)S(1)}, f32[16]{0:T(128)}, u32[]{:S(2)}) copy-start(f32[16]{0:T(128)} %fusion.90) | copy-start | bytes 196
  30.4 26.0 %copy-start.24 = (bf16[768,768]{1,0:T(8,128)(2,1)S(1)}, bf16[768,768]{1,0:T(8,128)(2,1)}, u32[]{:S(2)}) copy-start(bf16[768,768]{1,0:T(8,128)(2,1)} %param.29) | copy-start | bytes 3538948
  30.4 26.0 %copy-start.25 = (bf16[768,768]{1,0:T(8,128)(2,1)S(1)}, bf16[768,768]{1,0:T(8,128)(2,1)}, u32[]{:S(2)}) copy-start(bf16[768,768]{1,0:T(8,128)(2,1)} %param.28) | copy-start | bytes 3538948
  59.1 1.0 %copy-start.4 = (f32[16,16,256]{2,1,0:T(8,128)S(1)}, f32[16,16,256]{2,1,0:T(8,128)}, u32[]{:S(2)}) copy-start(f32[16,16,256]{2,1,0:T(8,128)} %copy.43) | copy-start | bytes 786436
  59.1 1.0 %copy-start.22 = (pred[256]{0:T(512)(128)(4,1)S(1)}, pred[256]{0:T(512)(128)(4,1)}, u32[]{:S(2)}) copy-start(pred[256]{0:T(512)(128)(4,1)} %broadcast_compare_fusion) | copy-start | bytes 772
  60.0 1.5 %copy-start.5 = (bf16[256,2,768]{0,2,1:T(8,128)(2,1)S(1)}, bf16[256,2,768]{0,2,1:T(8,128)(2,1)}, u32[]{:S(2)}) copy-start(bf16[256,2,768]{0,2,1:T(8,128)(2,1)} %copy.44) | copy-start | bytes 2359300
  60.4 0.8 %copy-start.7 = (f32[2,16,16,256]{3,2,1,0:T(8,128)}, f32[2,16,16,256]{3,2,1,0:T(8,128)S(1)}, u32[]{:S(2)}) copy-start(f32[2,16,16,256]{3,2,1,0:T(8,128)S(1)} %fusion.17) | copy-start | bytes 1572868
  61.5 1.9 %copy-start.2 = (bf16[768,768]{1,0:T(8,128)(2,1)S(1)}, bf16[768,768]{1,0:T(8,128)(2,1)}, u32[]{:S(2)}) copy-start(bf16[768,768]{1,0:T(8,128)(2,1)} %param.30) | copy-start | bytes 3538948

commit v2 on v1

--- a/solution.py
+++ b/solution.py
@@ -1,6 +1,11 @@
+import functools
+import math
+
 import jax
 import jax.numpy as jnp
 from jax import lax
+from jax.experimental import pallas as pl
+from jax.experimental.pallas import tpu as pltpu
 from jax.sharding import PartitionSpec as P
 
 ATOM_HEADS = 4
@@ -25,6 +30,79 @@
     count = lax.axis_size(axis)
     route = [(i, i + step) for i in range(count) if 0 <= i + step < count]
     return lax.ppermute(block, axis, route)
+
+
+def atom_kernel(
+    ext_ref,
+    keep_ref,
+    wq_ref,
+    wk_ref,
+    wv_ref,
+    wo_ref,
+    wt_ref,
+    onehot_ref,
+    count_ref,
+    token_ref,
+    atom_ref,
+    state_ref,
+    *,
+    atom_dev,
+    blocks,
+    low_rows,
+    span,
+    head_dim,
+):
+    f32, bf16 = jnp.float32, jnp.bfloat16
+    samples, _, width = ext_ref.shape
+    rows = blocks * QBLOCK
+    lane = lax.broadcasted_iota(jnp.int32, (1, width), 1) // head_dim
+    head_masks = [(lane == h).astype(f32) for h in range(ATOM_HEADS)]
+    root = jnp.float32(math.sqrt(head_dim))
+    onehot = onehot_ref[...].astype(bf16)
+    counts = count_ref[...]
+    for s in range(samples):
+        x = ext_ref[s].astype(f32)
+        mean = jnp.mean(x, axis=-1, keepdims=True)
+        var = jnp.mean((x - mean) ** 2, axis=-1, keepdims=True)
+        xn = ((x - mean) / jnp.sqrt(var + 1e-05)).astype(bf16)
+        q = jnp.dot(xn[low_rows : low_rows + rows], wq_ref[...], preferred_element_type=f32)
+        q = q.astype(bf16)
+        k = jnp.dot(xn, wk_ref[...], preferred_element_type=f32).astype(bf16)
+        v = jnp.dot(xn, wv_ref[...], preferred_element_type=f32).astype(bf16)
+        pieces = []
+        for j in range(blocks):
+            qj = q[j * QBLOCK : (j + 1) * QBLOCK]
+            kj = k[j * QBLOCK : j * QBLOCK + span]
+            vj = v[j * QBLOCK : j * QBLOCK + span]
+            keep = keep_ref[j : j + 1, :] > 0.5
+            acc = jnp.zeros((QBLOCK, width), f32)
+            for h in range(ATOM_HEADS):
+                qh = qj * head_masks[h].astype(bf16)
+                sc = lax.dot_general(
+                    qh, kj, (((1,), (1,)), ((), ())), preferred_element_type=f32
+                ) / root
+                sc = jnp.where(keep, sc, -1e30)
+                top = jnp.max(sc, axis=-1, keepdims=True)
+                e = jnp.where(keep, jnp.exp(sc - top), 0.0)
+                tot = jnp.sum(e, axis=-1, keepdims=True)
+                o = jnp.dot(e.astype(bf16), vj, preferred_element_type=f32)
+                acc = acc + (o / tot) * head_masks[h]
+            pieces.append(acc.astype(bf16))
+        mixed = jnp.concatenate(pieces, axis=0)
+        base = x[low_rows : low_rows + rows]
+        out = (base + jnp.dot(mixed, wo_ref[...], preferred_element_type=f32)).astype(bf16)
+        atom_ref[s] = out[:atom_dev]
+        hidden = jnp.maximum(jnp.dot(out, wt_ref[...], preferred_element_type=f32), 0.0)
+        top_part = hidden.astype(bf16)
+        rest = hidden - top_part.astype(f32)
+        mid_part = rest.astype(bf16)
+        low_part = (rest - mid_part.astype(f32)).astype(bf16)
+        sums = (
+            jnp.dot(onehot, top_part, preferred_element_type=f32)
+            + jnp.dot(onehot, mid_part, preferred_element_type=f32)
+            + jnp.dot(onehot, low_part, preferred_element_type=f32)
+        )
+        state_ref[s] = (token_ref[s].astype(f32) + sums / counts).astype(bf16)
 
 
 def on_device(
@@ -69,17 +147,8 @@
     next_shift = upper[high_rows, 0, 0].astype(jnp.int32)
     upper = upper[:high_rows]
 
-    w_qkv = jnp.concatenate([w_atom_query, w_atom_key, w_atom_value], axis=1)
-    w_kv = jnp.concatenate([w_atom_key, w_atom_value], axis=1)
-    own_p = project(layer_norm(atom_feat).astype(jnp.bfloat16), w_qkv).astype(jnp.bfloat16)
-    low_p = project(layer_norm(low).astype(jnp.bfloat16), w_kv).astype(jnp.bfloat16)
-    high_p = project(layer_norm(upper).astype(jnp.bfloat16), w_qkv).astype(jnp.bfloat16)
-    query = jnp.concatenate([own_p[..., :width], high_p[:QBLOCK, :, :width]], axis=0)
-    kv = jnp.concatenate([low_p, own_p[..., width:], high_p[..., width:]], axis=0)
-
     head_dim = width // ATOM_HEADS
     shifts = jnp.concatenate([window_shift, next_shift[None]], axis=0)
-    kwin = jnp.stack([kv[j * QBLOCK : j * QBLOCK + span] for j in range(blocks)], axis=0)
     position = jnp.arange(span, dtype=jnp.int32)
     first = (SHIFT + shifts)[:, None]
     absolute = (
@@ -94,36 +163,59 @@
         & (absolute >= 0)
         & (absolute < total_atoms)
     )
-    qblock = query.reshape(blocks, QBLOCK, samples, ATOM_HEADS, head_dim)
-    kblock = kwin[..., :width].reshape(blocks, span, samples, ATOM_HEADS, head_dim)
-    vblock = kwin[..., width:].reshape(blocks, span, samples, ATOM_HEADS, head_dim)
-    scores = jnp.einsum(
-        "bqshd,bkshd->bshqk", qblock, kblock, preferred_element_type=jnp.float32
-    ) / jnp.sqrt(jnp.float32(head_dim))
-    keep = valid[:, None, None, None, :]
-    scores = jnp.where(keep, scores, -1e30)
-    top = jnp.max(scores, axis=-1, keepdims=True)
-    expo = jnp.where(keep, jnp.exp(scores - top), 0.0)
-    total = jnp.sum(expo, axis=-1)
-    mixed = jnp.einsum(
-        "bshqk,bkshd->bqshd", expo.astype(jnp.bfloat16), vblock, preferred_element_type=jnp.float32
-    )
-    mixed = mixed / jnp.transpose(total, (0, 3, 1, 2))[..., None]
     rows = blocks * QBLOCK
-    mixed = mixed.astype(jnp.bfloat16).reshape(rows, samples, width)
-    feat = jnp.concatenate([atom_feat, upper[:QBLOCK]], axis=0)
-    atom_rows = (feat.astype(jnp.float32) + project(mixed, w_atom_out)).astype(jnp.bfloat16)
-    atom_out = atom_rows[:atom_dev]
-
     own_ids = rank * tok_dev + jnp.arange(tok_dev, dtype=jnp.int32)
     row_ids = lax.dynamic_slice_in_dim(
         jnp.concatenate([atom_token, jnp.full((QBLOCK,), -1, jnp.int32)]), atom_base, rows
     )
-    hidden = jax.nn.relu(project(atom_rows, w_to_token))
     onehot = (own_ids[:, None] == row_ids[None, :]).astype(jnp.float32)
-    counts = jnp.sum(onehot, axis=1)
-    sums = jnp.einsum("ta,asd->tsd", onehot, hidden, precision=high)
-    state = (token_in.astype(jnp.float32) + sums / counts[:, None, None]).astype(jnp.bfloat16)
+    counts = jnp.sum(onehot, axis=1, keepdims=True)
+    extended = jnp.transpose(jnp.concatenate([low, atom_feat, upper], axis=0), (1, 0, 2))
+    kernel = functools.partial(
+        atom_kernel,
+        atom_dev=atom_dev,
+        blocks=blocks,
+        low_rows=low_rows,
+        span=span,
+        head_dim=head_dim,
+    )
+    vmem = pl.BlockSpec(memory_space=pltpu.VMEM)
+    ext_rows = extended.shape[1]
+    flops = 2 * samples * (
+        ext_rows * width * 3 * width
+        + rows * width * (width + tok_width)
+        + blocks * ATOM_HEADS * QBLOCK * span * width * 2
+        + 3 * tok_dev * rows * tok_width
+    )
+    atom_t, state_t = pl.pallas_call(
+        kernel,
+        out_shape=(
+            jax.ShapeDtypeStruct((samples, atom_dev, width), jnp.bfloat16),
+            jax.ShapeDtypeStruct((samples, tok_dev, tok_width), jnp.bfloat16),
+        ),
+        in_specs=[vmem] * 10,
+        out_specs=(vmem, vmem),
+        cost_estimate=pl.CostEstimate(
+            flops=flops,
+            transcendentals=samples * blocks * ATOM_HEADS * QBLOCK * span,
+            bytes_accessed=2 * (ext_rows + atom_dev) * samples * width
+            + 2 * width * (3 * width + width + tok_width)
+            + 4 * samples * tok_dev * tok_width,
+        ),
+    )(
+        extended,
+        valid.astype(jnp.float32),
+        w_atom_query,
+        w_atom_key,
+        w_atom_value,
+        w_atom_out,
+        w_to_token,
+        onehot,
+        counts,
+        jnp.transpose(token_in, (1, 0, 2)),
+    )
+    atom_out = jnp.transpose(atom_t, (1, 0, 2))
+    state = jnp.transpose(state_t, (1, 0, 2))
 
     tdim = tok_width // TOKEN_HEADS
     tq = project(layer_norm(state).astype(jnp.bfloat16), w_query).astype(jnp.bfloat16)

time: 65.1 us -> 65.4 us (level)
  Pallas kernels: 0 us -> 12.8 us
  matrix products: 12 us -> 5.74 us
  local copies, waits for them, and re-layouts: 11.7 us -> 8.85 us
  other arithmetic: 8.99 us -> 6.27 us
    pallas_call x0 -> x1, Pallas kernels: none -> 12.8 us  [on_device(): pl.pallas_call(kernel, out_shape=(jax.ShapeDtypeStruct((samples, atom_dev...]
    dot_general x3 -> x0, matrix products: 3.77 us -> none  [the longest x1 1.94 us: on_device(): jnp.einsum('bshqk,bkshd->bqshd', expo.astype(jnp.bfloat16), vblock, prefe...]
    dot_general x8 -> x3, matrix products: 3.99 us -> 2.2 us  [project(): jnp.einsum('asc,cd->asd', values, weight, preferred_element_type=jnp.floa...]
    reduce_sum x5 -> x2, other arithmetic: 2.14 us -> 0.54 us  [layer_norm(): var = jnp.mean((values - mean) ** 2, axis=-1, keepdims=True)]
    slice x10 -> x1, local copies, waits for them, and re-layouts: 1.42 us -> 0.01 us  [on_device(): upper = upper[:high_rows]]
    sub x1 -> x0, matrix products: 1.27 us -> none  [on_device(): expo = jnp.where(keep, jnp.exp(scores - top), 0.0)]
    convert_element_type x1 -> x0, local copies, waits for them, and re-layouts: 1.22 us -> none  [on_device(): mixed = mixed.astype(jnp.bfloat16).reshape(rows, samples, width)]
    unnamed x55 -> x22, local copies, waits for them, and re-layouts: 3.9 us -> 4.72 us
  transfers between devices with their start and end apart: 2 -> 2, of which waited for: 0 -> 0; matrix products, arithmetic and copies ran while one was open for 15% -> 10% of each run, Pallas kernels for 0% -> 0%
where the time goes in v2:
time: 65.4 us; the launch traced here: 65 us
  blocking collectives  25.5 us (39%)
  Pallas kernels  12.8 us (20%)
  local copies, waits for them, and re-layouts  8.85 us (14%)
  other arithmetic  6.27 us (10%)
  matrix products  5.74 us (9%)
  starting transfers between devices  4.32 us (7%)
  between operations  1.55 us (2%)
    all_gather x1, blocking collectives, on_device(): every = lax.all_gather(state, 'row', axis=0, tiled=True)  25.5 us
    pallas_call x1, Pallas kernels, on_device(): pl.pallas_call(kernel, out_shape=(jax.ShapeDtypeStruct((samples, atom_dev...  12.8 us
    unnamed x22, local copies, waits for them, and re-layouts  4.72 us
    ppermute x2, starting transfers between devices, shifted(): return lax.ppermute(block, axis, route)  4.32 us
    dot_general x3, matrix products, project(): jnp.einsum('asc,cd->asd', values, weight, preferred_element_type=jnp.floa...  2.2 us
    dot_general x1, matrix products, on_device(): jnp.einsum('shqk,kshd->shqd', expo_t.astype(jnp.bfloat16), vheads, prefer...  1.69 us
    dot_general x1, matrix products, on_device(): jnp.einsum('qkc,ch->hqk', pair, w_bias, preferred_element_type=jnp.float32)  1.61 us
  transfers between devices with their start and end apart: 2, of which 0 were waited for; matrix products, arithmetic and copies ran while one was open for 10% of the time, Pallas kernels for 0%

profile of v2, /device:TPU:0, one launch (start us, length us, event | category | flops | bytes accessed | tf_op | source)
XLA Modules:
  0.0 65.0 jit_solution(13216155926495091417)
XLA Ops:
  0.6 0.0 copy-start
  0.6 0.0 copy-start.6
  0.7 0.0 copy-start.5
  0.7 1.0 %copy.29 = bf16[128,2,128]{2,0,1:T(8,128)(2,1)S(1)} copy(bf16[128,2,128]{2,1,0:T(2,128)(2,1)} %param.16) | data formatting | bytes 131072 | tf_op args[0]
  1.6 0.7 %convert.4 = bf16[4]{0:T(256)(128)(2,1)S(1)} convert(s32[4]{0:T(128)} %param.17) | non-fusion elementwise | flops 4 | bytes 24 | tf_op jit(solution)/shard_map/convert.1
  2.3 0.8 %slice_select_fusion = bf16[97,2,128]{2,0,1:T(8,128)(2,1)S(1)} fusion(bf16[128,2,128]{2,0,1:T(8,128)(2,1)S(1)} %copy.29, pred[97]{0:T(512)(128)(4,1)} %constant.17.clone.1, bf16[]{:T(256)S(1)} %bitcast.64), kind=kLoop, calls=%fused_computation.38 | loop fusion | flops 24832 | bytes 99427 | tf_op jit(solution)/shard_map/concatenate | solution.py:145
  3.1 1.3 %collective-permute-start.1 = (bf16[97,2,128]{2,0,1:T(8,128)(2,1)S(1)}, bf16[97,2,128]{2,0,1:T(8,128)(2,1)S(1)}, u32[]{:S(2)}, u32[]{:S(2)}) collective-permute-start(bf16[97,2,128]{2,0,1:T(8,128)(2,1)S(1)} %slice_select_fusion), channel_id=1, source_target_pairs={{1,0},{2,1},{3,2},{4,3},{5,4},{6,5},{7,6},{8,7},{9,8},{10,9},{11,1... | collective-permute-start | bytes 149000 | tf_op jit(solution)/shard_map/ppermute | solution.py:32
  4.4 3.0 %collective-permute-start = (bf16[64,2,128]{2,0,1:T(8,128)(2,1)S(1)}, bf16[64,2,128]{2,0,1:T(8,128)(2,1)S(1)}, u32[]{:S(2)}, u32[]{:S(2)}) collective-permute-start(bf16[64,2,128]{2,0,1:T(8,128)(2,1)S(1)} %slice.30), channel_id=1, source_target_pairs={{0,1},{1,2},{2,3},{3,4},{4,5},{5,6},{6,7},{7,8},{8,9},{9,10},{10,1... | collective-permute-start | bytes 98312 | tf_op jit(solution)/shard_map/ppermute | solution.py:32
  7.4 0.8 %pad_dynamic-slice_fusion = s32[160]{0:T(256)S(1)} fusion(s32[]{:T(128)S(6)} %select_n.10, s32[2048]{0:T(1024)} %param.18), kind=kLoop, calls=%fused_computation.43 | loop fusion | bytes 8836 | tf_op jit(solution)/shard_map/dynamic_slice | solution.py:168
  8.2 0.7 %compare_convert_fusion.onehot_ref = f32[16,160]{1,0:T(8,128)} fusion(s32[160]{0:T(256)S(1)} %pad_dynamic-slice_fusion, s32[16]{0:T(128)S(1)} %iota_add_fusion.1), kind=kLoop, calls=%fused_computation.42 | loop fusion | flops 5120 | bytes 10944 | tf_op jit(solution)/shard_map/convert_element_type | solution.py:171
  8.9 0.2 fusion.45
  9.1 0.7 %broadcast_compare_fusion = pred[256]{0:T(512)(128)(4,1)S(1)} fusion(s32[256]{0:T(256)} %param.21), kind=kLoop, calls=%fused_computation.62 | loop fusion | flops 256 | bytes 1280 | tf_op jit(solution)/shard_map/gt | solution.py:232
  9.8 1.6 %fusion.46 = f32[16,16,256]{2,0,1:T(8,128)S(1)} fusion(bf16[16,256,128]{2,1,0:T(8,128)(2,1)} %param.20, bf16[128,16]{0,1:T(8,128)(2,1)} %param.31), kind=kOutput, calls=%fused_computation.54 | convolution fusion | flops 16777216 | bytes 1314816 | tf_op jit(solution)/shard_map/qkc,ch->hqk/dot_general | solution.py:223
  11.4 0.7 %copy.33.count_ref = f32[16,1]{1,0:T(8,128)} copy(f32[16,1]{0,1:T(1,128)S(1)} %bitcast.63) | data formatting | bytes 128 | tf_op jit(solution)/shard_map/broadcast_in_dim | solution.py:172
  12.1 0.0 copy-done.5
  12.1 0.6 copy.44
  12.7 0.2 copy.36
  12.9 0.0 collective-permute-done.1
  12.9 0.6 slice.33
  14.2 0.0 copy-done.6
  14.2 0.1 broadcast_add_fusion.1
  14.3 0.7 %fusion.44.keep_ref = f32[5,160]{1,0:T(8,128)} fusion(s32[5]{0:T(128)S(1)} %add_add_fusion, s32[5]{0:T(128)S(1)} %get-tuple-element.13, s32[5]{0:T(128)S(1)} %get-tuple-element.12), kind=kLoop, calls=%fused_computation.52 | loop fusion | flops 7200 | bytes 3260 | tf_op jit(solution)/shard_map/convert_element_type | solution.py:207
  14.9 0.0 collective-permute-done
  14.9 0.7 %maximum_bitcast_fusion.2.ext_ref = bf16[2,288,128]{2,1,0:T(8,128)(2,1)} fusion(bf16[96,2,128]{2,0,1:T(8,128)(2,1)S(1)} %slice.32, bf16[128,2,128]{2,0,1:T(8,128)(2,1)S(1)} %copy.29, bf16[64,2,128]{2,0,1:T(8,128)(2,1)S(1)} %collective-permute-done), kind=kLoop, calls=%fused_computation.32 | loop fusion | flops 442368 | bytes 294912 | tf_op jit(solution)/shard_map/transpose | solution.py:173
  15.6 0.0 copy-start.7
  15.6 12.8 %shard_map.167 = (bf16[2,128,128]{2,1,0:T(8,128)(2,1)}, bf16[2,16,768]{2,1,0:T(8,128)(2,1)}) custom-call(bf16[2,288,128]{2,1,0:T(8,128)(2,1)} %maximum_bitcast_fusion.2.ext_ref, f32[5,160]{1,0:T(8,128)} %fusion.44.keep_ref, bf16[128,128]{1,0:T(8,128)(2,1)} %wq_ref.1, bf16[128,128]{1,0:T(8,128)(2,1)} %wk_ref.1, bf16[128,128]{1,0:T(8,128)(2,1)} %wv_ref.1, ...), custom_call_target="tpu_custom_call" | custom-call | flops 258473984 | bytes 638976 | tf_op jit(solution)/shard_map/pallas_call | solution.py:190
  28.4 0.0 copy-start.8
  28.4 1.6 %copy.39 = bf16[128,2,128]{2,1,0:T(2,128)(2,1)} copy(bf16[128,2,128]{2,0,1:T(8,128)(2,1)} %bitcast.61) | data formatting | bytes 131072
  30.0 0.9 %convert_reduce_fusion.1 = f32[16,2]{0,1:T(2,128)S(1)} fusion(bf16[2,16,768]{2,1,0:T(8,128)(2,1)} %get-tuple-element.5), kind=kLoop, calls=%fused_computation.31 | loop fusion | flops 49120 | bytes 49280 | tf_op jit(solution)/shard_map/reduce_sum | solution.py:20
  30.9 25.5 %all_gather.3 = bf16[256,2,768]{2,0,1:T(8,128)(2,1)S(1)} all-gather(bf16[16,2,768]{2,0,1:T(8,128)(2,1)} %bitcast.59), channel_id=1, replica_groups=mesh['groups'=2,'row'=16] {'row'}, dimensions={0}, use_global_device_ids=true | all-gather | bytes 835584 | tf_op jit(solution)/shard_map/all_gather | solution.py:226
  56.4 0.2 convert_reduce_fusion
  56.6 0.4 fusion.5
  57.0 0.0 copy-done.7
  57.0 0.0 copy-done.8
  57.0 1.5 %convolution_convert_fusion = bf16[256,2,1536]{2,0,1:T(8,128)(2,1)S(1)} fusion(bf16[768,768]{1,0:T(8,128)(2,1)S(1)} %copy-done.7, bf16[768,768]{1,0:T(8,128)(2,1)S(1)} %copy-done.8, bf16[256,2,768]{2,0,1:T(8,128)(2,1)S(1)} %all_gather.3, f32[256,2]{0,1:T(2,128)S(1)} %add_sqrt_fusion, f32[256,2]{0,1:T(2,128)S(1)} %broadcast_multiply_fusion), kind=kOutput, calls=%fused_computation.1 | convolution fusion | flops 1215037440 | bytes 4722688 | tf_op jit(solution)/shard_map/asc,cd->asd/dot_general | solution.py:26
  58.5 0.1 fusion.52
  58.6 0.0 copy-start.1
  58.6 1.2 %copy.37 = bf16[256,2,768]{0,2,1:T(8,128)(2,1)} copy(bf16[256,2,768]{2,0,1:T(8,128)(2,1)S(1)} %get-tuple-element.11) | data formatting | bytes 1572864 | tf_op jit(solution)/shard_map/slice | solution.py:231
  59.8 0.3 copy.34
  60.1 0.0 copy-done.1
  60.1 0.2 fusion.34
  60.2 0.0 copy-done
  60.2 0.4 fusion.24
  60.6 0.0 copy-start.3
  60.6 0.2 reshape.95
  60.8 0.2 fusion.11
  61.0 0.0 copy-start.4
  61.1 0.8 %copy-done.4 = f32[2,16,16,256]{3,2,1,0:T(8,128)} copy-done((f32[2,16,16,256]{3,2,1,0:T(8,128)}, f32[2,16,16,256]{3,2,1,0:T(8,128)S(1)}, u32[]{:S(2)}) %copy-start.4) | copy-done | bytes 524312
  61.8 0.0 copy-start.2
  61.8 0.2 fusion.53
  62.1 0.0 copy-done.3
  62.1 1.7 %fusion.17 = bf16[16,2,16,48]{3,0,2,1:T(8,128)(2,1)S(1)} fusion(bf16[256,2,16,48]{0,3,2,1:T(8,128)(2,1)S(1)} %bitcast.60, f32[16,2,16]{0,2,1:T(8,128)S(1)} %bitcast.65, f32[2,16,16,256]{3,2,1,0:T(8,128)} %copy-done.4, pred[256]{0:T(512)(128)(4,1)S(1)} %broadcast_compare_fusion), kind=kOutput, calls=%fused_computation.23 | convolution fusion | flops 13026047 | bytes 1362176 | tf_op jit(solution)/shard_map/shqk,kshd->shqd/dot_general | solution.py:241
  63.8 0.2 reshape.98
  64.0 0.0 copy-done.2
  64.0 0.3 fusion.21
  64.3 0.7 %copy.40 = bf16[16,2,768]{2,1,0:T(2,128)(2,1)} copy(bf16[16,2,768]{2,0,1:T(8,128)(2,1)S(1)} %fusion.21) | data formatting | bytes 98304
  (9 shorter events, 0.1 us)
Async XLA Ops:
  0.6 59.6 %copy-start = (bf16[768,768]{1,0:T(8,128)(2,1)S(1)}, bf16[768,768]{1,0:T(8,128)(2,1)}, u32[]{:S(2)}) copy-start(bf16[768,768]{1,0:T(8,128)(2,1)} %param.27) | copy-start | bytes 3538948
  0.6 13.5 %copy-start.6 = (s32[4]{0:T(128)S(1)}, s32[4]{0:T(128)}, u32[]{:S(2)}) copy-start(s32[4]{0:T(128)} %param.17) | copy-start | bytes 52
  0.7 11.4 %copy-start.5 = (bf16[16,2,768]{2,1,0:T(2,128)(2,1)S(1)}, bf16[16,2,768]{2,1,0:T(2,128)(2,1)}, u32[]{:S(2)}) copy-start(bf16[16,2,768]{2,1,0:T(2,128)(2,1)} %param.19) | copy-start | bytes 147460
  3.1 9.8 %collective-permute-start.1 = (bf16[97,2,128]{2,0,1:T(8,128)(2,1)S(1)}, bf16[97,2,128]{2,0,1:T(8,128)(2,1)S(1)}, u32[]{:S(2)}, u32[]{:S(2)}) collective-permute-start(bf16[97,2,128]{2,0,1:T(8,128)(2,1)S(1)} %slice_select_fusion), channel_id=1, source_target_pairs={{1,0},{2,1},{3,2},{4,3},{5,4},{6,5},{7,6},{8,7},{9,8},{10,9},{11,1... | collective-permute-start | bytes 149000 | tf_op jit(solution)/shard_map/ppermute | solution.py:32
  4.4 10.6 %collective-permute-start = (bf16[64,2,128]{2,0,1:T(8,128)(2,1)S(1)}, bf16[64,2,128]{2,0,1:T(8,128)(2,1)S(1)}, u32[]{:S(2)}, u32[]{:S(2)}) collective-permute-start(bf16[64,2,128]{2,0,1:T(8,128)(2,1)S(1)} %slice.30), channel_id=1, source_target_pairs={{0,1},{1,2},{2,3},{3,4},{4,5},{5,6},{6,7},{7,8},{8,9},{9,10},{10,1... | collective-permute-start | bytes 98312 | tf_op jit(solution)/shard_map/ppermute | solution.py:32
  15.6 41.4 %copy-start.7 = (bf16[768,768]{1,0:T(8,128)(2,1)S(1)}, bf16[768,768]{1,0:T(8,128)(2,1)}, u32[]{:S(2)}) copy-start(bf16[768,768]{1,0:T(8,128)(2,1)} %param.29) | copy-start | bytes 3538948
  28.4 28.6 %copy-start.8 = (bf16[768,768]{1,0:T(8,128)(2,1)S(1)}, bf16[768,768]{1,0:T(8,128)(2,1)}, u32[]{:S(2)}) copy-start(bf16[768,768]{1,0:T(8,128)(2,1)} %param.28) | copy-start | bytes 3538948
  58.6 1.4 %copy-start.1 = (bf16[2,16,768]{2,1,0:T(8,128)(2,1)S(1)}, bf16[2,16,768]{2,1,0:T(8,128)(2,1)}, u32[]{:S(2)}) copy-start(bf16[2,16,768]{2,1,0:T(8,128)(2,1)} %get-tuple-element.5) | copy-start | bytes 147460
  60.6 1.5 %copy-start.3 = (bf16[256,2,768]{0,2,1:T(8,128)(2,1)S(1)}, bf16[256,2,768]{0,2,1:T(8,128)(2,1)}, u32[]{:S(2)}) copy-start(bf16[256,2,768]{0,2,1:T(8,128)(2,1)} %copy.37) | copy-start | bytes 2359300
  61.0 0.8 %copy-start.4 = (f32[2,16,16,256]{3,2,1,0:T(8,128)}, f32[2,16,16,256]{3,2,1,0:T(8,128)S(1)}, u32[]{:S(2)}) copy-start(f32[2,16,16,256]{3,2,1,0:T(8,128)S(1)} %fusion.11) | copy-start | bytes 1572868
  61.8 2.2 %copy-start.2 = (bf16[768,768]{1,0:T(8,128)(2,1)S(1)}, bf16[768,768]{1,0:T(8,128)(2,1)}, u32[]{:S(2)}) copy-start(bf16[768,768]{1,0:T(8,128)(2,1)} %param.30) | copy-start | bytes 3538948

commit v3 on v2

--- a/solution.py
+++ b/solution.py
@@ -34,32 +34,33 @@
 
 def atom_kernel(
     ext_ref,
-    keep_ref,
+    bounds_ref,
     wq_ref,
     wk_ref,
     wv_ref,
     wo_ref,
     wt_ref,
-    onehot_ref,
-    count_ref,
+    row_ids_ref,
+    own_ids_ref,
     token_ref,
     atom_ref,
     state_ref,
     *,
     atom_dev,
-    blocks,
+    rows,
     low_rows,
-    span,
     head_dim,
 ):
     f32, bf16 = jnp.float32, jnp.bfloat16
-    samples, _, width = ext_ref.shape
-    rows = blocks * QBLOCK
+    samples, ext_rows, width = ext_ref.shape
     lane = lax.broadcasted_iota(jnp.int32, (1, width), 1) // head_dim
     head_masks = [(lane == h).astype(f32) for h in range(ATOM_HEADS)]
     root = jnp.float32(math.sqrt(head_dim))
-    onehot = onehot_ref[...].astype(bf16)
-    counts = count_ref[...]
+    column = lax.broadcasted_iota(jnp.int32, (rows, ext_rows), 1)
+    keep = (column >= bounds_ref[:, 0:1]) & (column < bounds_ref[:, 1:2])
+    onehot = (own_ids_ref[...] == row_ids_ref[...]).astype(f32)
+    counts = jnp.sum(onehot, axis=1, keepdims=True)
+    onehot = onehot.astype(bf16)
     for s in range(samples):
         x = ext_ref[s].astype(f32)
         mean = jnp.mean(x, axis=-1, keepdims=True)
@@ -69,26 +70,19 @@
         q = q.astype(bf16)
         k = jnp.dot(xn, wk_ref[...], preferred_element_type=f32).astype(bf16)
         v = jnp.dot(xn, wv_ref[...], preferred_element_type=f32).astype(bf16)
-        pieces = []
-        for j in range(blocks):
-            qj = q[j * QBLOCK : (j + 1) * QBLOCK]
-            kj = k[j * QBLOCK : j * QBLOCK + span]
-            vj = v[j * QBLOCK : j * QBLOCK + span]
-            keep = keep_ref[j : j + 1, :] > 0.5
-            acc = jnp.zeros((QBLOCK, width), f32)
-            for h in range(ATOM_HEADS):
-                qh = qj * head_masks[h].astype(bf16)
-                sc = lax.dot_general(
-                    qh, kj, (((1,), (1,)), ((), ())), preferred_element_type=f32
-                ) / root
-                sc = jnp.where(keep, sc, -1e30)
-                top = jnp.max(sc, axis=-1, keepdims=True)
-                e = jnp.where(keep, jnp.exp(sc - top), 0.0)
-                tot = jnp.sum(e, axis=-1, keepdims=True)
-                o = jnp.dot(e.astype(bf16), vj, preferred_element_type=f32)
-                acc = acc + (o / tot) * head_masks[h]
-            pieces.append(acc.astype(bf16))
-        mixed = jnp.concatenate(pieces, axis=0)
+        acc = jnp.zeros((rows, width), f32)
+        for h in range(ATOM_HEADS):
+            qh = q * head_masks[h].astype(bf16)
+            sc = lax.dot_general(
+                qh, k, (((1,), (1,)), ((), ())), preferred_element_type=f32
+            ) / root
+            sc = jnp.where(keep, sc, -1e30)
+            top = jnp.max(sc, axis=-1, keepdims=True)
+            e = jnp.where(keep, jnp.exp(sc - top), 0.0)
+            tot = jnp.sum(e, axis=-1, keepdims=True)
+            o = jnp.dot(e.astype(bf16), v, preferred_element_type=f32)
+            acc = acc + (o / tot) * head_masks[h]
+        mixed = acc.astype(bf16)
         base = x[low_rows : low_rows + rows]
         out = (base + jnp.dot(mixed, wo_ref[...], preferred_element_type=f32)).astype(bf16)
         atom_ref[s] = out[:atom_dev]
@@ -149,42 +143,30 @@
 
     head_dim = width // ATOM_HEADS
     shifts = jnp.concatenate([window_shift, next_shift[None]], axis=0)
-    position = jnp.arange(span, dtype=jnp.int32)
-    first = (SHIFT + shifts)[:, None]
-    absolute = (
-        atom_base
-        + jnp.arange(blocks, dtype=jnp.int32)[:, None] * QBLOCK
-        - low_rows
-        + position[None, :]
-    )
-    valid = (
-        (position[None, :] >= first)
-        & (position[None, :] < first + KWIN)
-        & (absolute >= 0)
-        & (absolute < total_atoms)
-    )
     rows = blocks * QBLOCK
+    ext_rows = low_rows + atom_dev + high_rows
+    row_block = jnp.arange(rows, dtype=jnp.int32) // QBLOCK
+    first = row_block * QBLOCK + SHIFT + jnp.repeat(shifts, QBLOCK)
+    bounds = jnp.stack(
+        [
+            jnp.maximum(first, low_rows - atom_base),
+            jnp.minimum(first + KWIN, total_atoms - atom_base + low_rows),
+        ],
+        axis=1,
+    )
     own_ids = rank * tok_dev + jnp.arange(tok_dev, dtype=jnp.int32)
     row_ids = lax.dynamic_slice_in_dim(
         jnp.concatenate([atom_token, jnp.full((QBLOCK,), -1, jnp.int32)]), atom_base, rows
     )
-    onehot = (own_ids[:, None] == row_ids[None, :]).astype(jnp.float32)
-    counts = jnp.sum(onehot, axis=1, keepdims=True)
     extended = jnp.transpose(jnp.concatenate([low, atom_feat, upper], axis=0), (1, 0, 2))
     kernel = functools.partial(
-        atom_kernel,
-        atom_dev=atom_dev,
-        blocks=blocks,
-        low_rows=low_rows,
-        span=span,
-        head_dim=head_dim,
+        atom_kernel, atom_dev=atom_dev, rows=rows, low_rows=low_rows, head_dim=head_dim
     )
     vmem = pl.BlockSpec(memory_space=pltpu.VMEM)
-    ext_rows = extended.shape[1]
     flops = 2 * samples * (
         ext_rows * width * 3 * width
         + rows * width * (width + tok_width)
-        + blocks * ATOM_HEADS * QBLOCK * span * width * 2
+        + ATOM_HEADS * rows * ext_rows * width * 2
         + 3 * tok_dev * rows * tok_width
     )
     atom_t, state_t = pl.pallas_call(
@@ -197,21 +179,21 @@
         out_specs=(vmem, vmem),
         cost_estimate=pl.CostEstimate(
             flops=flops,
-            transcendentals=samples * blocks * ATOM_HEADS * QBLOCK * span,
+            transcendentals=samples * ATOM_HEADS * rows * ext_rows,
             bytes_accessed=2 * (ext_rows + atom_dev) * samples * width
             + 2 * width * (3 * width + width + tok_width)
             + 4 * samples * tok_dev * tok_width,
         ),
     )(
         extended,
-        valid.astype(jnp.float32),
+        bounds,
         w_atom_query,
         w_atom_key,
         w_atom_value,
         w_atom_out,
         w_to_token,
-        onehot,
-        counts,
+        row_ids[None, :],
+        own_ids[:, None],
         jnp.transpose(token_in, (1, 0, 2)),
     )
     atom_out = jnp.transpose(atom_t, (1, 0, 2))

time: 65.4 us -> 57.4 us (0.88)
  Pallas kernels: 12.8 us -> 5.58 us
  other arithmetic: 6.27 us -> 5.36 us
    pallas_call x1, Pallas kernels: 12.8 us -> 5.58 us  [on_device(): pl.pallas_call(kernel, out_shape=(jax.ShapeDtypeStruct((samples, atom_dev...]
    convert_element_type x2 -> x0, other arithmetic: 1.35 us -> none  [the longest x1 0.68 us: on_device(): onehot = (own_ids[:, None] == row_ids[None, :]).astype(jnp.float32)]
    another operation x0 -> x1, local copies, waits for them, and re-layouts: none -> 0.75 us  [on_device(): jnp.stack([jnp.maximum(first, low_rows - atom_base), jnp.minimum(first +...]
    unnamed x22 -> x24, local copies, waits for them, and re-layouts: 4.72 us -> 4.75 us
where the time goes in v3:
time: 57.4 us; the launch traced here: 57.1 us
  blocking collectives  25.5 us (44%)
  local copies, waits for them, and re-layouts  8.99 us (16%)
  matrix products  5.75 us (10%)
  Pallas kernels  5.58 us (10%)
  other arithmetic  5.36 us (9%)
  starting transfers between devices  4.32 us (8%)
  between operations  1.57 us (3%)
    all_gather x1, blocking collectives, on_device(): every = lax.all_gather(state, 'row', axis=0, tiled=True)  25.5 us
    pallas_call x1, Pallas kernels, on_device(): pl.pallas_call(kernel, out_shape=(jax.ShapeDtypeStruct((samples, atom_dev...  5.58 us
    unnamed x24, local copies, waits for them, and re-layouts  4.75 us
    ppermute x2, starting transfers between devices, shifted(): return lax.ppermute(block, axis, route)  4.32 us
    dot_general x3, matrix products, project(): jnp.einsum('asc,cd->asd', values, weight, preferred_element_type=jnp.floa...  2.21 us
    dot_general x1, matrix products, on_device(): jnp.einsum('shqk,kshd->shqd', expo_t.astype(jnp.bfloat16), vheads, prefer...  1.69 us
    dot_general x1, matrix products, on_device(): jnp.einsum('qkc,ch->hqk', pair, w_bias, preferred_element_type=jnp.float32)  1.61 us
    slice x1, local copies, waits for them, and re-layouts, on_device(): vheads = tkv[..., tok_width:].reshape(count, samples, TOKEN_HEADS, tdim)  1.15 us
  transfers between devices with their start and end apart: 2, of which 0 were waited for; matrix products, arithmetic and copies ran while one was open for 10% of the time, Pallas kernels for 0%

profile of v3, /device:TPU:0, one launch (start us, length us, event | category | flops | bytes accessed | tf_op | source)
XLA Modules:
  0.0 57.1 jit_solution(432028243470507216)
XLA Ops:
  0.6 0.0 copy-start
  0.6 0.0 copy-start.9
  0.7 0.0 copy-start.6
  0.7 0.0 copy-start.5
  0.7 0.9 %copy.40 = bf16[128,2,128]{2,0,1:T(8,128)(2,1)S(1)} copy(bf16[128,2,128]{2,1,0:T(2,128)(2,1)} %param.16) | data formatting | bytes 131072 | tf_op args[0]
  1.6 0.7 %convert.4 = bf16[4]{0:T(256)(128)(2,1)S(1)} convert(s32[4]{0:T(128)} %param.17) | non-fusion elementwise | flops 4 | bytes 24 | tf_op jit(solution)/shard_map/convert.1
  2.3 0.8 %slice_select_fusion = bf16[97,2,128]{2,0,1:T(8,128)(2,1)S(1)} fusion(bf16[128,2,128]{2,0,1:T(8,128)(2,1)S(1)} %copy.40, pred[97]{0:T(512)(128)(4,1)} %constant.19.clone.1, bf16[]{:T(256)S(1)} %bitcast.64), kind=kLoop, calls=%fused_computation.38 | loop fusion | flops 24832 | bytes 99427 | tf_op jit(solution)/shard_map/concatenate | solution.py:139
  3.1 1.3 %collective-permute-start.1 = (bf16[97,2,128]{2,0,1:T(8,128)(2,1)S(1)}, bf16[97,2,128]{2,0,1:T(8,128)(2,1)S(1)}, u32[]{:S(2)}, u32[]{:S(2)}) collective-permute-start(bf16[97,2,128]{2,0,1:T(8,128)(2,1)S(1)} %slice_select_fusion), channel_id=1, source_target_pairs={{1,0},{2,1},{3,2},{4,3},{5,4},{6,5},{7,6},{8,7},{9,8},{10,9},{11,1... | collective-permute-start | bytes 149000 | tf_op jit(solution)/shard_map/ppermute | solution.py:32
  4.4 3.0 %collective-permute-start = (bf16[64,2,128]{2,0,1:T(8,128)(2,1)S(1)}, bf16[64,2,128]{2,0,1:T(8,128)(2,1)S(1)}, u32[]{:S(2)}, u32[]{:S(2)}) collective-permute-start(bf16[64,2,128]{2,0,1:T(8,128)(2,1)S(1)} %slice.30), channel_id=1, source_target_pairs={{0,1},{1,2},{2,3},{3,4},{4,5},{5,6},{6,7},{7,8},{8,9},{9,10},{10,1... | collective-permute-start | bytes 98312 | tf_op jit(solution)/shard_map/ppermute | solution.py:32
  7.4 0.6 %iota_add_fusion.own_ids_ref = s32[16,1]{1,0:T(8,128)} fusion(s32[]{:T(128)S(6)} %mul.29), kind=kLoop, calls=%fused_computation.43 | loop fusion | flops 16 | bytes 68 | tf_op jit(solution)/shard_map/add | solution.py:157
  8.0 0.7 %broadcast_compare_fusion = pred[256]{0:T(512)(128)(4,1)S(1)} fusion(s32[256]{0:T(256)} %param.21), kind=kLoop, calls=%fused_computation.61 | loop fusion | flops 256 | bytes 1280 | tf_op jit(solution)/shard_map/gt | solution.py:214
  8.7 1.6 %fusion.39 = f32[16,16,256]{2,0,1:T(8,128)S(1)} fusion(bf16[16,256,128]{2,1,0:T(8,128)(2,1)} %param.20, bf16[128,16]{0,1:T(8,128)(2,1)} %param.31), kind=kOutput, calls=%fused_computation.44 | convolution fusion | flops 16777216 | bytes 1314816 | tf_op jit(solution)/shard_map/qkc,ch->hqk/dot_general | solution.py:205
  10.3 0.0 copy-done.6
  10.3 0.7 %pad_dynamic-slice_fusion = s32[160]{0:T(256)} fusion(s32[]{:T(128)S(6)} %select_n.27, s32[2048]{0:T(1024)S(1)} %copy-done.6), kind=kLoop, calls=%fused_computation.42 | loop fusion | bytes 8836 | tf_op jit(solution)/shard_map/dynamic_slice | solution.py:158
  11.0 0.0 copy-done.5
  11.0 0.6 %copy.55 = bf16[16,2,768]{2,0,1:T(8,128)(2,1)} copy(bf16[16,2,768]{2,1,0:T(2,128)(2,1)S(1)} %copy-done.5) | data formatting | bytes 98304 | tf_op args[3]
  11.6 0.2 copy.47
  11.8 0.0 collective-permute-done.1
  11.8 0.6 %slice.33 = bf16[1,1,1]{2,0,1:T(2,128)(2,1)} slice(bf16[97,2,128]{2,0,1:T(8,128)(2,1)S(1)} %collective-permute-done.1), slice={[96:97], [0:1], [0:1]} | slice | bytes 4 | tf_op jit(solution)/shard_map/slice | solution.py:141
  13.1 0.0 copy-done.9
  13.1 0.1 pad_add_fusion.1
  13.2 0.1 broadcast_in_dim.43
  13.2 0.1 reshape.121
  13.4 0.8 %copy.44.bounds_ref = s32[160,2]{1,0:T(8,128)} copy(s32[160,2]{0,1:T(2,128)S(1)} %pad_add_fusion) | data formatting | bytes 2560 | tf_op jit(solution)/shard_map/stack | solution.py:150
  14.1 0.0 collective-permute-done
  14.1 0.7 %maximum_bitcast_fusion.2.ext_ref = bf16[2,288,128]{2,1,0:T(8,128)(2,1)} fusion(bf16[96,2,128]{2,0,1:T(8,128)(2,1)S(1)} %slice.32, bf16[128,2,128]{2,0,1:T(8,128)(2,1)S(1)} %copy.40, bf16[64,2,128]{2,0,1:T(8,128)(2,1)S(1)} %collective-permute-done), kind=kLoop, calls=%fused_computation.32 | loop fusion | flops 442368 | bytes 294912 | tf_op jit(solution)/shard_map/transpose | solution.py:161
  14.8 5.6 %shard_map.167 = (bf16[2,128,128]{2,1,0:T(8,128)(2,1)}, bf16[2,16,768]{2,1,0:T(8,128)(2,1)}) custom-call(bf16[2,288,128]{2,1,0:T(8,128)(2,1)} %maximum_bitcast_fusion.2.ext_ref, s32[160,2]{1,0:T(8,128)} %copy.44.bounds_ref, bf16[128,128]{1,0:T(8,128)(2,1)} %wq_ref.1, bf16[128,128]{1,0:T(8,128)(2,1)} %wk_ref.1, bf16[128,128]{1,0:T(8,128)(2,1)} %wv_ref.1, ...), custom_call_target="tpu_custom_call" | custom-call | flops 342360064 | bytes 638976 | tf_op jit(solution)/shard_map/pallas_call | solution.py:172
  20.4 0.0 copy-start.7
  20.4 0.0 copy-start.8
  20.4 1.7 %copy.50 = bf16[128,2,128]{2,1,0:T(2,128)(2,1)} copy(bf16[128,2,128]{2,0,1:T(8,128)(2,1)} %bitcast.61) | data formatting | bytes 131072
  22.1 0.9 %convert_reduce_fusion.1 = f32[16,2]{0,1:T(2,128)S(1)} fusion(bf16[2,16,768]{2,1,0:T(8,128)(2,1)} %get-tuple-element.5), kind=kLoop, calls=%fused_computation.31 | loop fusion | flops 49120 | bytes 49280 | tf_op jit(solution)/shard_map/reduce_sum | solution.py:20
  23.0 25.5 %all_gather.3 = bf16[256,2,768]{2,0,1:T(8,128)(2,1)S(1)} all-gather(bf16[16,2,768]{2,0,1:T(8,128)(2,1)} %bitcast.59), channel_id=1, replica_groups=mesh['groups'=2,'row'=16] {'row'}, dimensions={0}, use_global_device_ids=true | all-gather | bytes 835584 | tf_op jit(solution)/shard_map/all_gather | solution.py:208
  48.4 0.2 convert_reduce_fusion
  48.6 0.4 fusion.5
  49.0 0.0 copy-done.7
  49.0 0.0 copy-done.8
  49.0 1.5 %convolution_convert_fusion = bf16[256,2,1536]{2,0,1:T(8,128)(2,1)S(1)} fusion(bf16[768,768]{1,0:T(8,128)(2,1)S(1)} %copy-done.7, bf16[768,768]{1,0:T(8,128)(2,1)S(1)} %copy-done.8, bf16[256,2,768]{2,0,1:T(8,128)(2,1)S(1)} %all_gather.3, f32[256,2]{0,1:T(2,128)S(1)} %add_sqrt_fusion, f32[256,2]{0,1:T(2,128)S(1)} %broadcast_multiply_fusion), kind=kOutput, calls=%fused_computation.1 | convolution fusion | flops 1215037440 | bytes 4722688 | tf_op jit(solution)/shard_map/asc,cd->asd/dot_general | solution.py:26
  50.5 0.1 fusion.49
  50.7 0.0 copy-start.1
  50.7 1.2 %copy.48 = bf16[256,2,768]{0,2,1:T(8,128)(2,1)} copy(bf16[256,2,768]{2,0,1:T(8,128)(2,1)S(1)} %get-tuple-element.15) | data formatting | bytes 1572864 | tf_op jit(solution)/shard_map/slice | solution.py:213
  51.8 0.3 copy.45
  52.1 0.0 copy-done.1
  52.1 0.2 fusion.34
  52.3 0.0 copy-done
  52.3 0.4 fusion.24
  52.7 0.0 copy-start.3
  52.7 0.2 reshape.122
  52.9 0.2 fusion.11
  53.1 0.0 copy-start.4
  53.1 0.8 %copy-done.4 = f32[2,16,16,256]{3,2,1,0:T(8,128)} copy-done((f32[2,16,16,256]{3,2,1,0:T(8,128)}, f32[2,16,16,256]{3,2,1,0:T(8,128)S(1)}, u32[]{:S(2)}) %copy-start.4) | copy-done | bytes 524312
  53.9 0.0 copy-start.2
  53.9 0.2 fusion.50
  54.1 0.0 copy-done.3
  54.1 1.7 %fusion.17 = bf16[16,2,16,48]{3,0,2,1:T(8,128)(2,1)S(1)} fusion(bf16[256,2,16,48]{0,3,2,1:T(8,128)(2,1)S(1)} %bitcast.60, f32[16,2,16]{0,2,1:T(8,128)S(1)} %bitcast.65, f32[2,16,16,256]{3,2,1,0:T(8,128)} %copy-done.4, pred[256]{0:T(512)(128)(4,1)S(1)} %broadcast_compare_fusion), kind=kOutput, calls=%fused_computation.23 | convolution fusion | flops 13026047 | bytes 1362176 | tf_op jit(solution)/shard_map/shqk,kshd->shqd/dot_general | solution.py:223
  55.9 0.2 reshape.125
  56.1 0.0 copy-done.2
  56.1 0.3 fusion.21
  56.4 0.7 %copy.51 = bf16[16,2,768]{2,1,0:T(2,128)(2,1)} copy(bf16[16,2,768]{2,0,1:T(8,128)(2,1)S(1)} %fusion.21) | data formatting | bytes 98304
  (10 shorter events, 0.1 us)
Async XLA Ops:
  0.6 51.7 %copy-start = (bf16[768,768]{1,0:T(8,128)(2,1)S(1)}, bf16[768,768]{1,0:T(8,128)(2,1)}, u32[]{:S(2)}) copy-start(bf16[768,768]{1,0:T(8,128)(2,1)} %param.27) | copy-start | bytes 3538948
  0.6 12.4 %copy-start.9 = (s32[4]{0:T(128)S(1)}, s32[4]{0:T(128)}, u32[]{:S(2)}) copy-start(s32[4]{0:T(128)} %param.17) | copy-start | bytes 52
  0.7 9.7 %copy-start.6 = (s32[2048]{0:T(1024)S(1)}, s32[2048]{0:T(1024)}, u32[]{:S(2)}) copy-start(s32[2048]{0:T(1024)} %param.18) | copy-start | bytes 24580
  0.7 10.3 %copy-start.5 = (bf16[16,2,768]{2,1,0:T(2,128)(2,1)S(1)}, bf16[16,2,768]{2,1,0:T(2,128)(2,1)}, u32[]{:S(2)}) copy-start(bf16[16,2,768]{2,1,0:T(2,128)(2,1)} %param.19) | copy-start | bytes 147460
  3.1 8.7 %collective-permute-start.1 = (bf16[97,2,128]{2,0,1:T(8,128)(2,1)S(1)}, bf16[97,2,128]{2,0,1:T(8,128)(2,1)S(1)}, u32[]{:S(2)}, u32[]{:S(2)}) collective-permute-start(bf16[97,2,128]{2,0,1:T(8,128)(2,1)S(1)} %slice_select_fusion), channel_id=1, source_target_pairs={{1,0},{2,1},{3,2},{4,3},{5,4},{6,5},{7,6},{8,7},{9,8},{10,9},{11,1... | collective-permute-start | bytes 149000 | tf_op jit(solution)/shard_map/ppermute | solution.py:32
  4.4 9.8 %collective-permute-start = (bf16[64,2,128]{2,0,1:T(8,128)(2,1)S(1)}, bf16[64,2,128]{2,0,1:T(8,128)(2,1)S(1)}, u32[]{:S(2)}, u32[]{:S(2)}) collective-permute-start(bf16[64,2,128]{2,0,1:T(8,128)(2,1)S(1)} %slice.30), channel_id=1, source_target_pairs={{0,1},{1,2},{2,3},{3,4},{4,5},{5,6},{6,7},{7,8},{8,9},{9,10},{10,1... | collective-permute-start | bytes 98312 | tf_op jit(solution)/shard_map/ppermute | solution.py:32
  20.4 28.6 %copy-start.7 = (bf16[768,768]{1,0:T(8,128)(2,1)S(1)}, bf16[768,768]{1,0:T(8,128)(2,1)}, u32[]{:S(2)}) copy-start(bf16[768,768]{1,0:T(8,128)(2,1)} %param.29) | copy-start | bytes 3538948
  20.4 28.6 %copy-start.8 = (bf16[768,768]{1,0:T(8,128)(2,1)S(1)}, bf16[768,768]{1,0:T(8,128)(2,1)}, u32[]{:S(2)}) copy-start(bf16[768,768]{1,0:T(8,128)(2,1)} %param.28) | copy-start | bytes 3538948
  50.7 1.4 %copy-start.1 = (bf16[2,16,768]{2,1,0:T(8,128)(2,1)S(1)}, bf16[2,16,768]{2,1,0:T(8,128)(2,1)}, u32[]{:S(2)}) copy-start(bf16[2,16,768]{2,1,0:T(8,128)(2,1)} %get-tuple-element.5) | copy-start | bytes 147460
  52.7 1.5 %copy-start.3 = (bf16[256,2,768]{0,2,1:T(8,128)(2,1)S(1)}, bf16[256,2,768]{0,2,1:T(8,128)(2,1)}, u32[]{:S(2)}) copy-start(bf16[256,2,768]{0,2,1:T(8,128)(2,1)} %copy.48) | copy-start | bytes 2359300
  53.1 0.8 %copy-start.4 = (f32[2,16,16,256]{3,2,1,0:T(8,128)}, f32[2,16,16,256]{3,2,1,0:T(8,128)S(1)}, u32[]{:S(2)}) copy-start(f32[2,16,16,256]{3,2,1,0:T(8,128)S(1)} %fusion.11) | copy-start | bytes 1572868
  53.9 2.2 %copy-start.2 = (bf16[768,768]{1,0:T(8,128)(2,1)S(1)}, bf16[768,768]{1,0:T(8,128)(2,1)}, u32[]{:S(2)}) copy-start(bf16[768,768]{1,0:T(8,128)(2,1)} %param.30) | copy-start | bytes 3538948

commit v4 on v3

--- a/solution.py
+++ b/solution.py
@@ -99,6 +99,55 @@
         state_ref[s] = (token_ref[s].astype(f32) + sums / counts).astype(bf16)
 
 
+def token_kernel(
+    every_ref,
+    own_ref,
+    bias_ref,
+    flags_ref,
+    wq_ref,
+    wk_ref,
+    wv_ref,
+    wo_ref,
+    out_ref,
+    *,
+    heads,
+):
+    f32, bf16 = jnp.float32, jnp.bfloat16
+    samples, tok_dev, width = own_ref.shape
+    head_dim = width // heads
+    lane = lax.broadcasted_iota(jnp.int32, (1, width), 1) // head_dim
+    head_masks = [(lane == h).astype(f32) for h in range(heads)]
+    root = jnp.float32(math.sqrt(head_dim))
+    keep = flags_ref[...] > 0
+    bias = bias_ref[...]
+
+    def normed(x):
+        mean = jnp.mean(x, axis=-1, keepdims=True)
+        var = jnp.mean((x - mean) ** 2, axis=-1, keepdims=True)
+        return ((x - mean) / jnp.sqrt(var + 1e-05)).astype(bf16)
+
+    for s in range(samples):
+        allx = normed(every_ref[s].astype(f32))
+        own = own_ref[s].astype(f32)
+        q = jnp.dot(normed(own), wq_ref[...], preferred_element_type=f32).astype(bf16)
+        k = jnp.dot(allx, wk_ref[...], preferred_element_type=f32).astype(bf16)
+        v = jnp.dot(allx, wv_ref[...], preferred_element_type=f32).astype(bf16)
+        stacked = jnp.concatenate([q * head_masks[h].astype(bf16) for h in range(heads)], axis=0)
+        sc = lax.dot_general(
+            stacked, k, (((1,), (1,)), ((), ())), preferred_element_type=f32
+        ) / root + bias
+        sc = jnp.where(keep, sc, -1e30)
+        top = jnp.max(sc, axis=-1, keepdims=True)
+        e = jnp.where(keep, jnp.exp(sc - top), 0.0)
+        tot = jnp.sum(e, axis=-1, keepdims=True)
+        o = jnp.dot(e.astype(bf16), v, preferred_element_type=f32) / tot
+        mix = o[0:tok_dev] * head_masks[0]
+        for h in range(1, heads):
+            mix = mix + o[h * tok_dev : (h + 1) * tok_dev] * head_masks[h]
+        mix = mix.astype(bf16)
+        out_ref[s] = (own + jnp.dot(mix, wo_ref[...], preferred_element_type=f32)).astype(bf16)
+
+
 def on_device(
     atom_feat,
     window_shift,
@@ -197,35 +246,35 @@
         jnp.transpose(token_in, (1, 0, 2)),
     )
     atom_out = jnp.transpose(atom_t, (1, 0, 2))
-    state = jnp.transpose(state_t, (1, 0, 2))
-
-    tdim = tok_width // TOKEN_HEADS
-    tq = project(layer_norm(state).astype(jnp.bfloat16), w_query).astype(jnp.bfloat16)
-    tq = tq.reshape(tok_dev, samples, TOKEN_HEADS, tdim)
+
     bias = jnp.einsum("qkc,ch->hqk", pair, w_bias, preferred_element_type=jnp.float32)
-    scale = 1.0 / jnp.sqrt(jnp.float32(tdim))
-
-    every = lax.all_gather(state, "row", axis=0, tiled=True)
-    count = every.shape[0]
-    tkv = project(layer_norm(every).astype(jnp.bfloat16), jnp.concatenate([w_key, w_value], axis=1))
-    tkv = tkv.astype(jnp.bfloat16)
-    kheads = tkv[..., :tok_width].reshape(count, samples, TOKEN_HEADS, tdim)
-    vheads = tkv[..., tok_width:].reshape(count, samples, TOKEN_HEADS, tdim)
-    flags = (key_mask > 0)[None, None, None, :]
-    score = (
-        jnp.einsum("qshd,kshd->shqk", tq, kheads, preferred_element_type=jnp.float32) * scale
-        + bias[None]
-    )
-    score = jnp.where(flags, score, -1e30)
-    peak = jnp.max(score, axis=-1)
-    expo_t = jnp.where(flags, jnp.exp(score - peak[..., None]), 0.0)
-    denom = jnp.sum(expo_t, axis=-1)
-    accum = jnp.einsum(
-        "shqk,kshd->shqd", expo_t.astype(jnp.bfloat16), vheads, preferred_element_type=jnp.float32
-    )
-    tmix = (accum / denom[..., None]).astype(jnp.bfloat16)
-    tmix = jnp.transpose(tmix, (2, 0, 1, 3)).reshape(tok_dev, samples, tok_width)
-    token_out = (state.astype(jnp.float32) + project(tmix, w_out)).astype(jnp.bfloat16)
+    every = lax.all_gather(state_t, "row", axis=1, tiled=True)
+    count = every.shape[1]
+    token_t = pl.pallas_call(
+        functools.partial(token_kernel, heads=TOKEN_HEADS),
+        out_shape=jax.ShapeDtypeStruct((samples, tok_dev, tok_width), jnp.bfloat16),
+        in_specs=[vmem] * 8,
+        out_specs=vmem,
+        cost_estimate=pl.CostEstimate(
+            flops=2 * samples * tok_width * (
+                2 * count * tok_width + 2 * tok_dev * tok_width + 2 * TOKEN_HEADS * tok_dev * count
+            ),
+            transcendentals=samples * TOKEN_HEADS * tok_dev * count,
+            bytes_accessed=2 * 4 * tok_width * tok_width
+            + 2 * samples * (count + 2 * tok_dev) * tok_width
+            + 4 * TOKEN_HEADS * tok_dev * count,
+        ),
+    )(
+        every,
+        state_t,
+        bias.reshape(TOKEN_HEADS * tok_dev, count),
+        key_mask[None, :],
+        w_query,
+        w_key,
+        w_value,
+        w_out,
+    )
+    token_out = jnp.transpose(token_t, (1, 0, 2))
     return (atom_out, token_out)
 
 

time: 57.4 us -> 57.8 us (level)
  Pallas kernels: 5.58 us -> 12.3 us
  matrix products: 5.75 us -> 1.06 us
  blocking collectives: 25.5 us -> 28.7 us
  other arithmetic: 5.36 us -> 2.81 us
  local copies, waits for them, and re-layouts: 8.99 us -> 7.53 us
  starting transfers between devices: 4.32 us -> 3.65 us
    pallas_call x0 -> x1, Pallas kernels: none -> 6.7 us  [on_device(): pl.pallas_call(functools.partial(token_kernel, heads=TOKEN_HEADS), out_sh...]
    dot_general x5 -> x0, matrix products: 4.14 us -> none  [the longest x3 2.21 us: project(): jnp.einsum('asc,cd->asd', values, weight, preferred_element_type=jnp.floa...]
    all_gather x1, blocking collectives: 25.5 us -> 28.7 us  [on_device(): every = lax.all_gather(state_t, 'row', axis=1, tiled=True)]
    reduce_sum x4 -> x0, other arithmetic: 1.6 us -> none  [the longest x2 1.06 us: layer_norm(): mean = jnp.mean(values, axis=-1, keepdims=True)]
    slice x3 -> x0, local copies, waits for them, and re-layouts: 1.52 us -> none  [the longest x1 1.15 us: on_device(): vheads = tkv[..., tok_width:].reshape(count, samples, TOKEN_HEADS, tdim)]
    dot_general x1, local copies, waits for them, and re-layouts: 0.16 us -> 0.85 us  [on_device(): jnp.einsum('qkc,ch->hqk', pair, w_bias, preferred_element_type=jnp.float32)]
    gt x1 -> x0, other arithmetic: 0.68 us -> none  [on_device(): flags = (key_mask > 0)[None, None, None, :]]
    ppermute x2, starting transfers between devices: 4.32 us -> 3.65 us  [shifted(): return lax.ppermute(block, axis, route)]
  transfers between devices with their start and end apart: 2 -> 2, of which waited for: 0 -> 1; matrix products, arithmetic and copies ran while one was open for 10% -> 12% of each run, Pallas kernels for 0% -> 0%
where the time goes in v4:
time: 57.8 us; the launch traced here: 57.4 us
  blocking collectives  28.7 us (50%)
  Pallas kernels  12.3 us (21%)
  local copies, waits for them, and re-layouts  7.53 us (13%)
  starting transfers between devices  3.65 us (6%)
  other arithmetic  2.81 us (5%)
  between operations  1.31 us (2%)
  matrix products  1.06 us (2%)
    all_gather x1, blocking collectives, on_device(): every = lax.all_gather(state_t, 'row', axis=1, tiled=True)  28.7 us
    pallas_call x1, Pallas kernels, on_device(): pl.pallas_call(functools.partial(token_kernel, heads=TOKEN_HEADS), out_sh...  6.7 us
    pallas_call x1, Pallas kernels, on_device(): pl.pallas_call(kernel, out_shape=(jax.ShapeDtypeStruct((samples, atom_dev...  5.58 us
    unnamed x12, local copies, waits for them, and re-layouts  4.57 us
    ppermute x2, starting transfers between devices, shifted(): return lax.ppermute(block, axis, route)  3.65 us
  transfers between devices with their start and end apart: 2, of which 1 were waited for; matrix products, arithmetic and copies ran while one was open for 12% of the time, Pallas kernels for 0%

profile of v4, /device:TPU:0, one launch (start us, length us, event | category | flops | bytes accessed | tf_op | source)
XLA Modules:
  0.0 57.4 jit_solution(12859682283339762903)
XLA Ops:
  0.6 0.0 copy-start
  0.6 0.0 copy-start.3
  0.7 0.0 copy-start.2
  0.7 0.0 copy-start.1
  0.7 0.9 %copy.33 = bf16[128,2,128]{2,0,1:T(8,128)(2,1)S(1)} copy(bf16[128,2,128]{2,1,0:T(2,128)(2,1)} %param.16) | data formatting | bytes 131072 | tf_op args[0]
  1.6 2.4 %collective-permute-start = (bf16[64,2,128]{2,0,1:T(8,128)(2,1)S(1)}, bf16[64,2,128]{2,0,1:T(8,128)(2,1)S(1)}, u32[]{:S(2)}, u32[]{:S(2)}) collective-permute-start(bf16[64,2,128]{2,0,1:T(8,128)(2,1)S(1)} %slice.22), channel_id=1, source_target_pairs={{0,1},{1,2},{2,3},{3,4},{4,5},{5,6},{6,7},{7,8},{8,9},{9,10},{10,1... | collective-permute-start | bytes 98312 | tf_op jit(solution)/shard_map/ppermute | solution.py:32
  4.0 0.7 %convert.4 = bf16[4]{0:T(256)(128)(2,1)S(1)} convert(s32[4]{0:T(128)} %param.17) | non-fusion elementwise | flops 4 | bytes 24 | tf_op jit(solution)/shard_map/convert.1
  4.7 0.8 %slice_select_fusion = bf16[97,2,128]{2,0,1:T(8,128)(2,1)S(1)} fusion(bf16[128,2,128]{2,0,1:T(8,128)(2,1)S(1)} %copy.33, pred[97]{0:T(512)(128)(4,1)} %constant.30.clone.1, bf16[]{:T(256)S(1)} %bitcast.23), kind=kLoop, calls=%fused_computation.1 | loop fusion | flops 24832 | bytes 99427 | tf_op jit(solution)/shard_map/concatenate | solution.py:188
  5.4 1.3 %collective-permute-start.1 = (bf16[97,2,128]{2,0,1:T(8,128)(2,1)S(1)}, bf16[97,2,128]{2,0,1:T(8,128)(2,1)S(1)}, u32[]{:S(2)}, u32[]{:S(2)}) collective-permute-start(bf16[97,2,128]{2,0,1:T(8,128)(2,1)S(1)} %slice_select_fusion), channel_id=1, source_target_pairs={{1,0},{2,1},{3,2},{4,3},{5,4},{6,5},{7,6},{8,7},{9,8},{10,9},{11,1... | collective-permute-start | bytes 149000 | tf_op jit(solution)/shard_map/ppermute | solution.py:32
  6.7 0.6 %iota_add_fusion.own_ids_ref = s32[16,1]{1,0:T(8,128)} fusion(s32[]{:T(128)S(6)} %mul.23), kind=kLoop, calls=%fused_computation.4 | loop fusion | flops 16 | bytes 68 | tf_op jit(solution)/shard_map/add | solution.py:206
  7.3 0.0 copy-done
  7.3 1.1 %fusion = f32[16,16,256]{2,0,1:T(8,128)S(1)} fusion(bf16[16,256,128]{2,1,0:T(8,128)(2,1)S(1)} %copy-done, bf16[128,16]{0,1:T(8,128)(2,1)} %param.31), kind=kOutput, calls=%fused_computation.5 | convolution fusion | flops 16777216 | bytes 1314816 | tf_op jit(solution)/shard_map/qkc,ch->hqk/dot_general | solution.py:250
  8.4 0.0 copy-done.2
  8.4 0.7 %pad_dynamic-slice_fusion = s32[160]{0:T(256)} fusion(s32[]{:T(128)S(6)} %select_n.20, s32[2048]{0:T(1024)S(1)} %copy-done.2), kind=kLoop, calls=%fused_computation.3 | loop fusion | bytes 8836 | tf_op jit(solution)/shard_map/dynamic_slice | solution.py:207
  9.1 0.0 copy-done.1
  9.1 0.6 %copy.42 = bf16[16,2,768]{2,0,1:T(8,128)(2,1)} copy(bf16[16,2,768]{2,1,0:T(2,128)(2,1)S(1)} %copy-done.1) | data formatting | bytes 98304 | tf_op args[3]
  9.7 0.8 %copy.38 = f32[16,16,256]{2,1,0:T(8,128)} copy(f32[16,16,256]{2,0,1:T(8,128)S(1)} %fusion) | data formatting | bytes 524288 | tf_op jit(solution)/shard_map/qkc,ch->hqk/dot_general | solution.py:250
  10.6 0.1 collective-permute-done.1
  10.7 0.5 slice.25
  11.8 0.0 copy-done.3
  11.8 0.1 pad_add_fusion.1
  11.9 0.1 broadcast_in_dim.20
  11.9 0.1 reshape.84
  12.1 0.8 %copy.37.bounds_ref = s32[160,2]{1,0:T(8,128)} copy(s32[160,2]{0,1:T(2,128)S(1)} %pad_add_fusion) | data formatting | bytes 2560 | tf_op jit(solution)/shard_map/stack | solution.py:199
  12.8 0.0 collective-permute-done
  12.8 0.7 %maximum_bitcast_fusion.ext_ref = bf16[2,288,128]{2,1,0:T(8,128)(2,1)} fusion(bf16[96,2,128]{2,0,1:T(8,128)(2,1)S(1)} %slice.24, bf16[128,2,128]{2,0,1:T(8,128)(2,1)S(1)} %copy.33, bf16[64,2,128]{2,0,1:T(8,128)(2,1)S(1)} %collective-permute-done), kind=kLoop, calls=%fused_computation | loop fusion | flops 442368 | bytes 294912 | tf_op jit(solution)/shard_map/transpose | solution.py:210
  13.5 5.6 %shard_map.167 = (bf16[2,128,128]{2,1,0:T(8,128)(2,1)}, bf16[2,16,768]{2,1,0:T(8,128)(2,1)}) custom-call(bf16[2,288,128]{2,1,0:T(8,128)(2,1)} %maximum_bitcast_fusion.ext_ref, s32[160,2]{1,0:T(8,128)} %copy.37.bounds_ref, bf16[128,128]{1,0:T(8,128)(2,1)} %wq_ref.2, bf16[128,128]{1,0:T(8,128)(2,1)} %wk_ref.2, bf16[128,128]{1,0:T(8,128)(2,1)} %wv_ref.2, ...), custom_call_target="tpu_custom_call" | custom-call | flops 342360064 | bytes 638976 | tf_op jit(solution)/shard_map/pallas_call | solution.py:221
  19.1 1.5 %copy.39 = bf16[128,2,128]{2,1,0:T(2,128)(2,1)} copy(bf16[128,2,128]{2,0,1:T(8,128)(2,1)} %bitcast.19) | data formatting | bytes 131072
  20.6 28.7 %all_gather.3.every_ref = bf16[2,256,768]{2,1,0:T(8,128)(2,1)} all-gather(bf16[2,16,768]{2,1,0:T(8,128)(2,1)} %get-tuple-element.5.own_ref), channel_id=1, replica_groups=mesh['groups'=2,'row'=16] {'row'}, dimensions={1}, use_global_device_ids=true | all-gather | bytes 835584 | tf_op jit(solution)/shard_map/all_gather | solution.py:251
  49.3 6.7 %shard_map.168 = bf16[2,16,768]{2,1,0:T(8,128)(2,1)} custom-call(bf16[2,256,768]{2,1,0:T(8,128)(2,1)} %all_gather.3.every_ref, bf16[2,16,768]{2,1,0:T(8,128)(2,1)} %get-tuple-element.5.own_ref, f32[256,256]{1,0:T(8,128)} %bitcast.18, s32[1,256]{1,0:T(1,128)} %bitcast.24, bf16[768,768]{1,0:T(8,128)(2,1)} %wq_ref.3, bf16[768,768]{1,0:T(8,128)(2,1)} %wk_ref.3, ...), custom_call_target="tpu_custom_call" | custom-call | flops 1686110208 | bytes 5865472 | tf_op jit(solution)/shard_map/pallas_call | solution.py:253
  56.0 1.5 %copy.40 = bf16[16,2,768]{2,1,0:T(2,128)(2,1)} copy(bf16[16,2,768]{2,0,1:T(8,128)(2,1)} %bitcast.21) | data formatting | bytes 98304
  (5 shorter events, 0.0 us)
Async XLA Ops:
  0.6 6.7 %copy-start = (bf16[16,256,128]{2,1,0:T(8,128)(2,1)S(1)}, bf16[16,256,128]{2,1,0:T(8,128)(2,1)}, u32[]{:S(2)}) copy-start(bf16[16,256,128]{2,1,0:T(8,128)(2,1)} %param.20) | copy-start | bytes 3145732
  0.6 11.1 %copy-start.3 = (s32[4]{0:T(128)S(1)}, s32[4]{0:T(128)}, u32[]{:S(2)}) copy-start(s32[4]{0:T(128)} %param.17) | copy-start | bytes 52
  0.7 7.7 %copy-start.2 = (s32[2048]{0:T(1024)S(1)}, s32[2048]{0:T(1024)}, u32[]{:S(2)}) copy-start(s32[2048]{0:T(1024)} %param.18) | copy-start | bytes 24580
  0.7 8.4 %copy-start.1 = (bf16[16,2,768]{2,1,0:T(2,128)(2,1)S(1)}, bf16[16,2,768]{2,1,0:T(2,128)(2,1)}, u32[]{:S(2)}) copy-start(bf16[16,2,768]{2,1,0:T(2,128)(2,1)} %param.19) | copy-start | bytes 147460
  1.6 11.2 %collective-permute-start = (bf16[64,2,128]{2,0,1:T(8,128)(2,1)S(1)}, bf16[64,2,128]{2,0,1:T(8,128)(2,1)S(1)}, u32[]{:S(2)}, u32[]{:S(2)}) collective-permute-start(bf16[64,2,128]{2,0,1:T(8,128)(2,1)S(1)} %slice.22), channel_id=1, source_target_pairs={{0,1},{1,2},{2,3},{3,4},{4,5},{5,6},{6,7},{7,8},{8,9},{9,10},{10,1... | collective-permute-start | bytes 98312 | tf_op jit(solution)/shard_map/ppermute | solution.py:32
  5.4 5.3 %collective-permute-start.1 = (bf16[97,2,128]{2,0,1:T(8,128)(2,1)S(1)}, bf16[97,2,128]{2,0,1:T(8,128)(2,1)S(1)}, u32[]{:S(2)}, u32[]{:S(2)}) collective-permute-start(bf16[97,2,128]{2,0,1:T(8,128)(2,1)S(1)} %slice_select_fusion), channel_id=1, source_target_pairs={{1,0},{2,1},{3,2},{4,3},{5,4},{6,5},{7,6},{8,7},{9,8},{10,9},{11,1... | collective-permute-start | bytes 149000 | tf_op jit(solution)/shard_map/ppermute | solution.py:32

commit v5 on v4

--- a/solution.py
+++ b/solution.py
@@ -33,7 +33,9 @@
 
 
 def atom_kernel(
-    ext_ref,
+    own_ref,
+    low_ref,
+    upper_ref,
     bounds_ref,
     wq_ref,
     wk_ref,
@@ -49,10 +51,12 @@
     atom_dev,
     rows,
     low_rows,
+    high_rows,
     head_dim,
 ):
     f32, bf16 = jnp.float32, jnp.bfloat16
-    samples, ext_rows, width = ext_ref.shape
+    _, samples, width = own_ref.shape
+    ext_rows = low_rows + atom_dev + high_rows
     lane = lax.broadcasted_iota(jnp.int32, (1, width), 1) // head_dim
     head_masks = [(lane == h).astype(f32) for h in range(ATOM_HEADS)]
     root = jnp.float32(math.sqrt(head_dim))
@@ -62,7 +66,9 @@
     counts = jnp.sum(onehot, axis=1, keepdims=True)
     onehot = onehot.astype(bf16)
     for s in range(samples):
-        x = ext_ref[s].astype(f32)
+        x = jnp.concatenate(
+            [low_ref[:, s, :], own_ref[:, s, :], upper_ref[0:high_rows, s, :]], axis=0
+        ).astype(f32)
         mean = jnp.mean(x, axis=-1, keepdims=True)
         var = jnp.mean((x - mean) ** 2, axis=-1, keepdims=True)
         xn = ((x - mean) / jnp.sqrt(var + 1e-05)).astype(bf16)
@@ -85,7 +91,7 @@
         mixed = acc.astype(bf16)
         base = x[low_rows : low_rows + rows]
         out = (base + jnp.dot(mixed, wo_ref[...], preferred_element_type=f32)).astype(bf16)
-        atom_ref[s] = out[:atom_dev]
+        atom_ref[:, s, :] = out[:atom_dev]
         hidden = jnp.maximum(jnp.dot(out, wt_ref[...], preferred_element_type=f32), 0.0)
         top_part = hidden.astype(bf16)
         rest = hidden - top_part.astype(f32)
@@ -96,7 +102,7 @@
             + jnp.dot(onehot, mid_part, preferred_element_type=f32)
             + jnp.dot(onehot, low_part, preferred_element_type=f32)
         )
-        state_ref[s] = (token_ref[s].astype(f32) + sums / counts).astype(bf16)
+        state_ref[s] = (token_ref[:, s, :].astype(f32) + sums / counts).astype(bf16)
 
 
 def token_kernel(
@@ -145,7 +151,7 @@
         for h in range(1, heads):
             mix = mix + o[h * tok_dev : (h + 1) * tok_dev] * head_masks[h]
         mix = mix.astype(bf16)
-        out_ref[s] = (own + jnp.dot(mix, wo_ref[...], preferred_element_type=f32)).astype(bf16)
+        out_ref[:, s, :] = (own + jnp.dot(mix, wo_ref[...], preferred_element_type=f32)).astype(bf16)
 
 
 def on_device(
@@ -188,7 +194,6 @@
         jnp.concatenate([atom_feat[:high_rows], shift_row], axis=0), "row", -1
     )
     next_shift = upper[high_rows, 0, 0].astype(jnp.int32)
-    upper = upper[:high_rows]
 
     head_dim = width // ATOM_HEADS
     shifts = jnp.concatenate([window_shift, next_shift[None]], axis=0)
@@ -207,9 +212,13 @@
     row_ids = lax.dynamic_slice_in_dim(
         jnp.concatenate([atom_token, jnp.full((QBLOCK,), -1, jnp.int32)]), atom_base, rows
     )
-    extended = jnp.transpose(jnp.concatenate([low, atom_feat, upper], axis=0), (1, 0, 2))
     kernel = functools.partial(
-        atom_kernel, atom_dev=atom_dev, rows=rows, low_rows=low_rows, head_dim=head_dim
+        atom_kernel,
+        atom_dev=atom_dev,
+        rows=rows,
+        low_rows=low_rows,
+        high_rows=high_rows,
+        head_dim=head_dim,
     )
     vmem = pl.BlockSpec(memory_space=pltpu.VMEM)
     flops = 2 * samples * (
@@ -218,13 +227,13 @@
         + ATOM_HEADS * rows * ext_rows * width * 2
         + 3 * tok_dev * rows * tok_width
     )
-    atom_t, state_t = pl.pallas_call(
+    atom_out, state_t = pl.pallas_call(
         kernel,
         out_shape=(
-            jax.ShapeDtypeStruct((samples, atom_dev, width), jnp.bfloat16),
+            jax.ShapeDtypeStruct((atom_dev, samples, width), jnp.bfloat16),
             jax.ShapeDtypeStruct((samples, tok_dev, tok_width), jnp.bfloat16),
         ),
-        in_specs=[vmem] * 10,
+        in_specs=[vmem] * 12,
         out_specs=(vmem, vmem),
         cost_estimate=pl.CostEstimate(
             flops=flops,
@@ -234,7 +243,9 @@
             + 4 * samples * tok_dev * tok_width,
         ),
     )(
-        extended,
+        atom_feat,
+        low,
+        upper,
         bounds,
         w_atom_query,
         w_atom_key,
@@ -243,16 +254,15 @@
         w_to_token,
         row_ids[None, :],
         own_ids[:, None],
-        jnp.transpose(token_in, (1, 0, 2)),
-    )
-    atom_out = jnp.transpose(atom_t, (1, 0, 2))
+        token_in,
+    )
 
     bias = jnp.einsum("qkc,ch->hqk", pair, w_bias, preferred_element_type=jnp.float32)
     every = lax.all_gather(state_t, "row", axis=1, tiled=True)
     count = every.shape[1]
-    token_t = pl.pallas_call(
+    token_out = pl.pallas_call(
         functools.partial(token_kernel, heads=TOKEN_HEADS),
-        out_shape=jax.ShapeDtypeStruct((samples, tok_dev, tok_width), jnp.bfloat16),
+        out_shape=jax.ShapeDtypeStruct((tok_dev, samples, tok_width), jnp.bfloat16),
         in_specs=[vmem] * 8,
         out_specs=vmem,
         cost_estimate=pl.CostEstimate(
@@ -274,7 +284,6 @@
         w_value,
         w_out,
     )
-    token_out = jnp.transpose(token_t, (1, 0, 2))
     return (atom_out, token_out)
 
 

time: 57.8 us -> 54.6 us (0.945)
  local copies, waits for them, and re-layouts: 7.53 us -> 4.48 us
  blocking collectives: 28.7 us -> 28 us
  waiting for transfers between devices: 0.13 us -> 0.75 us
    unnamed x12 -> x10, local copies, waits for them, and re-layouts: 4.57 us -> 0.64 us
    slice x1, local copies, waits for them, and re-layouts: 0.01 us -> 0.87 us  [on_device(): low = shifted(atom_feat[atom_dev - low_rows:], 'row', 1)]
    transpose x1 -> x0, other arithmetic: 0.66 us -> none  [on_device(): jnp.transpose(jnp.concatenate([low, atom_feat, upper], axis=0), (1, 0, 2))]
    all_gather x1, blocking collectives: 28.7 us -> 28 us  [on_device(): every = lax.all_gather(state_t, 'row', axis=1, tiled=True)]
    ppermute x2, waiting for transfers between devices: 0.13 us -> 0.75 us  [shifted(): return lax.ppermute(block, axis, route)]
where the time goes in v5:
time: 54.6 us; the launch traced here: 54.3 us
  blocking collectives  28 us (51%)
  Pallas kernels  12.6 us (23%)
  local copies, waits for them, and re-layouts  4.48 us (8%)
  starting transfers between devices  3.65 us (7%)
  other arithmetic  2.4 us (4%)
  between operations  1.38 us (3%)
  matrix products  1.06 us (2%)
  waiting for transfers between devices  0.75 us (1%)
    all_gather x1, blocking collectives, on_device(): every = lax.all_gather(state_t, 'row', axis=1, tiled=True)  28 us
    pallas_call x1, Pallas kernels, on_device(): pl.pallas_call(functools.partial(token_kernel, heads=TOKEN_HEADS), out_sh...  6.72 us
    pallas_call x1, Pallas kernels, on_device(): pl.pallas_call(kernel, out_shape=(jax.ShapeDtypeStruct((atom_dev, samples...  5.85 us
    ppermute x2, starting transfers between devices, shifted(): return lax.ppermute(block, axis, route)  3.65 us
  transfers between devices with their start and end apart: 2, of which 1 were waited for; matrix products, arithmetic and copies ran while one was open for 12% of the time, Pallas kernels for 0%

profile of v5, /device:TPU:0, one launch (start us, length us, event | category | flops | bytes accessed | tf_op | source)
XLA Modules:
  0.0 54.3 jit_solution(1336660822995429801)
XLA Ops:
  0.6 0.0 copy-start
  0.6 0.0 copy-start.4
  0.7 0.0 copy-start.1
  0.7 0.9 %slice.14 = bf16[64,2,128]{2,1,0:T(2,128)(2,1)S(1)} slice(bf16[128,2,128]{2,1,0:T(2,128)(2,1)} %own_ref.1), slice={[64:128], [0:2], [0:128]} | slice | bytes 65536 | tf_op jit(solution)/shard_map/slice | solution.py:192
  1.5 2.4 %collective-permute-start = (bf16[64,2,128]{2,1,0:T(2,128)(2,1)S(1)}, bf16[64,2,128]{2,1,0:T(2,128)(2,1)S(1)}, u32[]{:S(2)}, u32[]{:S(2)}) collective-permute-start(bf16[64,2,128]{2,1,0:T(2,128)(2,1)S(1)} %slice.14), channel_id=1, source_target_pairs={{0,1},{1,2},{2,3},{3,4},{4,5},{5,6},{6,7},{7,8},{8,9},{9,10},{10,1... | collective-permute-start | bytes 98312 | tf_op jit(solution)/shard_map/ppermute | solution.py:32
  3.9 0.7 %convert.4 = bf16[4]{0:T(256)(128)(2,1)S(1)} convert(s32[4]{0:T(128)} %param.17) | non-fusion elementwise | flops 4 | bytes 24 | tf_op jit(solution)/shard_map/convert.1
  4.6 1.0 %broadcast_select_fusion = bf16[97,2,128]{2,1,0:T(2,128)(2,1)S(1)} fusion(pred[97]{0:T(512)(128)(4,1)} %constant.30.clone.1, bf16[128,2,128]{2,1,0:T(2,128)(2,1)} %own_ref.1, bf16[]{:T(256)S(1)} %bitcast.13), kind=kLoop, calls=%fused_computation | loop fusion | flops 24832 | bytes 99427 | tf_op jit(solution)/shard_map/concatenate | solution.py:194
  5.6 1.3 %collective-permute-start.1 = (bf16[97,2,128]{2,1,0:T(2,128)(2,1)S(1)}, bf16[97,2,128]{2,1,0:T(2,128)(2,1)S(1)}, u32[]{:S(2)}, u32[]{:S(2)}) collective-permute-start(bf16[97,2,128]{2,1,0:T(2,128)(2,1)S(1)} %broadcast_select_fusion), channel_id=1, source_target_pairs={{1,0},{2,1},{3,2},{4,3},{5,4},{6,5},{7,6},{8,7},{9,8},{10,9},{11,1... | collective-permute-start | bytes 149000 | tf_op jit(solution)/shard_map/ppermute | solution.py:32
  6.9 0.6 %iota_add_fusion.own_ids_ref = s32[16,1]{1,0:T(8,128)} fusion(s32[]{:T(128)S(6)} %mul.23), kind=kLoop, calls=%fused_computation.2 | loop fusion | flops 16 | bytes 68 | tf_op jit(solution)/shard_map/add | solution.py:211
  7.5 0.0 copy-done
  7.5 1.1 %fusion = f32[16,16,256]{2,0,1:T(8,128)S(1)} fusion(bf16[16,256,128]{2,1,0:T(8,128)(2,1)S(1)} %copy-done, bf16[128,16]{0,1:T(8,128)(2,1)} %param.31), kind=kOutput, calls=%fused_computation.3 | convolution fusion | flops 16777216 | bytes 1314816 | tf_op jit(solution)/shard_map/qkc,ch->hqk/dot_general | solution.py:260
  8.6 0.0 copy-done.1
  8.6 0.7 %pad_dynamic-slice_fusion = s32[160]{0:T(256)} fusion(s32[]{:T(128)S(6)} %select_n.20, s32[2048]{0:T(1024)S(1)} %copy-done.1), kind=kLoop, calls=%fused_computation.1 | loop fusion | bytes 8836 | tf_op jit(solution)/shard_map/dynamic_slice | solution.py:212
  9.3 0.9 %copy.22 = f32[16,16,256]{2,1,0:T(8,128)} copy(f32[16,16,256]{2,0,1:T(8,128)S(1)} %fusion) | data formatting | bytes 524288 | tf_op jit(solution)/shard_map/qkc,ch->hqk/dot_general | solution.py:260
  10.1 0.7 %collective-permute-done.1.upper_ref = bf16[97,2,128]{2,1,0:T(2,128)(2,1)S(1)} collective-permute-done((bf16[97,2,128]{2,1,0:T(2,128)(2,1)S(1)}, bf16[97,2,128]{2,1,0:T(2,128)(2,1)S(1)}, u32[]{:S(2)}, u32[]{:S(2)}) %collective-permute-start.1) | collective-permute-done | bytes 49696 | tf_op jit(solution)/shard_map/ppermute | solution.py:32
  10.9 0.0 copy-start.2
  10.9 0.5 slice.18
  12.0 0.0 copy-done.4
  12.1 0.1 pad_add_fusion.1
  12.1 0.1 broadcast_in_dim.20
  12.2 0.1 reshape.84
  12.3 0.8 %copy.21.bounds_ref = s32[160,2]{1,0:T(8,128)} copy(s32[160,2]{0,1:T(2,128)S(1)} %pad_add_fusion) | data formatting | bytes 2560 | tf_op jit(solution)/shard_map/stack | solution.py:204
  13.1 0.0 collective-permute-done.low_ref
  13.1 0.0 copy-start.3
  13.1 0.0 copy-done.2
  13.1 0.6 %copy-done.3 = bf16[64,2,128]{2,1,0:T(2,128)(2,1)} copy-done((bf16[64,2,128]{2,1,0:T(2,128)(2,1)}, bf16[64,2,128]{2,1,0:T(2,128)(2,1)S(1)}, u32[]{:S(2)}) %copy-start.3) | copy-done | bytes 32792
  13.7 5.8 %shard_map.167 = (bf16[128,2,128]{2,1,0:T(2,128)(2,1)}, bf16[2,16,768]{2,1,0:T(8,128)(2,1)}) custom-call(bf16[128,2,128]{2,1,0:T(2,128)(2,1)} %own_ref.1, bf16[64,2,128]{2,1,0:T(2,128)(2,1)} %copy-done.3, bf16[97,2,128]{2,1,0:T(2,128)(2,1)} %copy-done.2, s32[160,2]{1,0:T(8,128)} %copy.21.bounds_ref, bf16[128,128]{1,0:T(8,128)(2,1)} %wq_ref.2, ...), custom_call_target="tpu_custom_call" | custom-call | flops 342360064 | bytes 638976 | tf_op jit(solution)/shard_map/pallas_call | solution.py:230
  19.6 28.0 %all_gather.3.every_ref = bf16[2,256,768]{2,1,0:T(8,128)(2,1)} all-gather(bf16[2,16,768]{2,1,0:T(8,128)(2,1)} %get-tuple-element.5.own_ref), channel_id=1, replica_groups=mesh['groups'=2,'row'=16] {'row'}, dimensions={1}, use_global_device_ids=true | all-gather | bytes 835584 | tf_op jit(solution)/shard_map/all_gather | solution.py:261
  47.6 6.7 %shard_map.168 = bf16[16,2,768]{2,1,0:T(2,128)(2,1)} custom-call(bf16[2,256,768]{2,1,0:T(8,128)(2,1)} %all_gather.3.every_ref, bf16[2,16,768]{2,1,0:T(8,128)(2,1)} %get-tuple-element.5.own_ref, f32[256,256]{1,0:T(8,128)} %bitcast.11, s32[1,256]{1,0:T(1,128)} %bitcast.14, bf16[768,768]{1,0:T(8,128)(2,1)} %wq_ref.3, bf16[768,768]{1,0:T(8,128)(2,1)} %wk_ref.3, ...), custom_call_target="tpu_custom_call" | custom-call | flops 1686110208 | bytes 5865472 | tf_op jit(solution)/shard_map/pallas_call | solution.py:263
  (3 shorter events, 0.0 us)
Async XLA Ops:
  0.6 6.9 %copy-start = (bf16[16,256,128]{2,1,0:T(8,128)(2,1)S(1)}, bf16[16,256,128]{2,1,0:T(8,128)(2,1)}, u32[]{:S(2)}) copy-start(bf16[16,256,128]{2,1,0:T(8,128)(2,1)} %param.20) | copy-start | bytes 3145732
  0.6 11.4 %copy-start.4 = (s32[4]{0:T(128)S(1)}, s32[4]{0:T(128)}, u32[]{:S(2)}) copy-start(s32[4]{0:T(128)} %param.17) | copy-start | bytes 52
  0.7 7.9 %copy-start.1 = (s32[2048]{0:T(1024)S(1)}, s32[2048]{0:T(1024)}, u32[]{:S(2)}) copy-start(s32[2048]{0:T(1024)} %param.18) | copy-start | bytes 24580
  1.5 11.5 %collective-permute-start = (bf16[64,2,128]{2,1,0:T(2,128)(2,1)S(1)}, bf16[64,2,128]{2,1,0:T(2,128)(2,1)S(1)}, u32[]{:S(2)}, u32[]{:S(2)}) collective-permute-start(bf16[64,2,128]{2,1,0:T(2,128)(2,1)S(1)} %slice.14), channel_id=1, source_target_pairs={{0,1},{1,2},{2,3},{3,4},{4,5},{5,6},{6,7},{7,8},{8,9},{9,10},{10,1... | collective-permute-start | bytes 98312 | tf_op jit(solution)/shard_map/ppermute | solution.py:32
  5.6 5.3 %collective-permute-start.1 = (bf16[97,2,128]{2,1,0:T(2,128)(2,1)S(1)}, bf16[97,2,128]{2,1,0:T(2,128)(2,1)S(1)}, u32[]{:S(2)}, u32[]{:S(2)}) collective-permute-start(bf16[97,2,128]{2,1,0:T(2,128)(2,1)S(1)} %broadcast_select_fusion), channel_id=1, source_target_pairs={{1,0},{2,1},{3,2},{4,3},{5,4},{6,5},{7,6},{8,7},{9,8},{10,9},{11,1... | collective-permute-start | bytes 149000 | tf_op jit(solution)/shard_map/ppermute | solution.py:32
  10.9 2.2 %copy-start.2 = (bf16[97,2,128]{2,1,0:T(2,128)(2,1)}, bf16[97,2,128]{2,1,0:T(2,128)(2,1)S(1)}, u32[]{:S(2)}) copy-start(bf16[97,2,128]{2,1,0:T(2,128)(2,1)S(1)} %collective-permute-done.1.upper_ref) | copy-start | bytes 148996
  13.1 0.6 %copy-start.3 = (bf16[64,2,128]{2,1,0:T(2,128)(2,1)}, bf16[64,2,128]{2,1,0:T(2,128)(2,1)S(1)}, u32[]{:S(2)}) copy-start(bf16[64,2,128]{2,1,0:T(2,128)(2,1)S(1)} %collective-permute-done.low_ref) | copy-start | bytes 98308

commit v6 on v5

--- a/solution.py
+++ b/solution.py
@@ -36,14 +36,13 @@
     own_ref,
     low_ref,
     upper_ref,
-    bounds_ref,
+    shift_ref,
     wq_ref,
     wk_ref,
     wv_ref,
     wo_ref,
     wt_ref,
-    row_ids_ref,
-    own_ids_ref,
+    ids_ref,
     token_ref,
     atom_ref,
     state_ref,
@@ -53,6 +52,7 @@
     low_rows,
     high_rows,
     head_dim,
+    devices,
 ):
     f32, bf16 = jnp.float32, jnp.bfloat16
     _, samples, width = own_ref.shape
@@ -60,9 +60,27 @@
     lane = lax.broadcasted_iota(jnp.int32, (1, width), 1) // head_dim
     head_masks = [(lane == h).astype(f32) for h in range(ATOM_HEADS)]
     root = jnp.float32(math.sqrt(head_dim))
+    rank = lax.axis_index("row")
+    base = rank * atom_dev
+    total = devices * atom_dev
+    tok_dev = token_ref.shape[0]
+    row_block = lax.broadcasted_iota(jnp.int32, (rows, 1), 0) // QBLOCK
+    next_shift = upper_ref[pl.ds(high_rows, 1), 0, :].astype(f32)[:, 0:1].astype(jnp.int32)
+    shift = jnp.where(row_block == rows // QBLOCK - 1, next_shift, 0)
+    for j in range(rows // QBLOCK - 1):
+        shift = shift + jnp.where(row_block == j, shift_ref[j], 0)
+    first = row_block * QBLOCK + SHIFT + shift
+    lo = jnp.maximum(first, low_rows - base)
+    hi = jnp.minimum(first + KWIN, total - base + low_rows)
     column = lax.broadcasted_iota(jnp.int32, (rows, ext_rows), 1)
-    keep = (column >= bounds_ref[:, 0:1]) & (column < bounds_ref[:, 1:2])
-    onehot = (own_ids_ref[...] == row_ids_ref[...]).astype(f32)
+    keep = (column >= lo) & (column < hi)
+    own_start = pl.multiple_of(base, atom_dev)
+    next_start = pl.multiple_of(jnp.minimum(base + atom_dev, total - atom_dev), atom_dev)
+    next_ids = ids_ref[:, pl.ds(next_start, atom_dev)][:, 0 : rows - atom_dev]
+    next_ids = jnp.where(rank < devices - 1, next_ids, -1)
+    row_ids = jnp.concatenate([ids_ref[:, pl.ds(own_start, atom_dev)], next_ids], axis=1)
+    own_ids = rank * tok_dev + lax.broadcasted_iota(jnp.int32, (tok_dev, 1), 0)
+    onehot = (own_ids == row_ids).astype(f32)
     counts = jnp.sum(onehot, axis=1, keepdims=True)
     onehot = onehot.astype(bf16)
     for s in range(samples):
@@ -108,7 +126,8 @@
 def token_kernel(
     every_ref,
     own_ref,
-    bias_ref,
+    pair_ref,
+    wb_ref,
     flags_ref,
     wq_ref,
     wk_ref,
@@ -125,7 +144,15 @@
     head_masks = [(lane == h).astype(f32) for h in range(heads)]
     root = jnp.float32(math.sqrt(head_dim))
     keep = flags_ref[...] > 0
-    bias = bias_ref[...]
+    wb = wb_ref[...]
+    bias = jnp.concatenate(
+        [
+            lax.dot_general(wb, pair_ref[t], (((1,), (1,)), ((), ())), preferred_element_type=f32)
+            for t in range(tok_dev)
+        ],
+        axis=0,
+    )
+    mask_rows = jnp.concatenate(head_masks, axis=0)
 
     def normed(x):
         mean = jnp.mean(x, axis=-1, keepdims=True)
@@ -138,7 +165,9 @@
         q = jnp.dot(normed(own), wq_ref[...], preferred_element_type=f32).astype(bf16)
         k = jnp.dot(allx, wk_ref[...], preferred_element_type=f32).astype(bf16)
         v = jnp.dot(allx, wv_ref[...], preferred_element_type=f32).astype(bf16)
-        stacked = jnp.concatenate([q * head_masks[h].astype(bf16) for h in range(heads)], axis=0)
+        stacked = jnp.concatenate(
+            [q[t : t + 1].astype(f32) * mask_rows for t in range(tok_dev)], axis=0
+        ).astype(bf16)
         sc = lax.dot_general(
             stacked, k, (((1,), (1,)), ((), ())), preferred_element_type=f32
         ) / root + bias
@@ -147,10 +176,13 @@
         e = jnp.where(keep, jnp.exp(sc - top), 0.0)
         tot = jnp.sum(e, axis=-1, keepdims=True)
         o = jnp.dot(e.astype(bf16), v, preferred_element_type=f32) / tot
-        mix = o[0:tok_dev] * head_masks[0]
-        for h in range(1, heads):
-            mix = mix + o[h * tok_dev : (h + 1) * tok_dev] * head_masks[h]
-        mix = mix.astype(bf16)
+        mix = jnp.concatenate(
+            [
+                jnp.sum(o[t * heads : (t + 1) * heads] * mask_rows, axis=0, keepdims=True)
+                for t in range(tok_dev)
+            ],
+            axis=0,
+        ).astype(bf16)
         out_ref[:, s, :] = (own + jnp.dot(mix, wo_ref[...], preferred_element_type=f32)).astype(bf16)
 
 
@@ -193,25 +225,10 @@
     upper = shifted(
         jnp.concatenate([atom_feat[:high_rows], shift_row], axis=0), "row", -1
     )
-    next_shift = upper[high_rows, 0, 0].astype(jnp.int32)
 
     head_dim = width // ATOM_HEADS
-    shifts = jnp.concatenate([window_shift, next_shift[None]], axis=0)
     rows = blocks * QBLOCK
     ext_rows = low_rows + atom_dev + high_rows
-    row_block = jnp.arange(rows, dtype=jnp.int32) // QBLOCK
-    first = row_block * QBLOCK + SHIFT + jnp.repeat(shifts, QBLOCK)
-    bounds = jnp.stack(
-        [
-            jnp.maximum(first, low_rows - atom_base),
-            jnp.minimum(first + KWIN, total_atoms - atom_base + low_rows),
-        ],
-        axis=1,
-    )
-    own_ids = rank * tok_dev + jnp.arange(tok_dev, dtype=jnp.int32)
-    row_ids = lax.dynamic_slice_in_dim(
-        jnp.concatenate([atom_token, jnp.full((QBLOCK,), -1, jnp.int32)]), atom_base, rows
-    )
     kernel = functools.partial(
         atom_kernel,
         atom_dev=atom_dev,
@@ -219,6 +236,7 @@
         low_rows=low_rows,
         high_rows=high_rows,
         head_dim=head_dim,
+        devices=devices,
     )
     vmem = pl.BlockSpec(memory_space=pltpu.VMEM)
     flops = 2 * samples * (
@@ -233,8 +251,9 @@
             jax.ShapeDtypeStruct((atom_dev, samples, width), jnp.bfloat16),
             jax.ShapeDtypeStruct((samples, tok_dev, tok_width), jnp.bfloat16),
         ),
-        in_specs=[vmem] * 12,
+        in_specs=[vmem] * 3 + [pl.BlockSpec(memory_space=pltpu.SMEM)] + [vmem] * 7,
         out_specs=(vmem, vmem),
+        compiler_params=pltpu.CompilerParams(vmem_limit_bytes=8 * 1024 * 1024),
         cost_estimate=pl.CostEstimate(
             flops=flops,
             transcendentals=samples * ATOM_HEADS * rows * ext_rows,
@@ -246,25 +265,24 @@
         atom_feat,
         low,
         upper,
-        bounds,
+        window_shift,
         w_atom_query,
         w_atom_key,
         w_atom_value,
         w_atom_out,
         w_to_token,
-        row_ids[None, :],
-        own_ids[:, None],
+        atom_token[None, :],
         token_in,
     )
 
-    bias = jnp.einsum("qkc,ch->hqk", pair, w_bias, preferred_element_type=jnp.float32)
     every = lax.all_gather(state_t, "row", axis=1, tiled=True)
     count = every.shape[1]
     token_out = pl.pallas_call(
         functools.partial(token_kernel, heads=TOKEN_HEADS),
         out_shape=jax.ShapeDtypeStruct((tok_dev, samples, tok_width), jnp.bfloat16),
-        in_specs=[vmem] * 8,
+        in_specs=[vmem] * 9,
         out_specs=vmem,
+        compiler_params=pltpu.CompilerParams(vmem_limit_bytes=24 * 1024 * 1024),
         cost_estimate=pl.CostEstimate(
             flops=2 * samples * tok_width * (
                 2 * count * tok_width + 2 * tok_dev * tok_width + 2 * TOKEN_HEADS * tok_dev * count
@@ -277,7 +295,8 @@
     )(
         every,
         state_t,
-        bias.reshape(TOKEN_HEADS * tok_dev, count),
+        pair,
+        jnp.transpose(w_bias),
         key_mask[None, :],
         w_query,
         w_key,

time: 54.6 us -> 56.5 us (1.035)
  local copies, waits for them, and re-layouts: 4.48 us -> 11.6 us
  Pallas kernels: 12.6 us -> 9.26 us
  matrix products: 1.06 us -> 0 us
  blocking collectives: 28 us -> 27.2 us
  between operations: 1.38 us -> 0.7 us
  starting transfers between devices: 3.65 us -> 4.32 us
  other arithmetic: 2.4 us -> 1.83 us
    unnamed x10 -> x32, local copies, waits for them, and re-layouts: 0.64 us -> 10.8 us
    pallas_call x1, Pallas kernels: 6.72 us -> 4.29 us  [on_device(): pl.pallas_call(functools.partial(token_kernel, heads=TOKEN_HEADS), out_sh...]
    dot_general x1 -> x0, matrix products: 1.06 us -> none  [on_device(): jnp.einsum('qkc,ch->hqk', pair, w_bias, preferred_element_type=jnp.float32)]
    pallas_call x1, Pallas kernels: 5.85 us -> 4.97 us  [on_device(): pl.pallas_call(kernel, out_shape=(jax.ShapeDtypeStruct((atom_dev, samples...]
    dot_general x1 -> x0, local copies, waits for them, and re-layouts: 0.86 us -> none  [on_device(): jnp.einsum('qkc,ch->hqk', pair, w_bias, preferred_element_type=jnp.float32)]
    all_gather x1, blocking collectives: 28 us -> 27.2 us  [on_device(): every = lax.all_gather(state_t, 'row', axis=1, tiled=True)]
    another operation x1 -> x0, local copies, waits for them, and re-layouts: 0.75 us -> none  [on_device(): jnp.stack([jnp.maximum(first, low_rows - atom_base), jnp.minimum(first +...]
    dynamic_slice x1 -> x0, local copies, waits for them, and re-layouts: 0.68 us -> none  [on_device(): lax.dynamic_slice_in_dim(jnp.concatenate([atom_token, jnp.full((QBLOCK,),...]
  transfers between devices with their start and end apart: 2 -> 2, of which waited for: 1 -> 1; matrix products, arithmetic and copies ran while one was open for 12% -> 1% of each run, Pallas kernels for 0% -> 0%
where the time goes in v6:
time: 56.5 us; the launch traced here: 55.7 us
  blocking collectives  27.2 us (48%)
  local copies, waits for them, and re-layouts  11.6 us (21%)
  Pallas kernels  9.26 us (16%)
  starting transfers between devices  4.32 us (8%)
  other arithmetic  1.83 us (3%)
  waiting for transfers between devices  0.84 us (1%)
  between operations  0.7 us (1%)
    all_gather x1, blocking collectives, on_device(): every = lax.all_gather(state_t, 'row', axis=1, tiled=True)  27.2 us
    unnamed x32, local copies, waits for them, and re-layouts  10.8 us
    pallas_call x1, Pallas kernels, on_device(): pl.pallas_call(kernel, out_shape=(jax.ShapeDtypeStruct((atom_dev, samples...  4.97 us
    ppermute x2, starting transfers between devices, shifted(): return lax.ppermute(block, axis, route)  4.32 us
    pallas_call x1, Pallas kernels, on_device(): pl.pallas_call(functools.partial(token_kernel, heads=TOKEN_HEADS), out_sh...  4.29 us
  transfers between devices with their start and end apart: 2, of which 1 were waited for; matrix products, arithmetic and copies ran while one was open for 1% of the time, Pallas kernels for 0%

profile of v6, /device:TPU:0, one launch (start us, length us, event | category | flops | bytes accessed | tf_op | source)
XLA Modules:
  0.0 55.7 jit_solution(3877170178067914724)
XLA Ops:
  0.6 0.0 copy-start
  0.6 0.0 copy-start.4
  0.6 0.8 %convert.3 = bf16[4]{0:T(256)(128)(2,1)S(1)} convert(s32[4]{0:T(128)} %shift_ref.1) | non-fusion elementwise | flops 4 | bytes 24 | tf_op jit(solution)/shard_map/convert
  1.5 1.0 %broadcast_select_fusion = bf16[97,2,128]{2,1,0:T(2,128)(2,1)S(1)} fusion(pred[97]{0:T(512)(128)(4,1)} %constant.1.clone.1, bf16[128,2,128]{2,1,0:T(2,128)(2,1)} %own_ref.1, bf16[]{:T(256)S(1)} %bitcast.8), kind=kLoop, calls=%fused_computation | loop fusion | flops 24832 | bytes 99427 | tf_op jit(solution)/shard_map/concatenate | solution.py:226
  2.5 1.3 %collective-permute-start.1 = (bf16[97,2,128]{2,1,0:T(2,128)(2,1)S(1)}, bf16[97,2,128]{2,1,0:T(2,128)(2,1)S(1)}, u32[]{:S(2)}, u32[]{:S(2)}) collective-permute-start(bf16[97,2,128]{2,1,0:T(2,128)(2,1)S(1)} %broadcast_select_fusion), channel_id=1, source_target_pairs={{1,0},{2,1},{3,2},{4,3},{5,4},{6,5},{7,6},{8,7},{9,8},{10,9},{11,1... | collective-permute-start | bytes 149000 | tf_op jit(solution)/shard_map/ppermute | solution.py:32
  3.8 0.8 %slice.11 = bf16[64,2,128]{2,1,0:T(2,128)(2,1)S(1)} slice(bf16[128,2,128]{2,1,0:T(2,128)(2,1)} %own_ref.1), slice={[64:128], [0:2], [0:128]} | slice | bytes 65536 | tf_op jit(solution)/shard_map/slice | solution.py:224
  4.6 3.0 %collective-permute-start = (bf16[64,2,128]{2,1,0:T(2,128)(2,1)S(1)}, bf16[64,2,128]{2,1,0:T(2,128)(2,1)S(1)}, u32[]{:S(2)}, u32[]{:S(2)}) collective-permute-start(bf16[64,2,128]{2,1,0:T(2,128)(2,1)S(1)} %slice.11), channel_id=1, source_target_pairs={{0,1},{1,2},{2,3},{3,4},{4,5},{5,6},{6,7},{7,8},{8,9},{9,10},{10,1... | collective-permute-start | bytes 98312 | tf_op jit(solution)/shard_map/ppermute | solution.py:32
  7.6 0.8 %collective-permute-done.low_ref = bf16[64,2,128]{2,1,0:T(2,128)(2,1)S(1)} collective-permute-done((bf16[64,2,128]{2,1,0:T(2,128)(2,1)S(1)}, bf16[64,2,128]{2,1,0:T(2,128)(2,1)S(1)}, u32[]{:S(2)}, u32[]{:S(2)}) %collective-permute-start) | collective-permute-done | bytes 32800 | tf_op jit(solution)/shard_map/ppermute | solution.py:32
  8.5 0.0 collective-permute-done.1.upper_ref
  8.5 0.0 copy-start.5
  8.5 0.8 %copy-done.5 = bf16[128,2,128]{2,1,0:T(2,128)(2,1)S(1)} copy-done((bf16[128,2,128]{2,1,0:T(2,128)(2,1)S(1)}, bf16[128,2,128]{2,1,0:T(2,128)(2,1)}, u32[]{:S(2)}) %copy-start.5) | copy-done | bytes 65560
  9.3 0.0 copy-start.8
  9.3 0.9 %copy-done.8 = bf16[128,768]{1,0:T(8,128)(2,1)S(1)} copy-done((bf16[128,768]{1,0:T(8,128)(2,1)S(1)}, bf16[128,768]{1,0:T(8,128)(2,1)}, u32[]{:S(2)}) %copy-start.8) | copy-done | bytes 196632
  10.2 0.0 copy-start.9
  10.2 0.8 %copy-done.9 = bf16[16,2,768]{2,1,0:T(2,128)(2,1)S(1)} copy-done((bf16[16,2,768]{2,1,0:T(2,128)(2,1)S(1)}, bf16[16,2,768]{2,1,0:T(2,128)(2,1)}, u32[]{:S(2)}) %copy-start.9) | copy-done | bytes 49176
  11.0 0.0 copy-start.10
  11.0 0.8 %copy-done.10 = bf16[128,128]{1,0:T(8,128)(2,1)S(1)} copy-done((bf16[128,128]{1,0:T(8,128)(2,1)S(1)}, bf16[128,128]{1,0:T(8,128)(2,1)}, u32[]{:S(2)}) %copy-start.10) | copy-done | bytes 32792
  11.8 0.0 copy-start.11
  11.8 0.8 %copy-done.11 = bf16[128,128]{1,0:T(8,128)(2,1)S(1)} copy-done((bf16[128,128]{1,0:T(8,128)(2,1)S(1)}, bf16[128,128]{1,0:T(8,128)(2,1)}, u32[]{:S(2)}) %copy-start.11) | copy-done | bytes 32792
  12.5 0.0 copy-start.12
  12.6 0.8 %copy-done.12 = bf16[128,128]{1,0:T(8,128)(2,1)S(1)} copy-done((bf16[128,128]{1,0:T(8,128)(2,1)S(1)}, bf16[128,128]{1,0:T(8,128)(2,1)}, u32[]{:S(2)}) %copy-start.12) | copy-done | bytes 32792
  13.3 0.0 copy-start.13
  13.3 0.8 %copy-done.13 = bf16[128,128]{1,0:T(8,128)(2,1)S(1)} copy-done((bf16[128,128]{1,0:T(8,128)(2,1)S(1)}, bf16[128,128]{1,0:T(8,128)(2,1)}, u32[]{:S(2)}) %copy-start.13) | copy-done | bytes 32792
  14.1 0.0 copy-start.14
  14.1 0.7 %copy-done.14 = s32[2048]{0:T(1024)S(1)} copy-done((s32[2048]{0:T(1024)S(1)}, s32[2048]{0:T(1024)}, u32[]{:S(2)}) %copy-start.14) | copy-done | bytes 8216
  14.8 0.0 copy-start.15
  14.8 0.7 %copy-done.15 = s32[4]{0:T(128)S(1)} copy-done((s32[4]{0:T(128)S(1)}, s32[4]{0:T(128)}, u32[]{:S(2)}) %copy-start.15) | copy-done | bytes 40
  15.4 0.0 copy-start.6
  15.4 0.0 copy-start.7
  15.4 5.0 %shard_map.167 = (bf16[128,2,128]{2,1,0:T(2,128)(2,1)}, bf16[2,16,768]{2,1,0:T(8,128)(2,1)S(1)}) custom-call(bf16[128,2,128]{2,1,0:T(2,128)(2,1)S(1)} %copy-done.5, bf16[64,2,128]{2,1,0:T(2,128)(2,1)S(1)} %collective-permute-done.low_ref, bf16[97,2,128]{2,1,0:T(2,128)(2,1)S(1)} %collective-permute-done.1.upper_ref, s32[4]{0:T(128)S(1)} %copy-done.15, ...), custom_call_target="tpu_custom_call" | custom-call | flops 342360064 | bytes 638976 | tf_op jit(solution)/shard_map/pallas_call | solution.py:248
  20.4 27.2 %all_gather.3.every_ref = bf16[2,256,768]{2,1,0:T(8,128)(2,1)S(1)} all-gather(bf16[2,16,768]{2,1,0:T(8,128)(2,1)S(1)} %get-tuple-element.5.own_ref), channel_id=1, replica_groups=mesh['groups'=2,'row'=16] {'row'}, dimensions={1}, use_global_device_ids=true | all-gather | bytes 835584 | tf_op jit(solution)/shard_map/all_gather | solution.py:278
  47.6 0.0 copy-done
  47.6 0.0 copy-done.4
  47.6 0.0 copy-done.6
  47.6 0.0 copy-done.7
  47.6 0.0 copy-start.1
  47.6 1.3 %copy-done.1 = bf16[768,768]{1,0:T(8,128)(2,1)S(1)} copy-done((bf16[768,768]{1,0:T(8,128)(2,1)S(1)}, bf16[768,768]{1,0:T(8,128)(2,1)}, u32[]{:S(2)}) %copy-start.1) | copy-done | bytes 1179672
  48.9 0.0 copy-start.2
  48.9 1.3 %copy-done.2 = bf16[768,768]{1,0:T(8,128)(2,1)S(1)} copy-done((bf16[768,768]{1,0:T(8,128)(2,1)S(1)}, bf16[768,768]{1,0:T(8,128)(2,1)}, u32[]{:S(2)}) %copy-start.2) | copy-done | bytes 1179672
  50.2 0.0 copy-start.3
  50.2 1.3 %copy-done.3 = bf16[768,768]{1,0:T(8,128)(2,1)S(1)} copy-done((bf16[768,768]{1,0:T(8,128)(2,1)S(1)}, bf16[768,768]{1,0:T(8,128)(2,1)}, u32[]{:S(2)}) %copy-start.3) | copy-done | bytes 1179672
  51.4 4.3 %shard_map.168 = bf16[16,2,768]{2,1,0:T(2,128)(2,1)} custom-call(bf16[2,256,768]{2,1,0:T(8,128)(2,1)S(1)} %all_gather.3.every_ref, bf16[2,16,768]{2,1,0:T(8,128)(2,1)S(1)} %get-tuple-element.5.own_ref, bf16[16,256,128]{2,1,0:T(8,128)(2,1)S(1)} %copy-done.4, bf16[16,128]{1,0:T(8,128)(2,1)S(1)} %bitcast.5, s32[1,256]{1,0:T(1,128)S(1)} %bitcast.6, ...), custom_call_target="tpu_custom_call" | custom-call | flops 1686110208 | bytes 5865472 | tf_op jit(solution)/shard_map/pallas_call | solution.py:280
Async XLA Ops:
  0.6 47.0 %copy-start = (bf16[768,768]{1,0:T(8,128)(2,1)S(1)}, bf16[768,768]{1,0:T(8,128)(2,1)}, u32[]{:S(2)}) copy-start(bf16[768,768]{1,0:T(8,128)(2,1)} %wq_ref.3) | copy-start | bytes 3538948
  0.6 47.0 %copy-start.4 = (bf16[16,256,128]{2,1,0:T(8,128)(2,1)S(1)}, bf16[16,256,128]{2,1,0:T(8,128)(2,1)}, u32[]{:S(2)}) copy-start(bf16[16,256,128]{2,1,0:T(8,128)(2,1)} %pair_ref.1) | copy-start | bytes 3145732
  2.5 6.0 %collective-permute-start.1 = (bf16[97,2,128]{2,1,0:T(2,128)(2,1)S(1)}, bf16[97,2,128]{2,1,0:T(2,128)(2,1)S(1)}, u32[]{:S(2)}, u32[]{:S(2)}) collective-permute-start(bf16[97,2,128]{2,1,0:T(2,128)(2,1)S(1)} %broadcast_select_fusion), channel_id=1, source_target_pairs={{1,0},{2,1},{3,2},{4,3},{5,4},{6,5},{7,6},{8,7},{9,8},{10,9},{11,1... | collective-permute-start | bytes 149000 | tf_op jit(solution)/shard_map/ppermute | solution.py:32
  4.6 3.9 %collective-permute-start = (bf16[64,2,128]{2,1,0:T(2,128)(2,1)S(1)}, bf16[64,2,128]{2,1,0:T(2,128)(2,1)S(1)}, u32[]{:S(2)}, u32[]{:S(2)}) collective-permute-start(bf16[64,2,128]{2,1,0:T(2,128)(2,1)S(1)} %slice.11), channel_id=1, source_target_pairs={{0,1},{1,2},{2,3},{3,4},{4,5},{5,6},{6,7},{7,8},{8,9},{9,10},{10,1... | collective-permute-start | bytes 98312 | tf_op jit(solution)/shard_map/ppermute | solution.py:32
  8.5 0.8 %copy-start.5 = (bf16[128,2,128]{2,1,0:T(2,128)(2,1)S(1)}, bf16[128,2,128]{2,1,0:T(2,128)(2,1)}, u32[]{:S(2)}) copy-start(bf16[128,2,128]{2,1,0:T(2,128)(2,1)} %own_ref.1) | copy-start | bytes 196612
  9.3 0.9 %copy-start.8 = (bf16[128,768]{1,0:T(8,128)(2,1)S(1)}, bf16[128,768]{1,0:T(8,128)(2,1)}, u32[]{:S(2)}) copy-start(bf16[128,768]{1,0:T(8,128)(2,1)} %wt_ref.1) | copy-start | bytes 589828
  10.2 0.8 %copy-start.9 = (bf16[16,2,768]{2,1,0:T(2,128)(2,1)S(1)}, bf16[16,2,768]{2,1,0:T(2,128)(2,1)}, u32[]{:S(2)}) copy-start(bf16[16,2,768]{2,1,0:T(2,128)(2,1)} %token_ref.1) | copy-start | bytes 147460
  11.0 0.8 %copy-start.10 = (bf16[128,128]{1,0:T(8,128)(2,1)S(1)}, bf16[128,128]{1,0:T(8,128)(2,1)}, u32[]{:S(2)}) copy-start(bf16[128,128]{1,0:T(8,128)(2,1)} %wq_ref.2) | copy-start | bytes 98308
  11.8 0.8 %copy-start.11 = (bf16[128,128]{1,0:T(8,128)(2,1)S(1)}, bf16[128,128]{1,0:T(8,128)(2,1)}, u32[]{:S(2)}) copy-start(bf16[128,128]{1,0:T(8,128)(2,1)} %wk_ref.2) | copy-start | bytes 98308
  12.5 0.8 %copy-start.12 = (bf16[128,128]{1,0:T(8,128)(2,1)S(1)}, bf16[128,128]{1,0:T(8,128)(2,1)}, u32[]{:S(2)}) copy-start(bf16[128,128]{1,0:T(8,128)(2,1)} %wv_ref.2) | copy-start | bytes 98308
  13.3 0.8 %copy-start.13 = (bf16[128,128]{1,0:T(8,128)(2,1)S(1)}, bf16[128,128]{1,0:T(8,128)(2,1)}, u32[]{:S(2)}) copy-start(bf16[128,128]{1,0:T(8,128)(2,1)} %wo_ref.2) | copy-start | bytes 98308
  14.1 0.7 %copy-start.14 = (s32[2048]{0:T(1024)S(1)}, s32[2048]{0:T(1024)}, u32[]{:S(2)}) copy-start(s32[2048]{0:T(1024)} %param.18) | copy-start | bytes 24580
  14.8 0.7 %copy-start.15 = (s32[4]{0:T(128)S(1)}, s32[4]{0:T(128)}, u32[]{:S(2)}) copy-start(s32[4]{0:T(128)} %shift_ref.1) | copy-start | bytes 52
  15.4 32.2 %copy-start.6 = (bf16[128,16]{0,1:T(8,128)(2,1)S(1)}, bf16[128,16]{0,1:T(8,128)(2,1)}, u32[]{:S(2)}) copy-start(bf16[128,16]{0,1:T(8,128)(2,1)} %param.31) | copy-start | bytes 12292
  15.4 32.2 %copy-start.7 = (s32[256]{0:T(256)S(1)}, s32[256]{0:T(256)}, u32[]{:S(2)}) copy-start(s32[256]{0:T(256)} %param.21) | copy-start | bytes 3076
  47.6 1.3 %copy-start.1 = (bf16[768,768]{1,0:T(8,128)(2,1)S(1)}, bf16[768,768]{1,0:T(8,128)(2,1)}, u32[]{:S(2)}) copy-start(bf16[768,768]{1,0:T(8,128)(2,1)} %wk_ref.3) | copy-start | bytes 3538948
  48.9 1.3 %copy-start.2 = (bf16[768,768]{1,0:T(8,128)(2,1)S(1)}, bf16[768,768]{1,0:T(8,128)(2,1)}, u32[]{:S(2)}) copy-start(bf16[768,768]{1,0:T(8,128)(2,1)} %wv_ref.3) | copy-start | bytes 3538948
  50.2 1.3 %copy-start.3 = (bf16[768,768]{1,0:T(8,128)(2,1)S(1)}, bf16[768,768]{1,0:T(8,128)(2,1)}, u32[]{:S(2)}) copy-start(bf16[768,768]{1,0:T(8,128)(2,1)} %wo_ref.3) | copy-start | bytes 3538948

commit v7 on v6

--- a/solution.py
+++ b/solution.py
@@ -126,17 +126,31 @@
 def token_kernel(
     every_ref,
     own_ref,
-    pair_ref,
+    pair_hbm,
     wb_ref,
     flags_ref,
+    wq_hbm,
+    wk_hbm,
+    wv_hbm,
+    wo_hbm,
+    out_ref,
+    pair_ref,
     wq_ref,
     wk_ref,
     wv_ref,
     wo_ref,
-    out_ref,
+    sems,
     *,
     heads,
 ):
+    copies = [
+        pltpu.make_async_copy(src, dst, sems.at[i])
+        for i, (src, dst) in enumerate(
+            [(wk_hbm, wk_ref), (wv_hbm, wv_ref), (pair_hbm, pair_ref), (wq_hbm, wq_ref), (wo_hbm, wo_ref)]
+        )
+    ]
+    for copy in copies:
+        copy.start()
     f32, bf16 = jnp.float32, jnp.bfloat16
     samples, tok_dev, width = own_ref.shape
     head_dim = width // heads
@@ -145,6 +159,19 @@
     root = jnp.float32(math.sqrt(head_dim))
     keep = flags_ref[...] > 0
     wb = wb_ref[...]
+    mask_rows = jnp.concatenate(head_masks, axis=0)
+
+    def normed(x):
+        mean = jnp.mean(x, axis=-1, keepdims=True)
+        var = jnp.mean((x - mean) ** 2, axis=-1, keepdims=True)
+        return ((x - mean) / jnp.sqrt(var + 1e-05)).astype(bf16)
+
+    allx = [normed(every_ref[s].astype(f32)) for s in range(samples)]
+    copies[0].wait()
+    ks = [jnp.dot(x, wk_ref[...], preferred_element_type=f32).astype(bf16) for x in allx]
+    copies[1].wait()
+    vs = [jnp.dot(x, wv_ref[...], preferred_element_type=f32).astype(bf16) for x in allx]
+    copies[2].wait()
     bias = jnp.concatenate(
         [
             lax.dot_general(wb, pair_ref[t], (((1,), (1,)), ((), ())), preferred_element_type=f32)
@@ -152,37 +179,35 @@
         ],
         axis=0,
     )
-    mask_rows = jnp.concatenate(head_masks, axis=0)
-
-    def normed(x):
-        mean = jnp.mean(x, axis=-1, keepdims=True)
-        var = jnp.mean((x - mean) ** 2, axis=-1, keepdims=True)
-        return ((x - mean) / jnp.sqrt(var + 1e-05)).astype(bf16)
-
+    copies[3].wait()
+    mixes = []
     for s in range(samples):
-        allx = normed(every_ref[s].astype(f32))
         own = own_ref[s].astype(f32)
         q = jnp.dot(normed(own), wq_ref[...], preferred_element_type=f32).astype(bf16)
-        k = jnp.dot(allx, wk_ref[...], preferred_element_type=f32).astype(bf16)
-        v = jnp.dot(allx, wv_ref[...], preferred_element_type=f32).astype(bf16)
         stacked = jnp.concatenate(
             [q[t : t + 1].astype(f32) * mask_rows for t in range(tok_dev)], axis=0
         ).astype(bf16)
         sc = lax.dot_general(
-            stacked, k, (((1,), (1,)), ((), ())), preferred_element_type=f32
+            stacked, ks[s], (((1,), (1,)), ((), ())), preferred_element_type=f32
         ) / root + bias
         sc = jnp.where(keep, sc, -1e30)
         top = jnp.max(sc, axis=-1, keepdims=True)
         e = jnp.where(keep, jnp.exp(sc - top), 0.0)
         tot = jnp.sum(e, axis=-1, keepdims=True)
-        o = jnp.dot(e.astype(bf16), v, preferred_element_type=f32) / tot
-        mix = jnp.concatenate(
-            [
-                jnp.sum(o[t * heads : (t + 1) * heads] * mask_rows, axis=0, keepdims=True)
-                for t in range(tok_dev)
-            ],
-            axis=0,
-        ).astype(bf16)
+        o = jnp.dot(e.astype(bf16), vs[s], preferred_element_type=f32) / tot
+        mixes.append(
+            jnp.concatenate(
+                [
+                    jnp.sum(o[t * heads : (t + 1) * heads] * mask_rows, axis=0, keepdims=True)
+                    for t in range(tok_dev)
+                ],
+                axis=0,
+            ).astype(bf16)
+        )
+    copies[4].wait()
+    for s in range(samples):
+        own = own_ref[s].astype(f32)
+        mix = mixes[s]
         out_ref[:, s, :] = (own + jnp.dot(mix, wo_ref[...], preferred_element_type=f32)).astype(bf16)
 
 
@@ -253,7 +278,6 @@
         ),
         in_specs=[vmem] * 3 + [pl.BlockSpec(memory_space=pltpu.SMEM)] + [vmem] * 7,
         out_specs=(vmem, vmem),
-        compiler_params=pltpu.CompilerParams(vmem_limit_bytes=8 * 1024 * 1024),
         cost_estimate=pl.CostEstimate(
             flops=flops,
             transcendentals=samples * ATOM_HEADS * rows * ext_rows,
@@ -277,12 +301,20 @@
 
     every = lax.all_gather(state_t, "row", axis=1, tiled=True)
     count = every.shape[1]
+    hbm = pl.BlockSpec(memory_space=pl.ANY)
     token_out = pl.pallas_call(
         functools.partial(token_kernel, heads=TOKEN_HEADS),
         out_shape=jax.ShapeDtypeStruct((tok_dev, samples, tok_width), jnp.bfloat16),
-        in_specs=[vmem] * 9,
+        in_specs=[vmem, vmem, hbm, vmem, vmem, hbm, hbm, hbm, hbm],
         out_specs=vmem,
-        compiler_params=pltpu.CompilerParams(vmem_limit_bytes=24 * 1024 * 1024),
+        scratch_shapes=[
+            pltpu.VMEM(pair.shape, pair.dtype),
+            pltpu.VMEM(w_query.shape, w_query.dtype),
+            pltpu.VMEM(w_key.shape, w_key.dtype),
+            pltpu.VMEM(w_value.shape, w_value.dtype),
+            pltpu.VMEM(w_out.shape, w_out.dtype),
+            pltpu.SemaphoreType.DMA((5,)),
+        ],
         cost_estimate=pl.CostEstimate(
             flops=2 * samples * tok_width * (
                 2 * count * tok_width + 2 * tok_dev * tok_width + 2 * TOKEN_HEADS * tok_dev * count

time: 56.5 us -> 51.2 us (0.906)
  local copies, waits for them, and re-layouts: 11.6 us -> 1.4 us
  Pallas kernels: 9.26 us -> 13.1 us
  blocking collectives: 27.2 us -> 28.9 us
    unnamed x32 -> x4, local copies, waits for them, and re-layouts: 10.8 us -> 0.61 us
    pallas_call x1, Pallas kernels: 4.29 us -> 7.27 us  [on_device(): pl.pallas_call(functools.partial(token_kernel, heads=TOKEN_HEADS), out_sh...]
    all_gather x1, blocking collectives: 27.2 us -> 28.9 us  [on_device(): every = lax.all_gather(state_t, 'row', axis=1, tiled=True)]
    pallas_call x1, Pallas kernels: 4.97 us -> 5.79 us  [on_device(): pl.pallas_call(kernel, out_shape=(jax.ShapeDtypeStruct((atom_dev, samples...]
  transfers between devices with their start and end apart: 2 -> 2, of which waited for: 1 -> 1; matrix products, arithmetic and copies ran while one was open for 1% -> 2% of each run, Pallas kernels for 0% -> 0%
where the time goes in v7:
time: 51.2 us; the launch traced here: 50.8 us
  blocking collectives  28.9 us (56%)
  Pallas kernels  13.1 us (26%)
  starting transfers between devices  4.32 us (8%)
  other arithmetic  1.68 us (3%)
  local copies, waits for them, and re-layouts  1.4 us (3%)
  waiting for transfers between devices  0.84 us (2%)
  between operations  0.66 us (1%)
    all_gather x1, blocking collectives, on_device(): every = lax.all_gather(state_t, 'row', axis=1, tiled=True)  28.9 us
    pallas_call x1, Pallas kernels, on_device(): pl.pallas_call(functools.partial(token_kernel, heads=TOKEN_HEADS), out_sh...  7.27 us
    pallas_call x1, Pallas kernels, on_device(): pl.pallas_call(kernel, out_shape=(jax.ShapeDtypeStruct((atom_dev, samples...  5.79 us
    ppermute x2, starting transfers between devices, shifted(): return lax.ppermute(block, axis, route)  4.32 us
  transfers between devices with their start and end apart: 2, of which 1 were waited for; matrix products, arithmetic and copies ran while one was open for 2% of the time, Pallas kernels for 0%

profile of v7, /device:TPU:0, one launch (start us, length us, event | category | flops | bytes accessed | tf_op | source)
XLA Modules:
  0.0 50.8 jit_solution(7696674743611456683)
XLA Ops:
  0.6 0.7 %convert.3 = bf16[4]{0:T(256)(128)(2,1)S(1)} convert(s32[4]{0:T(128)} %shift_ref.1) | non-fusion elementwise | flops 4 | bytes 24 | tf_op jit(solution)/shard_map/convert
  1.3 1.0 %broadcast_select_fusion = bf16[97,2,128]{2,1,0:T(2,128)(2,1)S(1)} fusion(pred[97]{0:T(512)(128)(4,1)} %constant.1.clone.1, bf16[128,2,128]{2,1,0:T(2,128)(2,1)} %own_ref.1, bf16[]{:T(256)S(1)} %bitcast.7), kind=kLoop, calls=%fused_computation | loop fusion | flops 24832 | bytes 99427 | tf_op jit(solution)/shard_map/concatenate | solution.py:251
  2.3 1.3 %collective-permute-start.1 = (bf16[97,2,128]{2,1,0:T(2,128)(2,1)S(1)}, bf16[97,2,128]{2,1,0:T(2,128)(2,1)S(1)}, u32[]{:S(2)}, u32[]{:S(2)}) collective-permute-start(bf16[97,2,128]{2,1,0:T(2,128)(2,1)S(1)} %broadcast_select_fusion), channel_id=1, source_target_pairs={{1,0},{2,1},{3,2},{4,3},{5,4},{6,5},{7,6},{8,7},{9,8},{10,9},{11,1... | collective-permute-start | bytes 149000 | tf_op jit(solution)/shard_map/ppermute | solution.py:32
  3.6 0.8 %slice.11 = bf16[64,2,128]{2,1,0:T(2,128)(2,1)S(1)} slice(bf16[128,2,128]{2,1,0:T(2,128)(2,1)} %own_ref.1), slice={[64:128], [0:2], [0:128]} | slice | bytes 65536 | tf_op jit(solution)/shard_map/slice | solution.py:249
  4.4 3.0 %collective-permute-start = (bf16[64,2,128]{2,1,0:T(2,128)(2,1)S(1)}, bf16[64,2,128]{2,1,0:T(2,128)(2,1)S(1)}, u32[]{:S(2)}, u32[]{:S(2)}) collective-permute-start(bf16[64,2,128]{2,1,0:T(2,128)(2,1)S(1)} %slice.11), channel_id=1, source_target_pairs={{0,1},{1,2},{2,3},{3,4},{4,5},{5,6},{6,7},{7,8},{8,9},{9,10},{10,1... | collective-permute-start | bytes 98312 | tf_op jit(solution)/shard_map/ppermute | solution.py:32
  7.4 0.8 %collective-permute-done.low_ref = bf16[64,2,128]{2,1,0:T(2,128)(2,1)S(1)} collective-permute-done((bf16[64,2,128]{2,1,0:T(2,128)(2,1)S(1)}, bf16[64,2,128]{2,1,0:T(2,128)(2,1)S(1)}, u32[]{:S(2)}, u32[]{:S(2)}) %collective-permute-start) | collective-permute-done | bytes 32800 | tf_op jit(solution)/shard_map/ppermute | solution.py:32
  8.3 0.0 copy-start.1
  8.3 0.0 collective-permute-done.1.upper_ref
  8.3 0.0 copy-start
  8.3 0.6 %copy-done.1 = bf16[64,2,128]{2,1,0:T(2,128)(2,1)} copy-done((bf16[64,2,128]{2,1,0:T(2,128)(2,1)}, bf16[64,2,128]{2,1,0:T(2,128)(2,1)S(1)}, u32[]{:S(2)}) %copy-start.1) | copy-done | bytes 32792
  8.9 0.0 copy-done
  8.9 5.8 %shard_map.167 = (bf16[128,2,128]{2,1,0:T(2,128)(2,1)}, bf16[2,16,768]{2,1,0:T(8,128)(2,1)}) custom-call(bf16[128,2,128]{2,1,0:T(2,128)(2,1)} %own_ref.1, bf16[64,2,128]{2,1,0:T(2,128)(2,1)} %copy-done.1, bf16[97,2,128]{2,1,0:T(2,128)(2,1)} %copy-done, s32[4]{0:T(128)} %shift_ref.1, bf16[128,128]{1,0:T(8,128)(2,1)} %wq_ref.1, bf16[128,128]{1,0:T(8,128)(2,1)} %wk_ref.1, ...), custom_call_target="tpu_custom_call" | custom-call | flops 342360064 | bytes 638976 | tf_op jit(solution)/shard_map/pallas_call | solution.py:273
  14.7 28.9 %all_gather.3.every_ref = bf16[2,256,768]{2,1,0:T(8,128)(2,1)} all-gather(bf16[2,16,768]{2,1,0:T(8,128)(2,1)} %get-tuple-element.5.own_ref), channel_id=1, replica_groups=mesh['groups'=2,'row'=16] {'row'}, dimensions={1}, use_global_device_ids=true | all-gather | bytes 835584 | tf_op jit(solution)/shard_map/all_gather | solution.py:302
  43.6 7.3 %shard_map.168 = bf16[16,2,768]{2,1,0:T(2,128)(2,1)} custom-call(bf16[2,256,768]{2,1,0:T(8,128)(2,1)} %all_gather.3.every_ref, bf16[2,16,768]{2,1,0:T(8,128)(2,1)} %get-tuple-element.5.own_ref, bf16[16,256,128]{2,1,0:T(8,128)(2,1)} %pair_hbm.1, bf16[16,128]{1,0:T(8,128)(2,1)} %bitcast.5, s32[1,256]{1,0:T(1,128)} %bitcast.6, bf16[768,768]{1,0:T(8,128)(2,1)} %wq_hbm.1, ...), custom_call_target="tpu_custom_call" | custom-call | flops 1686110208 | bytes 5865472 | tf_op jit(solution)/shard_map/pallas_call | solution.py:305
Async XLA Ops:
  2.3 6.0 %collective-permute-start.1 = (bf16[97,2,128]{2,1,0:T(2,128)(2,1)S(1)}, bf16[97,2,128]{2,1,0:T(2,128)(2,1)S(1)}, u32[]{:S(2)}, u32[]{:S(2)}) collective-permute-start(bf16[97,2,128]{2,1,0:T(2,128)(2,1)S(1)} %broadcast_select_fusion), channel_id=1, source_target_pairs={{1,0},{2,1},{3,2},{4,3},{5,4},{6,5},{7,6},{8,7},{9,8},{10,9},{11,1... | collective-permute-start | bytes 149000 | tf_op jit(solution)/shard_map/ppermute | solution.py:32
  4.4 3.9 %collective-permute-start = (bf16[64,2,128]{2,1,0:T(2,128)(2,1)S(1)}, bf16[64,2,128]{2,1,0:T(2,128)(2,1)S(1)}, u32[]{:S(2)}, u32[]{:S(2)}) collective-permute-start(bf16[64,2,128]{2,1,0:T(2,128)(2,1)S(1)} %slice.11), channel_id=1, source_target_pairs={{0,1},{1,2},{2,3},{3,4},{4,5},{5,6},{6,7},{7,8},{8,9},{9,10},{10,1... | collective-permute-start | bytes 98312 | tf_op jit(solution)/shard_map/ppermute | solution.py:32
  8.3 0.6 %copy-start.1 = (bf16[64,2,128]{2,1,0:T(2,128)(2,1)}, bf16[64,2,128]{2,1,0:T(2,128)(2,1)S(1)}, u32[]{:S(2)}) copy-start(bf16[64,2,128]{2,1,0:T(2,128)(2,1)S(1)} %collective-permute-done.low_ref) | copy-start | bytes 98308
  8.3 0.6 %copy-start = (bf16[97,2,128]{2,1,0:T(2,128)(2,1)}, bf16[97,2,128]{2,1,0:T(2,128)(2,1)S(1)}, u32[]{:S(2)}) copy-start(bf16[97,2,128]{2,1,0:T(2,128)(2,1)S(1)} %collective-permute-done.1.upper_ref) | copy-start | bytes 148996

commit v8 on v7

--- a/solution.py
+++ b/solution.py
@@ -44,8 +44,16 @@
     wt_ref,
     ids_ref,
     token_ref,
+    wq_hbm,
+    pair_hbm,
+    wb_ref,
     atom_ref,
     state_ref,
+    query_ref,
+    bias_ref,
+    wtq_ref,
+    pair_ref,
+    sems,
     *,
     atom_dev,
     rows,
@@ -55,6 +63,12 @@
     devices,
 ):
     f32, bf16 = jnp.float32, jnp.bfloat16
+    copies = [
+        pltpu.make_async_copy(wq_hbm, wtq_ref, sems.at[0]),
+        pltpu.make_async_copy(pair_hbm, pair_ref, sems.at[1]),
+    ]
+    for copy in copies:
+        copy.start()
     _, samples, width = own_ref.shape
     ext_rows = low_rows + atom_dev + high_rows
     lane = lax.broadcasted_iota(jnp.int32, (1, width), 1) // head_dim
@@ -121,21 +135,34 @@
             + jnp.dot(onehot, low_part, preferred_element_type=f32)
         )
         state_ref[s] = (token_ref[:, s, :].astype(f32) + sums / counts).astype(bf16)
+    copies[1].wait()
+    wb = wb_ref[...]
+    bias_ref[...] = jnp.concatenate(
+        [
+            lax.dot_general(wb, pair_ref[t], (((1,), (1,)), ((), ())), preferred_element_type=f32)
+            for t in range(tok_dev)
+        ],
+        axis=0,
+    )
+    copies[0].wait()
+    for s in range(samples):
+        st = state_ref[s].astype(f32)
+        mean = jnp.mean(st, axis=-1, keepdims=True)
+        var = jnp.mean((st - mean) ** 2, axis=-1, keepdims=True)
+        tn = ((st - mean) / jnp.sqrt(var + 1e-05)).astype(bf16)
+        query_ref[s] = jnp.dot(tn, wtq_ref[...], preferred_element_type=f32).astype(bf16)
 
 
 def token_kernel(
     every_ref,
     own_ref,
-    pair_hbm,
-    wb_ref,
+    query_ref,
+    bias_ref,
     flags_ref,
-    wq_hbm,
     wk_hbm,
     wv_hbm,
     wo_hbm,
     out_ref,
-    pair_ref,
-    wq_ref,
     wk_ref,
     wv_ref,
     wo_ref,
@@ -145,9 +172,7 @@
 ):
     copies = [
         pltpu.make_async_copy(src, dst, sems.at[i])
-        for i, (src, dst) in enumerate(
-            [(wk_hbm, wk_ref), (wv_hbm, wv_ref), (pair_hbm, pair_ref), (wq_hbm, wq_ref), (wo_hbm, wo_ref)]
-        )
+        for i, (src, dst) in enumerate([(wk_hbm, wk_ref), (wv_hbm, wv_ref), (wo_hbm, wo_ref)])
     ]
     for copy in copies:
         copy.start()
@@ -158,7 +183,6 @@
     head_masks = [(lane == h).astype(f32) for h in range(heads)]
     root = jnp.float32(math.sqrt(head_dim))
     keep = flags_ref[...] > 0
-    wb = wb_ref[...]
     mask_rows = jnp.concatenate(head_masks, axis=0)
 
     def normed(x):
@@ -171,19 +195,10 @@
     ks = [jnp.dot(x, wk_ref[...], preferred_element_type=f32).astype(bf16) for x in allx]
     copies[1].wait()
     vs = [jnp.dot(x, wv_ref[...], preferred_element_type=f32).astype(bf16) for x in allx]
-    copies[2].wait()
-    bias = jnp.concatenate(
-        [
-            lax.dot_general(wb, pair_ref[t], (((1,), (1,)), ((), ())), preferred_element_type=f32)
-            for t in range(tok_dev)
-        ],
-        axis=0,
-    )
-    copies[3].wait()
+    bias = bias_ref[...]
     mixes = []
     for s in range(samples):
-        own = own_ref[s].astype(f32)
-        q = jnp.dot(normed(own), wq_ref[...], preferred_element_type=f32).astype(bf16)
+        q = query_ref[s]
         stacked = jnp.concatenate(
             [q[t : t + 1].astype(f32) * mask_rows for t in range(tok_dev)], axis=0
         ).astype(bf16)
@@ -204,7 +219,7 @@
                 axis=0,
             ).astype(bf16)
         )
-    copies[4].wait()
+    copies[2].wait()
     for s in range(samples):
         own = own_ref[s].astype(f32)
         mix = mixes[s]
@@ -270,14 +285,26 @@
         + ATOM_HEADS * rows * ext_rows * width * 2
         + 3 * tok_dev * rows * tok_width
     )
-    atom_out, state_t = pl.pallas_call(
+    hbm = pl.BlockSpec(memory_space=pl.ANY)
+    count = tok_dev * devices
+    atom_out, state_t, query_t, bias = pl.pallas_call(
         kernel,
         out_shape=(
             jax.ShapeDtypeStruct((atom_dev, samples, width), jnp.bfloat16),
             jax.ShapeDtypeStruct((samples, tok_dev, tok_width), jnp.bfloat16),
+            jax.ShapeDtypeStruct((samples, tok_dev, tok_width), jnp.bfloat16),
+            jax.ShapeDtypeStruct((TOKEN_HEADS * tok_dev, count), jnp.float32),
         ),
-        in_specs=[vmem] * 3 + [pl.BlockSpec(memory_space=pltpu.SMEM)] + [vmem] * 7,
-        out_specs=(vmem, vmem),
+        in_specs=[vmem] * 3
+        + [pl.BlockSpec(memory_space=pltpu.SMEM)]
+        + [vmem] * 7
+        + [hbm, hbm, vmem],
+        out_specs=(vmem, vmem, vmem, vmem),
+        scratch_shapes=[
+            pltpu.VMEM(w_query.shape, w_query.dtype),
+            pltpu.VMEM(pair.shape, pair.dtype),
+            pltpu.SemaphoreType.DMA((2,)),
+        ],
         cost_estimate=pl.CostEstimate(
             flops=flops,
             transcendentals=samples * ATOM_HEADS * rows * ext_rows,
@@ -297,23 +324,22 @@
         w_to_token,
         atom_token[None, :],
         token_in,
+        w_query,
+        pair,
+        jnp.transpose(w_bias),
     )
 
     every = lax.all_gather(state_t, "row", axis=1, tiled=True)
-    count = every.shape[1]
-    hbm = pl.BlockSpec(memory_space=pl.ANY)
     token_out = pl.pallas_call(
         functools.partial(token_kernel, heads=TOKEN_HEADS),
         out_shape=jax.ShapeDtypeStruct((tok_dev, samples, tok_width), jnp.bfloat16),
-        in_specs=[vmem, vmem, hbm, vmem, vmem, hbm, hbm, hbm, hbm],
+        in_specs=[vmem, vmem, vmem, vmem, vmem, hbm, hbm, hbm],
         out_specs=vmem,
         scratch_shapes=[
-            pltpu.VMEM(pair.shape, pair.dtype),
-            pltpu.VMEM(w_query.shape, w_query.dtype),
             pltpu.VMEM(w_key.shape, w_key.dtype),
             pltpu.VMEM(w_value.shape, w_value.dtype),
             pltpu.VMEM(w_out.shape, w_out.dtype),
-            pltpu.SemaphoreType.DMA((5,)),
+            pltpu.SemaphoreType.DMA((3,)),
         ],
         cost_estimate=pl.CostEstimate(
             flops=2 * samples * tok_width * (
@@ -327,10 +353,9 @@
     )(
         every,
         state_t,
-        pair,
-        jnp.transpose(w_bias),
+        query_t,
+        bias,
         key_mask[None, :],
-        w_query,
         w_key,
         w_value,
         w_out,

time: 51.2 us -> 51 us (level)
    pallas_call x1, Pallas kernels: 7.27 us -> 5.98 us  [on_device(): pl.pallas_call(functools.partial(token_kernel, heads=TOKEN_HEADS), out_sh...]
    pallas_call x1, Pallas kernels: 5.79 us -> 6.84 us  [on_device(): pl.pallas_call(kernel, out_shape=(jax.ShapeDtypeStruct((atom_dev, samples...]
where the time goes in v8:
time: 51 us; the launch traced here: 50.6 us
  blocking collectives  28.9 us (57%)
  Pallas kernels  12.8 us (25%)
  starting transfers between devices  4.32 us (8%)
  other arithmetic  1.68 us (3%)
  local copies, waits for them, and re-layouts  1.4 us (3%)
  waiting for transfers between devices  0.84 us (2%)
  between operations  0.67 us (1%)
    all_gather x1, blocking collectives, on_device(): every = lax.all_gather(state_t, 'row', axis=1, tiled=True)  28.9 us
    pallas_call x1, Pallas kernels, on_device(): pl.pallas_call(kernel, out_shape=(jax.ShapeDtypeStruct((atom_dev, samples...  6.84 us
    pallas_call x1, Pallas kernels, on_device(): pl.pallas_call(functools.partial(token_kernel, heads=TOKEN_HEADS), out_sh...  5.98 us
    ppermute x2, starting transfers between devices, shifted(): return lax.ppermute(block, axis, route)  4.32 us
    concatenate x1, other arithmetic, on_device(): jnp.concatenate([atom_feat[:high_rows], shift_row], axis=0)  1.02 us
  transfers between devices with their start and end apart: 2, of which 1 were waited for; matrix products, arithmetic and copies ran while one was open for 2% of the time, Pallas kernels for 0%

profile of v8, /device:TPU:0, one launch (start us, length us, event | category | flops | bytes accessed | tf_op | source)
XLA Modules:
  0.0 50.6 jit_solution(12789634270234019754)
XLA Ops:
  0.6 0.7 %convert.3 = bf16[4]{0:T(256)(128)(2,1)S(1)} convert(s32[4]{0:T(128)} %shift_ref.1) | non-fusion elementwise | flops 4 | bytes 24 | tf_op jit(solution)/shard_map/convert
  1.3 1.0 %broadcast_select_fusion = bf16[97,2,128]{2,1,0:T(2,128)(2,1)S(1)} fusion(pred[97]{0:T(512)(128)(4,1)} %constant.1.clone.1, bf16[128,2,128]{2,1,0:T(2,128)(2,1)} %own_ref.1, bf16[]{:T(256)S(1)} %bitcast.7), kind=kLoop, calls=%fused_computation | loop fusion | flops 24832 | bytes 99427 | tf_op jit(solution)/shard_map/concatenate | solution.py:266
  2.3 1.3 %collective-permute-start.1 = (bf16[97,2,128]{2,1,0:T(2,128)(2,1)S(1)}, bf16[97,2,128]{2,1,0:T(2,128)(2,1)S(1)}, u32[]{:S(2)}, u32[]{:S(2)}) collective-permute-start(bf16[97,2,128]{2,1,0:T(2,128)(2,1)S(1)} %broadcast_select_fusion), channel_id=1, source_target_pairs={{1,0},{2,1},{3,2},{4,3},{5,4},{6,5},{7,6},{8,7},{9,8},{10,9},{11,1... | collective-permute-start | bytes 149000 | tf_op jit(solution)/shard_map/ppermute | solution.py:32
  3.6 0.8 %slice.11 = bf16[64,2,128]{2,1,0:T(2,128)(2,1)S(1)} slice(bf16[128,2,128]{2,1,0:T(2,128)(2,1)} %own_ref.1), slice={[64:128], [0:2], [0:128]} | slice | bytes 65536 | tf_op jit(solution)/shard_map/slice | solution.py:264
  4.4 3.0 %collective-permute-start = (bf16[64,2,128]{2,1,0:T(2,128)(2,1)S(1)}, bf16[64,2,128]{2,1,0:T(2,128)(2,1)S(1)}, u32[]{:S(2)}, u32[]{:S(2)}) collective-permute-start(bf16[64,2,128]{2,1,0:T(2,128)(2,1)S(1)} %slice.11), channel_id=1, source_target_pairs={{0,1},{1,2},{2,3},{3,4},{4,5},{5,6},{6,7},{7,8},{8,9},{9,10},{10,1... | collective-permute-start | bytes 98312 | tf_op jit(solution)/shard_map/ppermute | solution.py:32
  7.4 0.8 %collective-permute-done.low_ref = bf16[64,2,128]{2,1,0:T(2,128)(2,1)S(1)} collective-permute-done((bf16[64,2,128]{2,1,0:T(2,128)(2,1)S(1)}, bf16[64,2,128]{2,1,0:T(2,128)(2,1)S(1)}, u32[]{:S(2)}, u32[]{:S(2)}) %collective-permute-start) | collective-permute-done | bytes 32800 | tf_op jit(solution)/shard_map/ppermute | solution.py:32
  8.3 0.0 copy-start.1
  8.3 0.0 collective-permute-done.1.upper_ref
  8.3 0.0 copy-start
  8.3 0.6 %copy-done.1 = bf16[64,2,128]{2,1,0:T(2,128)(2,1)} copy-done((bf16[64,2,128]{2,1,0:T(2,128)(2,1)}, bf16[64,2,128]{2,1,0:T(2,128)(2,1)S(1)}, u32[]{:S(2)}) %copy-start.1) | copy-done | bytes 32792
  8.9 0.0 copy-done
  8.9 6.8 %shard_map.167 = (bf16[128,2,128]{2,1,0:T(2,128)(2,1)}, bf16[2,16,768]{2,1,0:T(8,128)(2,1)}, bf16[2,16,768]{2,1,0:T(8,128)(2,1)}, f32[256,256]{1,0:T(8,128)}) custom-call(bf16[128,2,128]{2,1,0:T(2,128)(2,1)} %own_ref.1, bf16[64,2,128]{2,1,0:T(2,128)(2,1)} %copy-done.1, bf16[97,2,128]{2,1,0:T(2,128)(2,1)} %copy-done, s32[4]{0:T(128)} %shift_ref.1, ...), custom_call_target="tpu_custom_call" | custom-call | flops 342360064 | bytes 638976 | tf_op jit(solution)/shard_map/pallas_call | solution.py:290
  15.8 28.9 %all_gather.3.every_ref = bf16[2,256,768]{2,1,0:T(8,128)(2,1)} all-gather(bf16[2,16,768]{2,1,0:T(8,128)(2,1)} %get-tuple-element.7.own_ref), channel_id=1, replica_groups=mesh['groups'=2,'row'=16] {'row'}, dimensions={1}, use_global_device_ids=true | all-gather | bytes 835584 | tf_op jit(solution)/shard_map/all_gather | solution.py:332
  44.6 6.0 %shard_map.168 = bf16[16,2,768]{2,1,0:T(2,128)(2,1)} custom-call(bf16[2,256,768]{2,1,0:T(8,128)(2,1)} %all_gather.3.every_ref, bf16[2,16,768]{2,1,0:T(8,128)(2,1)} %get-tuple-element.7.own_ref, bf16[2,16,768]{2,1,0:T(8,128)(2,1)} %get-tuple-element.8.query_ref, f32[256,256]{1,0:T(8,128)} %get-tuple-element.9.bias_ref, s32[1,256]{1,0:T(1,128)} %bitcast.8, ...), custom_call_target="tpu_custom_call" | custom-call | flops 1686110208 | bytes 5865472 | tf_op jit(solution)/shard_map/pallas_call | solution.py:333
Async XLA Ops:
  2.3 6.0 %collective-permute-start.1 = (bf16[97,2,128]{2,1,0:T(2,128)(2,1)S(1)}, bf16[97,2,128]{2,1,0:T(2,128)(2,1)S(1)}, u32[]{:S(2)}, u32[]{:S(2)}) collective-permute-start(bf16[97,2,128]{2,1,0:T(2,128)(2,1)S(1)} %broadcast_select_fusion), channel_id=1, source_target_pairs={{1,0},{2,1},{3,2},{4,3},{5,4},{6,5},{7,6},{8,7},{9,8},{10,9},{11,1... | collective-permute-start | bytes 149000 | tf_op jit(solution)/shard_map/ppermute | solution.py:32
  4.4 3.9 %collective-permute-start = (bf16[64,2,128]{2,1,0:T(2,128)(2,1)S(1)}, bf16[64,2,128]{2,1,0:T(2,128)(2,1)S(1)}, u32[]{:S(2)}, u32[]{:S(2)}) collective-permute-start(bf16[64,2,128]{2,1,0:T(2,128)(2,1)S(1)} %slice.11), channel_id=1, source_target_pairs={{0,1},{1,2},{2,3},{3,4},{4,5},{5,6},{6,7},{7,8},{8,9},{9,10},{10,1... | collective-permute-start | bytes 98312 | tf_op jit(solution)/shard_map/ppermute | solution.py:32
  8.3 0.6 %copy-start.1 = (bf16[64,2,128]{2,1,0:T(2,128)(2,1)}, bf16[64,2,128]{2,1,0:T(2,128)(2,1)S(1)}, u32[]{:S(2)}) copy-start(bf16[64,2,128]{2,1,0:T(2,128)(2,1)S(1)} %collective-permute-done.low_ref) | copy-start | bytes 98308
  8.3 0.6 %copy-start = (bf16[97,2,128]{2,1,0:T(2,128)(2,1)}, bf16[97,2,128]{2,1,0:T(2,128)(2,1)S(1)}, u32[]{:S(2)}) copy-start(bf16[97,2,128]{2,1,0:T(2,128)(2,1)S(1)} %collective-permute-done.1.upper_ref) | copy-start | bytes 148996

commit v9 on v8

--- a/solution.py
+++ b/solution.py
@@ -45,14 +45,10 @@
     ids_ref,
     token_ref,
     wq_hbm,
-    pair_hbm,
-    wb_ref,
     atom_ref,
     state_ref,
     query_ref,
-    bias_ref,
     wtq_ref,
-    pair_ref,
     sems,
     *,
     atom_dev,
@@ -63,10 +59,7 @@
     devices,
 ):
     f32, bf16 = jnp.float32, jnp.bfloat16
-    copies = [
-        pltpu.make_async_copy(wq_hbm, wtq_ref, sems.at[0]),
-        pltpu.make_async_copy(pair_hbm, pair_ref, sems.at[1]),
-    ]
+    copies = [pltpu.make_async_copy(wq_hbm, wtq_ref, sems.at[0])]
     for copy in copies:
         copy.start()
     _, samples, width = own_ref.shape
@@ -135,15 +128,6 @@
             + jnp.dot(onehot, low_part, preferred_element_type=f32)
         )
         state_ref[s] = (token_ref[:, s, :].astype(f32) + sums / counts).astype(bf16)
-    copies[1].wait()
-    wb = wb_ref[...]
-    bias_ref[...] = jnp.concatenate(
-        [
-            lax.dot_general(wb, pair_ref[t], (((1,), (1,)), ((), ())), preferred_element_type=f32)
-            for t in range(tok_dev)
-        ],
-        axis=0,
-    )
     copies[0].wait()
     for s in range(samples):
         st = state_ref[s].astype(f32)
@@ -287,23 +271,21 @@
     )
     hbm = pl.BlockSpec(memory_space=pl.ANY)
     count = tok_dev * devices
-    atom_out, state_t, query_t, bias = pl.pallas_call(
+    atom_out, state_t, query_t = pl.pallas_call(
         kernel,
         out_shape=(
             jax.ShapeDtypeStruct((atom_dev, samples, width), jnp.bfloat16),
             jax.ShapeDtypeStruct((samples, tok_dev, tok_width), jnp.bfloat16),
             jax.ShapeDtypeStruct((samples, tok_dev, tok_width), jnp.bfloat16),
-            jax.ShapeDtypeStruct((TOKEN_HEADS * tok_dev, count), jnp.float32),
         ),
         in_specs=[vmem] * 3
         + [pl.BlockSpec(memory_space=pltpu.SMEM)]
         + [vmem] * 7
-        + [hbm, hbm, vmem],
-        out_specs=(vmem, vmem, vmem, vmem),
+        + [hbm],
+        out_specs=(vmem, vmem, vmem),
         scratch_shapes=[
             pltpu.VMEM(w_query.shape, w_query.dtype),
-            pltpu.VMEM(pair.shape, pair.dtype),
-            pltpu.SemaphoreType.DMA((2,)),
+            pltpu.SemaphoreType.DMA((1,)),
         ],
         cost_estimate=pl.CostEstimate(
             flops=flops,
@@ -325,9 +307,9 @@
         atom_token[None, :],
         token_in,
         w_query,
-        pair,
-        jnp.transpose(w_bias),
-    )
+    )
+    bias = jnp.einsum("qkc,ch->qhk", pair, w_bias, preferred_element_type=jnp.float32)
+    bias = bias.reshape(tok_dev * TOKEN_HEADS, count)
 
     every = lax.all_gather(state_t, "row", axis=1, tiled=True)
     token_out = pl.pallas_call(

time: 51 us -> 50.8 us (level)
  blocking collectives: 28.9 us -> 26.7 us
  matrix products: 0 us -> 1.78 us
  waiting for transfers between devices: 0.84 us -> 2.17 us
  starting transfers between devices: 4.32 us -> 3.65 us
    all_gather x1, blocking collectives: 28.9 us -> 26.7 us  [on_device(): every = lax.all_gather(state_t, 'row', axis=1, tiled=True)]
    dot_general x0 -> x1, matrix products: none -> 1.78 us  [on_device(): jnp.einsum('qkc,ch->qhk', pair, w_bias, preferred_element_type=jnp.float32)]
    ppermute x2, waiting for transfers between devices: 0.84 us -> 2.17 us  [shifted(): return lax.ppermute(block, axis, route)]
    ppermute x2, starting transfers between devices: 4.32 us -> 3.65 us  [shifted(): return lax.ppermute(block, axis, route)]
  transfers between devices with their start and end apart: 2 -> 2, of which waited for: 1 -> 1; matrix products, arithmetic and copies ran while one was open for 2% -> 7% of each run, Pallas kernels for 0% -> 0%
where the time goes in v9:
time: 50.8 us; the launch traced here: 50.5 us
  blocking collectives  26.7 us (53%)
  Pallas kernels  12.4 us (24%)
  starting transfers between devices  3.65 us (7%)
  waiting for transfers between devices  2.17 us (4%)
  matrix products  1.78 us (4%)
  other arithmetic  1.68 us (3%)
  local copies, waits for them, and re-layouts  1.5 us (3%)
  between operations  0.68 us (1%)
    all_gather x1, blocking collectives, on_device(): every = lax.all_gather(state_t, 'row', axis=1, tiled=True)  26.7 us
    pallas_call x1, Pallas kernels, on_device(): pl.pallas_call(kernel, out_shape=(jax.ShapeDtypeStruct((atom_dev, samples...  6.38 us
    pallas_call x1, Pallas kernels, on_device(): pl.pallas_call(functools.partial(token_kernel, heads=TOKEN_HEADS), out_sh...  5.98 us
    ppermute x2, starting transfers between devices, shifted(): return lax.ppermute(block, axis, route)  3.65 us
    ppermute x2, waiting for transfers between devices, shifted(): return lax.ppermute(block, axis, route)  2.17 us
    dot_general x1, matrix products, on_device(): jnp.einsum('qkc,ch->qhk', pair, w_bias, preferred_element_type=jnp.float32)  1.78 us
    concatenate x1, other arithmetic, on_device(): jnp.concatenate([atom_feat[:high_rows], shift_row], axis=0)  1.02 us
  transfers between devices with their start and end apart: 2, of which 1 were waited for; matrix products, arithmetic and copies ran while one was open for 7% of the time, Pallas kernels for 0%

profile of v9, /device:TPU:0, one launch (start us, length us, event | category | flops | bytes accessed | tf_op | source)
XLA Modules:
  0.0 50.5 jit_solution(375788494094059975)
XLA Ops:
  0.6 0.0 copy-start
  0.6 0.9 %slice.11 = bf16[64,2,128]{2,1,0:T(2,128)(2,1)S(1)} slice(bf16[128,2,128]{2,1,0:T(2,128)(2,1)} %own_ref.1), slice={[64:128], [0:2], [0:128]} | slice | bytes 65536 | tf_op jit(solution)/shard_map/slice | solution.py:248
  1.5 2.4 %collective-permute-start = (bf16[64,2,128]{2,1,0:T(2,128)(2,1)S(1)}, bf16[64,2,128]{2,1,0:T(2,128)(2,1)S(1)}, u32[]{:S(2)}, u32[]{:S(2)}) collective-permute-start(bf16[64,2,128]{2,1,0:T(2,128)(2,1)S(1)} %slice.11), channel_id=1, source_target_pairs={{0,1},{1,2},{2,3},{3,4},{4,5},{5,6},{6,7},{7,8},{8,9},{9,10},{10,1... | collective-permute-start | bytes 98312 | tf_op jit(solution)/shard_map/ppermute | solution.py:32
  3.9 0.7 %convert.3 = bf16[4]{0:T(256)(128)(2,1)S(1)} convert(s32[4]{0:T(128)} %shift_ref.1) | non-fusion elementwise | flops 4 | bytes 24 | tf_op jit(solution)/shard_map/convert
  4.5 1.0 %broadcast_select_fusion = bf16[97,2,128]{2,1,0:T(2,128)(2,1)S(1)} fusion(pred[97]{0:T(512)(128)(4,1)} %constant.1.clone.1, bf16[128,2,128]{2,1,0:T(2,128)(2,1)} %own_ref.1, bf16[]{:T(256)S(1)} %bitcast.13), kind=kLoop, calls=%fused_computation | loop fusion | flops 24832 | bytes 99427 | tf_op jit(solution)/shard_map/concatenate | solution.py:250
  5.6 1.3 %collective-permute-start.1 = (bf16[97,2,128]{2,1,0:T(2,128)(2,1)S(1)}, bf16[97,2,128]{2,1,0:T(2,128)(2,1)S(1)}, u32[]{:S(2)}, u32[]{:S(2)}) collective-permute-start(bf16[97,2,128]{2,1,0:T(2,128)(2,1)S(1)} %broadcast_select_fusion), channel_id=1, source_target_pairs={{1,0},{2,1},{3,2},{4,3},{5,4},{6,5},{7,6},{8,7},{9,8},{10,9},{11,1... | collective-permute-start | bytes 149000 | tf_op jit(solution)/shard_map/ppermute | solution.py:32
  6.9 0.0 copy-done
  6.9 1.8 %fusion = f32[16,16,256]{2,0,1:T(8,128)} fusion(bf16[16,256,128]{2,1,0:T(8,128)(2,1)S(1)} %copy-done, bf16[128,16]{0,1:T(8,128)(2,1)} %param.31), kind=kOutput, calls=%fused_computation.1 | convolution fusion | flops 16777216 | bytes 1314816 | tf_op jit(solution)/shard_map/qkc,ch->qhk/dot_general | solution.py:311
  8.7 0.0 collective-permute-done.low_ref
  8.7 0.0 copy-start.2
  8.7 2.2 %collective-permute-done.1.upper_ref = bf16[97,2,128]{2,1,0:T(2,128)(2,1)S(1)} collective-permute-done((bf16[97,2,128]{2,1,0:T(2,128)(2,1)S(1)}, bf16[97,2,128]{2,1,0:T(2,128)(2,1)S(1)}, u32[]{:S(2)}, u32[]{:S(2)}) %collective-permute-start.1) | collective-permute-done | bytes 49696 | tf_op jit(solution)/shard_map/ppermute | solution.py:32
  10.8 0.0 copy-start.1
  10.8 0.0 copy-done.2
  10.8 0.6 %copy-done.1 = bf16[97,2,128]{2,1,0:T(2,128)(2,1)} copy-done((bf16[97,2,128]{2,1,0:T(2,128)(2,1)}, bf16[97,2,128]{2,1,0:T(2,128)(2,1)S(1)}, u32[]{:S(2)}) %copy-start.1) | copy-done | bytes 49688
  11.5 6.4 %shard_map.167 = (bf16[128,2,128]{2,1,0:T(2,128)(2,1)}, bf16[2,16,768]{2,1,0:T(8,128)(2,1)}, bf16[2,16,768]{2,1,0:T(8,128)(2,1)}) custom-call(bf16[128,2,128]{2,1,0:T(2,128)(2,1)} %own_ref.1, bf16[64,2,128]{2,1,0:T(2,128)(2,1)} %copy-done.2, bf16[97,2,128]{2,1,0:T(2,128)(2,1)} %copy-done.1, s32[4]{0:T(128)} %shift_ref.1, bf16[128,128]{1,0:T(8,128)(2,1)} %wq_ref.1, ...), custom_call_target="tpu_custom_call" | custom-call | flops 342360064 | bytes 638976 | tf_op jit(solution)/shard_map/pallas_call | solution.py:274
  17.8 26.7 %all_gather.3.every_ref = bf16[2,256,768]{2,1,0:T(8,128)(2,1)} all-gather(bf16[2,16,768]{2,1,0:T(8,128)(2,1)} %get-tuple-element.6.own_ref), channel_id=1, replica_groups=mesh['groups'=2,'row'=16] {'row'}, dimensions={1}, use_global_device_ids=true | all-gather | bytes 835584 | tf_op jit(solution)/shard_map/all_gather | solution.py:314
  44.5 6.0 %shard_map.168 = bf16[16,2,768]{2,1,0:T(2,128)(2,1)} custom-call(bf16[2,256,768]{2,1,0:T(8,128)(2,1)} %all_gather.3.every_ref, bf16[2,16,768]{2,1,0:T(8,128)(2,1)} %get-tuple-element.6.own_ref, bf16[2,16,768]{2,1,0:T(8,128)(2,1)} %get-tuple-element.7.query_ref, f32[256,256]{1,0:T(8,128)} %bitcast.11, s32[1,256]{1,0:T(1,128)} %bitcast.14, ...), custom_call_target="tpu_custom_call" | custom-call | flops 1686110208 | bytes 5865472 | tf_op jit(solution)/shard_map/pallas_call | solution.py:315
Async XLA Ops:
  0.6 6.3 %copy-start = (bf16[16,256,128]{2,1,0:T(8,128)(2,1)S(1)}, bf16[16,256,128]{2,1,0:T(8,128)(2,1)}, u32[]{:S(2)}) copy-start(bf16[16,256,128]{2,1,0:T(8,128)(2,1)} %param.20) | copy-start | bytes 3145732
  1.5 7.2 %collective-permute-start = (bf16[64,2,128]{2,1,0:T(2,128)(2,1)S(1)}, bf16[64,2,128]{2,1,0:T(2,128)(2,1)S(1)}, u32[]{:S(2)}, u32[]{:S(2)}) collective-permute-start(bf16[64,2,128]{2,1,0:T(2,128)(2,1)S(1)} %slice.11), channel_id=1, source_target_pairs={{0,1},{1,2},{2,3},{3,4},{4,5},{5,6},{6,7},{7,8},{8,9},{9,10},{10,1... | collective-permute-start | bytes 98312 | tf_op jit(solution)/shard_map/ppermute | solution.py:32
  5.6 5.3 %collective-permute-start.1 = (bf16[97,2,128]{2,1,0:T(2,128)(2,1)S(1)}, bf16[97,2,128]{2,1,0:T(2,128)(2,1)S(1)}, u32[]{:S(2)}, u32[]{:S(2)}) collective-permute-start(bf16[97,2,128]{2,1,0:T(2,128)(2,1)S(1)} %broadcast_select_fusion), channel_id=1, source_target_pairs={{1,0},{2,1},{3,2},{4,3},{5,4},{6,5},{7,6},{8,7},{9,8},{10,9},{11,1... | collective-permute-start | bytes 149000 | tf_op jit(solution)/shard_map/ppermute | solution.py:32
  8.7 2.2 %copy-start.2 = (bf16[64,2,128]{2,1,0:T(2,128)(2,1)}, bf16[64,2,128]{2,1,0:T(2,128)(2,1)S(1)}, u32[]{:S(2)}) copy-start(bf16[64,2,128]{2,1,0:T(2,128)(2,1)S(1)} %collective-permute-done.low_ref) | copy-start | bytes 98308
  10.8 0.6 %copy-start.1 = (bf16[97,2,128]{2,1,0:T(2,128)(2,1)}, bf16[97,2,128]{2,1,0:T(2,128)(2,1)S(1)}, u32[]{:S(2)}) copy-start(bf16[97,2,128]{2,1,0:T(2,128)(2,1)S(1)} %collective-permute-done.1.upper_ref) | copy-start | bytes 148996

commit v10 on v9

--- a/solution.py
+++ b/solution.py
@@ -138,7 +138,7 @@
 
 
 def token_kernel(
-    every_ref,
+    every_hbm,
     own_ref,
     query_ref,
     bias_ref,
@@ -147,17 +147,27 @@
     wv_hbm,
     wo_hbm,
     out_ref,
+    every_ref,
     wk_ref,
     wv_ref,
     wo_ref,
     sems,
     *,
     heads,
+    chunk,
 ):
-    copies = [
-        pltpu.make_async_copy(src, dst, sems.at[i])
-        for i, (src, dst) in enumerate([(wk_hbm, wk_ref), (wv_hbm, wv_ref), (wo_hbm, wo_ref)])
-    ]
+    f32, bf16 = jnp.float32, jnp.bfloat16
+    samples = every_ref.shape[0]
+    width = wk_ref.shape[0]
+    chunks = width // chunk
+    pairs = [(every_hbm.at[s], every_ref.at[s]) for s in range(samples)]
+    for w_hbm, w_ref in ((wk_hbm, wk_ref), (wv_hbm, wv_ref)):
+        pairs += [
+            (w_hbm.at[pl.ds(c * chunk, chunk)], w_ref.at[pl.ds(c * chunk, chunk)])
+            for c in range(chunks)
+        ]
+    pairs.append((wo_hbm, wo_ref))
+    copies = [pltpu.make_async_copy(src, dst, sems.at[i]) for i, (src, dst) in enumerate(pairs)]
     for copy in copies:
         copy.start()
     f32, bf16 = jnp.float32, jnp.bfloat16
@@ -174,11 +184,25 @@
         var = jnp.mean((x - mean) ** 2, axis=-1, keepdims=True)
         return ((x - mean) / jnp.sqrt(var + 1e-05)).astype(bf16)
 
-    allx = [normed(every_ref[s].astype(f32)) for s in range(samples)]
-    copies[0].wait()
-    ks = [jnp.dot(x, wk_ref[...], preferred_element_type=f32).astype(bf16) for x in allx]
-    copies[1].wait()
-    vs = [jnp.dot(x, wv_ref[...], preferred_element_type=f32).astype(bf16) for x in allx]
+    allx = []
+    for s in range(samples):
+        copies[s].wait()
+        allx.append(normed(every_ref[s].astype(f32)))
+
+    def projected(w_ref, first):
+        acc = [None] * samples
+        for c in range(chunks):
+            copies[first + c].wait()
+            part = w_ref[c * chunk : (c + 1) * chunk, :]
+            for s in range(samples):
+                term = jnp.dot(
+                    allx[s][:, c * chunk : (c + 1) * chunk], part, preferred_element_type=f32
+                )
+                acc[s] = term if acc[s] is None else acc[s] + term
+        return [a.astype(bf16) for a in acc]
+
+    ks = projected(wk_ref, samples)
+    vs = projected(wv_ref, samples + chunks)
     bias = bias_ref[...]
     mixes = []
     for s in range(samples):
@@ -203,7 +227,7 @@
                 axis=0,
             ).astype(bf16)
         )
-    copies[2].wait()
+    copies[-1].wait()
     for s in range(samples):
         own = own_ref[s].astype(f32)
         mix = mixes[s]
@@ -313,15 +337,16 @@
 
     every = lax.all_gather(state_t, "row", axis=1, tiled=True)
     token_out = pl.pallas_call(
-        functools.partial(token_kernel, heads=TOKEN_HEADS),
+        functools.partial(token_kernel, heads=TOKEN_HEADS, chunk=128),
         out_shape=jax.ShapeDtypeStruct((tok_dev, samples, tok_width), jnp.bfloat16),
-        in_specs=[vmem, vmem, vmem, vmem, vmem, hbm, hbm, hbm],
+        in_specs=[hbm, vmem, vmem, vmem, vmem, hbm, hbm, hbm],
         out_specs=vmem,
         scratch_shapes=[
+            pltpu.VMEM(every.shape, every.dtype),
             pltpu.VMEM(w_key.shape, w_key.dtype),
             pltpu.VMEM(w_value.shape, w_value.dtype),
             pltpu.VMEM(w_out.shape, w_out.dtype),
-            pltpu.SemaphoreType.DMA((3,)),
+            pltpu.SemaphoreType.DMA((samples + 2 * (tok_width // 128) + 1,)),
         ],
         cost_estimate=pl.CostEstimate(
             flops=2 * samples * tok_width * (

time: 50.8 us -> 52.3 us (1.030)
  Pallas kernels: 12.4 us -> 13.9 us
    pallas_call x1, Pallas kernels: 5.98 us -> 7.53 us  [on_device(): pl.pallas_call(functools.partial(token_kernel, heads=TOKEN_HEADS, chunk=1...]
where the time goes in v10:
time: 52.3 us; the launch traced here: 52 us
  blocking collectives  26.7 us (51%)
  Pallas kernels  13.9 us (27%)
  starting transfers between devices  3.65 us (7%)
  waiting for transfers between devices  2.17 us (4%)
  matrix products  1.78 us (3%)
  other arithmetic  1.68 us (3%)
  local copies, waits for them, and re-layouts  1.5 us (3%)
  between operations  0.68 us (1%)
    all_gather x1, blocking collectives, on_device(): every = lax.all_gather(state_t, 'row', axis=1, tiled=True)  26.7 us
    pallas_call x1, Pallas kernels, on_device(): pl.pallas_call(functools.partial(token_kernel, heads=TOKEN_HEADS, chunk=1...  7.53 us
    pallas_call x1, Pallas kernels, on_device(): pl.pallas_call(kernel, out_shape=(jax.ShapeDtypeStruct((atom_dev, samples...  6.38 us
    ppermute x2, starting transfers between devices, shifted(): return lax.ppermute(block, axis, route)  3.65 us
    ppermute x2, waiting for transfers between devices, shifted(): return lax.ppermute(block, axis, route)  2.17 us
    dot_general x1, matrix products, on_device(): jnp.einsum('qkc,ch->qhk', pair, w_bias, preferred_element_type=jnp.float32)  1.78 us
  transfers between devices with their start and end apart: 2, of which 1 were waited for; matrix products, arithmetic and copies ran while one was open for 7% of the time, Pallas kernels for 0%

profile of v10, /device:TPU:0, one launch (start us, length us, event | category | flops | bytes accessed | tf_op | source)
XLA Modules:
  0.0 52.0 jit_solution(16448436001964476992)
XLA Ops:
  0.6 0.0 copy-start
  0.6 0.9 %slice.11 = bf16[64,2,128]{2,1,0:T(2,128)(2,1)S(1)} slice(bf16[128,2,128]{2,1,0:T(2,128)(2,1)} %own_ref.1), slice={[64:128], [0:2], [0:128]} | slice | bytes 65536 | tf_op jit(solution)/shard_map/slice | solution.py:272
  1.5 2.4 %collective-permute-start = (bf16[64,2,128]{2,1,0:T(2,128)(2,1)S(1)}, bf16[64,2,128]{2,1,0:T(2,128)(2,1)S(1)}, u32[]{:S(2)}, u32[]{:S(2)}) collective-permute-start(bf16[64,2,128]{2,1,0:T(2,128)(2,1)S(1)} %slice.11), channel_id=1, source_target_pairs={{0,1},{1,2},{2,3},{3,4},{4,5},{5,6},{6,7},{7,8},{8,9},{9,10},{10,1... | collective-permute-start | bytes 98312 | tf_op jit(solution)/shard_map/ppermute | solution.py:32
  3.9 0.7 %convert.3 = bf16[4]{0:T(256)(128)(2,1)S(1)} convert(s32[4]{0:T(128)} %shift_ref.1) | non-fusion elementwise | flops 4 | bytes 24 | tf_op jit(solution)/shard_map/convert
  4.5 1.0 %broadcast_select_fusion = bf16[97,2,128]{2,1,0:T(2,128)(2,1)S(1)} fusion(pred[97]{0:T(512)(128)(4,1)} %constant.1.clone.1, bf16[128,2,128]{2,1,0:T(2,128)(2,1)} %own_ref.1, bf16[]{:T(256)S(1)} %bitcast.13), kind=kLoop, calls=%fused_computation | loop fusion | flops 24832 | bytes 99427 | tf_op jit(solution)/shard_map/concatenate | solution.py:274
  5.6 1.3 %collective-permute-start.1 = (bf16[97,2,128]{2,1,0:T(2,128)(2,1)S(1)}, bf16[97,2,128]{2,1,0:T(2,128)(2,1)S(1)}, u32[]{:S(2)}, u32[]{:S(2)}) collective-permute-start(bf16[97,2,128]{2,1,0:T(2,128)(2,1)S(1)} %broadcast_select_fusion), channel_id=1, source_target_pairs={{1,0},{2,1},{3,2},{4,3},{5,4},{6,5},{7,6},{8,7},{9,8},{10,9},{11,1... | collective-permute-start | bytes 149000 | tf_op jit(solution)/shard_map/ppermute | solution.py:32
  6.9 0.0 copy-done
  6.9 1.8 %fusion = f32[16,16,256]{2,0,1:T(8,128)} fusion(bf16[16,256,128]{2,1,0:T(8,128)(2,1)S(1)} %copy-done, bf16[128,16]{0,1:T(8,128)(2,1)} %param.31), kind=kOutput, calls=%fused_computation.1 | convolution fusion | flops 16777216 | bytes 1314816 | tf_op jit(solution)/shard_map/qkc,ch->qhk/dot_general | solution.py:335
  8.7 0.0 collective-permute-done.low_ref
  8.7 0.0 copy-start.2
  8.7 2.2 %collective-permute-done.1.upper_ref = bf16[97,2,128]{2,1,0:T(2,128)(2,1)S(1)} collective-permute-done((bf16[97,2,128]{2,1,0:T(2,128)(2,1)S(1)}, bf16[97,2,128]{2,1,0:T(2,128)(2,1)S(1)}, u32[]{:S(2)}, u32[]{:S(2)}) %collective-permute-start.1) | collective-permute-done | bytes 49696 | tf_op jit(solution)/shard_map/ppermute | solution.py:32
  10.8 0.0 copy-start.1
  10.8 0.0 copy-done.2
  10.8 0.6 %copy-done.1 = bf16[97,2,128]{2,1,0:T(2,128)(2,1)} copy-done((bf16[97,2,128]{2,1,0:T(2,128)(2,1)}, bf16[97,2,128]{2,1,0:T(2,128)(2,1)S(1)}, u32[]{:S(2)}) %copy-start.1) | copy-done | bytes 49688
  11.5 6.4 %shard_map.167 = (bf16[128,2,128]{2,1,0:T(2,128)(2,1)}, bf16[2,16,768]{2,1,0:T(8,128)(2,1)}, bf16[2,16,768]{2,1,0:T(8,128)(2,1)}) custom-call(bf16[128,2,128]{2,1,0:T(2,128)(2,1)} %own_ref.1, bf16[64,2,128]{2,1,0:T(2,128)(2,1)} %copy-done.2, bf16[97,2,128]{2,1,0:T(2,128)(2,1)} %copy-done.1, s32[4]{0:T(128)} %shift_ref.1, bf16[128,128]{1,0:T(8,128)(2,1)} %wq_ref.1, ...), custom_call_target="tpu_custom_call" | custom-call | flops 342360064 | bytes 638976 | tf_op jit(solution)/shard_map/pallas_call | solution.py:298
  17.8 26.7 %all_gather.3.every_hbm = bf16[2,256,768]{2,1,0:T(8,128)(2,1)} all-gather(bf16[2,16,768]{2,1,0:T(8,128)(2,1)} %get-tuple-element.6.own_ref), channel_id=1, replica_groups=mesh['groups'=2,'row'=16] {'row'}, dimensions={1}, use_global_device_ids=true | all-gather | bytes 835584 | tf_op jit(solution)/shard_map/all_gather | solution.py:338
  44.5 7.5 %shard_map.168 = bf16[16,2,768]{2,1,0:T(2,128)(2,1)} custom-call(bf16[2,256,768]{2,1,0:T(8,128)(2,1)} %all_gather.3.every_hbm, bf16[2,16,768]{2,1,0:T(8,128)(2,1)} %get-tuple-element.6.own_ref, bf16[2,16,768]{2,1,0:T(8,128)(2,1)} %get-tuple-element.7.query_ref, f32[256,256]{1,0:T(8,128)} %bitcast.11, s32[1,256]{1,0:T(1,128)} %bitcast.14, ...), custom_call_target="tpu_custom_call" | custom-call | flops 1686110208 | bytes 5865472 | tf_op jit(solution)/shard_map/pallas_call | solution.py:339
Async XLA Ops:
  0.6 6.3 %copy-start = (bf16[16,256,128]{2,1,0:T(8,128)(2,1)S(1)}, bf16[16,256,128]{2,1,0:T(8,128)(2,1)}, u32[]{:S(2)}) copy-start(bf16[16,256,128]{2,1,0:T(8,128)(2,1)} %param.20) | copy-start | bytes 3145732
  1.5 7.2 %collective-permute-start = (bf16[64,2,128]{2,1,0:T(2,128)(2,1)S(1)}, bf16[64,2,128]{2,1,0:T(2,128)(2,1)S(1)}, u32[]{:S(2)}, u32[]{:S(2)}) collective-permute-start(bf16[64,2,128]{2,1,0:T(2,128)(2,1)S(1)} %slice.11), channel_id=1, source_target_pairs={{0,1},{1,2},{2,3},{3,4},{4,5},{5,6},{6,7},{7,8},{8,9},{9,10},{10,1... | collective-permute-start | bytes 98312 | tf_op jit(solution)/shard_map/ppermute | solution.py:32
  5.6 5.3 %collective-permute-start.1 = (bf16[97,2,128]{2,1,0:T(2,128)(2,1)S(1)}, bf16[97,2,128]{2,1,0:T(2,128)(2,1)S(1)}, u32[]{:S(2)}, u32[]{:S(2)}) collective-permute-start(bf16[97,2,128]{2,1,0:T(2,128)(2,1)S(1)} %broadcast_select_fusion), channel_id=1, source_target_pairs={{1,0},{2,1},{3,2},{4,3},{5,4},{6,5},{7,6},{8,7},{9,8},{10,9},{11,1... | collective-permute-start | bytes 149000 | tf_op jit(solution)/shard_map/ppermute | solution.py:32
  8.7 2.2 %copy-start.2 = (bf16[64,2,128]{2,1,0:T(2,128)(2,1)}, bf16[64,2,128]{2,1,0:T(2,128)(2,1)S(1)}, u32[]{:S(2)}) copy-start(bf16[64,2,128]{2,1,0:T(2,128)(2,1)S(1)} %collective-permute-done.low_ref) | copy-start | bytes 98308
  10.8 0.6 %copy-start.1 = (bf16[97,2,128]{2,1,0:T(2,128)(2,1)}, bf16[97,2,128]{2,1,0:T(2,128)(2,1)S(1)}, u32[]{:S(2)}) copy-start(bf16[97,2,128]{2,1,0:T(2,128)(2,1)S(1)} %collective-permute-done.1.upper_ref) | copy-start | bytes 148996

commit v11 on v9

--- a/solution.py
+++ b/solution.py
@@ -90,17 +90,28 @@
     onehot = (own_ids == row_ids).astype(f32)
     counts = jnp.sum(onehot, axis=1, keepdims=True)
     onehot = onehot.astype(bf16)
+    xs, xns = [], []
     for s in range(samples):
         x = jnp.concatenate(
             [low_ref[:, s, :], own_ref[:, s, :], upper_ref[0:high_rows, s, :]], axis=0
         ).astype(f32)
         mean = jnp.mean(x, axis=-1, keepdims=True)
         var = jnp.mean((x - mean) ** 2, axis=-1, keepdims=True)
-        xn = ((x - mean) / jnp.sqrt(var + 1e-05)).astype(bf16)
-        q = jnp.dot(xn[low_rows : low_rows + rows], wq_ref[...], preferred_element_type=f32)
-        q = q.astype(bf16)
-        k = jnp.dot(xn, wk_ref[...], preferred_element_type=f32).astype(bf16)
-        v = jnp.dot(xn, wv_ref[...], preferred_element_type=f32).astype(bf16)
+        xs.append(x)
+        xns.append(((x - mean) / jnp.sqrt(var + 1e-05)).astype(bf16))
+    xn_all = jnp.concatenate(xns, axis=0)
+    q_all = jnp.dot(
+        jnp.concatenate([xn[low_rows : low_rows + rows] for xn in xns], axis=0),
+        wq_ref[...],
+        preferred_element_type=f32,
+    ).astype(bf16)
+    k_all = jnp.dot(xn_all, wk_ref[...], preferred_element_type=f32).astype(bf16)
+    v_all = jnp.dot(xn_all, wv_ref[...], preferred_element_type=f32).astype(bf16)
+    mixed = []
+    for s in range(samples):
+        q = q_all[s * rows : (s + 1) * rows]
+        k = k_all[s * ext_rows : (s + 1) * ext_rows]
+        v = v_all[s * ext_rows : (s + 1) * ext_rows]
         acc = jnp.zeros((rows, width), f32)
         for h in range(ATOM_HEADS):
             qh = q * head_masks[h].astype(bf16)
@@ -113,28 +124,45 @@
             tot = jnp.sum(e, axis=-1, keepdims=True)
             o = jnp.dot(e.astype(bf16), v, preferred_element_type=f32)
             acc = acc + (o / tot) * head_masks[h]
-        mixed = acc.astype(bf16)
-        base = x[low_rows : low_rows + rows]
-        out = (base + jnp.dot(mixed, wo_ref[...], preferred_element_type=f32)).astype(bf16)
-        atom_ref[:, s, :] = out[:atom_dev]
-        hidden = jnp.maximum(jnp.dot(out, wt_ref[...], preferred_element_type=f32), 0.0)
-        top_part = hidden.astype(bf16)
-        rest = hidden - top_part.astype(f32)
-        mid_part = rest.astype(bf16)
-        low_part = (rest - mid_part.astype(f32)).astype(bf16)
-        sums = (
-            jnp.dot(onehot, top_part, preferred_element_type=f32)
-            + jnp.dot(onehot, mid_part, preferred_element_type=f32)
-            + jnp.dot(onehot, low_part, preferred_element_type=f32)
-        )
-        state_ref[s] = (token_ref[:, s, :].astype(f32) + sums / counts).astype(bf16)
-    copies[0].wait()
-    for s in range(samples):
-        st = state_ref[s].astype(f32)
+        mixed.append(acc.astype(bf16))
+    base = jnp.concatenate([x[low_rows : low_rows + rows] for x in xs], axis=0)
+    out = (
+        base + jnp.dot(jnp.concatenate(mixed, axis=0), wo_ref[...], preferred_element_type=f32)
+    ).astype(bf16)
+    for s in range(samples):
+        atom_ref[:, s, :] = out[s * rows : s * rows + atom_dev]
+    hidden = jnp.maximum(jnp.dot(out, wt_ref[...], preferred_element_type=f32), 0.0)
+    top_part = hidden.astype(bf16)
+    rest = hidden - top_part.astype(f32)
+    mid_part = rest.astype(bf16)
+    low_part = (rest - mid_part.astype(f32)).astype(bf16)
+    zero = jnp.zeros_like(onehot)
+    diagonal = jnp.concatenate(
+        [
+            jnp.concatenate([onehot if c == r else zero for c in range(samples)], axis=1)
+            for r in range(samples)
+        ],
+        axis=0,
+    )
+    sums = (
+        jnp.dot(diagonal, top_part, preferred_element_type=f32)
+        + jnp.dot(diagonal, mid_part, preferred_element_type=f32)
+        + jnp.dot(diagonal, low_part, preferred_element_type=f32)
+    )
+    tns = []
+    for s in range(samples):
+        st = (token_ref[:, s, :].astype(f32) + sums[s * tok_dev : (s + 1) * tok_dev] / counts)
+        st = st.astype(bf16)
+        state_ref[s] = st
+        st = st.astype(f32)
         mean = jnp.mean(st, axis=-1, keepdims=True)
         var = jnp.mean((st - mean) ** 2, axis=-1, keepdims=True)
-        tn = ((st - mean) / jnp.sqrt(var + 1e-05)).astype(bf16)
-        query_ref[s] = jnp.dot(tn, wtq_ref[...], preferred_element_type=f32).astype(bf16)
+        tns.append(((st - mean) / jnp.sqrt(var + 1e-05)).astype(bf16))
+    copies[0].wait()
+    query = jnp.dot(jnp.concatenate(tns, axis=0), wtq_ref[...], preferred_element_type=f32)
+    query = query.astype(bf16)
+    for s in range(samples):
+        query_ref[s] = query[s * tok_dev : (s + 1) * tok_dev]
 
 
 def token_kernel(
@@ -174,11 +202,14 @@
         var = jnp.mean((x - mean) ** 2, axis=-1, keepdims=True)
         return ((x - mean) / jnp.sqrt(var + 1e-05)).astype(bf16)
 
-    allx = [normed(every_ref[s].astype(f32)) for s in range(samples)]
+    allx = jnp.concatenate([normed(every_ref[s].astype(f32)) for s in range(samples)], axis=0)
+    count = every_ref.shape[1]
     copies[0].wait()
-    ks = [jnp.dot(x, wk_ref[...], preferred_element_type=f32).astype(bf16) for x in allx]
+    k_all = jnp.dot(allx, wk_ref[...], preferred_element_type=f32).astype(bf16)
     copies[1].wait()
-    vs = [jnp.dot(x, wv_ref[...], preferred_element_type=f32).astype(bf16) for x in allx]
+    v_all = jnp.dot(allx, wv_ref[...], preferred_element_type=f32).astype(bf16)
+    ks = [k_all[s * count : (s + 1) * count] for s in range(samples)]
+    vs = [v_all[s * count : (s + 1) * count] for s in range(samples)]
     bias = bias_ref[...]
     mixes = []
     for s in range(samples):
@@ -204,10 +235,10 @@
             ).astype(bf16)
         )
     copies[2].wait()
+    projected = jnp.dot(jnp.concatenate(mixes, axis=0), wo_ref[...], preferred_element_type=f32)
     for s in range(samples):
         own = own_ref[s].astype(f32)
-        mix = mixes[s]
-        out_ref[:, s, :] = (own + jnp.dot(mix, wo_ref[...], preferred_element_type=f32)).astype(bf16)
+        out_ref[:, s, :] = (own + projected[s * tok_dev : (s + 1) * tok_dev]).astype(bf16)
 
 
 def on_device(

time: 50.8 us -> 50.2 us (0.988)
  Pallas kernels: 12.4 us -> 11.8 us
    pallas_call x1, Pallas kernels: 6.38 us -> 5.84 us  [on_device(): pl.pallas_call(kernel, out_shape=(jax.ShapeDtypeStruct((atom_dev, samples...]
where the time goes in v11:
time: 50.2 us; the launch traced here: 49.9 us
  blocking collectives  26.7 us (53%)
  Pallas kernels  11.8 us (24%)
  starting transfers between devices  3.65 us (7%)
  waiting for transfers between devices  2.17 us (4%)
  matrix products  1.78 us (4%)
  other arithmetic  1.68 us (3%)
  local copies, waits for them, and re-layouts  1.5 us (3%)
  between operations  0.68 us (1%)
    all_gather x1, blocking collectives, on_device(): every = lax.all_gather(state_t, 'row', axis=1, tiled=True)  26.7 us
    pallas_call x1, Pallas kernels, on_device(): pl.pallas_call(functools.partial(token_kernel, heads=TOKEN_HEADS), out_sh...  5.94 us
    pallas_call x1, Pallas kernels, on_device(): pl.pallas_call(kernel, out_shape=(jax.ShapeDtypeStruct((atom_dev, samples...  5.84 us
    ppermute x2, starting transfers between devices, shifted(): return lax.ppermute(block, axis, route)  3.65 us
    ppermute x2, waiting for transfers between devices, shifted(): return lax.ppermute(block, axis, route)  2.17 us
    dot_general x1, matrix products, on_device(): jnp.einsum('qkc,ch->qhk', pair, w_bias, preferred_element_type=jnp.float32)  1.78 us
    concatenate x1, other arithmetic, on_device(): jnp.concatenate([atom_feat[:high_rows], shift_row], axis=0)  1.02 us
  transfers between devices with their start and end apart: 2, of which 1 were waited for; matrix products, arithmetic and copies ran while one was open for 7% of the time, Pallas kernels for 0%

profile of v11, /device:TPU:0, one launch (start us, length us, event | category | flops | bytes accessed | tf_op | source)
XLA Modules:
  0.0 49.9 jit_solution(8282736969289155057)
XLA Ops:
  0.6 0.0 copy-start
  0.6 0.9 %slice.11 = bf16[64,2,128]{2,1,0:T(2,128)(2,1)S(1)} slice(bf16[128,2,128]{2,1,0:T(2,128)(2,1)} %own_ref.1), slice={[64:128], [0:2], [0:128]} | slice | bytes 65536 | tf_op jit(solution)/shard_map/slice | solution.py:279
  1.5 2.4 %collective-permute-start = (bf16[64,2,128]{2,1,0:T(2,128)(2,1)S(1)}, bf16[64,2,128]{2,1,0:T(2,128)(2,1)S(1)}, u32[]{:S(2)}, u32[]{:S(2)}) collective-permute-start(bf16[64,2,128]{2,1,0:T(2,128)(2,1)S(1)} %slice.11), channel_id=1, source_target_pairs={{0,1},{1,2},{2,3},{3,4},{4,5},{5,6},{6,7},{7,8},{8,9},{9,10},{10,1... | collective-permute-start | bytes 98312 | tf_op jit(solution)/shard_map/ppermute | solution.py:32
  3.9 0.7 %convert.3 = bf16[4]{0:T(256)(128)(2,1)S(1)} convert(s32[4]{0:T(128)} %shift_ref.1) | non-fusion elementwise | flops 4 | bytes 24 | tf_op jit(solution)/shard_map/convert
  4.5 1.0 %broadcast_select_fusion = bf16[97,2,128]{2,1,0:T(2,128)(2,1)S(1)} fusion(pred[97]{0:T(512)(128)(4,1)} %constant.1.clone.1, bf16[128,2,128]{2,1,0:T(2,128)(2,1)} %own_ref.1, bf16[]{:T(256)S(1)} %bitcast.13), kind=kLoop, calls=%fused_computation | loop fusion | flops 24832 | bytes 99427 | tf_op jit(solution)/shard_map/concatenate | solution.py:281
  5.6 1.3 %collective-permute-start.1 = (bf16[97,2,128]{2,1,0:T(2,128)(2,1)S(1)}, bf16[97,2,128]{2,1,0:T(2,128)(2,1)S(1)}, u32[]{:S(2)}, u32[]{:S(2)}) collective-permute-start(bf16[97,2,128]{2,1,0:T(2,128)(2,1)S(1)} %broadcast_select_fusion), channel_id=1, source_target_pairs={{1,0},{2,1},{3,2},{4,3},{5,4},{6,5},{7,6},{8,7},{9,8},{10,9},{11,1... | collective-permute-start | bytes 149000 | tf_op jit(solution)/shard_map/ppermute | solution.py:32
  6.9 0.0 copy-done
  6.9 1.8 %fusion = f32[16,16,256]{2,0,1:T(8,128)} fusion(bf16[16,256,128]{2,1,0:T(8,128)(2,1)S(1)} %copy-done, bf16[128,16]{0,1:T(8,128)(2,1)} %param.31), kind=kOutput, calls=%fused_computation.1 | convolution fusion | flops 16777216 | bytes 1314816 | tf_op jit(solution)/shard_map/qkc,ch->qhk/dot_general | solution.py:342
  8.7 0.0 collective-permute-done.low_ref
  8.7 0.0 copy-start.2
  8.7 2.2 %collective-permute-done.1.upper_ref = bf16[97,2,128]{2,1,0:T(2,128)(2,1)S(1)} collective-permute-done((bf16[97,2,128]{2,1,0:T(2,128)(2,1)S(1)}, bf16[97,2,128]{2,1,0:T(2,128)(2,1)S(1)}, u32[]{:S(2)}, u32[]{:S(2)}) %collective-permute-start.1) | collective-permute-done | bytes 49696 | tf_op jit(solution)/shard_map/ppermute | solution.py:32
  10.8 0.0 copy-start.1
  10.8 0.0 copy-done.2
  10.8 0.6 %copy-done.1 = bf16[97,2,128]{2,1,0:T(2,128)(2,1)} copy-done((bf16[97,2,128]{2,1,0:T(2,128)(2,1)}, bf16[97,2,128]{2,1,0:T(2,128)(2,1)S(1)}, u32[]{:S(2)}) %copy-start.1) | copy-done | bytes 49688
  11.5 5.8 %shard_map.167 = (bf16[128,2,128]{2,1,0:T(2,128)(2,1)}, bf16[2,16,768]{2,1,0:T(8,128)(2,1)}, bf16[2,16,768]{2,1,0:T(8,128)(2,1)}) custom-call(bf16[128,2,128]{2,1,0:T(2,128)(2,1)} %own_ref.1, bf16[64,2,128]{2,1,0:T(2,128)(2,1)} %copy-done.2, bf16[97,2,128]{2,1,0:T(2,128)(2,1)} %copy-done.1, s32[4]{0:T(128)} %shift_ref.1, bf16[128,128]{1,0:T(8,128)(2,1)} %wq_ref.1, ...), custom_call_target="tpu_custom_call" | custom-call | flops 342360064 | bytes 638976 | tf_op jit(solution)/shard_map/pallas_call | solution.py:305
  17.3 26.7 %all_gather.3.every_ref = bf16[2,256,768]{2,1,0:T(8,128)(2,1)} all-gather(bf16[2,16,768]{2,1,0:T(8,128)(2,1)} %get-tuple-element.6.own_ref), channel_id=1, replica_groups=mesh['groups'=2,'row'=16] {'row'}, dimensions={1}, use_global_device_ids=true | all-gather | bytes 835584 | tf_op jit(solution)/shard_map/all_gather | solution.py:345
  44.0 5.9 %shard_map.168 = bf16[16,2,768]{2,1,0:T(2,128)(2,1)} custom-call(bf16[2,256,768]{2,1,0:T(8,128)(2,1)} %all_gather.3.every_ref, bf16[2,16,768]{2,1,0:T(8,128)(2,1)} %get-tuple-element.6.own_ref, bf16[2,16,768]{2,1,0:T(8,128)(2,1)} %get-tuple-element.7.query_ref, f32[256,256]{1,0:T(8,128)} %bitcast.11, s32[1,256]{1,0:T(1,128)} %bitcast.14, ...), custom_call_target="tpu_custom_call" | custom-call | flops 1686110208 | bytes 5865472 | tf_op jit(solution)/shard_map/pallas_call | solution.py:346
Async XLA Ops:
  0.6 6.3 %copy-start = (bf16[16,256,128]{2,1,0:T(8,128)(2,1)S(1)}, bf16[16,256,128]{2,1,0:T(8,128)(2,1)}, u32[]{:S(2)}) copy-start(bf16[16,256,128]{2,1,0:T(8,128)(2,1)} %param.20) | copy-start | bytes 3145732
  1.5 7.2 %collective-permute-start = (bf16[64,2,128]{2,1,0:T(2,128)(2,1)S(1)}, bf16[64,2,128]{2,1,0:T(2,128)(2,1)S(1)}, u32[]{:S(2)}, u32[]{:S(2)}) collective-permute-start(bf16[64,2,128]{2,1,0:T(2,128)(2,1)S(1)} %slice.11), channel_id=1, source_target_pairs={{0,1},{1,2},{2,3},{3,4},{4,5},{5,6},{6,7},{7,8},{8,9},{9,10},{10,1... | collective-permute-start | bytes 98312 | tf_op jit(solution)/shard_map/ppermute | solution.py:32
  5.6 5.3 %collective-permute-start.1 = (bf16[97,2,128]{2,1,0:T(2,128)(2,1)S(1)}, bf16[97,2,128]{2,1,0:T(2,128)(2,1)S(1)}, u32[]{:S(2)}, u32[]{:S(2)}) collective-permute-start(bf16[97,2,128]{2,1,0:T(2,128)(2,1)S(1)} %broadcast_select_fusion), channel_id=1, source_target_pairs={{1,0},{2,1},{3,2},{4,3},{5,4},{6,5},{7,6},{8,7},{9,8},{10,9},{11,1... | collective-permute-start | bytes 149000 | tf_op jit(solution)/shard_map/ppermute | solution.py:32
  8.7 2.2 %copy-start.2 = (bf16[64,2,128]{2,1,0:T(2,128)(2,1)}, bf16[64,2,128]{2,1,0:T(2,128)(2,1)S(1)}, u32[]{:S(2)}) copy-start(bf16[64,2,128]{2,1,0:T(2,128)(2,1)S(1)} %collective-permute-done.low_ref) | copy-start | bytes 98308
  10.8 0.6 %copy-start.1 = (bf16[97,2,128]{2,1,0:T(2,128)(2,1)}, bf16[97,2,128]{2,1,0:T(2,128)(2,1)S(1)}, u32[]{:S(2)}) copy-start(bf16[97,2,128]{2,1,0:T(2,128)(2,1)S(1)} %collective-permute-done.1.upper_ref) | copy-start | bytes 148996

commit v12 on v11

--- a/solution.py
+++ b/solution.py
@@ -37,6 +37,7 @@
     low_ref,
     upper_ref,
     shift_ref,
+    next_ref,
     wq_ref,
     wk_ref,
     wv_ref,
@@ -72,8 +73,7 @@
     total = devices * atom_dev
     tok_dev = token_ref.shape[0]
     row_block = lax.broadcasted_iota(jnp.int32, (rows, 1), 0) // QBLOCK
-    next_shift = upper_ref[pl.ds(high_rows, 1), 0, :].astype(f32)[:, 0:1].astype(jnp.int32)
-    shift = jnp.where(row_block == rows // QBLOCK - 1, next_shift, 0)
+    shift = jnp.where(row_block == rows // QBLOCK - 1, next_ref[0], 0)
     for j in range(rows // QBLOCK - 1):
         shift = shift + jnp.where(row_block == j, shift_ref[j], 0)
     first = row_block * QBLOCK + SHIFT + shift
@@ -93,7 +93,12 @@
     xs, xns = [], []
     for s in range(samples):
         x = jnp.concatenate(
-            [low_ref[:, s, :], own_ref[:, s, :], upper_ref[0:high_rows, s, :]], axis=0
+            [
+                low_ref[atom_dev - low_rows : atom_dev, s, :],
+                own_ref[:, s, :],
+                upper_ref[0:high_rows, s, :],
+            ],
+            axis=0,
         ).astype(f32)
         mean = jnp.mean(x, axis=-1, keepdims=True)
         var = jnp.mean((x - mean) ** 2, axis=-1, keepdims=True)
@@ -273,13 +278,8 @@
     high_rows = span - low_rows
     blocks = atom_dev // QBLOCK + 1
 
-    shift_row = jnp.broadcast_to(
-        window_shift[0].astype(jnp.bfloat16), (1, samples, width)
-    )
-    low = shifted(atom_feat[atom_dev - low_rows :], "row", 1)
-    upper = shifted(
-        jnp.concatenate([atom_feat[:high_rows], shift_row], axis=0), "row", -1
-    )
+    low = shifted(atom_feat, "row", 1)
+    upper, next_shifts = shifted((atom_feat, window_shift), "row", -1)
 
     head_dim = width // ATOM_HEADS
     rows = blocks * QBLOCK
@@ -310,7 +310,7 @@
             jax.ShapeDtypeStruct((samples, tok_dev, tok_width), jnp.bfloat16),
         ),
         in_specs=[vmem] * 3
-        + [pl.BlockSpec(memory_space=pltpu.SMEM)]
+        + [pl.BlockSpec(memory_space=pltpu.SMEM)] * 2
         + [vmem] * 7
         + [hbm],
         out_specs=(vmem, vmem, vmem),
@@ -330,6 +330,7 @@
         low,
         upper,
         window_shift,
+        next_shifts,
         w_atom_query,
         w_atom_key,
         w_atom_value,

time: 50.2 us -> 49.7 us (0.990)
  other arithmetic: 1.68 us -> 0 us
  starting transfers between devices: 3.65 us -> 5.08 us
  local copies, waits for them, and re-layouts: 1.5 us -> 0.64 us
  waiting for transfers between devices: 2.17 us -> 2.84 us
    ppermute x2 -> x3, starting transfers between devices: 3.65 us -> 5.08 us  [shifted(): return lax.ppermute(block, axis, route)]
    concatenate x1 -> x0, other arithmetic: 1.02 us -> none  [on_device(): jnp.concatenate([atom_feat[:high_rows], shift_row], axis=0)]
    slice x1 -> x0, local copies, waits for them, and re-layouts: 0.87 us -> none  [on_device(): low = shifted(atom_feat[atom_dev - low_rows:], 'row', 1)]
    ppermute x2 -> x3, waiting for transfers between devices: 2.17 us -> 2.84 us  [shifted(): return lax.ppermute(block, axis, route)]
    another operation x1 -> x0, other arithmetic: 0.66 us -> none
  transfers between devices with their start and end apart: 2 -> 3, of which waited for: 1 -> 1; matrix products, arithmetic and copies ran while one was open for 7% -> 4% of each run, Pallas kernels for 0% -> 0%
where the time goes in v12:
time: 49.7 us; the launch traced here: 49.5 us
  blocking collectives  26.7 us (54%)
  Pallas kernels  11.8 us (24%)
  starting transfers between devices  5.08 us (10%)
  waiting for transfers between devices  2.84 us (6%)
  matrix products  1.77 us (4%)
  between operations  0.69 us (1%)
  local copies, waits for them, and re-layouts  0.64 us (1%)
    all_gather x1, blocking collectives, on_device(): every = lax.all_gather(state_t, 'row', axis=1, tiled=True)  26.7 us
    pallas_call x1, Pallas kernels, on_device(): pl.pallas_call(functools.partial(token_kernel, heads=TOKEN_HEADS), out_sh...  5.94 us
    pallas_call x1, Pallas kernels, on_device(): pl.pallas_call(kernel, out_shape=(jax.ShapeDtypeStruct((atom_dev, samples...  5.88 us
    ppermute x3, starting transfers between devices, shifted(): return lax.ppermute(block, axis, route)  5.08 us
    ppermute x3, waiting for transfers between devices, shifted(): return lax.ppermute(block, axis, route)  2.84 us
    dot_general x1, matrix products, on_device(): jnp.einsum('qkc,ch->qhk', pair, w_bias, preferred_element_type=jnp.float32)  1.77 us
  transfers between devices with their start and end apart: 3, of which 1 were waited for; matrix products, arithmetic and copies ran while one was open for 4% of the time, Pallas kernels for 0%

profile of v12, /device:TPU:0, one launch (start us, length us, event | category | flops | bytes accessed | tf_op | source)
XLA Modules:
  0.0 49.5 jit_solution(12272934314942878910)
XLA Ops:
  0.6 0.0 copy-start
  0.6 2.5 %collective-permute-start = (bf16[128,2,128]{2,1,0:T(2,128)(2,1)}, bf16[128,2,128]{2,1,0:T(2,128)(2,1)S(1)}, u32[]{:S(2)}, u32[]{:S(2)}) collective-permute-start(bf16[128,2,128]{2,1,0:T(2,128)(2,1)} %own_ref.1), channel_id=1, source_target_pairs={{0,1},{1,2},{2,3},{3,4},{4,5},{5,6},{6,7},{7,8},{8,9},{9,10},{10,1... | collective-permute-start | bytes 196616 | tf_op jit(solution)/shard_map/ppermute | solution.py:32
  3.1 1.3 %collective-permute-start.1 = (bf16[128,2,128]{2,1,0:T(2,128)(2,1)}, bf16[128,2,128]{2,1,0:T(2,128)(2,1)S(1)}, u32[]{:S(2)}, u32[]{:S(2)}) collective-permute-start(bf16[128,2,128]{2,1,0:T(2,128)(2,1)} %own_ref.1), channel_id=1, source_target_pairs={{1,0},{2,1},{3,2},{4,3},{5,4},{6,5},{7,6},{8,7},{9,8},{10,9},{11,1... | collective-permute-start | bytes 196616 | tf_op jit(solution)/shard_map/ppermute | solution.py:32
  4.4 1.3 %collective-permute-start.2 = (s32[4]{0:T(128)}, s32[4]{0:T(128)S(1)}, u32[]{:S(2)}, u32[]{:S(2)}) collective-permute-start(s32[4]{0:T(128)} %shift_ref.1), channel_id=1, source_target_pairs={{1,0},{2,1},{3,2},{4,3},{5,4},{6,5},{7,6},{8,7},{9,8},{10,9},{11,1... | collective-permute-start | bytes 56 | tf_op jit(solution)/shard_map/ppermute | solution.py:32
  5.7 0.0 copy-done
  5.8 1.8 %fusion = f32[16,16,256]{2,0,1:T(8,128)} fusion(bf16[16,256,128]{2,1,0:T(8,128)(2,1)S(1)} %copy-done, bf16[128,16]{0,1:T(8,128)(2,1)} %param.31), kind=kOutput, calls=%fused_computation | convolution fusion | flops 16777216 | bytes 1314816 | tf_op jit(solution)/shard_map/qkc,ch->qhk/dot_general | solution.py:343
  7.5 2.8 %collective-permute-done.2.next_ref = s32[4]{0:T(128)S(1)} collective-permute-done((s32[4]{0:T(128)}, s32[4]{0:T(128)S(1)}, u32[]{:S(2)}, u32[]{:S(2)}) %collective-permute-start.2) | collective-permute-done | bytes 48 | tf_op jit(solution)/shard_map/ppermute | solution.py:32
  10.4 0.0 copy-start.3
  10.4 0.0 collective-permute-done.low_ref
  10.4 0.0 copy-start.1
  10.4 0.0 collective-permute-done.1.upper_ref
  10.4 0.0 copy-start.2
  10.4 0.5 copy-done.3
  10.9 0.1 copy-done.1
  11.0 0.0 copy-done.2
  11.0 5.9 %shard_map.167 = (bf16[128,2,128]{2,1,0:T(2,128)(2,1)}, bf16[2,16,768]{2,1,0:T(8,128)(2,1)}, bf16[2,16,768]{2,1,0:T(8,128)(2,1)}) custom-call(bf16[128,2,128]{2,1,0:T(2,128)(2,1)} %own_ref.1, bf16[128,2,128]{2,1,0:T(2,128)(2,1)} %copy-done.1, bf16[128,2,128]{2,1,0:T(2,128)(2,1)} %copy-done.2, s32[4]{0:T(128)} %shift_ref.1, s32[4]{0:T(128)} %copy-done.3, ...), custom_call_target="tpu_custom_call" | custom-call | flops 342360064 | bytes 638976 | tf_op jit(solution)/shard_map/pallas_call | solution.py:305
  16.9 26.7 %all_gather.3.every_ref = bf16[2,256,768]{2,1,0:T(8,128)(2,1)} all-gather(bf16[2,16,768]{2,1,0:T(8,128)(2,1)} %get-tuple-element.6.own_ref), channel_id=1, replica_groups=mesh['groups'=2,'row'=16] {'row'}, dimensions={1}, use_global_device_ids=true | all-gather | bytes 835584 | tf_op jit(solution)/shard_map/all_gather | solution.py:346
  43.5 5.9 %shard_map.168 = bf16[16,2,768]{2,1,0:T(2,128)(2,1)} custom-call(bf16[2,256,768]{2,1,0:T(8,128)(2,1)} %all_gather.3.every_ref, bf16[2,16,768]{2,1,0:T(8,128)(2,1)} %get-tuple-element.6.own_ref, bf16[2,16,768]{2,1,0:T(8,128)(2,1)} %get-tuple-element.7.query_ref, f32[256,256]{1,0:T(8,128)} %bitcast.9, s32[1,256]{1,0:T(1,128)} %bitcast.11, ...), custom_call_target="tpu_custom_call" | custom-call | flops 1686110208 | bytes 5865472 | tf_op jit(solution)/shard_map/pallas_call | solution.py:347
Async XLA Ops:
  0.6 5.1 %copy-start = (bf16[16,256,128]{2,1,0:T(8,128)(2,1)S(1)}, bf16[16,256,128]{2,1,0:T(8,128)(2,1)}, u32[]{:S(2)}) copy-start(bf16[16,256,128]{2,1,0:T(8,128)(2,1)} %param.20) | copy-start | bytes 3145732
  0.6 9.7 %collective-permute-start = (bf16[128,2,128]{2,1,0:T(2,128)(2,1)}, bf16[128,2,128]{2,1,0:T(2,128)(2,1)S(1)}, u32[]{:S(2)}, u32[]{:S(2)}) collective-permute-start(bf16[128,2,128]{2,1,0:T(2,128)(2,1)} %own_ref.1), channel_id=1, source_target_pairs={{0,1},{1,2},{2,3},{3,4},{4,5},{5,6},{6,7},{7,8},{8,9},{9,10},{10,1... | collective-permute-start | bytes 196616 | tf_op jit(solution)/shard_map/ppermute | solution.py:32
  3.1 7.2 %collective-permute-start.1 = (bf16[128,2,128]{2,1,0:T(2,128)(2,1)}, bf16[128,2,128]{2,1,0:T(2,128)(2,1)S(1)}, u32[]{:S(2)}, u32[]{:S(2)}) collective-permute-start(bf16[128,2,128]{2,1,0:T(2,128)(2,1)} %own_ref.1), channel_id=1, source_target_pairs={{1,0},{2,1},{3,2},{4,3},{5,4},{6,5},{7,6},{8,7},{9,8},{10,9},{11,1... | collective-permute-start | bytes 196616 | tf_op jit(solution)/shard_map/ppermute | solution.py:32
  4.4 5.9 %collective-permute-start.2 = (s32[4]{0:T(128)}, s32[4]{0:T(128)S(1)}, u32[]{:S(2)}, u32[]{:S(2)}) collective-permute-start(s32[4]{0:T(128)} %shift_ref.1), channel_id=1, source_target_pairs={{1,0},{2,1},{3,2},{4,3},{5,4},{6,5},{7,6},{8,7},{9,8},{10,9},{11,1... | collective-permute-start | bytes 56 | tf_op jit(solution)/shard_map/ppermute | solution.py:32
  10.4 0.5 %copy-start.3 = (s32[4]{0:T(128)}, s32[4]{0:T(128)S(1)}, u32[]{:S(2)}) copy-start(s32[4]{0:T(128)S(1)} %collective-permute-done.2.next_ref) | copy-start | bytes 52
  10.4 0.6 %copy-start.1 = (bf16[128,2,128]{2,1,0:T(2,128)(2,1)}, bf16[128,2,128]{2,1,0:T(2,128)(2,1)S(1)}, u32[]{:S(2)}) copy-start(bf16[128,2,128]{2,1,0:T(2,128)(2,1)S(1)} %collective-permute-done.low_ref) | copy-start | bytes 196612
  10.4 0.6 %copy-start.2 = (bf16[128,2,128]{2,1,0:T(2,128)(2,1)}, bf16[128,2,128]{2,1,0:T(2,128)(2,1)S(1)}, u32[]{:S(2)}) copy-start(bf16[128,2,128]{2,1,0:T(2,128)(2,1)S(1)} %collective-permute-done.1.upper_ref) | copy-start | bytes 196612

commit v13 on v12

--- a/solution.py
+++ b/solution.py
@@ -37,7 +37,6 @@
     low_ref,
     upper_ref,
     shift_ref,
-    next_ref,
     wq_ref,
     wk_ref,
     wv_ref,
@@ -73,7 +72,8 @@
     total = devices * atom_dev
     tok_dev = token_ref.shape[0]
     row_block = lax.broadcasted_iota(jnp.int32, (rows, 1), 0) // QBLOCK
-    shift = jnp.where(row_block == rows // QBLOCK - 1, next_ref[0], 0)
+    next_shift = upper_ref[pl.ds(atom_dev, 1), 0, :].astype(f32)[:, 0:1].astype(jnp.int32)
+    shift = jnp.where(row_block == rows // QBLOCK - 1, next_shift, 0)
     for j in range(rows // QBLOCK - 1):
         shift = shift + jnp.where(row_block == j, shift_ref[j], 0)
     first = row_block * QBLOCK + SHIFT + shift
@@ -279,7 +279,8 @@
     blocks = atom_dev // QBLOCK + 1
 
     low = shifted(atom_feat, "row", 1)
-    upper, next_shifts = shifted((atom_feat, window_shift), "row", -1)
+    shift_row = jnp.broadcast_to(window_shift[0], (1, samples, width)).astype(jnp.bfloat16)
+    upper = shifted(jnp.concatenate([atom_feat, shift_row], axis=0), "row", -1)
 
     head_dim = width // ATOM_HEADS
     rows = blocks * QBLOCK
@@ -310,7 +311,7 @@
             jax.ShapeDtypeStruct((samples, tok_dev, tok_width), jnp.bfloat16),
         ),
         in_specs=[vmem] * 3
-        + [pl.BlockSpec(memory_space=pltpu.SMEM)] * 2
+        + [pl.BlockSpec(memory_space=pltpu.SMEM)]
         + [vmem] * 7
         + [hbm],
         out_specs=(vmem, vmem, vmem),
@@ -330,7 +331,6 @@
         low,
         upper,
         window_shift,
-        next_shifts,
         w_atom_query,
         w_atom_key,
         w_atom_value,

time: 49.7 us -> 49.5 us (level)
  starting transfers between devices: 5.08 us -> 3.79 us
  local copies, waits for them, and re-layouts: 0.64 us -> 1.56 us
  other arithmetic: 0 us -> 0.66 us
  waiting for transfers between devices: 2.84 us -> 2.19 us
    ppermute x3 -> x2, starting transfers between devices: 5.08 us -> 3.79 us  [shifted(): return lax.ppermute(block, axis, route)]
    concatenate x0 -> x1, local copies, waits for them, and re-layouts: none -> 0.93 us  [on_device(): upper = shifted(jnp.concatenate([atom_feat, shift_row], axis=0), 'row', -1)]
    another operation x0 -> x1, other arithmetic: none -> 0.66 us
    ppermute x3 -> x2, waiting for transfers between devices: 2.84 us -> 2.19 us  [shifted(): return lax.ppermute(block, axis, route)]
  transfers between devices with their start and end apart: 3 -> 2, of which waited for: 1 -> 1; matrix products, arithmetic and copies ran while one was open for 4% -> 7% of each run, Pallas kernels for 0% -> 0%
where the time goes in v13:
time: 49.5 us; the launch traced here: 49.2 us
  blocking collectives  26.7 us (54%)
  Pallas kernels  11.8 us (24%)
  starting transfers between devices  3.79 us (8%)
  waiting for transfers between devices  2.19 us (4%)
  matrix products  1.78 us (4%)
  local copies, waits for them, and re-layouts  1.56 us (3%)
  between operations  0.68 us (1%)
  other arithmetic  0.66 us (1%)
    all_gather x1, blocking collectives, on_device(): every = lax.all_gather(state_t, 'row', axis=1, tiled=True)  26.7 us
    pallas_call x1, Pallas kernels, on_device(): pl.pallas_call(functools.partial(token_kernel, heads=TOKEN_HEADS), out_sh...  5.94 us
    pallas_call x1, Pallas kernels, on_device(): pl.pallas_call(kernel, out_shape=(jax.ShapeDtypeStruct((atom_dev, samples...  5.9 us
    ppermute x2, starting transfers between devices, shifted(): return lax.ppermute(block, axis, route)  3.79 us
    ppermute x2, waiting for transfers between devices, shifted(): return lax.ppermute(block, axis, route)  2.19 us
    dot_general x1, matrix products, on_device(): jnp.einsum('qkc,ch->qhk', pair, w_bias, preferred_element_type=jnp.float32)  1.78 us
  transfers between devices with their start and end apart: 2, of which 1 were waited for; matrix products, arithmetic and copies ran while one was open for 7% of the time, Pallas kernels for 0%

profile of v13, /device:TPU:0, one launch (start us, length us, event | category | flops | bytes accessed | tf_op | source)
XLA Modules:
  0.0 49.2 jit_solution(1318352850334740372)
XLA Ops:
  0.6 0.0 copy-start
  0.6 2.5 %collective-permute-start = (bf16[128,2,128]{2,1,0:T(2,128)(2,1)}, bf16[128,2,128]{2,1,0:T(2,128)(2,1)S(1)}, u32[]{:S(2)}, u32[]{:S(2)}) collective-permute-start(bf16[128,2,128]{2,1,0:T(2,128)(2,1)} %own_ref.1), channel_id=1, source_target_pairs={{0,1},{1,2},{2,3},{3,4},{4,5},{5,6},{6,7},{7,8},{8,9},{9,10},{10,1... | collective-permute-start | bytes 196616 | tf_op jit(solution)/shard_map/ppermute | solution.py:32
  3.1 0.7 %convert.3 = bf16[4]{0:T(256)(128)(2,1)S(1)} convert(s32[4]{0:T(128)} %shift_ref.1) | non-fusion elementwise | flops 4 | bytes 24 | tf_op jit(solution)/shard_map/convert
  3.8 0.9 %concatenate.3 = bf16[129,2,128]{2,1,0:T(2,128)(2,1)S(1)} pad(bf16[128,2,128]{2,1,0:T(2,128)(2,1)} %own_ref.1, bf16[]{:T(256)S(1)} %bitcast.13), padding=0_1x0_0x0_0 | pad | bytes 131586 | tf_op jit(solution)/shard_map/concatenate | solution.py:283
  4.7 1.3 %collective-permute-start.1 = (bf16[129,2,128]{2,1,0:T(2,128)(2,1)S(1)}, bf16[129,2,128]{2,1,0:T(2,128)(2,1)S(1)}, u32[]{:S(2)}, u32[]{:S(2)}) collective-permute-start(bf16[129,2,128]{2,1,0:T(2,128)(2,1)S(1)} %concatenate.3), channel_id=1, source_target_pairs={{1,0},{2,1},{3,2},{4,3},{5,4},{6,5},{7,6},{8,7},{9,8},{10,9},{11,1... | collective-permute-start | bytes 198152 | tf_op jit(solution)/shard_map/ppermute | solution.py:32
  6.0 0.0 copy-done
  6.1 1.8 %fusion = f32[16,16,256]{2,0,1:T(8,128)} fusion(bf16[16,256,128]{2,1,0:T(8,128)(2,1)S(1)} %copy-done, bf16[128,16]{0,1:T(8,128)(2,1)} %param.31), kind=kOutput, calls=%fused_computation | convolution fusion | flops 16777216 | bytes 1314816 | tf_op jit(solution)/shard_map/qkc,ch->qhk/dot_general | solution.py:343
  7.8 0.0 collective-permute-done.low_ref
  7.8 0.0 copy-start.2
  7.8 2.2 %collective-permute-done.1.upper_ref = bf16[129,2,128]{2,1,0:T(2,128)(2,1)S(1)} collective-permute-done((bf16[129,2,128]{2,1,0:T(2,128)(2,1)S(1)}, bf16[129,2,128]{2,1,0:T(2,128)(2,1)S(1)}, u32[]{:S(2)}, u32[]{:S(2)}) %collective-permute-start.1) | collective-permute-done | bytes 66080 | tf_op jit(solution)/shard_map/ppermute | solution.py:32
  10.0 0.0 copy-start.1
  10.0 0.0 copy-done.2
  10.0 0.6 %copy-done.1 = bf16[129,2,128]{2,1,0:T(2,128)(2,1)} copy-done((bf16[129,2,128]{2,1,0:T(2,128)(2,1)}, bf16[129,2,128]{2,1,0:T(2,128)(2,1)S(1)}, u32[]{:S(2)}) %copy-start.1) | copy-done | bytes 66072
  10.6 5.9 %shard_map.167 = (bf16[128,2,128]{2,1,0:T(2,128)(2,1)}, bf16[2,16,768]{2,1,0:T(8,128)(2,1)}, bf16[2,16,768]{2,1,0:T(8,128)(2,1)}) custom-call(bf16[128,2,128]{2,1,0:T(2,128)(2,1)} %own_ref.1, bf16[128,2,128]{2,1,0:T(2,128)(2,1)} %copy-done.2, bf16[129,2,128]{2,1,0:T(2,128)(2,1)} %copy-done.1, s32[4]{0:T(128)} %shift_ref.1, bf16[128,128]{1,0:T(8,128)(2,1)} %wq_ref.1, ...), custom_call_target="tpu_custom_call" | custom-call | flops 342360064 | bytes 638976 | tf_op jit(solution)/shard_map/pallas_call | solution.py:306
  16.5 26.7 %all_gather.3.every_ref = bf16[2,256,768]{2,1,0:T(8,128)(2,1)} all-gather(bf16[2,16,768]{2,1,0:T(8,128)(2,1)} %get-tuple-element.6.own_ref), channel_id=1, replica_groups=mesh['groups'=2,'row'=16] {'row'}, dimensions={1}, use_global_device_ids=true | all-gather | bytes 835584 | tf_op jit(solution)/shard_map/all_gather | solution.py:346
  43.3 5.9 %shard_map.168 = bf16[16,2,768]{2,1,0:T(2,128)(2,1)} custom-call(bf16[2,256,768]{2,1,0:T(8,128)(2,1)} %all_gather.3.every_ref, bf16[2,16,768]{2,1,0:T(8,128)(2,1)} %get-tuple-element.6.own_ref, bf16[2,16,768]{2,1,0:T(8,128)(2,1)} %get-tuple-element.7.query_ref, f32[256,256]{1,0:T(8,128)} %bitcast.11, s32[1,256]{1,0:T(1,128)} %bitcast.14, ...), custom_call_target="tpu_custom_call" | custom-call | flops 1686110208 | bytes 5865472 | tf_op jit(solution)/shard_map/pallas_call | solution.py:347
Async XLA Ops:
  0.6 5.4 %copy-start = (bf16[16,256,128]{2,1,0:T(8,128)(2,1)S(1)}, bf16[16,256,128]{2,1,0:T(8,128)(2,1)}, u32[]{:S(2)}) copy-start(bf16[16,256,128]{2,1,0:T(8,128)(2,1)} %param.20) | copy-start | bytes 3145732
  0.6 7.2 %collective-permute-start = (bf16[128,2,128]{2,1,0:T(2,128)(2,1)}, bf16[128,2,128]{2,1,0:T(2,128)(2,1)S(1)}, u32[]{:S(2)}, u32[]{:S(2)}) collective-permute-start(bf16[128,2,128]{2,1,0:T(2,128)(2,1)} %own_ref.1), channel_id=1, source_target_pairs={{0,1},{1,2},{2,3},{3,4},{4,5},{5,6},{6,7},{7,8},{8,9},{9,10},{10,1... | collective-permute-start | bytes 196616 | tf_op jit(solution)/shard_map/ppermute | solution.py:32
  4.7 5.3 %collective-permute-start.1 = (bf16[129,2,128]{2,1,0:T(2,128)(2,1)S(1)}, bf16[129,2,128]{2,1,0:T(2,128)(2,1)S(1)}, u32[]{:S(2)}, u32[]{:S(2)}) collective-permute-start(bf16[129,2,128]{2,1,0:T(2,128)(2,1)S(1)} %concatenate.3), channel_id=1, source_target_pairs={{1,0},{2,1},{3,2},{4,3},{5,4},{6,5},{7,6},{8,7},{9,8},{10,9},{11,1... | collective-permute-start | bytes 198152 | tf_op jit(solution)/shard_map/ppermute | solution.py:32
  7.8 2.2 %copy-start.2 = (bf16[128,2,128]{2,1,0:T(2,128)(2,1)}, bf16[128,2,128]{2,1,0:T(2,128)(2,1)S(1)}, u32[]{:S(2)}) copy-start(bf16[128,2,128]{2,1,0:T(2,128)(2,1)S(1)} %collective-permute-done.low_ref) | copy-start | bytes 196612
  10.0 0.6 %copy-start.1 = (bf16[129,2,128]{2,1,0:T(2,128)(2,1)}, bf16[129,2,128]{2,1,0:T(2,128)(2,1)S(1)}, u32[]{:S(2)}) copy-start(bf16[129,2,128]{2,1,0:T(2,128)(2,1)S(1)} %collective-permute-done.1.upper_ref) | copy-start | bytes 198148

commit v14 on v13

--- a/solution.py
+++ b/solution.py
@@ -191,8 +191,7 @@
         pltpu.make_async_copy(src, dst, sems.at[i])
         for i, (src, dst) in enumerate([(wk_hbm, wk_ref), (wv_hbm, wv_ref), (wo_hbm, wo_ref)])
     ]
-    for copy in copies:
-        copy.start()
+    copies[0].start()
     f32, bf16 = jnp.float32, jnp.bfloat16
     samples, tok_dev, width = own_ref.shape
     head_dim = width // heads
@@ -210,8 +209,10 @@
     allx = jnp.concatenate([normed(every_ref[s].astype(f32)) for s in range(samples)], axis=0)
     count = every_ref.shape[1]
     copies[0].wait()
+    copies[1].start()
     k_all = jnp.dot(allx, wk_ref[...], preferred_element_type=f32).astype(bf16)
     copies[1].wait()
+    copies[2].start()
     v_all = jnp.dot(allx, wv_ref[...], preferred_element_type=f32).astype(bf16)
     ks = [k_all[s * count : (s + 1) * count] for s in range(samples)]
     vs = [v_all[s * count : (s + 1) * count] for s in range(samples)]

time: 49.5 us -> 49.9 us (level)
  no operation moved by 1% of the time
where the time goes in v14:
time: 49.9 us; the launch traced here: 49.6 us
  blocking collectives  26.7 us (54%)
  Pallas kernels  12.2 us (24%)
  starting transfers between devices  3.79 us (8%)
  waiting for transfers between devices  2.19 us (4%)
  matrix products  1.78 us (4%)
  local copies, waits for them, and re-layouts  1.56 us (3%)
  between operations  0.68 us (1%)
  other arithmetic  0.66 us (1%)
    all_gather x1, blocking collectives, on_device(): every = lax.all_gather(state_t, 'row', axis=1, tiled=True)  26.7 us
    pallas_call x1, Pallas kernels, on_device(): pl.pallas_call(functools.partial(token_kernel, heads=TOKEN_HEADS), out_sh...  6.28 us
    pallas_call x1, Pallas kernels, on_device(): pl.pallas_call(kernel, out_shape=(jax.ShapeDtypeStruct((atom_dev, samples...  5.9 us
    ppermute x2, starting transfers between devices, shifted(): return lax.ppermute(block, axis, route)  3.79 us
    ppermute x2, waiting for transfers between devices, shifted(): return lax.ppermute(block, axis, route)  2.19 us
    dot_general x1, matrix products, on_device(): jnp.einsum('qkc,ch->qhk', pair, w_bias, preferred_element_type=jnp.float32)  1.78 us
  transfers between devices with their start and end apart: 2, of which 1 were waited for; matrix products, arithmetic and copies ran while one was open for 7% of the time, Pallas kernels for 0%

profile of v14, /device:TPU:0, one launch (start us, length us, event | category | flops | bytes accessed | tf_op | source)
XLA Modules:
  0.0 49.6 jit_solution(1092560708882606307)
XLA Ops:
  0.6 0.0 copy-start
  0.6 2.5 %collective-permute-start = (bf16[128,2,128]{2,1,0:T(2,128)(2,1)}, bf16[128,2,128]{2,1,0:T(2,128)(2,1)S(1)}, u32[]{:S(2)}, u32[]{:S(2)}) collective-permute-start(bf16[128,2,128]{2,1,0:T(2,128)(2,1)} %own_ref.1), channel_id=1, source_target_pairs={{0,1},{1,2},{2,3},{3,4},{4,5},{5,6},{6,7},{7,8},{8,9},{9,10},{10,1... | collective-permute-start | bytes 196616 | tf_op jit(solution)/shard_map/ppermute | solution.py:32
  3.1 0.7 %convert.3 = bf16[4]{0:T(256)(128)(2,1)S(1)} convert(s32[4]{0:T(128)} %shift_ref.1) | non-fusion elementwise | flops 4 | bytes 24 | tf_op jit(solution)/shard_map/convert
  3.8 0.9 %concatenate.3 = bf16[129,2,128]{2,1,0:T(2,128)(2,1)S(1)} pad(bf16[128,2,128]{2,1,0:T(2,128)(2,1)} %own_ref.1, bf16[]{:T(256)S(1)} %bitcast.13), padding=0_1x0_0x0_0 | pad | bytes 131586 | tf_op jit(solution)/shard_map/concatenate | solution.py:284
  4.7 1.3 %collective-permute-start.1 = (bf16[129,2,128]{2,1,0:T(2,128)(2,1)S(1)}, bf16[129,2,128]{2,1,0:T(2,128)(2,1)S(1)}, u32[]{:S(2)}, u32[]{:S(2)}) collective-permute-start(bf16[129,2,128]{2,1,0:T(2,128)(2,1)S(1)} %concatenate.3), channel_id=1, source_target_pairs={{1,0},{2,1},{3,2},{4,3},{5,4},{6,5},{7,6},{8,7},{9,8},{10,9},{11,1... | collective-permute-start | bytes 198152 | tf_op jit(solution)/shard_map/ppermute | solution.py:32
  6.0 0.0 copy-done
  6.1 1.8 %fusion = f32[16,16,256]{2,0,1:T(8,128)} fusion(bf16[16,256,128]{2,1,0:T(8,128)(2,1)S(1)} %copy-done, bf16[128,16]{0,1:T(8,128)(2,1)} %param.31), kind=kOutput, calls=%fused_computation | convolution fusion | flops 16777216 | bytes 1314816 | tf_op jit(solution)/shard_map/qkc,ch->qhk/dot_general | solution.py:344
  7.8 0.0 collective-permute-done.low_ref
  7.8 0.0 copy-start.2
  7.8 2.2 %collective-permute-done.1.upper_ref = bf16[129,2,128]{2,1,0:T(2,128)(2,1)S(1)} collective-permute-done((bf16[129,2,128]{2,1,0:T(2,128)(2,1)S(1)}, bf16[129,2,128]{2,1,0:T(2,128)(2,1)S(1)}, u32[]{:S(2)}, u32[]{:S(2)}) %collective-permute-start.1) | collective-permute-done | bytes 66080 | tf_op jit(solution)/shard_map/ppermute | solution.py:32
  10.0 0.0 copy-start.1
  10.0 0.0 copy-done.2
  10.0 0.6 %copy-done.1 = bf16[129,2,128]{2,1,0:T(2,128)(2,1)} copy-done((bf16[129,2,128]{2,1,0:T(2,128)(2,1)}, bf16[129,2,128]{2,1,0:T(2,128)(2,1)S(1)}, u32[]{:S(2)}) %copy-start.1) | copy-done | bytes 66072
  10.6 5.9 %shard_map.167 = (bf16[128,2,128]{2,1,0:T(2,128)(2,1)}, bf16[2,16,768]{2,1,0:T(8,128)(2,1)}, bf16[2,16,768]{2,1,0:T(8,128)(2,1)}) custom-call(bf16[128,2,128]{2,1,0:T(2,128)(2,1)} %own_ref.1, bf16[128,2,128]{2,1,0:T(2,128)(2,1)} %copy-done.2, bf16[129,2,128]{2,1,0:T(2,128)(2,1)} %copy-done.1, s32[4]{0:T(128)} %shift_ref.1, bf16[128,128]{1,0:T(8,128)(2,1)} %wq_ref.1, ...), custom_call_target="tpu_custom_call" | custom-call | flops 342360064 | bytes 638976 | tf_op jit(solution)/shard_map/pallas_call | solution.py:307
  16.5 26.7 %all_gather.3.every_ref = bf16[2,256,768]{2,1,0:T(8,128)(2,1)} all-gather(bf16[2,16,768]{2,1,0:T(8,128)(2,1)} %get-tuple-element.6.own_ref), channel_id=1, replica_groups=mesh['groups'=2,'row'=16] {'row'}, dimensions={1}, use_global_device_ids=true | all-gather | bytes 835584 | tf_op jit(solution)/shard_map/all_gather | solution.py:347
  43.3 6.3 %shard_map.168 = bf16[16,2,768]{2,1,0:T(2,128)(2,1)} custom-call(bf16[2,256,768]{2,1,0:T(8,128)(2,1)} %all_gather.3.every_ref, bf16[2,16,768]{2,1,0:T(8,128)(2,1)} %get-tuple-element.6.own_ref, bf16[2,16,768]{2,1,0:T(8,128)(2,1)} %get-tuple-element.7.query_ref, f32[256,256]{1,0:T(8,128)} %bitcast.11, s32[1,256]{1,0:T(1,128)} %bitcast.14, ...), custom_call_target="tpu_custom_call" | custom-call | flops 1686110208 | bytes 5865472 | tf_op jit(solution)/shard_map/pallas_call | solution.py:348
Async XLA Ops:
  0.6 5.4 %copy-start = (bf16[16,256,128]{2,1,0:T(8,128)(2,1)S(1)}, bf16[16,256,128]{2,1,0:T(8,128)(2,1)}, u32[]{:S(2)}) copy-start(bf16[16,256,128]{2,1,0:T(8,128)(2,1)} %param.20) | copy-start | bytes 3145732
  0.6 7.2 %collective-permute-start = (bf16[128,2,128]{2,1,0:T(2,128)(2,1)}, bf16[128,2,128]{2,1,0:T(2,128)(2,1)S(1)}, u32[]{:S(2)}, u32[]{:S(2)}) collective-permute-start(bf16[128,2,128]{2,1,0:T(2,128)(2,1)} %own_ref.1), channel_id=1, source_target_pairs={{0,1},{1,2},{2,3},{3,4},{4,5},{5,6},{6,7},{7,8},{8,9},{9,10},{10,1... | collective-permute-start | bytes 196616 | tf_op jit(solution)/shard_map/ppermute | solution.py:32
  4.7 5.3 %collective-permute-start.1 = (bf16[129,2,128]{2,1,0:T(2,128)(2,1)S(1)}, bf16[129,2,128]{2,1,0:T(2,128)(2,1)S(1)}, u32[]{:S(2)}, u32[]{:S(2)}) collective-permute-start(bf16[129,2,128]{2,1,0:T(2,128)(2,1)S(1)} %concatenate.3), channel_id=1, source_target_pairs={{1,0},{2,1},{3,2},{4,3},{5,4},{6,5},{7,6},{8,7},{9,8},{10,9},{11,1... | collective-permute-start | bytes 198152 | tf_op jit(solution)/shard_map/ppermute | solution.py:32
  7.8 2.2 %copy-start.2 = (bf16[128,2,128]{2,1,0:T(2,128)(2,1)}, bf16[128,2,128]{2,1,0:T(2,128)(2,1)S(1)}, u32[]{:S(2)}) copy-start(bf16[128,2,128]{2,1,0:T(2,128)(2,1)S(1)} %collective-permute-done.low_ref) | copy-start | bytes 196612
  10.0 0.6 %copy-start.1 = (bf16[129,2,128]{2,1,0:T(2,128)(2,1)}, bf16[129,2,128]{2,1,0:T(2,128)(2,1)S(1)}, u32[]{:S(2)}) copy-start(bf16[129,2,128]{2,1,0:T(2,128)(2,1)S(1)} %collective-permute-done.1.upper_ref) | copy-start | bytes 198148

commit v15 on v13

--- a/solution.py
+++ b/solution.py
@@ -171,7 +171,7 @@
 
 
 def token_kernel(
-    every_ref,
+    every_hbm,
     own_ref,
     query_ref,
     bias_ref,
@@ -180,19 +180,37 @@
     wv_hbm,
     wo_hbm,
     out_ref,
+    every_ref,
     wk_ref,
     wv_ref,
     wo_ref,
     sems,
     *,
     heads,
+    pieces,
 ):
-    copies = [
-        pltpu.make_async_copy(src, dst, sems.at[i])
-        for i, (src, dst) in enumerate([(wk_hbm, wk_ref), (wv_hbm, wv_ref), (wo_hbm, wo_ref)])
-    ]
-    for copy in copies:
-        copy.start()
+    samples = every_ref.shape[0]
+    step = wk_ref.shape[0] // pieces
+    groups = [[(every_hbm.at[s], every_ref.at[s])] for s in range(samples)]
+    for w_hbm, w_ref in ((wk_hbm, wk_ref), (wv_hbm, wv_ref), (wo_hbm, wo_ref)):
+        groups.append(
+            [(w_hbm.at[pl.ds(c * step, step)], w_ref.at[pl.ds(c * step, step)]) for c in range(pieces)]
+        )
+    copies, index = [], 0
+    for group in groups:
+        made = []
+        for src, dst in group:
+            made.append(pltpu.make_async_copy(src, dst, sems.at[index]))
+            index += 1
+        copies.append(made)
+    for group in copies:
+        for copy in group:
+            copy.start()
+
+    def arrived(group):
+        for copy in copies[group]:
+            copy.wait()
+
     f32, bf16 = jnp.float32, jnp.bfloat16
     samples, tok_dev, width = own_ref.shape
     head_dim = width // heads
@@ -207,11 +225,15 @@
         var = jnp.mean((x - mean) ** 2, axis=-1, keepdims=True)
         return ((x - mean) / jnp.sqrt(var + 1e-05)).astype(bf16)
 
-    allx = jnp.concatenate([normed(every_ref[s].astype(f32)) for s in range(samples)], axis=0)
+    normal = []
+    for s in range(samples):
+        arrived(s)
+        normal.append(normed(every_ref[s].astype(f32)))
+    allx = jnp.concatenate(normal, axis=0)
     count = every_ref.shape[1]
-    copies[0].wait()
+    arrived(samples)
     k_all = jnp.dot(allx, wk_ref[...], preferred_element_type=f32).astype(bf16)
-    copies[1].wait()
+    arrived(samples + 1)
     v_all = jnp.dot(allx, wv_ref[...], preferred_element_type=f32).astype(bf16)
     ks = [k_all[s * count : (s + 1) * count] for s in range(samples)]
     vs = [v_all[s * count : (s + 1) * count] for s in range(samples)]
@@ -239,7 +261,7 @@
                 axis=0,
             ).astype(bf16)
         )
-    copies[2].wait()
+    arrived(samples + 2)
     projected = jnp.dot(jnp.concatenate(mixes, axis=0), wo_ref[...], preferred_element_type=f32)
     for s in range(samples):
         own = own_ref[s].astype(f32)
@@ -345,15 +367,16 @@
 
     every = lax.all_gather(state_t, "row", axis=1, tiled=True)
     token_out = pl.pallas_call(
-        functools.partial(token_kernel, heads=TOKEN_HEADS),
+        functools.partial(token_kernel, heads=TOKEN_HEADS, pieces=4),
         out_shape=jax.ShapeDtypeStruct((tok_dev, samples, tok_width), jnp.bfloat16),
-        in_specs=[vmem, vmem, vmem, vmem, vmem, hbm, hbm, hbm],
+        in_specs=[hbm, vmem, vmem, vmem, vmem, hbm, hbm, hbm],
         out_specs=vmem,
         scratch_shapes=[
+            pltpu.VMEM(every.shape, every.dtype),
             pltpu.VMEM(w_key.shape, w_key.dtype),
             pltpu.VMEM(w_value.shape, w_value.dtype),
             pltpu.VMEM(w_out.shape, w_out.dtype),
-            pltpu.SemaphoreType.DMA((3,)),
+            pltpu.SemaphoreType.DMA((samples + 3 * 4,)),
         ],
         cost_estimate=pl.CostEstimate(
             flops=2 * samples * tok_width * (

time: 49.5 us -> 49.7 us (level)
  no operation moved by 1% of the time
where the time goes in v15:
time: 49.7 us; the launch traced here: 49.4 us
  blocking collectives  26.7 us (54%)
  Pallas kernels  12 us (24%)
  starting transfers between devices  3.79 us (8%)
  waiting for transfers between devices  2.19 us (4%)
  matrix products  1.78 us (4%)
  local copies, waits for them, and re-layouts  1.56 us (3%)
  between operations  0.68 us (1%)
  other arithmetic  0.66 us (1%)
    all_gather x1, blocking collectives, on_device(): every = lax.all_gather(state_t, 'row', axis=1, tiled=True)  26.7 us
    pallas_call x1, Pallas kernels, on_device(): pl.pallas_call(functools.partial(token_kernel, heads=TOKEN_HEADS, pieces=...  6.11 us
    pallas_call x1, Pallas kernels, on_device(): pl.pallas_call(kernel, out_shape=(jax.ShapeDtypeStruct((atom_dev, samples...  5.9 us
    ppermute x2, starting transfers between devices, shifted(): return lax.ppermute(block, axis, route)  3.79 us
    ppermute x2, waiting for transfers between devices, shifted(): return lax.ppermute(block, axis, route)  2.19 us
    dot_general x1, matrix products, on_device(): jnp.einsum('qkc,ch->qhk', pair, w_bias, preferred_element_type=jnp.float32)  1.78 us
  transfers between devices with their start and end apart: 2, of which 1 were waited for; matrix products, arithmetic and copies ran while one was open for 7% of the time, Pallas kernels for 0%

profile of v15, /device:TPU:0, one launch (start us, length us, event | category | flops | bytes accessed | tf_op | source)
XLA Modules:
  0.0 49.4 jit_solution(6162840597368146442)
XLA Ops:
  0.6 0.0 copy-start
  0.6 2.5 %collective-permute-start = (bf16[128,2,128]{2,1,0:T(2,128)(2,1)}, bf16[128,2,128]{2,1,0:T(2,128)(2,1)S(1)}, u32[]{:S(2)}, u32[]{:S(2)}) collective-permute-start(bf16[128,2,128]{2,1,0:T(2,128)(2,1)} %own_ref.1), channel_id=1, source_target_pairs={{0,1},{1,2},{2,3},{3,4},{4,5},{5,6},{6,7},{7,8},{8,9},{9,10},{10,1... | collective-permute-start | bytes 196616 | tf_op jit(solution)/shard_map/ppermute | solution.py:32
  3.1 0.7 %convert.3 = bf16[4]{0:T(256)(128)(2,1)S(1)} convert(s32[4]{0:T(128)} %shift_ref.1) | non-fusion elementwise | flops 4 | bytes 24 | tf_op jit(solution)/shard_map/convert
  3.8 0.9 %concatenate.3 = bf16[129,2,128]{2,1,0:T(2,128)(2,1)S(1)} pad(bf16[128,2,128]{2,1,0:T(2,128)(2,1)} %own_ref.1, bf16[]{:T(256)S(1)} %bitcast.13), padding=0_1x0_0x0_0 | pad | bytes 131586 | tf_op jit(solution)/shard_map/concatenate | solution.py:305
  4.7 1.3 %collective-permute-start.1 = (bf16[129,2,128]{2,1,0:T(2,128)(2,1)S(1)}, bf16[129,2,128]{2,1,0:T(2,128)(2,1)S(1)}, u32[]{:S(2)}, u32[]{:S(2)}) collective-permute-start(bf16[129,2,128]{2,1,0:T(2,128)(2,1)S(1)} %concatenate.3), channel_id=1, source_target_pairs={{1,0},{2,1},{3,2},{4,3},{5,4},{6,5},{7,6},{8,7},{9,8},{10,9},{11,1... | collective-permute-start | bytes 198152 | tf_op jit(solution)/shard_map/ppermute | solution.py:32
  6.0 0.0 copy-done
  6.1 1.8 %fusion = f32[16,16,256]{2,0,1:T(8,128)} fusion(bf16[16,256,128]{2,1,0:T(8,128)(2,1)S(1)} %copy-done, bf16[128,16]{0,1:T(8,128)(2,1)} %param.31), kind=kOutput, calls=%fused_computation | convolution fusion | flops 16777216 | bytes 1314816 | tf_op jit(solution)/shard_map/qkc,ch->qhk/dot_general | solution.py:365
  7.8 0.0 collective-permute-done.low_ref
  7.8 0.0 copy-start.2
  7.8 2.2 %collective-permute-done.1.upper_ref = bf16[129,2,128]{2,1,0:T(2,128)(2,1)S(1)} collective-permute-done((bf16[129,2,128]{2,1,0:T(2,128)(2,1)S(1)}, bf16[129,2,128]{2,1,0:T(2,128)(2,1)S(1)}, u32[]{:S(2)}, u32[]{:S(2)}) %collective-permute-start.1) | collective-permute-done | bytes 66080 | tf_op jit(solution)/shard_map/ppermute | solution.py:32
  10.0 0.0 copy-start.1
  10.0 0.0 copy-done.2
  10.0 0.6 %copy-done.1 = bf16[129,2,128]{2,1,0:T(2,128)(2,1)} copy-done((bf16[129,2,128]{2,1,0:T(2,128)(2,1)}, bf16[129,2,128]{2,1,0:T(2,128)(2,1)S(1)}, u32[]{:S(2)}) %copy-start.1) | copy-done | bytes 66072
  10.6 5.9 %shard_map.167 = (bf16[128,2,128]{2,1,0:T(2,128)(2,1)}, bf16[2,16,768]{2,1,0:T(8,128)(2,1)}, bf16[2,16,768]{2,1,0:T(8,128)(2,1)}) custom-call(bf16[128,2,128]{2,1,0:T(2,128)(2,1)} %own_ref.1, bf16[128,2,128]{2,1,0:T(2,128)(2,1)} %copy-done.2, bf16[129,2,128]{2,1,0:T(2,128)(2,1)} %copy-done.1, s32[4]{0:T(128)} %shift_ref.1, bf16[128,128]{1,0:T(8,128)(2,1)} %wq_ref.1, ...), custom_call_target="tpu_custom_call" | custom-call | flops 342360064 | bytes 638976 | tf_op jit(solution)/shard_map/pallas_call | solution.py:328
  16.5 26.7 %all_gather.3.every_hbm = bf16[2,256,768]{2,1,0:T(8,128)(2,1)} all-gather(bf16[2,16,768]{2,1,0:T(8,128)(2,1)} %get-tuple-element.6.own_ref), channel_id=1, replica_groups=mesh['groups'=2,'row'=16] {'row'}, dimensions={1}, use_global_device_ids=true | all-gather | bytes 835584 | tf_op jit(solution)/shard_map/all_gather | solution.py:368
  43.3 6.1 %shard_map.168 = bf16[16,2,768]{2,1,0:T(2,128)(2,1)} custom-call(bf16[2,256,768]{2,1,0:T(8,128)(2,1)} %all_gather.3.every_hbm, bf16[2,16,768]{2,1,0:T(8,128)(2,1)} %get-tuple-element.6.own_ref, bf16[2,16,768]{2,1,0:T(8,128)(2,1)} %get-tuple-element.7.query_ref, f32[256,256]{1,0:T(8,128)} %bitcast.11, s32[1,256]{1,0:T(1,128)} %bitcast.14, ...), custom_call_target="tpu_custom_call" | custom-call | flops 1686110208 | bytes 5865472 | tf_op jit(solution)/shard_map/pallas_call | solution.py:369
Async XLA Ops:
  0.6 5.4 %copy-start = (bf16[16,256,128]{2,1,0:T(8,128)(2,1)S(1)}, bf16[16,256,128]{2,1,0:T(8,128)(2,1)}, u32[]{:S(2)}) copy-start(bf16[16,256,128]{2,1,0:T(8,128)(2,1)} %param.20) | copy-start | bytes 3145732
  0.6 7.2 %collective-permute-start = (bf16[128,2,128]{2,1,0:T(2,128)(2,1)}, bf16[128,2,128]{2,1,0:T(2,128)(2,1)S(1)}, u32[]{:S(2)}, u32[]{:S(2)}) collective-permute-start(bf16[128,2,128]{2,1,0:T(2,128)(2,1)} %own_ref.1), channel_id=1, source_target_pairs={{0,1},{1,2},{2,3},{3,4},{4,5},{5,6},{6,7},{7,8},{8,9},{9,10},{10,1... | collective-permute-start | bytes 196616 | tf_op jit(solution)/shard_map/ppermute | solution.py:32
  4.7 5.3 %collective-permute-start.1 = (bf16[129,2,128]{2,1,0:T(2,128)(2,1)S(1)}, bf16[129,2,128]{2,1,0:T(2,128)(2,1)S(1)}, u32[]{:S(2)}, u32[]{:S(2)}) collective-permute-start(bf16[129,2,128]{2,1,0:T(2,128)(2,1)S(1)} %concatenate.3), channel_id=1, source_target_pairs={{1,0},{2,1},{3,2},{4,3},{5,4},{6,5},{7,6},{8,7},{9,8},{10,9},{11,1... | collective-permute-start | bytes 198152 | tf_op jit(solution)/shard_map/ppermute | solution.py:32
  7.8 2.2 %copy-start.2 = (bf16[128,2,128]{2,1,0:T(2,128)(2,1)}, bf16[128,2,128]{2,1,0:T(2,128)(2,1)S(1)}, u32[]{:S(2)}) copy-start(bf16[128,2,128]{2,1,0:T(2,128)(2,1)S(1)} %collective-permute-done.low_ref) | copy-start | bytes 196612
  10.0 0.6 %copy-start.1 = (bf16[129,2,128]{2,1,0:T(2,128)(2,1)}, bf16[129,2,128]{2,1,0:T(2,128)(2,1)S(1)}, u32[]{:S(2)}) copy-start(bf16[129,2,128]{2,1,0:T(2,128)(2,1)S(1)} %collective-permute-done.1.upper_ref) | copy-start | bytes 198148

commit v16 on v13

--- a/solution.py
+++ b/solution.py
@@ -30,6 +30,22 @@
     count = lax.axis_size(axis)
     route = [(i, i + step) for i in range(count) if 0 <= i + step < count]
     return lax.ppermute(block, axis, route)
+
+
+def own_kernel(own_ref, wq_ref, wk_ref, wv_ref, q_ref, k_ref, v_ref):
+    f32, bf16 = jnp.float32, jnp.bfloat16
+    rows, samples, _ = own_ref.shape
+    normal = []
+    for s in range(samples):
+        x = own_ref[:, s, :].astype(f32)
+        mean = jnp.mean(x, axis=-1, keepdims=True)
+        var = jnp.mean((x - mean) ** 2, axis=-1, keepdims=True)
+        normal.append(((x - mean) / jnp.sqrt(var + 1e-05)).astype(bf16))
+    xn = jnp.concatenate(normal, axis=0)
+    for w_ref, o_ref in ((wq_ref, q_ref), (wk_ref, k_ref), (wv_ref, v_ref)):
+        y = jnp.dot(xn, w_ref[...], preferred_element_type=f32).astype(bf16)
+        for s in range(samples):
+            o_ref[s] = y[s * rows : (s + 1) * rows]
 
 
 def atom_kernel(
@@ -45,6 +61,9 @@
     ids_ref,
     token_ref,
     wq_hbm,
+    q_own_ref,
+    k_own_ref,
+    v_own_ref,
     atom_ref,
     state_ref,
     query_ref,
@@ -90,7 +109,7 @@
     onehot = (own_ids == row_ids).astype(f32)
     counts = jnp.sum(onehot, axis=1, keepdims=True)
     onehot = onehot.astype(bf16)
-    xs, xns = [], []
+    xs, halo = [], []
     for s in range(samples):
         x = jnp.concatenate(
             [
@@ -100,18 +119,34 @@
             ],
             axis=0,
         ).astype(f32)
-        mean = jnp.mean(x, axis=-1, keepdims=True)
-        var = jnp.mean((x - mean) ** 2, axis=-1, keepdims=True)
         xs.append(x)
-        xns.append(((x - mean) / jnp.sqrt(var + 1e-05)).astype(bf16))
-    xn_all = jnp.concatenate(xns, axis=0)
-    q_all = jnp.dot(
-        jnp.concatenate([xn[low_rows : low_rows + rows] for xn in xns], axis=0),
+        for part in (x[0:low_rows], x[low_rows + atom_dev :]):
+            mean = jnp.mean(part, axis=-1, keepdims=True)
+            var = jnp.mean((part - mean) ** 2, axis=-1, keepdims=True)
+            halo.append(((part - mean) / jnp.sqrt(var + 1e-05)).astype(bf16))
+    halo_rows = low_rows + high_rows
+    halo_all = jnp.concatenate(halo, axis=0)
+    kh = jnp.dot(halo_all, wk_ref[...], preferred_element_type=f32).astype(bf16)
+    vh = jnp.dot(halo_all, wv_ref[...], preferred_element_type=f32).astype(bf16)
+    extra = rows - atom_dev
+    qh = jnp.dot(
+        jnp.concatenate([halo[2 * s + 1][0:extra] for s in range(samples)], axis=0),
         wq_ref[...],
         preferred_element_type=f32,
     ).astype(bf16)
-    k_all = jnp.dot(xn_all, wk_ref[...], preferred_element_type=f32).astype(bf16)
-    v_all = jnp.dot(xn_all, wv_ref[...], preferred_element_type=f32).astype(bf16)
+
+    def assembled(h, own, s):
+        start = s * halo_rows
+        return jnp.concatenate(
+            [h[start : start + low_rows], own[s], h[start + low_rows : start + halo_rows]], axis=0
+        )
+
+    q_all = jnp.concatenate(
+        [jnp.concatenate([q_own_ref[s], qh[s * extra : (s + 1) * extra]], axis=0) for s in range(samples)],
+        axis=0,
+    )
+    k_all = jnp.concatenate([assembled(kh, k_own_ref, s) for s in range(samples)], axis=0)
+    v_all = jnp.concatenate([assembled(vh, v_own_ref, s) for s in range(samples)], axis=0)
     mixed = []
     for s in range(samples):
         q = q_all[s * rows : (s + 1) * rows]
@@ -303,6 +338,18 @@
     )
     hbm = pl.BlockSpec(memory_space=pl.ANY)
     count = tok_dev * devices
+    own_shape = jax.ShapeDtypeStruct((samples, atom_dev, width), jnp.bfloat16)
+    q_own, k_own, v_own = pl.pallas_call(
+        own_kernel,
+        out_shape=(own_shape, own_shape, own_shape),
+        in_specs=[vmem] * 4,
+        out_specs=(vmem, vmem, vmem),
+        cost_estimate=pl.CostEstimate(
+            flops=2 * samples * atom_dev * width * 3 * width,
+            transcendentals=0,
+            bytes_accessed=2 * 4 * samples * atom_dev * width + 2 * 3 * width * width,
+        ),
+    )(atom_feat, w_atom_query, w_atom_key, w_atom_value)
     atom_out, state_t, query_t = pl.pallas_call(
         kernel,
         out_shape=(
@@ -313,7 +360,7 @@
         in_specs=[vmem] * 3
         + [pl.BlockSpec(memory_space=pltpu.SMEM)]
         + [vmem] * 7
-        + [hbm],
+        + [hbm, vmem, vmem, vmem],
         out_specs=(vmem, vmem, vmem),
         scratch_shapes=[
             pltpu.VMEM(w_query.shape, w_query.dtype),
@@ -339,6 +386,9 @@
         atom_token[None, :],
         token_in,
         w_query,
+        q_own,
+        k_own,
+        v_own,
     )
     bias = jnp.einsum("qkc,ch->qhk", pair, w_bias, preferred_element_type=jnp.float32)
     bias = bias.reshape(tok_dev * TOKEN_HEADS, count)

time: 49.5 us -> 51.6 us (1.042)
  Pallas kernels: 11.8 us -> 13.9 us
  waiting for transfers between devices: 2.19 us -> 0.22 us
  blocking collectives: 26.7 us -> 28.6 us
    pallas_call x0 -> x1, Pallas kernels: none -> 1.98 us  [on_device(): pl.pallas_call(own_kernel, out_shape=(own_shape, own_shape, own_shape), i...]
    ppermute x2, waiting for transfers between devices: 2.19 us -> 0.22 us  [shifted(): return lax.ppermute(block, axis, route)]
    all_gather x1, blocking collectives: 26.7 us -> 28.6 us  [on_device(): every = lax.all_gather(state_t, 'row', axis=1, tiled=True)]
  transfers between devices with their start and end apart: 2 -> 2, of which waited for: 1 -> 1; matrix products, arithmetic and copies ran while one was open for 7% -> 7% of each run, Pallas kernels for 0% -> 4%
where the time goes in v16:
time: 51.6 us; the launch traced here: 51.2 us
  blocking collectives  28.6 us (55%)
  Pallas kernels  13.9 us (27%)
  starting transfers between devices  3.79 us (7%)
  matrix products  1.77 us (3%)
  local copies, waits for them, and re-layouts  1.57 us (3%)
  between operations  0.68 us (1%)
  other arithmetic  0.66 us (1%)
    all_gather x1, blocking collectives, on_device(): every = lax.all_gather(state_t, 'row', axis=1, tiled=True)  28.6 us
    pallas_call x1, Pallas kernels, on_device(): pl.pallas_call(kernel, out_shape=(jax.ShapeDtypeStruct((atom_dev, samples...  5.98 us
    pallas_call x1, Pallas kernels, on_device(): pl.pallas_call(functools.partial(token_kernel, heads=TOKEN_HEADS), out_sh...  5.94 us
    ppermute x2, starting transfers between devices, shifted(): return lax.ppermute(block, axis, route)  3.79 us
    pallas_call x1, Pallas kernels, on_device(): pl.pallas_call(own_kernel, out_shape=(own_shape, own_shape, own_shape), i...  1.98 us
    dot_general x1, matrix products, on_device(): jnp.einsum('qkc,ch->qhk', pair, w_bias, preferred_element_type=jnp.float32)  1.77 us
  transfers between devices with their start and end apart: 2, of which 1 were waited for; matrix products, arithmetic and copies ran while one was open for 7% of the time, Pallas kernels for 4%

profile of v16, /device:TPU:0, one launch (start us, length us, event | category | flops | bytes accessed | tf_op | source)
XLA Modules:
  0.0 51.2 jit_solution(2413014568359667781)
XLA Ops:
  0.6 0.0 copy-start
  0.6 2.5 %collective-permute-start = (bf16[128,2,128]{2,1,0:T(2,128)(2,1)}, bf16[128,2,128]{2,1,0:T(2,128)(2,1)S(1)}, u32[]{:S(2)}, u32[]{:S(2)}) collective-permute-start(bf16[128,2,128]{2,1,0:T(2,128)(2,1)} %own_ref.3), channel_id=1, source_target_pairs={{0,1},{1,2},{2,3},{3,4},{4,5},{5,6},{6,7},{7,8},{8,9},{9,10},{10,1... | collective-permute-start | bytes 196616 | tf_op jit(solution)/shard_map/ppermute | solution.py:32
  3.1 0.7 %convert.3 = bf16[4]{0:T(256)(128)(2,1)S(1)} convert(s32[4]{0:T(128)} %shift_ref.1) | non-fusion elementwise | flops 4 | bytes 24 | tf_op jit(solution)/shard_map/convert
  3.8 0.9 %concatenate.3 = bf16[129,2,128]{2,1,0:T(2,128)(2,1)S(1)} pad(bf16[128,2,128]{2,1,0:T(2,128)(2,1)} %own_ref.3, bf16[]{:T(256)S(1)} %bitcast.13), padding=0_1x0_0x0_0 | pad | bytes 131586 | tf_op jit(solution)/shard_map/concatenate | solution.py:318
  4.7 1.3 %collective-permute-start.1 = (bf16[129,2,128]{2,1,0:T(2,128)(2,1)S(1)}, bf16[129,2,128]{2,1,0:T(2,128)(2,1)S(1)}, u32[]{:S(2)}, u32[]{:S(2)}) collective-permute-start(bf16[129,2,128]{2,1,0:T(2,128)(2,1)S(1)} %concatenate.3), channel_id=1, source_target_pairs={{1,0},{2,1},{3,2},{4,3},{5,4},{6,5},{7,6},{8,7},{9,8},{10,9},{11,1... | collective-permute-start | bytes 198152 | tf_op jit(solution)/shard_map/ppermute | solution.py:32
  6.0 0.0 copy-done
  6.1 1.8 %fusion = f32[16,16,256]{2,0,1:T(8,128)} fusion(bf16[16,256,128]{2,1,0:T(8,128)(2,1)S(1)} %copy-done, bf16[128,16]{0,1:T(8,128)(2,1)} %param.31), kind=kOutput, calls=%fused_computation | convolution fusion | flops 16777216 | bytes 1314816 | tf_op jit(solution)/shard_map/qkc,ch->qhk/dot_general | solution.py:393
  7.8 2.0 %shard_map.167 = (bf16[2,128,128]{2,1,0:T(8,128)(2,1)}, bf16[2,128,128]{2,1,0:T(8,128)(2,1)}, bf16[2,128,128]{2,1,0:T(8,128)(2,1)}) custom-call(bf16[128,2,128]{2,1,0:T(2,128)(2,1)} %own_ref.3, bf16[128,128]{1,0:T(8,128)(2,1)} %wq_ref.3, bf16[128,128]{1,0:T(8,128)(2,1)} %wk_ref.3, bf16[128,128]{1,0:T(8,128)(2,1)} %wv_ref.3), custom_call_target="tpu_custom_call" | custom-call | flops 25165824 | bytes 360448 | tf_op jit(solution)/shard_map/pallas_call | solution.py:342
  9.8 0.0 collective-permute-done.low_ref
  9.8 0.0 copy-start.2
  9.8 0.2 collective-permute-done.1.upper_ref
  10.0 0.0 copy-start.1
  10.0 0.4 copy-done.2
  10.4 0.2 copy-done.1
  10.7 6.0 %shard_map.168 = (bf16[128,2,128]{2,1,0:T(2,128)(2,1)}, bf16[2,16,768]{2,1,0:T(8,128)(2,1)}, bf16[2,16,768]{2,1,0:T(8,128)(2,1)}) custom-call(bf16[128,2,128]{2,1,0:T(2,128)(2,1)} %own_ref.3, bf16[128,2,128]{2,1,0:T(2,128)(2,1)} %copy-done.2, bf16[129,2,128]{2,1,0:T(2,128)(2,1)} %copy-done.1, s32[4]{0:T(128)} %shift_ref.1, bf16[128,128]{1,0:T(8,128)(2,1)} %wq_ref.3, ...), custom_call_target="tpu_custom_call" | custom-call | flops 342360064 | bytes 638976 | tf_op jit(solution)/shard_map/pallas_call | solution.py:353
  16.6 28.6 %all_gather.3.every_ref = bf16[2,256,768]{2,1,0:T(8,128)(2,1)} all-gather(bf16[2,16,768]{2,1,0:T(8,128)(2,1)} %get-tuple-element.12.own_ref), channel_id=1, replica_groups=mesh['groups'=2,'row'=16] {'row'}, dimensions={1}, use_global_device_ids=true | all-gather | bytes 835584 | tf_op jit(solution)/shard_map/all_gather | solution.py:396
  45.3 5.9 %shard_map.169 = bf16[16,2,768]{2,1,0:T(2,128)(2,1)} custom-call(bf16[2,256,768]{2,1,0:T(8,128)(2,1)} %all_gather.3.every_ref, bf16[2,16,768]{2,1,0:T(8,128)(2,1)} %get-tuple-element.12.own_ref, bf16[2,16,768]{2,1,0:T(8,128)(2,1)} %get-tuple-element.13.query_ref, f32[256,256]{1,0:T(8,128)} %bitcast.11, s32[1,256]{1,0:T(1,128)} %bitcast.14, ...), custom_call_target="tpu_custom_call" | custom-call | flops 1686110208 | bytes 5865472 | tf_op jit(solution)/shard_map/pallas_call | solution.py:397
Async XLA Ops:
  0.6 5.4 %copy-start = (bf16[16,256,128]{2,1,0:T(8,128)(2,1)S(1)}, bf16[16,256,128]{2,1,0:T(8,128)(2,1)}, u32[]{:S(2)}) copy-start(bf16[16,256,128]{2,1,0:T(8,128)(2,1)} %param.20) | copy-start | bytes 3145732
  0.6 9.2 %collective-permute-start = (bf16[128,2,128]{2,1,0:T(2,128)(2,1)}, bf16[128,2,128]{2,1,0:T(2,128)(2,1)S(1)}, u32[]{:S(2)}, u32[]{:S(2)}) collective-permute-start(bf16[128,2,128]{2,1,0:T(2,128)(2,1)} %own_ref.3), channel_id=1, source_target_pairs={{0,1},{1,2},{2,3},{3,4},{4,5},{5,6},{6,7},{7,8},{8,9},{9,10},{10,1... | collective-permute-start | bytes 196616 | tf_op jit(solution)/shard_map/ppermute | solution.py:32
  4.7 5.3 %collective-permute-start.1 = (bf16[129,2,128]{2,1,0:T(2,128)(2,1)S(1)}, bf16[129,2,128]{2,1,0:T(2,128)(2,1)S(1)}, u32[]{:S(2)}, u32[]{:S(2)}) collective-permute-start(bf16[129,2,128]{2,1,0:T(2,128)(2,1)S(1)} %concatenate.3), channel_id=1, source_target_pairs={{1,0},{2,1},{3,2},{4,3},{5,4},{6,5},{7,6},{8,7},{9,8},{10,9},{11,1... | collective-permute-start | bytes 198152 | tf_op jit(solution)/shard_map/ppermute | solution.py:32
  9.8 0.6 %copy-start.2 = (bf16[128,2,128]{2,1,0:T(2,128)(2,1)}, bf16[128,2,128]{2,1,0:T(2,128)(2,1)S(1)}, u32[]{:S(2)}) copy-start(bf16[128,2,128]{2,1,0:T(2,128)(2,1)S(1)} %collective-permute-done.low_ref) | copy-start | bytes 196612
  10.0 0.6 %copy-start.1 = (bf16[129,2,128]{2,1,0:T(2,128)(2,1)}, bf16[129,2,128]{2,1,0:T(2,128)(2,1)S(1)}, u32[]{:S(2)}) copy-start(bf16[129,2,128]{2,1,0:T(2,128)(2,1)S(1)} %collective-permute-done.1.upper_ref) | copy-start | bytes 198148

commit v17 on v13

--- a/solution.py
+++ b/solution.py
@@ -81,6 +81,7 @@
     hi = jnp.minimum(first + KWIN, total - base + low_rows)
     column = lax.broadcasted_iota(jnp.int32, (rows, ext_rows), 1)
     keep = (column >= lo) & (column < hi)
+    keep_all = jnp.concatenate([keep] * ATOM_HEADS, axis=0)
     own_start = pl.multiple_of(base, atom_dev)
     next_start = pl.multiple_of(jnp.minimum(base + atom_dev, total - atom_dev), atom_dev)
     next_ids = ids_ref[:, pl.ds(next_start, atom_dev)][:, 0 : rows - atom_dev]
@@ -117,18 +118,20 @@
         q = q_all[s * rows : (s + 1) * rows]
         k = k_all[s * ext_rows : (s + 1) * ext_rows]
         v = v_all[s * ext_rows : (s + 1) * ext_rows]
-        acc = jnp.zeros((rows, width), f32)
-        for h in range(ATOM_HEADS):
-            qh = q * head_masks[h].astype(bf16)
-            sc = lax.dot_general(
-                qh, k, (((1,), (1,)), ((), ())), preferred_element_type=f32
-            ) / root
-            sc = jnp.where(keep, sc, -1e30)
-            top = jnp.max(sc, axis=-1, keepdims=True)
-            e = jnp.where(keep, jnp.exp(sc - top), 0.0)
-            tot = jnp.sum(e, axis=-1, keepdims=True)
-            o = jnp.dot(e.astype(bf16), v, preferred_element_type=f32)
-            acc = acc + (o / tot) * head_masks[h]
+        stacked = jnp.concatenate(
+            [q * head_masks[h].astype(bf16) for h in range(ATOM_HEADS)], axis=0
+        )
+        sc = lax.dot_general(
+            stacked, k, (((1,), (1,)), ((), ())), preferred_element_type=f32
+        ) / root
+        sc = jnp.where(keep_all, sc, -1e30)
+        top = jnp.max(sc, axis=-1, keepdims=True)
+        e = jnp.where(keep_all, jnp.exp(sc - top), 0.0)
+        tot = jnp.sum(e, axis=-1, keepdims=True)
+        o = jnp.dot(e.astype(bf16), v, preferred_element_type=f32) / tot
+        acc = o[0:rows] * head_masks[0]
+        for h in range(1, ATOM_HEADS):
+            acc = acc + o[h * rows : (h + 1) * rows] * head_masks[h]
         mixed.append(acc.astype(bf16))
     base = jnp.concatenate([x[low_rows : low_rows + rows] for x in xs], axis=0)
     out = (

time: 49.5 us -> 48.4 us (0.978)
  Pallas kernels: 11.8 us -> 10.7 us
    pallas_call x1, Pallas kernels: 5.9 us -> 4.74 us  [on_device(): pl.pallas_call(kernel, out_shape=(jax.ShapeDtypeStruct((atom_dev, samples...]
where the time goes in v17:
time: 48.4 us; the launch traced here: 48.1 us
  blocking collectives  26.7 us (55%)
  Pallas kernels  10.7 us (22%)
  starting transfers between devices  3.79 us (8%)
  waiting for transfers between devices  2.19 us (5%)
  matrix products  1.78 us (4%)
  local copies, waits for them, and re-layouts  1.56 us (3%)
  between operations  0.68 us (1%)
  other arithmetic  0.66 us (1%)
    all_gather x1, blocking collectives, on_device(): every = lax.all_gather(state_t, 'row', axis=1, tiled=True)  26.7 us
    pallas_call x1, Pallas kernels, on_device(): pl.pallas_call(functools.partial(token_kernel, heads=TOKEN_HEADS), out_sh...  5.94 us
    pallas_call x1, Pallas kernels, on_device(): pl.pallas_call(kernel, out_shape=(jax.ShapeDtypeStruct((atom_dev, samples...  4.74 us
    ppermute x2, starting transfers between devices, shifted(): return lax.ppermute(block, axis, route)  3.79 us
    ppermute x2, waiting for transfers between devices, shifted(): return lax.ppermute(block, axis, route)  2.19 us
    dot_general x1, matrix products, on_device(): jnp.einsum('qkc,ch->qhk', pair, w_bias, preferred_element_type=jnp.float32)  1.78 us
  transfers between devices with their start and end apart: 2, of which 1 were waited for; matrix products, arithmetic and copies ran while one was open for 7% of the time, Pallas kernels for 0%

profile of v17, /device:TPU:0, one launch (start us, length us, event | category | flops | bytes accessed | tf_op | source)
XLA Modules:
  0.0 48.1 jit_solution(7420760161238340175)
XLA Ops:
  0.6 0.0 copy-start
  0.6 2.5 %collective-permute-start = (bf16[128,2,128]{2,1,0:T(2,128)(2,1)}, bf16[128,2,128]{2,1,0:T(2,128)(2,1)S(1)}, u32[]{:S(2)}, u32[]{:S(2)}) collective-permute-start(bf16[128,2,128]{2,1,0:T(2,128)(2,1)} %own_ref.1), channel_id=1, source_target_pairs={{0,1},{1,2},{2,3},{3,4},{4,5},{5,6},{6,7},{7,8},{8,9},{9,10},{10,1... | collective-permute-start | bytes 196616 | tf_op jit(solution)/shard_map/ppermute | solution.py:32
  3.1 0.7 %convert.3 = bf16[4]{0:T(256)(128)(2,1)S(1)} convert(s32[4]{0:T(128)} %shift_ref.1) | non-fusion elementwise | flops 4 | bytes 24 | tf_op jit(solution)/shard_map/convert
  3.8 0.9 %concatenate.3 = bf16[129,2,128]{2,1,0:T(2,128)(2,1)S(1)} pad(bf16[128,2,128]{2,1,0:T(2,128)(2,1)} %own_ref.1, bf16[]{:T(256)S(1)} %bitcast.13), padding=0_1x0_0x0_0 | pad | bytes 131586 | tf_op jit(solution)/shard_map/concatenate | solution.py:286
  4.7 1.3 %collective-permute-start.1 = (bf16[129,2,128]{2,1,0:T(2,128)(2,1)S(1)}, bf16[129,2,128]{2,1,0:T(2,128)(2,1)S(1)}, u32[]{:S(2)}, u32[]{:S(2)}) collective-permute-start(bf16[129,2,128]{2,1,0:T(2,128)(2,1)S(1)} %concatenate.3), channel_id=1, source_target_pairs={{1,0},{2,1},{3,2},{4,3},{5,4},{6,5},{7,6},{8,7},{9,8},{10,9},{11,1... | collective-permute-start | bytes 198152 | tf_op jit(solution)/shard_map/ppermute | solution.py:32
  6.0 0.0 copy-done
  6.1 1.8 %fusion = f32[16,16,256]{2,0,1:T(8,128)} fusion(bf16[16,256,128]{2,1,0:T(8,128)(2,1)S(1)} %copy-done, bf16[128,16]{0,1:T(8,128)(2,1)} %param.31), kind=kOutput, calls=%fused_computation | convolution fusion | flops 16777216 | bytes 1314816 | tf_op jit(solution)/shard_map/qkc,ch->qhk/dot_general | solution.py:346
  7.8 0.0 collective-permute-done.low_ref
  7.8 0.0 copy-start.2
  7.8 2.2 %collective-permute-done.1.upper_ref = bf16[129,2,128]{2,1,0:T(2,128)(2,1)S(1)} collective-permute-done((bf16[129,2,128]{2,1,0:T(2,128)(2,1)S(1)}, bf16[129,2,128]{2,1,0:T(2,128)(2,1)S(1)}, u32[]{:S(2)}, u32[]{:S(2)}) %collective-permute-start.1) | collective-permute-done | bytes 66080 | tf_op jit(solution)/shard_map/ppermute | solution.py:32
  10.0 0.0 copy-start.1
  10.0 0.0 copy-done.2
  10.0 0.6 %copy-done.1 = bf16[129,2,128]{2,1,0:T(2,128)(2,1)} copy-done((bf16[129,2,128]{2,1,0:T(2,128)(2,1)}, bf16[129,2,128]{2,1,0:T(2,128)(2,1)S(1)}, u32[]{:S(2)}) %copy-start.1) | copy-done | bytes 66072
  10.6 4.7 %shard_map.167 = (bf16[128,2,128]{2,1,0:T(2,128)(2,1)}, bf16[2,16,768]{2,1,0:T(8,128)(2,1)}, bf16[2,16,768]{2,1,0:T(8,128)(2,1)}) custom-call(bf16[128,2,128]{2,1,0:T(2,128)(2,1)} %own_ref.1, bf16[128,2,128]{2,1,0:T(2,128)(2,1)} %copy-done.2, bf16[129,2,128]{2,1,0:T(2,128)(2,1)} %copy-done.1, s32[4]{0:T(128)} %shift_ref.1, bf16[128,128]{1,0:T(8,128)(2,1)} %wq_ref.1, ...), custom_call_target="tpu_custom_call" | custom-call | flops 342360064 | bytes 638976 | tf_op jit(solution)/shard_map/pallas_call | solution.py:309
  15.4 26.7 %all_gather.3.every_ref = bf16[2,256,768]{2,1,0:T(8,128)(2,1)} all-gather(bf16[2,16,768]{2,1,0:T(8,128)(2,1)} %get-tuple-element.6.own_ref), channel_id=1, replica_groups=mesh['groups'=2,'row'=16] {'row'}, dimensions={1}, use_global_device_ids=true | all-gather | bytes 835584 | tf_op jit(solution)/shard_map/all_gather | solution.py:349
  42.1 5.9 %shard_map.168 = bf16[16,2,768]{2,1,0:T(2,128)(2,1)} custom-call(bf16[2,256,768]{2,1,0:T(8,128)(2,1)} %all_gather.3.every_ref, bf16[2,16,768]{2,1,0:T(8,128)(2,1)} %get-tuple-element.6.own_ref, bf16[2,16,768]{2,1,0:T(8,128)(2,1)} %get-tuple-element.7.query_ref, f32[256,256]{1,0:T(8,128)} %bitcast.11, s32[1,256]{1,0:T(1,128)} %bitcast.14, ...), custom_call_target="tpu_custom_call" | custom-call | flops 1686110208 | bytes 5865472 | tf_op jit(solution)/shard_map/pallas_call | solution.py:350
Async XLA Ops:
  0.6 5.4 %copy-start = (bf16[16,256,128]{2,1,0:T(8,128)(2,1)S(1)}, bf16[16,256,128]{2,1,0:T(8,128)(2,1)}, u32[]{:S(2)}) copy-start(bf16[16,256,128]{2,1,0:T(8,128)(2,1)} %param.20) | copy-start | bytes 3145732
  0.6 7.2 %collective-permute-start = (bf16[128,2,128]{2,1,0:T(2,128)(2,1)}, bf16[128,2,128]{2,1,0:T(2,128)(2,1)S(1)}, u32[]{:S(2)}, u32[]{:S(2)}) collective-permute-start(bf16[128,2,128]{2,1,0:T(2,128)(2,1)} %own_ref.1), channel_id=1, source_target_pairs={{0,1},{1,2},{2,3},{3,4},{4,5},{5,6},{6,7},{7,8},{8,9},{9,10},{10,1... | collective-permute-start | bytes 196616 | tf_op jit(solution)/shard_map/ppermute | solution.py:32
  4.7 5.3 %collective-permute-start.1 = (bf16[129,2,128]{2,1,0:T(2,128)(2,1)S(1)}, bf16[129,2,128]{2,1,0:T(2,128)(2,1)S(1)}, u32[]{:S(2)}, u32[]{:S(2)}) collective-permute-start(bf16[129,2,128]{2,1,0:T(2,128)(2,1)S(1)} %concatenate.3), channel_id=1, source_target_pairs={{1,0},{2,1},{3,2},{4,3},{5,4},{6,5},{7,6},{8,7},{9,8},{10,9},{11,1... | collective-permute-start | bytes 198152 | tf_op jit(solution)/shard_map/ppermute | solution.py:32
  7.8 2.2 %copy-start.2 = (bf16[128,2,128]{2,1,0:T(2,128)(2,1)}, bf16[128,2,128]{2,1,0:T(2,128)(2,1)S(1)}, u32[]{:S(2)}) copy-start(bf16[128,2,128]{2,1,0:T(2,128)(2,1)S(1)} %collective-permute-done.low_ref) | copy-start | bytes 196612
  10.0 0.6 %copy-start.1 = (bf16[129,2,128]{2,1,0:T(2,128)(2,1)}, bf16[129,2,128]{2,1,0:T(2,128)(2,1)S(1)}, u32[]{:S(2)}) copy-start(bf16[129,2,128]{2,1,0:T(2,128)(2,1)S(1)} %collective-permute-done.1.upper_ref) | copy-start | bytes 198148

commit v18 on v17

--- a/solution.py
+++ b/solution.py
@@ -111,8 +111,13 @@
         wq_ref[...],
         preferred_element_type=f32,
     ).astype(bf16)
-    k_all = jnp.dot(xn_all, wk_ref[...], preferred_element_type=f32).astype(bf16)
-    v_all = jnp.dot(xn_all, wv_ref[...], preferred_element_type=f32).astype(bf16)
+    kv_all = jnp.dot(
+        xn_all,
+        jnp.concatenate([wk_ref[...], wv_ref[...]], axis=1),
+        preferred_element_type=f32,
+    ).astype(bf16)
+    k_all = kv_all[:, 0:width]
+    v_all = kv_all[:, width:]
     mixed = []
     for s in range(samples):
         q = q_all[s * rows : (s + 1) * rows]
@@ -152,10 +157,10 @@
         ],
         axis=0,
     )
-    sums = (
-        jnp.dot(diagonal, top_part, preferred_element_type=f32)
-        + jnp.dot(diagonal, mid_part, preferred_element_type=f32)
-        + jnp.dot(diagonal, low_part, preferred_element_type=f32)
+    sums = jnp.dot(
+        jnp.concatenate([diagonal] * 3, axis=1),
+        jnp.concatenate([top_part, mid_part, low_part], axis=0),
+        preferred_element_type=f32,
     )
     tns = []
     for s in range(samples):

time: 48.4 us -> 49.1 us (1.014)
  Pallas kernels: 10.7 us -> 11.3 us
    pallas_call x1, Pallas kernels: 4.74 us -> 5.4 us  [on_device(): pl.pallas_call(kernel, out_shape=(jax.ShapeDtypeStruct((atom_dev, samples...]
where the time goes in v18:
time: 49.1 us; the launch traced here: 48.7 us
  blocking collectives  26.7 us (54%)
  Pallas kernels  11.3 us (23%)
  starting transfers between devices  3.79 us (8%)
  waiting for transfers between devices  2.19 us (4%)
  matrix products  1.78 us (4%)
  local copies, waits for them, and re-layouts  1.56 us (3%)
  between operations  0.68 us (1%)
  other arithmetic  0.66 us (1%)
    all_gather x1, blocking collectives, on_device(): every = lax.all_gather(state_t, 'row', axis=1, tiled=True)  26.7 us
    pallas_call x1, Pallas kernels, on_device(): pl.pallas_call(functools.partial(token_kernel, heads=TOKEN_HEADS), out_sh...  5.94 us
    pallas_call x1, Pallas kernels, on_device(): pl.pallas_call(kernel, out_shape=(jax.ShapeDtypeStruct((atom_dev, samples...  5.4 us
    ppermute x2, starting transfers between devices, shifted(): return lax.ppermute(block, axis, route)  3.79 us
    ppermute x2, waiting for transfers between devices, shifted(): return lax.ppermute(block, axis, route)  2.19 us
    dot_general x1, matrix products, on_device(): jnp.einsum('qkc,ch->qhk', pair, w_bias, preferred_element_type=jnp.float32)  1.78 us
  transfers between devices with their start and end apart: 2, of which 1 were waited for; matrix products, arithmetic and copies ran while one was open for 7% of the time, Pallas kernels for 0%

profile of v18, /device:TPU:0, one launch (start us, length us, event | category | flops | bytes accessed | tf_op | source)
XLA Modules:
  0.0 48.7 jit_solution(5163114123477703820)
XLA Ops:
  0.6 0.0 copy-start
  0.6 2.5 %collective-permute-start = (bf16[128,2,128]{2,1,0:T(2,128)(2,1)}, bf16[128,2,128]{2,1,0:T(2,128)(2,1)S(1)}, u32[]{:S(2)}, u32[]{:S(2)}) collective-permute-start(bf16[128,2,128]{2,1,0:T(2,128)(2,1)} %own_ref.1), channel_id=1, source_target_pairs={{0,1},{1,2},{2,3},{3,4},{4,5},{5,6},{6,7},{7,8},{8,9},{9,10},{10,1... | collective-permute-start | bytes 196616 | tf_op jit(solution)/shard_map/ppermute | solution.py:32
  3.1 0.7 %convert.3 = bf16[4]{0:T(256)(128)(2,1)S(1)} convert(s32[4]{0:T(128)} %shift_ref.1) | non-fusion elementwise | flops 4 | bytes 24 | tf_op jit(solution)/shard_map/convert
  3.8 0.9 %concatenate.3 = bf16[129,2,128]{2,1,0:T(2,128)(2,1)S(1)} pad(bf16[128,2,128]{2,1,0:T(2,128)(2,1)} %own_ref.1, bf16[]{:T(256)S(1)} %bitcast.13), padding=0_1x0_0x0_0 | pad | bytes 131586 | tf_op jit(solution)/shard_map/concatenate | solution.py:291
  4.7 1.3 %collective-permute-start.1 = (bf16[129,2,128]{2,1,0:T(2,128)(2,1)S(1)}, bf16[129,2,128]{2,1,0:T(2,128)(2,1)S(1)}, u32[]{:S(2)}, u32[]{:S(2)}) collective-permute-start(bf16[129,2,128]{2,1,0:T(2,128)(2,1)S(1)} %concatenate.3), channel_id=1, source_target_pairs={{1,0},{2,1},{3,2},{4,3},{5,4},{6,5},{7,6},{8,7},{9,8},{10,9},{11,1... | collective-permute-start | bytes 198152 | tf_op jit(solution)/shard_map/ppermute | solution.py:32
  6.0 0.0 copy-done
  6.1 1.8 %fusion = f32[16,16,256]{2,0,1:T(8,128)} fusion(bf16[16,256,128]{2,1,0:T(8,128)(2,1)S(1)} %copy-done, bf16[128,16]{0,1:T(8,128)(2,1)} %param.31), kind=kOutput, calls=%fused_computation | convolution fusion | flops 16777216 | bytes 1314816 | tf_op jit(solution)/shard_map/qkc,ch->qhk/dot_general | solution.py:351
  7.8 0.0 collective-permute-done.low_ref
  7.8 0.0 copy-start.2
  7.8 2.2 %collective-permute-done.1.upper_ref = bf16[129,2,128]{2,1,0:T(2,128)(2,1)S(1)} collective-permute-done((bf16[129,2,128]{2,1,0:T(2,128)(2,1)S(1)}, bf16[129,2,128]{2,1,0:T(2,128)(2,1)S(1)}, u32[]{:S(2)}, u32[]{:S(2)}) %collective-permute-start.1) | collective-permute-done | bytes 66080 | tf_op jit(solution)/shard_map/ppermute | solution.py:32
  10.0 0.0 copy-start.1
  10.0 0.0 copy-done.2
  10.0 0.6 %copy-done.1 = bf16[129,2,128]{2,1,0:T(2,128)(2,1)} copy-done((bf16[129,2,128]{2,1,0:T(2,128)(2,1)}, bf16[129,2,128]{2,1,0:T(2,128)(2,1)S(1)}, u32[]{:S(2)}) %copy-start.1) | copy-done | bytes 66072
  10.6 5.4 %shard_map.167 = (bf16[128,2,128]{2,1,0:T(2,128)(2,1)}, bf16[2,16,768]{2,1,0:T(8,128)(2,1)}, bf16[2,16,768]{2,1,0:T(8,128)(2,1)}) custom-call(bf16[128,2,128]{2,1,0:T(2,128)(2,1)} %own_ref.1, bf16[128,2,128]{2,1,0:T(2,128)(2,1)} %copy-done.2, bf16[129,2,128]{2,1,0:T(2,128)(2,1)} %copy-done.1, s32[4]{0:T(128)} %shift_ref.1, bf16[128,128]{1,0:T(8,128)(2,1)} %wq_ref.1, ...), custom_call_target="tpu_custom_call" | custom-call | flops 342360064 | bytes 638976 | tf_op jit(solution)/shard_map/pallas_call | solution.py:314
  16.0 26.7 %all_gather.3.every_ref = bf16[2,256,768]{2,1,0:T(8,128)(2,1)} all-gather(bf16[2,16,768]{2,1,0:T(8,128)(2,1)} %get-tuple-element.6.own_ref), channel_id=1, replica_groups=mesh['groups'=2,'row'=16] {'row'}, dimensions={1}, use_global_device_ids=true | all-gather | bytes 835584 | tf_op jit(solution)/shard_map/all_gather | solution.py:354
  42.8 5.9 %shard_map.168 = bf16[16,2,768]{2,1,0:T(2,128)(2,1)} custom-call(bf16[2,256,768]{2,1,0:T(8,128)(2,1)} %all_gather.3.every_ref, bf16[2,16,768]{2,1,0:T(8,128)(2,1)} %get-tuple-element.6.own_ref, bf16[2,16,768]{2,1,0:T(8,128)(2,1)} %get-tuple-element.7.query_ref, f32[256,256]{1,0:T(8,128)} %bitcast.11, s32[1,256]{1,0:T(1,128)} %bitcast.14, ...), custom_call_target="tpu_custom_call" | custom-call | flops 1686110208 | bytes 5865472 | tf_op jit(solution)/shard_map/pallas_call | solution.py:355
Async XLA Ops:
  0.6 5.4 %copy-start = (bf16[16,256,128]{2,1,0:T(8,128)(2,1)S(1)}, bf16[16,256,128]{2,1,0:T(8,128)(2,1)}, u32[]{:S(2)}) copy-start(bf16[16,256,128]{2,1,0:T(8,128)(2,1)} %param.20) | copy-start | bytes 3145732
  0.6 7.2 %collective-permute-start = (bf16[128,2,128]{2,1,0:T(2,128)(2,1)}, bf16[128,2,128]{2,1,0:T(2,128)(2,1)S(1)}, u32[]{:S(2)}, u32[]{:S(2)}) collective-permute-start(bf16[128,2,128]{2,1,0:T(2,128)(2,1)} %own_ref.1), channel_id=1, source_target_pairs={{0,1},{1,2},{2,3},{3,4},{4,5},{5,6},{6,7},{7,8},{8,9},{9,10},{10,1... | collective-permute-start | bytes 196616 | tf_op jit(solution)/shard_map/ppermute | solution.py:32
  4.7 5.3 %collective-permute-start.1 = (bf16[129,2,128]{2,1,0:T(2,128)(2,1)S(1)}, bf16[129,2,128]{2,1,0:T(2,128)(2,1)S(1)}, u32[]{:S(2)}, u32[]{:S(2)}) collective-permute-start(bf16[129,2,128]{2,1,0:T(2,128)(2,1)S(1)} %concatenate.3), channel_id=1, source_target_pairs={{1,0},{2,1},{3,2},{4,3},{5,4},{6,5},{7,6},{8,7},{9,8},{10,9},{11,1... | collective-permute-start | bytes 198152 | tf_op jit(solution)/shard_map/ppermute | solution.py:32
  7.8 2.2 %copy-start.2 = (bf16[128,2,128]{2,1,0:T(2,128)(2,1)}, bf16[128,2,128]{2,1,0:T(2,128)(2,1)S(1)}, u32[]{:S(2)}) copy-start(bf16[128,2,128]{2,1,0:T(2,128)(2,1)S(1)} %collective-permute-done.low_ref) | copy-start | bytes 196612
  10.0 0.6 %copy-start.1 = (bf16[129,2,128]{2,1,0:T(2,128)(2,1)}, bf16[129,2,128]{2,1,0:T(2,128)(2,1)S(1)}, u32[]{:S(2)}) copy-start(bf16[129,2,128]{2,1,0:T(2,128)(2,1)S(1)} %collective-permute-done.1.upper_ref) | copy-start | bytes 198148

commit v19 on v17

--- a/solution.py
+++ b/solution.py
@@ -222,9 +222,9 @@
     mixes = []
     for s in range(samples):
         q = query_ref[s]
-        stacked = jnp.concatenate(
-            [q[t : t + 1].astype(f32) * mask_rows for t in range(tok_dev)], axis=0
-        ).astype(bf16)
+        stacked = (q[:, None, :] * mask_rows.astype(bf16)[None, :, :]).reshape(
+            tok_dev * heads, width
+        )
         sc = lax.dot_general(
             stacked, ks[s], (((1,), (1,)), ((), ())), preferred_element_type=f32
         ) / root + bias
@@ -233,15 +233,8 @@
         e = jnp.where(keep, jnp.exp(sc - top), 0.0)
         tot = jnp.sum(e, axis=-1, keepdims=True)
         o = jnp.dot(e.astype(bf16), vs[s], preferred_element_type=f32) / tot
-        mixes.append(
-            jnp.concatenate(
-                [
-                    jnp.sum(o[t * heads : (t + 1) * heads] * mask_rows, axis=0, keepdims=True)
-                    for t in range(tok_dev)
-                ],
-                axis=0,
-            ).astype(bf16)
-        )
+        picked = o.reshape(tok_dev, heads, width) * mask_rows[None, :, :]
+        mixes.append(jnp.sum(picked, axis=1).astype(bf16))
     copies[2].wait()
     projected = jnp.dot(jnp.concatenate(mixes, axis=0), wo_ref[...], preferred_element_type=f32)
     for s in range(samples):

time: 48.4 us -> 48.3 us (level)
  no operation moved by 1% of the time
where the time goes in v19:
time: 48.3 us; the launch traced here: 48 us
  blocking collectives  26.7 us (55%)
  Pallas kernels  10.6 us (22%)
  starting transfers between devices  3.79 us (8%)
  waiting for transfers between devices  2.19 us (5%)
  matrix products  1.78 us (4%)
  local copies, waits for them, and re-layouts  1.56 us (3%)
  between operations  0.68 us (1%)
  other arithmetic  0.66 us (1%)
    all_gather x1, blocking collectives, on_device(): every = lax.all_gather(state_t, 'row', axis=1, tiled=True)  26.7 us
    pallas_call x1, Pallas kernels, on_device(): pl.pallas_call(functools.partial(token_kernel, heads=TOKEN_HEADS), out_sh...  5.89 us
    pallas_call x1, Pallas kernels, on_device(): pl.pallas_call(kernel, out_shape=(jax.ShapeDtypeStruct((atom_dev, samples...  4.74 us
    ppermute x2, starting transfers between devices, shifted(): return lax.ppermute(block, axis, route)  3.79 us
    ppermute x2, waiting for transfers between devices, shifted(): return lax.ppermute(block, axis, route)  2.19 us
    dot_general x1, matrix products, on_device(): jnp.einsum('qkc,ch->qhk', pair, w_bias, preferred_element_type=jnp.float32)  1.78 us
  transfers between devices with their start and end apart: 2, of which 1 were waited for; matrix products, arithmetic and copies ran while one was open for 7% of the time, Pallas kernels for 0%

profile of v19, /device:TPU:0, one launch (start us, length us, event | category | flops | bytes accessed | tf_op | source)
XLA Modules:
  0.0 48.0 jit_solution(8073606997154639816)
XLA Ops:
  0.6 0.0 copy-start
  0.6 2.5 %collective-permute-start = (bf16[128,2,128]{2,1,0:T(2,128)(2,1)}, bf16[128,2,128]{2,1,0:T(2,128)(2,1)S(1)}, u32[]{:S(2)}, u32[]{:S(2)}) collective-permute-start(bf16[128,2,128]{2,1,0:T(2,128)(2,1)} %own_ref.1), channel_id=1, source_target_pairs={{0,1},{1,2},{2,3},{3,4},{4,5},{5,6},{6,7},{7,8},{8,9},{9,10},{10,1... | collective-permute-start | bytes 196616 | tf_op jit(solution)/shard_map/ppermute | solution.py:32
  3.1 0.7 %convert.3 = bf16[4]{0:T(256)(128)(2,1)S(1)} convert(s32[4]{0:T(128)} %shift_ref.1) | non-fusion elementwise | flops 4 | bytes 24 | tf_op jit(solution)/shard_map/convert
  3.8 0.9 %concatenate.3 = bf16[129,2,128]{2,1,0:T(2,128)(2,1)S(1)} pad(bf16[128,2,128]{2,1,0:T(2,128)(2,1)} %own_ref.1, bf16[]{:T(256)S(1)} %bitcast.13), padding=0_1x0_0x0_0 | pad | bytes 131586 | tf_op jit(solution)/shard_map/concatenate | solution.py:279
  4.7 1.3 %collective-permute-start.1 = (bf16[129,2,128]{2,1,0:T(2,128)(2,1)S(1)}, bf16[129,2,128]{2,1,0:T(2,128)(2,1)S(1)}, u32[]{:S(2)}, u32[]{:S(2)}) collective-permute-start(bf16[129,2,128]{2,1,0:T(2,128)(2,1)S(1)} %concatenate.3), channel_id=1, source_target_pairs={{1,0},{2,1},{3,2},{4,3},{5,4},{6,5},{7,6},{8,7},{9,8},{10,9},{11,1... | collective-permute-start | bytes 198152 | tf_op jit(solution)/shard_map/ppermute | solution.py:32
  6.0 0.0 copy-done
  6.1 1.8 %fusion = f32[16,16,256]{2,0,1:T(8,128)} fusion(bf16[16,256,128]{2,1,0:T(8,128)(2,1)S(1)} %copy-done, bf16[128,16]{0,1:T(8,128)(2,1)} %param.31), kind=kOutput, calls=%fused_computation | convolution fusion | flops 16777216 | bytes 1314816 | tf_op jit(solution)/shard_map/qkc,ch->qhk/dot_general | solution.py:339
  7.8 0.0 collective-permute-done.low_ref
  7.8 0.0 copy-start.2
  7.8 2.2 %collective-permute-done.1.upper_ref = bf16[129,2,128]{2,1,0:T(2,128)(2,1)S(1)} collective-permute-done((bf16[129,2,128]{2,1,0:T(2,128)(2,1)S(1)}, bf16[129,2,128]{2,1,0:T(2,128)(2,1)S(1)}, u32[]{:S(2)}, u32[]{:S(2)}) %collective-permute-start.1) | collective-permute-done | bytes 66080 | tf_op jit(solution)/shard_map/ppermute | solution.py:32
  10.0 0.0 copy-start.1
  10.0 0.0 copy-done.2
  10.0 0.6 %copy-done.1 = bf16[129,2,128]{2,1,0:T(2,128)(2,1)} copy-done((bf16[129,2,128]{2,1,0:T(2,128)(2,1)}, bf16[129,2,128]{2,1,0:T(2,128)(2,1)S(1)}, u32[]{:S(2)}) %copy-start.1) | copy-done | bytes 66072
  10.6 4.7 %shard_map.167 = (bf16[128,2,128]{2,1,0:T(2,128)(2,1)}, bf16[2,16,768]{2,1,0:T(8,128)(2,1)}, bf16[2,16,768]{2,1,0:T(8,128)(2,1)}) custom-call(bf16[128,2,128]{2,1,0:T(2,128)(2,1)} %own_ref.1, bf16[128,2,128]{2,1,0:T(2,128)(2,1)} %copy-done.2, bf16[129,2,128]{2,1,0:T(2,128)(2,1)} %copy-done.1, s32[4]{0:T(128)} %shift_ref.1, bf16[128,128]{1,0:T(8,128)(2,1)} %wq_ref.1, ...), custom_call_target="tpu_custom_call" | custom-call | flops 342360064 | bytes 638976 | tf_op jit(solution)/shard_map/pallas_call | solution.py:302
  15.4 26.7 %all_gather.3.every_ref = bf16[2,256,768]{2,1,0:T(8,128)(2,1)} all-gather(bf16[2,16,768]{2,1,0:T(8,128)(2,1)} %get-tuple-element.6.own_ref), channel_id=1, replica_groups=mesh['groups'=2,'row'=16] {'row'}, dimensions={1}, use_global_device_ids=true | all-gather | bytes 835584 | tf_op jit(solution)/shard_map/all_gather | solution.py:342
  42.1 5.9 %shard_map.168 = bf16[16,2,768]{2,1,0:T(2,128)(2,1)} custom-call(bf16[2,256,768]{2,1,0:T(8,128)(2,1)} %all_gather.3.every_ref, bf16[2,16,768]{2,1,0:T(8,128)(2,1)} %get-tuple-element.6.own_ref, bf16[2,16,768]{2,1,0:T(8,128)(2,1)} %get-tuple-element.7.query_ref, f32[256,256]{1,0:T(8,128)} %bitcast.11, s32[1,256]{1,0:T(1,128)} %bitcast.14, ...), custom_call_target="tpu_custom_call" | custom-call | flops 1686110208 | bytes 5865472 | tf_op jit(solution)/shard_map/pallas_call | solution.py:343
Async XLA Ops:
  0.6 5.4 %copy-start = (bf16[16,256,128]{2,1,0:T(8,128)(2,1)S(1)}, bf16[16,256,128]{2,1,0:T(8,128)(2,1)}, u32[]{:S(2)}) copy-start(bf16[16,256,128]{2,1,0:T(8,128)(2,1)} %param.20) | copy-start | bytes 3145732
  0.6 7.2 %collective-permute-start = (bf16[128,2,128]{2,1,0:T(2,128)(2,1)}, bf16[128,2,128]{2,1,0:T(2,128)(2,1)S(1)}, u32[]{:S(2)}, u32[]{:S(2)}) collective-permute-start(bf16[128,2,128]{2,1,0:T(2,128)(2,1)} %own_ref.1), channel_id=1, source_target_pairs={{0,1},{1,2},{2,3},{3,4},{4,5},{5,6},{6,7},{7,8},{8,9},{9,10},{10,1... | collective-permute-start | bytes 196616 | tf_op jit(solution)/shard_map/ppermute | solution.py:32
  4.7 5.3 %collective-permute-start.1 = (bf16[129,2,128]{2,1,0:T(2,128)(2,1)S(1)}, bf16[129,2,128]{2,1,0:T(2,128)(2,1)S(1)}, u32[]{:S(2)}, u32[]{:S(2)}) collective-permute-start(bf16[129,2,128]{2,1,0:T(2,128)(2,1)S(1)} %concatenate.3), channel_id=1, source_target_pairs={{1,0},{2,1},{3,2},{4,3},{5,4},{6,5},{7,6},{8,7},{9,8},{10,9},{11,1... | collective-permute-start | bytes 198152 | tf_op jit(solution)/shard_map/ppermute | solution.py:32
  7.8 2.2 %copy-start.2 = (bf16[128,2,128]{2,1,0:T(2,128)(2,1)}, bf16[128,2,128]{2,1,0:T(2,128)(2,1)S(1)}, u32[]{:S(2)}) copy-start(bf16[128,2,128]{2,1,0:T(2,128)(2,1)S(1)} %collective-permute-done.low_ref) | copy-start | bytes 196612
  10.0 0.6 %copy-start.1 = (bf16[129,2,128]{2,1,0:T(2,128)(2,1)}, bf16[129,2,128]{2,1,0:T(2,128)(2,1)S(1)}, u32[]{:S(2)}) copy-start(bf16[129,2,128]{2,1,0:T(2,128)(2,1)S(1)} %collective-permute-done.1.upper_ref) | copy-start | bytes 198148

commit v20 on v19

--- a/solution.py
+++ b/solution.py
@@ -65,7 +65,10 @@
     _, samples, width = own_ref.shape
     ext_rows = low_rows + atom_dev + high_rows
     lane = lax.broadcasted_iota(jnp.int32, (1, width), 1) // head_dim
-    head_masks = [(lane == h).astype(f32) for h in range(ATOM_HEADS)]
+    head_block = (
+        lax.broadcasted_iota(jnp.int32, (ATOM_HEADS, 1, width), 2) // head_dim
+        == lax.broadcasted_iota(jnp.int32, (ATOM_HEADS, 1, width), 0)
+    ).astype(f32)
     root = jnp.float32(math.sqrt(head_dim))
     rank = lax.axis_index("row")
     base = rank * atom_dev
@@ -118,9 +121,7 @@
         q = q_all[s * rows : (s + 1) * rows]
         k = k_all[s * ext_rows : (s + 1) * ext_rows]
         v = v_all[s * ext_rows : (s + 1) * ext_rows]
-        stacked = jnp.concatenate(
-            [q * head_masks[h].astype(bf16) for h in range(ATOM_HEADS)], axis=0
-        )
+        stacked = (q[None, :, :] * head_block.astype(bf16)).reshape(ATOM_HEADS * rows, width)
         sc = lax.dot_general(
             stacked, k, (((1,), (1,)), ((), ())), preferred_element_type=f32
         ) / root
@@ -129,9 +130,7 @@
         e = jnp.where(keep_all, jnp.exp(sc - top), 0.0)
         tot = jnp.sum(e, axis=-1, keepdims=True)
         o = jnp.dot(e.astype(bf16), v, preferred_element_type=f32) / tot
-        acc = o[0:rows] * head_masks[0]
-        for h in range(1, ATOM_HEADS):
-            acc = acc + o[h * rows : (h + 1) * rows] * head_masks[h]
+        acc = jnp.sum(o.reshape(ATOM_HEADS, rows, width) * head_block, axis=0)
         mixed.append(acc.astype(bf16))
     base = jnp.concatenate([x[low_rows : low_rows + rows] for x in xs], axis=0)
     out = (

time: 48.3 us -> 48.3 us (level)
  no operation moved by 1% of the time
where the time goes in v20:
time: 48.3 us; the launch traced here: 48 us
  blocking collectives  26.7 us (55%)
  Pallas kernels  10.6 us (22%)
  starting transfers between devices  3.79 us (8%)
  waiting for transfers between devices  2.19 us (5%)
  matrix products  1.78 us (4%)
  local copies, waits for them, and re-layouts  1.56 us (3%)
  between operations  0.68 us (1%)
  other arithmetic  0.66 us (1%)
    all_gather x1, blocking collectives, on_device(): every = lax.all_gather(state_t, 'row', axis=1, tiled=True)  26.7 us
    pallas_call x1, Pallas kernels, on_device(): pl.pallas_call(functools.partial(token_kernel, heads=TOKEN_HEADS), out_sh...  5.89 us
    pallas_call x1, Pallas kernels, on_device(): pl.pallas_call(kernel, out_shape=(jax.ShapeDtypeStruct((atom_dev, samples...  4.74 us
    ppermute x2, starting transfers between devices, shifted(): return lax.ppermute(block, axis, route)  3.79 us
    ppermute x2, waiting for transfers between devices, shifted(): return lax.ppermute(block, axis, route)  2.19 us
    dot_general x1, matrix products, on_device(): jnp.einsum('qkc,ch->qhk', pair, w_bias, preferred_element_type=jnp.float32)  1.78 us
  transfers between devices with their start and end apart: 2, of which 1 were waited for; matrix products, arithmetic and copies ran while one was open for 7% of the time, Pallas kernels for 0%

profile of v20, /device:TPU:0, one launch (start us, length us, event | category | flops | bytes accessed | tf_op | source)
XLA Modules:
  0.0 48.0 jit_solution(7651148678049445688)
XLA Ops:
  0.6 0.0 copy-start
  0.6 2.5 %collective-permute-start = (bf16[128,2,128]{2,1,0:T(2,128)(2,1)}, bf16[128,2,128]{2,1,0:T(2,128)(2,1)S(1)}, u32[]{:S(2)}, u32[]{:S(2)}) collective-permute-start(bf16[128,2,128]{2,1,0:T(2,128)(2,1)} %own_ref.1), channel_id=1, source_target_pairs={{0,1},{1,2},{2,3},{3,4},{4,5},{5,6},{6,7},{7,8},{8,9},{9,10},{10,1... | collective-permute-start | bytes 196616 | tf_op jit(solution)/shard_map/ppermute | solution.py:32
  3.1 0.7 %convert.3 = bf16[4]{0:T(256)(128)(2,1)S(1)} convert(s32[4]{0:T(128)} %shift_ref.1) | non-fusion elementwise | flops 4 | bytes 24 | tf_op jit(solution)/shard_map/convert
  3.8 0.9 %concatenate.3 = bf16[129,2,128]{2,1,0:T(2,128)(2,1)S(1)} pad(bf16[128,2,128]{2,1,0:T(2,128)(2,1)} %own_ref.1, bf16[]{:T(256)S(1)} %bitcast.13), padding=0_1x0_0x0_0 | pad | bytes 131586 | tf_op jit(solution)/shard_map/concatenate | solution.py:278
  4.7 1.3 %collective-permute-start.1 = (bf16[129,2,128]{2,1,0:T(2,128)(2,1)S(1)}, bf16[129,2,128]{2,1,0:T(2,128)(2,1)S(1)}, u32[]{:S(2)}, u32[]{:S(2)}) collective-permute-start(bf16[129,2,128]{2,1,0:T(2,128)(2,1)S(1)} %concatenate.3), channel_id=1, source_target_pairs={{1,0},{2,1},{3,2},{4,3},{5,4},{6,5},{7,6},{8,7},{9,8},{10,9},{11,1... | collective-permute-start | bytes 198152 | tf_op jit(solution)/shard_map/ppermute | solution.py:32
  6.0 0.0 copy-done
  6.1 1.8 %fusion = f32[16,16,256]{2,0,1:T(8,128)} fusion(bf16[16,256,128]{2,1,0:T(8,128)(2,1)S(1)} %copy-done, bf16[128,16]{0,1:T(8,128)(2,1)} %param.31), kind=kOutput, calls=%fused_computation | convolution fusion | flops 16777216 | bytes 1314816 | tf_op jit(solution)/shard_map/qkc,ch->qhk/dot_general | solution.py:338
  7.8 0.0 collective-permute-done.low_ref
  7.8 0.0 copy-start.2
  7.8 2.2 %collective-permute-done.1.upper_ref = bf16[129,2,128]{2,1,0:T(2,128)(2,1)S(1)} collective-permute-done((bf16[129,2,128]{2,1,0:T(2,128)(2,1)S(1)}, bf16[129,2,128]{2,1,0:T(2,128)(2,1)S(1)}, u32[]{:S(2)}, u32[]{:S(2)}) %collective-permute-start.1) | collective-permute-done | bytes 66080 | tf_op jit(solution)/shard_map/ppermute | solution.py:32
  10.0 0.0 copy-start.1
  10.0 0.0 copy-done.2
  10.0 0.6 %copy-done.1 = bf16[129,2,128]{2,1,0:T(2,128)(2,1)} copy-done((bf16[129,2,128]{2,1,0:T(2,128)(2,1)}, bf16[129,2,128]{2,1,0:T(2,128)(2,1)S(1)}, u32[]{:S(2)}) %copy-start.1) | copy-done | bytes 66072
  10.6 4.7 %shard_map.167 = (bf16[128,2,128]{2,1,0:T(2,128)(2,1)}, bf16[2,16,768]{2,1,0:T(8,128)(2,1)}, bf16[2,16,768]{2,1,0:T(8,128)(2,1)}) custom-call(bf16[128,2,128]{2,1,0:T(2,128)(2,1)} %own_ref.1, bf16[128,2,128]{2,1,0:T(2,128)(2,1)} %copy-done.2, bf16[129,2,128]{2,1,0:T(2,128)(2,1)} %copy-done.1, s32[4]{0:T(128)} %shift_ref.1, bf16[128,128]{1,0:T(8,128)(2,1)} %wq_ref.1, ...), custom_call_target="tpu_custom_call" | custom-call | flops 342360064 | bytes 638976 | tf_op jit(solution)/shard_map/pallas_call | solution.py:301
  15.4 26.7 %all_gather.3.every_ref = bf16[2,256,768]{2,1,0:T(8,128)(2,1)} all-gather(bf16[2,16,768]{2,1,0:T(8,128)(2,1)} %get-tuple-element.6.own_ref), channel_id=1, replica_groups=mesh['groups'=2,'row'=16] {'row'}, dimensions={1}, use_global_device_ids=true | all-gather | bytes 835584 | tf_op jit(solution)/shard_map/all_gather | solution.py:341
  42.1 5.9 %shard_map.168 = bf16[16,2,768]{2,1,0:T(2,128)(2,1)} custom-call(bf16[2,256,768]{2,1,0:T(8,128)(2,1)} %all_gather.3.every_ref, bf16[2,16,768]{2,1,0:T(8,128)(2,1)} %get-tuple-element.6.own_ref, bf16[2,16,768]{2,1,0:T(8,128)(2,1)} %get-tuple-element.7.query_ref, f32[256,256]{1,0:T(8,128)} %bitcast.11, s32[1,256]{1,0:T(1,128)} %bitcast.14, ...), custom_call_target="tpu_custom_call" | custom-call | flops 1686110208 | bytes 5865472 | tf_op jit(solution)/shard_map/pallas_call | solution.py:342
Async XLA Ops:
  0.6 5.4 %copy-start = (bf16[16,256,128]{2,1,0:T(8,128)(2,1)S(1)}, bf16[16,256,128]{2,1,0:T(8,128)(2,1)}, u32[]{:S(2)}) copy-start(bf16[16,256,128]{2,1,0:T(8,128)(2,1)} %param.20) | copy-start | bytes 3145732
  0.6 7.2 %collective-permute-start = (bf16[128,2,128]{2,1,0:T(2,128)(2,1)}, bf16[128,2,128]{2,1,0:T(2,128)(2,1)S(1)}, u32[]{:S(2)}, u32[]{:S(2)}) collective-permute-start(bf16[128,2,128]{2,1,0:T(2,128)(2,1)} %own_ref.1), channel_id=1, source_target_pairs={{0,1},{1,2},{2,3},{3,4},{4,5},{5,6},{6,7},{7,8},{8,9},{9,10},{10,1... | collective-permute-start | bytes 196616 | tf_op jit(solution)/shard_map/ppermute | solution.py:32
  4.7 5.3 %collective-permute-start.1 = (bf16[129,2,128]{2,1,0:T(2,128)(2,1)S(1)}, bf16[129,2,128]{2,1,0:T(2,128)(2,1)S(1)}, u32[]{:S(2)}, u32[]{:S(2)}) collective-permute-start(bf16[129,2,128]{2,1,0:T(2,128)(2,1)S(1)} %concatenate.3), channel_id=1, source_target_pairs={{1,0},{2,1},{3,2},{4,3},{5,4},{6,5},{7,6},{8,7},{9,8},{10,9},{11,1... | collective-permute-start | bytes 198152 | tf_op jit(solution)/shard_map/ppermute | solution.py:32
  7.8 2.2 %copy-start.2 = (bf16[128,2,128]{2,1,0:T(2,128)(2,1)}, bf16[128,2,128]{2,1,0:T(2,128)(2,1)S(1)}, u32[]{:S(2)}) copy-start(bf16[128,2,128]{2,1,0:T(2,128)(2,1)S(1)} %collective-permute-done.low_ref) | copy-start | bytes 196612
  10.0 0.6 %copy-start.1 = (bf16[129,2,128]{2,1,0:T(2,128)(2,1)}, bf16[129,2,128]{2,1,0:T(2,128)(2,1)S(1)}, u32[]{:S(2)}) copy-start(bf16[129,2,128]{2,1,0:T(2,128)(2,1)S(1)} %collective-permute-done.1.upper_ref) | copy-start | bytes 198148

commit v21 on v19

--- a/solution.py
+++ b/solution.py
@@ -111,8 +111,13 @@
         wq_ref[...],
         preferred_element_type=f32,
     ).astype(bf16)
-    k_all = jnp.dot(xn_all, wk_ref[...], preferred_element_type=f32).astype(bf16)
-    v_all = jnp.dot(xn_all, wv_ref[...], preferred_element_type=f32).astype(bf16)
+    kv_all = jnp.dot(
+        xn_all,
+        jnp.concatenate([wk_ref[...], wv_ref[...]], axis=1),
+        preferred_element_type=f32,
+    ).astype(bf16)
+    k_all = kv_all[:, 0:width]
+    v_all = kv_all[:, width:]
     mixed = []
     for s in range(samples):
         q = q_all[s * rows : (s + 1) * rows]

time: 48.3 us -> 48.3 us (level)
  no operation moved by 1% of the time
where the time goes in v21:
time: 48.3 us; the launch traced here: 48 us
  blocking collectives  26.7 us (55%)
  Pallas kernels  10.6 us (22%)
  starting transfers between devices  3.79 us (8%)
  waiting for transfers between devices  2.19 us (5%)
  matrix products  1.78 us (4%)
  local copies, waits for them, and re-layouts  1.56 us (3%)
  between operations  0.68 us (1%)
  other arithmetic  0.66 us (1%)
    all_gather x1, blocking collectives, on_device(): every = lax.all_gather(state_t, 'row', axis=1, tiled=True)  26.7 us
    pallas_call x1, Pallas kernels, on_device(): pl.pallas_call(functools.partial(token_kernel, heads=TOKEN_HEADS), out_sh...  5.89 us
    pallas_call x1, Pallas kernels, on_device(): pl.pallas_call(kernel, out_shape=(jax.ShapeDtypeStruct((atom_dev, samples...  4.72 us
    ppermute x2, starting transfers between devices, shifted(): return lax.ppermute(block, axis, route)  3.79 us
    ppermute x2, waiting for transfers between devices, shifted(): return lax.ppermute(block, axis, route)  2.19 us
    dot_general x1, matrix products, on_device(): jnp.einsum('qkc,ch->qhk', pair, w_bias, preferred_element_type=jnp.float32)  1.78 us
  transfers between devices with their start and end apart: 2, of which 1 were waited for; matrix products, arithmetic and copies ran while one was open for 7% of the time, Pallas kernels for 0%

profile of v21, /device:TPU:0, one launch (start us, length us, event | category | flops | bytes accessed | tf_op | source)
XLA Modules:
  0.0 48.0 jit_solution(13667731797601293175)
XLA Ops:
  0.6 0.0 copy-start
  0.6 2.5 %collective-permute-start = (bf16[128,2,128]{2,1,0:T(2,128)(2,1)}, bf16[128,2,128]{2,1,0:T(2,128)(2,1)S(1)}, u32[]{:S(2)}, u32[]{:S(2)}) collective-permute-start(bf16[128,2,128]{2,1,0:T(2,128)(2,1)} %own_ref.1), channel_id=1, source_target_pairs={{0,1},{1,2},{2,3},{3,4},{4,5},{5,6},{6,7},{7,8},{8,9},{9,10},{10,1... | collective-permute-start | bytes 196616 | tf_op jit(solution)/shard_map/ppermute | solution.py:32
  3.1 0.7 %convert.3 = bf16[4]{0:T(256)(128)(2,1)S(1)} convert(s32[4]{0:T(128)} %shift_ref.1) | non-fusion elementwise | flops 4 | bytes 24 | tf_op jit(solution)/shard_map/convert
  3.8 0.9 %concatenate.3 = bf16[129,2,128]{2,1,0:T(2,128)(2,1)S(1)} pad(bf16[128,2,128]{2,1,0:T(2,128)(2,1)} %own_ref.1, bf16[]{:T(256)S(1)} %bitcast.13), padding=0_1x0_0x0_0 | pad | bytes 131586 | tf_op jit(solution)/shard_map/concatenate | solution.py:284
  4.7 1.3 %collective-permute-start.1 = (bf16[129,2,128]{2,1,0:T(2,128)(2,1)S(1)}, bf16[129,2,128]{2,1,0:T(2,128)(2,1)S(1)}, u32[]{:S(2)}, u32[]{:S(2)}) collective-permute-start(bf16[129,2,128]{2,1,0:T(2,128)(2,1)S(1)} %concatenate.3), channel_id=1, source_target_pairs={{1,0},{2,1},{3,2},{4,3},{5,4},{6,5},{7,6},{8,7},{9,8},{10,9},{11,1... | collective-permute-start | bytes 198152 | tf_op jit(solution)/shard_map/ppermute | solution.py:32
  6.0 0.0 copy-done
  6.1 1.8 %fusion = f32[16,16,256]{2,0,1:T(8,128)} fusion(bf16[16,256,128]{2,1,0:T(8,128)(2,1)S(1)} %copy-done, bf16[128,16]{0,1:T(8,128)(2,1)} %param.31), kind=kOutput, calls=%fused_computation | convolution fusion | flops 16777216 | bytes 1314816 | tf_op jit(solution)/shard_map/qkc,ch->qhk/dot_general | solution.py:344
  7.8 0.0 collective-permute-done.low_ref
  7.8 0.0 copy-start.2
  7.8 2.2 %collective-permute-done.1.upper_ref = bf16[129,2,128]{2,1,0:T(2,128)(2,1)S(1)} collective-permute-done((bf16[129,2,128]{2,1,0:T(2,128)(2,1)S(1)}, bf16[129,2,128]{2,1,0:T(2,128)(2,1)S(1)}, u32[]{:S(2)}, u32[]{:S(2)}) %collective-permute-start.1) | collective-permute-done | bytes 66080 | tf_op jit(solution)/shard_map/ppermute | solution.py:32
  10.0 0.0 copy-start.1
  10.0 0.0 copy-done.2
  10.0 0.6 %copy-done.1 = bf16[129,2,128]{2,1,0:T(2,128)(2,1)} copy-done((bf16[129,2,128]{2,1,0:T(2,128)(2,1)}, bf16[129,2,128]{2,1,0:T(2,128)(2,1)S(1)}, u32[]{:S(2)}) %copy-start.1) | copy-done | bytes 66072
  10.6 4.7 %shard_map.167 = (bf16[128,2,128]{2,1,0:T(2,128)(2,1)}, bf16[2,16,768]{2,1,0:T(8,128)(2,1)}, bf16[2,16,768]{2,1,0:T(8,128)(2,1)}) custom-call(bf16[128,2,128]{2,1,0:T(2,128)(2,1)} %own_ref.1, bf16[128,2,128]{2,1,0:T(2,128)(2,1)} %copy-done.2, bf16[129,2,128]{2,1,0:T(2,128)(2,1)} %copy-done.1, s32[4]{0:T(128)} %shift_ref.1, bf16[128,128]{1,0:T(8,128)(2,1)} %wq_ref.1, ...), custom_call_target="tpu_custom_call" | custom-call | flops 342360064 | bytes 638976 | tf_op jit(solution)/shard_map/pallas_call | solution.py:307
  15.4 26.7 %all_gather.3.every_ref = bf16[2,256,768]{2,1,0:T(8,128)(2,1)} all-gather(bf16[2,16,768]{2,1,0:T(8,128)(2,1)} %get-tuple-element.6.own_ref), channel_id=1, replica_groups=mesh['groups'=2,'row'=16] {'row'}, dimensions={1}, use_global_device_ids=true | all-gather | bytes 835584 | tf_op jit(solution)/shard_map/all_gather | solution.py:347
  42.1 5.9 %shard_map.168 = bf16[16,2,768]{2,1,0:T(2,128)(2,1)} custom-call(bf16[2,256,768]{2,1,0:T(8,128)(2,1)} %all_gather.3.every_ref, bf16[2,16,768]{2,1,0:T(8,128)(2,1)} %get-tuple-element.6.own_ref, bf16[2,16,768]{2,1,0:T(8,128)(2,1)} %get-tuple-element.7.query_ref, f32[256,256]{1,0:T(8,128)} %bitcast.11, s32[1,256]{1,0:T(1,128)} %bitcast.14, ...), custom_call_target="tpu_custom_call" | custom-call | flops 1686110208 | bytes 5865472 | tf_op jit(solution)/shard_map/pallas_call | solution.py:348
Async XLA Ops:
  0.6 5.4 %copy-start = (bf16[16,256,128]{2,1,0:T(8,128)(2,1)S(1)}, bf16[16,256,128]{2,1,0:T(8,128)(2,1)}, u32[]{:S(2)}) copy-start(bf16[16,256,128]{2,1,0:T(8,128)(2,1)} %param.20) | copy-start | bytes 3145732
  0.6 7.2 %collective-permute-start = (bf16[128,2,128]{2,1,0:T(2,128)(2,1)}, bf16[128,2,128]{2,1,0:T(2,128)(2,1)S(1)}, u32[]{:S(2)}, u32[]{:S(2)}) collective-permute-start(bf16[128,2,128]{2,1,0:T(2,128)(2,1)} %own_ref.1), channel_id=1, source_target_pairs={{0,1},{1,2},{2,3},{3,4},{4,5},{5,6},{6,7},{7,8},{8,9},{9,10},{10,1... | collective-permute-start | bytes 196616 | tf_op jit(solution)/shard_map/ppermute | solution.py:32
  4.7 5.3 %collective-permute-start.1 = (bf16[129,2,128]{2,1,0:T(2,128)(2,1)S(1)}, bf16[129,2,128]{2,1,0:T(2,128)(2,1)S(1)}, u32[]{:S(2)}, u32[]{:S(2)}) collective-permute-start(bf16[129,2,128]{2,1,0:T(2,128)(2,1)S(1)} %concatenate.3), channel_id=1, source_target_pairs={{1,0},{2,1},{3,2},{4,3},{5,4},{6,5},{7,6},{8,7},{9,8},{10,9},{11,1... | collective-permute-start | bytes 198152 | tf_op jit(solution)/shard_map/ppermute | solution.py:32
  7.8 2.2 %copy-start.2 = (bf16[128,2,128]{2,1,0:T(2,128)(2,1)}, bf16[128,2,128]{2,1,0:T(2,128)(2,1)S(1)}, u32[]{:S(2)}) copy-start(bf16[128,2,128]{2,1,0:T(2,128)(2,1)S(1)} %collective-permute-done.low_ref) | copy-start | bytes 196612
  10.0 0.6 %copy-start.1 = (bf16[129,2,128]{2,1,0:T(2,128)(2,1)}, bf16[129,2,128]{2,1,0:T(2,128)(2,1)S(1)}, u32[]{:S(2)}) copy-start(bf16[129,2,128]{2,1,0:T(2,128)(2,1)S(1)} %collective-permute-done.1.upper_ref) | copy-start | bytes 198148

commit v22 on v19

--- a/solution.py
+++ b/solution.py
@@ -143,7 +143,6 @@
     top_part = hidden.astype(bf16)
     rest = hidden - top_part.astype(f32)
     mid_part = rest.astype(bf16)
-    low_part = (rest - mid_part.astype(f32)).astype(bf16)
     zero = jnp.zeros_like(onehot)
     diagonal = jnp.concatenate(
         [
@@ -155,7 +154,6 @@
     sums = (
         jnp.dot(diagonal, top_part, preferred_element_type=f32)
         + jnp.dot(diagonal, mid_part, preferred_element_type=f32)
-        + jnp.dot(diagonal, low_part, preferred_element_type=f32)
     )
     tns = []
     for s in range(samples):

time: 48.3 us -> 48.1 us (level)
  no operation moved by 1% of the time
where the time goes in v22:
time: 48.1 us; the launch traced here: 47.8 us
  blocking collectives  26.7 us (56%)
  Pallas kernels  10.4 us (22%)
  starting transfers between devices  3.79 us (8%)
  waiting for transfers between devices  2.19 us (5%)
  matrix products  1.78 us (4%)
  local copies, waits for them, and re-layouts  1.56 us (3%)
  between operations  0.68 us (1%)
  other arithmetic  0.66 us (1%)
    all_gather x1, blocking collectives, on_device(): every = lax.all_gather(state_t, 'row', axis=1, tiled=True)  26.7 us
    pallas_call x1, Pallas kernels, on_device(): pl.pallas_call(functools.partial(token_kernel, heads=TOKEN_HEADS), out_sh...  5.89 us
    pallas_call x1, Pallas kernels, on_device(): pl.pallas_call(kernel, out_shape=(jax.ShapeDtypeStruct((atom_dev, samples...  4.54 us
    ppermute x2, starting transfers between devices, shifted(): return lax.ppermute(block, axis, route)  3.79 us
    ppermute x2, waiting for transfers between devices, shifted(): return lax.ppermute(block, axis, route)  2.19 us
    dot_general x1, matrix products, on_device(): jnp.einsum('qkc,ch->qhk', pair, w_bias, preferred_element_type=jnp.float32)  1.78 us
  transfers between devices with their start and end apart: 2, of which 1 were waited for; matrix products, arithmetic and copies ran while one was open for 7% of the time, Pallas kernels for 0%

profile of v22, /device:TPU:0, one launch (start us, length us, event | category | flops | bytes accessed | tf_op | source)
XLA Modules:
  0.0 47.8 jit_solution(15041907778180822155)
XLA Ops:
  0.6 0.0 copy-start
  0.6 2.5 %collective-permute-start = (bf16[128,2,128]{2,1,0:T(2,128)(2,1)}, bf16[128,2,128]{2,1,0:T(2,128)(2,1)S(1)}, u32[]{:S(2)}, u32[]{:S(2)}) collective-permute-start(bf16[128,2,128]{2,1,0:T(2,128)(2,1)} %own_ref.1), channel_id=1, source_target_pairs={{0,1},{1,2},{2,3},{3,4},{4,5},{5,6},{6,7},{7,8},{8,9},{9,10},{10,1... | collective-permute-start | bytes 196616 | tf_op jit(solution)/shard_map/ppermute | solution.py:32
  3.1 0.7 %convert.3 = bf16[4]{0:T(256)(128)(2,1)S(1)} convert(s32[4]{0:T(128)} %shift_ref.1) | non-fusion elementwise | flops 4 | bytes 24 | tf_op jit(solution)/shard_map/convert
  3.8 0.9 %concatenate.3 = bf16[129,2,128]{2,1,0:T(2,128)(2,1)S(1)} pad(bf16[128,2,128]{2,1,0:T(2,128)(2,1)} %own_ref.1, bf16[]{:T(256)S(1)} %bitcast.13), padding=0_1x0_0x0_0 | pad | bytes 131586 | tf_op jit(solution)/shard_map/concatenate | solution.py:277
  4.7 1.3 %collective-permute-start.1 = (bf16[129,2,128]{2,1,0:T(2,128)(2,1)S(1)}, bf16[129,2,128]{2,1,0:T(2,128)(2,1)S(1)}, u32[]{:S(2)}, u32[]{:S(2)}) collective-permute-start(bf16[129,2,128]{2,1,0:T(2,128)(2,1)S(1)} %concatenate.3), channel_id=1, source_target_pairs={{1,0},{2,1},{3,2},{4,3},{5,4},{6,5},{7,6},{8,7},{9,8},{10,9},{11,1... | collective-permute-start | bytes 198152 | tf_op jit(solution)/shard_map/ppermute | solution.py:32
  6.0 0.0 copy-done
  6.1 1.8 %fusion = f32[16,16,256]{2,0,1:T(8,128)} fusion(bf16[16,256,128]{2,1,0:T(8,128)(2,1)S(1)} %copy-done, bf16[128,16]{0,1:T(8,128)(2,1)} %param.31), kind=kOutput, calls=%fused_computation | convolution fusion | flops 16777216 | bytes 1314816 | tf_op jit(solution)/shard_map/qkc,ch->qhk/dot_general | solution.py:337
  7.8 0.0 collective-permute-done.low_ref
  7.8 0.0 copy-start.2
  7.8 2.2 %collective-permute-done.1.upper_ref = bf16[129,2,128]{2,1,0:T(2,128)(2,1)S(1)} collective-permute-done((bf16[129,2,128]{2,1,0:T(2,128)(2,1)S(1)}, bf16[129,2,128]{2,1,0:T(2,128)(2,1)S(1)}, u32[]{:S(2)}, u32[]{:S(2)}) %collective-permute-start.1) | collective-permute-done | bytes 66080 | tf_op jit(solution)/shard_map/ppermute | solution.py:32
  10.0 0.0 copy-start.1
  10.0 0.0 copy-done.2
  10.0 0.6 %copy-done.1 = bf16[129,2,128]{2,1,0:T(2,128)(2,1)} copy-done((bf16[129,2,128]{2,1,0:T(2,128)(2,1)}, bf16[129,2,128]{2,1,0:T(2,128)(2,1)S(1)}, u32[]{:S(2)}) %copy-start.1) | copy-done | bytes 66072
  10.6 4.5 %shard_map.167 = (bf16[128,2,128]{2,1,0:T(2,128)(2,1)}, bf16[2,16,768]{2,1,0:T(8,128)(2,1)}, bf16[2,16,768]{2,1,0:T(8,128)(2,1)}) custom-call(bf16[128,2,128]{2,1,0:T(2,128)(2,1)} %own_ref.1, bf16[128,2,128]{2,1,0:T(2,128)(2,1)} %copy-done.2, bf16[129,2,128]{2,1,0:T(2,128)(2,1)} %copy-done.1, s32[4]{0:T(128)} %shift_ref.1, bf16[128,128]{1,0:T(8,128)(2,1)} %wq_ref.1, ...), custom_call_target="tpu_custom_call" | custom-call | flops 342360064 | bytes 638976 | tf_op jit(solution)/shard_map/pallas_call | solution.py:300
  15.2 26.7 %all_gather.3.every_ref = bf16[2,256,768]{2,1,0:T(8,128)(2,1)} all-gather(bf16[2,16,768]{2,1,0:T(8,128)(2,1)} %get-tuple-element.6.own_ref), channel_id=1, replica_groups=mesh['groups'=2,'row'=16] {'row'}, dimensions={1}, use_global_device_ids=true | all-gather | bytes 835584 | tf_op jit(solution)/shard_map/all_gather | solution.py:340
  41.9 5.9 %shard_map.168 = bf16[16,2,768]{2,1,0:T(2,128)(2,1)} custom-call(bf16[2,256,768]{2,1,0:T(8,128)(2,1)} %all_gather.3.every_ref, bf16[2,16,768]{2,1,0:T(8,128)(2,1)} %get-tuple-element.6.own_ref, bf16[2,16,768]{2,1,0:T(8,128)(2,1)} %get-tuple-element.7.query_ref, f32[256,256]{1,0:T(8,128)} %bitcast.11, s32[1,256]{1,0:T(1,128)} %bitcast.14, ...), custom_call_target="tpu_custom_call" | custom-call | flops 1686110208 | bytes 5865472 | tf_op jit(solution)/shard_map/pallas_call | solution.py:341
Async XLA Ops:
  0.6 5.4 %copy-start = (bf16[16,256,128]{2,1,0:T(8,128)(2,1)S(1)}, bf16[16,256,128]{2,1,0:T(8,128)(2,1)}, u32[]{:S(2)}) copy-start(bf16[16,256,128]{2,1,0:T(8,128)(2,1)} %param.20) | copy-start | bytes 3145732
  0.6 7.2 %collective-permute-start = (bf16[128,2,128]{2,1,0:T(2,128)(2,1)}, bf16[128,2,128]{2,1,0:T(2,128)(2,1)S(1)}, u32[]{:S(2)}, u32[]{:S(2)}) collective-permute-start(bf16[128,2,128]{2,1,0:T(2,128)(2,1)} %own_ref.1), channel_id=1, source_target_pairs={{0,1},{1,2},{2,3},{3,4},{4,5},{5,6},{6,7},{7,8},{8,9},{9,10},{10,1... | collective-permute-start | bytes 196616 | tf_op jit(solution)/shard_map/ppermute | solution.py:32
  4.7 5.3 %collective-permute-start.1 = (bf16[129,2,128]{2,1,0:T(2,128)(2,1)S(1)}, bf16[129,2,128]{2,1,0:T(2,128)(2,1)S(1)}, u32[]{:S(2)}, u32[]{:S(2)}) collective-permute-start(bf16[129,2,128]{2,1,0:T(2,128)(2,1)S(1)} %concatenate.3), channel_id=1, source_target_pairs={{1,0},{2,1},{3,2},{4,3},{5,4},{6,5},{7,6},{8,7},{9,8},{10,9},{11,1... | collective-permute-start | bytes 198152 | tf_op jit(solution)/shard_map/ppermute | solution.py:32
  7.8 2.2 %copy-start.2 = (bf16[128,2,128]{2,1,0:T(2,128)(2,1)}, bf16[128,2,128]{2,1,0:T(2,128)(2,1)S(1)}, u32[]{:S(2)}) copy-start(bf16[128,2,128]{2,1,0:T(2,128)(2,1)S(1)} %collective-permute-done.low_ref) | copy-start | bytes 196612
  10.0 0.6 %copy-start.1 = (bf16[129,2,128]{2,1,0:T(2,128)(2,1)}, bf16[129,2,128]{2,1,0:T(2,128)(2,1)S(1)}, u32[]{:S(2)}) copy-start(bf16[129,2,128]{2,1,0:T(2,128)(2,1)S(1)} %collective-permute-done.1.upper_ref) | copy-start | bytes 198148
